TPU v7x, 256 devices: a whole 4x4x8 slice. The times are simulated.
256 devices in a mesh: head: 8 (over y, core), tile: 32 (over x, z).
Axes of the slice: x: 4, y: 4, z: 8, core: 2. Of those that a mesh axis runs over, the one named last changes fastest.
Arguments:
- query: bfloat16 [32768, 3072], P(('tile', 'head')), may hold values from -8 to 8
- key: bfloat16 [32768, 3072], P(('tile', 'head')), may hold values from -8 to 8
- value: bfloat16 [32768, 3072], P(('tile', 'head')), may hold values from -6 to 6
- grad_out: bfloat16 [32768, 3072], P(('tile', 'head')), may hold values from -6 to 6
- block_mask: int32 [256, 256], replicated, may hold values from 0 to 1, as said below
- tile_order: int32 [256], replicated, may hold values from 0 to 255, as said below
Outputs:
- attn_out: bfloat16 [32768, 3072], P(('tile', 'head'))
- grad_query: bfloat16 [32768, 3072], P(('tile', 'head'))
- grad_key: bfloat16 [32768, 3072], P(('tile', 'head'))
- grad_value: bfloat16 [32768, 3072], P(('tile', 'head'))
Inputs may be any that keep to these rules, and one draw needn't show every extreme that they name: block_mask[a, b] is 1 only where clip tiles a and b differ by at most one in frame, grid row and grid column; every diagonal entry is 1; a row has at most 9 ones, and some row has exactly 9. A permutation that keeps every tile in its frame: tile_order[s] // 8 == s // 8.
All inputs are finite; a program needn't handle non-finite values.
Results may differ from a plain program's by a relative error of at most 0.022.
Values may be sent and summed in bfloat16 or wider, within the bound.
No kernel may reach another device: no remote copies, remote signals or barrier semaphores. Data moves between devices by JAX's collectives and lax.ppermute only.
A program may use at most 192 MiB of HBM per device.

v0:
```python
import jax
import jax.numpy as jnp
from jax import lax
from jax.sharding import PartitionSpec as P

HD = 128


NEG = -1e30


def with_halo(array, sides, width):
    for axis, dim in sides:
        size, length = (lax.axis_size(axis), array.shape[dim])
        up = [(i, (i + 1) % size) for i in range(size - 1)]
        down = [(j, i) for i, j in up]
        last = lax.slice_in_dim(array, length - width, length, axis=dim)
        initial = lax.slice_in_dim(array, 0, width, axis=dim)
        before = lax.ppermute(last, axis, up)
        after = lax.ppermute(initial, axis, down)
        array = jnp.concatenate([before, array, after], axis=dim)
    return array


def passed_along(value, axis, steps):
    count = lax.axis_size(axis)
    initial, last = (max(0, -steps), min(count, count - steps))
    return lax.ppermute(value, axis, [(source, source + steps) for source in range(initial, last)])


def window_lists(block_mask, tile_order, frame_idx, frames, per_frame):
    tile_count = per_frame * frames
    query_clip = lax.dynamic_slice_in_dim(tile_order, frame_idx * per_frame, per_frame)
    cand_slot = (frame_idx - 1) * per_frame + jnp.arange(3 * per_frame, dtype=jnp.int32)
    valid_slot = ((cand_slot >= 0) & (cand_slot < tile_count)).astype(jnp.int32)
    cand_clip = jnp.take(tile_order, jnp.clip(cand_slot, 0, tile_count - 1))
    forward_active = block_mask[query_clip[:, None], cand_clip[None, :]] * valid_slot[None, :]
    backward_active = block_mask[cand_clip[:, None], query_clip[None, :]] * valid_slot[:, None]
    return (forward_active, backward_active)


def compact_slots(forward_active, max_keys):
    slot_key = jnp.argsort(1 - forward_active, axis=1, stable=True)[:, :max_keys]
    live_slot = jnp.take_along_axis(forward_active, slot_key, axis=1) > 0
    return (slot_key, live_slot)


def head_pass(query_h, key_win, value_win, grad_h, slot_key, live_slot, scaling):
    key_blocks = jnp.take(key_win, slot_key, axis=0)
    value_blocks = jnp.take(value_win, slot_key, axis=0)
    scores = (
        jnp.einsum("pqd,pskd->pqsk", query_h, key_blocks, preferred_element_type=jnp.float32)
        * scaling
    )
    scores = jnp.where(live_slot[:, None, :, None], scores, NEG)
    top = jnp.max(scores, axis=(2, 3), keepdims=True)
    log_total = top + jnp.log(jnp.sum(jnp.exp(scores - top), axis=(2, 3), keepdims=True))
    attn_prob = jnp.exp(scores - log_total)
    prob_bf = attn_prob.astype(jnp.bfloat16)
    output_h = jnp.einsum(
        "pqsk,pskd->pqd", prob_bf, value_blocks, preferred_element_type=jnp.float32
    ).astype(jnp.bfloat16)
    delta_h = jnp.sum(grad_h.astype(jnp.float32) * output_h.astype(jnp.float32), axis=2)
    dprob = jnp.einsum("pqd,pskd->pqsk", grad_h, value_blocks, preferred_element_type=jnp.float32)
    dscore = (attn_prob * (dprob - delta_h[:, :, None, None])).astype(jnp.bfloat16)
    grad_q = (
        jnp.einsum("pqsk,pskd->pqd", dscore, key_blocks, preferred_element_type=jnp.float32)
        * scaling
    )
    key_terms = (
        jnp.einsum("pqsk,pqd->pskd", dscore, query_h, preferred_element_type=jnp.float32) * scaling
    )
    value_terms = jnp.einsum("pqsk,pqd->pskd", prob_bf, grad_h, preferred_element_type=jnp.float32)
    onehot = (
        slot_key[:, :, None] == jnp.arange(key_win.shape[0], dtype=jnp.int32)[None, None, :]
    ).astype(jnp.float32)
    key_win_grad = jnp.einsum("psc,pskd->ckd", onehot, key_terms, precision=lax.Precision.HIGHEST)
    value_win_grad = jnp.einsum(
        "psc,pskd->ckd", onehot, value_terms, precision=lax.Precision.HIGHEST
    )
    return (output_h, grad_q, key_win_grad, value_win_grad, log_total[:, :, 0, 0], delta_h)


def local(query, key, value, grad_out, block_mask, tile_order):
    per_frame = lax.axis_size("head")
    frames = lax.axis_size("tile")
    frame_idx = lax.axis_index("tile")
    max_keys = 3 * min(3, per_frame // 2)
    tile_rows = query.shape[0]
    q_loc, k_loc, v_loc, g_loc = (
        lax.all_to_all(query, "head", split_axis=1, concat_axis=0, tiled=True),
        lax.all_to_all(key, "head", split_axis=1, concat_axis=0, tiled=True),
        lax.all_to_all(value, "head", split_axis=1, concat_axis=0, tiled=True),
        lax.all_to_all(grad_out, "head", split_axis=1, concat_axis=0, tiled=True),
    )
    width_dev = q_loc.shape[1]
    head_count = width_dev // HD
    rows_frame = per_frame * tile_rows
    scaling = HD ** (-0.5)
    kv_rims = with_halo(jnp.stack([k_loc, v_loc]), (("tile", 1),), rows_frame)
    forward_active, backward_active = window_lists(
        block_mask, tile_order, frame_idx, frames, per_frame
    )
    slot_key, live_slot = compact_slots(forward_active, max_keys)
    out_list, dq_list, dk_list, dv_list, lse_list, delta_list = ([], [], [], [], [], [])
    for head_idx in range(head_count):
        lo_col = head_idx * HD
        query_h = q_loc[:, lo_col : lo_col + HD].reshape(per_frame, tile_rows, HD)
        grad_h = g_loc[:, lo_col : lo_col + HD].reshape(per_frame, tile_rows, HD)
        key_win = kv_rims[0, :, lo_col : lo_col + HD].reshape(3 * per_frame, tile_rows, HD)
        value_win = kv_rims[1, :, lo_col : lo_col + HD].reshape(3 * per_frame, tile_rows, HD)
        output_h, grad_q, key_wg, value_wg, lse_h, delta_h = head_pass(
            query_h, key_win, value_win, grad_h, slot_key, live_slot, scaling
        )
        out_list.append(output_h.reshape(rows_frame, HD))
        dq_list.append(grad_q.reshape(rows_frame, HD))
        dk_list.append(key_wg.reshape(3 * rows_frame, HD))
        dv_list.append(value_wg.reshape(3 * rows_frame, HD))
        lse_list.append(lse_h.reshape(rows_frame))
        delta_list.append(delta_h.reshape(rows_frame))
    out_rows = jnp.concatenate(out_list, axis=1)
    dq_rows = jnp.concatenate(dq_list, axis=1).astype(jnp.bfloat16)
    grads_win = jnp.stack([jnp.concatenate(dk_list, axis=1), jnp.concatenate(dv_list, axis=1)])
    middle = grads_win[:, rows_frame : 2 * rows_frame]
    lower_part = grads_win[:, :rows_frame]
    upper_part = grads_win[:, 2 * rows_frame :]
    from_above = passed_along(lower_part.astype(jnp.bfloat16), "tile", -1).astype(lower_part.dtype)
    from_below = passed_along(upper_part.astype(jnp.bfloat16), "tile", 1).astype(upper_part.dtype)
    summed = middle + from_above + from_below
    key_out = summed[0].astype(jnp.bfloat16)
    value_out = summed[1].astype(jnp.bfloat16)
    attn_out, grad_query, grad_key, grad_value = (
        lax.all_to_all(out_rows, "head", split_axis=0, concat_axis=1, tiled=True),
        lax.all_to_all(dq_rows, "head", split_axis=0, concat_axis=1, tiled=True),
        lax.all_to_all(key_out, "head", split_axis=0, concat_axis=1, tiled=True),
        lax.all_to_all(value_out, "head", split_axis=0, concat_axis=1, tiled=True),
    )
    return (attn_out, grad_query, grad_key, grad_value)


def solution(mesh):
    in_specs = (
        P(("tile", "head"), None),
        P(("tile", "head"), None),
        P(("tile", "head"), None),
        P(("tile", "head"), None),
        P(),
        P(),
    )
    out_specs = (
        P(("tile", "head"), None),
        P(("tile", "head"), None),
        P(("tile", "head"), None),
        P(("tile", "head"), None),
    )
    return jax.shard_map(local, mesh=mesh, in_specs=in_specs, out_specs=out_specs, check_vma=False)
```

profile of v0, /device:TPU:6, one launch (start us, length us, event | category | flops | bytes accessed | tf_op | source)
XLA Modules:
  0.0 278.0 jit_solution(669168477288080226)
XLA Ops:
  3.0 4.6 %all-to-all-start.1 = ((bf16[128,8,384]{0,2,1:T(8,128)(2,1)}), bf16[128,8,384]{0,2,1:T(8,128)(2,1)S(1)}, u32[]{:S(2)}, u32[]{:S(2)}) async-start(bf16[128,8,384]{0,2,1:T(8,128)(2,1)} %bitcast.5), calls=%async_computation.1 | async-start | bytes 1572864 | tf_op jit(solution)/shard_map/all_to_all | solution.py:93
  8.8 12.0 %all-to-all-done.1 = bf16[128,8,384]{0,2,1:T(8,128)(2,1)S(1)} async-done(((bf16[128,8,384]{0,2,1:T(8,128)(2,1)}), bf16[128,8,384]{0,2,1:T(8,128)(2,1)S(1)}, u32[]{:S(2)}, u32[]{:S(2)}) %all-to-all-start.1) | async-done | bytes 786464 | tf_op jit(solution)/shard_map/all_to_all | solution.py:93
  30.0 7.4 %all-to-all-done = bf16[128,8,384]{0,2,1:T(8,128)(2,1)S(1)} async-done(((bf16[128,8,384]{0,2,1:T(8,128)(2,1)}), bf16[128,8,384]{0,2,1:T(8,128)(2,1)S(1)}, u32[]{:S(2)}, u32[]{:S(2)}) %all-to-all-start) | async-done | bytes 786464 | tf_op jit(solution)/shard_map/all_to_all | solution.py:92
  42.6 8.0 %collective-permute-start.1 = (bf16[2,1024,384]{2,1,0:T(8,128)(2,1)}, bf16[2,1024,384]{2,1,0:T(8,128)(2,1)}, u32[]{:S(2)}, u32[]{:S(2)}) collective-permute-start(bf16[2,1024,384]{2,1,0:T(8,128)(2,1)} %pad_maximum_fusion.2), channel_id=1, source_target_pairs={{1,0},{2,1},{3,2},{4,3},{5,4},{6,5},{7,6},{8,7},{9,8},{10,9},{11,1... | collective-permute-start | bytes 4718600 | tf_op jit(solution)/shard_map/ppermute | solution.py:20
  56.3 4.9 %all-to-all-start.2 = ((bf16[128,8,384]{2,0,1:T(8,128)(2,1)}), bf16[128,8,384]{2,0,1:T(8,128)(2,1)S(1)}, u32[]{:S(2)}, u32[]{:S(2)}) async-start(bf16[128,8,384]{2,0,1:T(8,128)(2,1)} %copy.209), calls=%async_computation.2 | async-start | bytes 1572864 | tf_op jit(solution)/shard_map/all_to_all | solution.py:91
  68.2 6.1 %all-to-all-done.2 = bf16[128,8,384]{2,0,1:T(8,128)(2,1)S(1)} async-done(((bf16[128,8,384]{2,0,1:T(8,128)(2,1)}), bf16[128,8,384]{2,0,1:T(8,128)(2,1)S(1)}, u32[]{:S(2)}, u32[]{:S(2)}) %all-to-all-start.2) | async-done | bytes 786464 | tf_op jit(solution)/shard_map/all_to_all | solution.py:91
  75.2 10.0 %collective-permute-done.1 = bf16[2,1024,384]{2,1,0:T(8,128)(2,1)} collective-permute-done((bf16[2,1024,384]{2,1,0:T(8,128)(2,1)}, bf16[2,1024,384]{2,1,0:T(8,128)(2,1)}, u32[]{:S(2)}, u32[]{:S(2)}) %collective-permute-start.1) | collective-permute-done | bytes 1572896 | tf_op jit(solution)/shard_map/ppermute | solution.py:20
  85.2 6.2 %collective-permute-done = bf16[2,1024,384]{2,1,0:T(8,128)(2,1)} collective-permute-done((bf16[2,1024,384]{2,1,0:T(8,128)(2,1)}, bf16[2,1024,384]{2,1,0:T(8,128)(2,1)}, u32[]{:S(2)}, u32[]{:S(2)}) %collective-permute-start) | collective-permute-done | bytes 1572896 | tf_op jit(solution)/shard_map/ppermute | solution.py:19
  100.0 3.6 %gather_fusion.7 = bf16[72,128,128]{2,1,0:T(8,128)(2,1)} fusion(bf16[24,128,128]{2,1,0:T(8,128)(2,1)} %bitcast.235, s32[1024]{0:T(1024)S(1)} %pad_clamp_fusion), kind=kCustom, calls=%fused_computation.4.clone | custom fusion | bytes 4718880 | tf_op jit(solution)/shard_map/jit(_take)/gather | solution.py:49
  103.6 4.3 %copy.225 = bf16[8,9,128,128]{2,3,1,0:T(8,128)(2,1)} copy(bf16[8,9,128,128]{3,2,1,0:T(8,128)(2,1)} %bitcast.237) | data formatting | bytes 4718592 | tf_op jit(solution)/shard_map/jit(_take)/gather | solution.py:49
  110.3 4.3 %copy.207 = bf16[8,9,128,128]{2,3,1,0:T(8,128)(2,1)} copy(bf16[8,9,128,128]{3,2,1,0:T(8,128)(2,1)} %bitcast.238) | data formatting | bytes 4718592 | tf_op jit(solution)/shard_map/jit(_take)/gather | solution.py:49
  117.1 4.3 %copy.217 = bf16[8,9,128,128]{2,3,1,0:T(8,128)(2,1)} copy(bf16[8,9,128,128]{3,2,1,0:T(8,128)(2,1)} %bitcast.239) | data formatting | bytes 4718592 | tf_op jit(solution)/shard_map/jit(_take)/gather | solution.py:49
  155.3 5.1 %fusion.47 = f32[24,128,128]{2,0,1:T(8,128)S(1)} fusion(f32[8,9,128,128]{3,2,1,0:T(8,128)S(1)} %broadcast_multiply_fusion, s32[8,9]{1,0:T(8,128)S(1)} %copy.239), kind=kOutput, calls=%fused_computation.83 | convolution fusion | flops 339740352 | bytes 6291744 | tf_op jit(solution)/shard_map/psc,pskd->ckd/dot_general | solution.py:77
  161.6 5.3 %fusion.44 = f32[24,128,128]{2,0,1:T(8,128)S(1)} fusion(f32[8,9,128,128]{3,2,1,0:T(8,128)S(1)} %broadcast_multiply_fusion.1, s32[8,9]{1,0:T(8,128)S(1)} %copy.239), kind=kOutput, calls=%fused_computation.82 | convolution fusion | flops 339740352 | bytes 6291744 | tf_op jit(solution)/shard_map/psc,pskd->ckd/dot_general | solution.py:77
  168.0 5.2 %fusion.41 = f32[24,128,128]{2,0,1:T(8,128)S(1)} fusion(f32[8,9,128,128]{3,2,1,0:T(8,128)S(1)} %broadcast_multiply_fusion.2, s32[8,9]{1,0:T(8,128)S(1)} %copy.239), kind=kOutput, calls=%fused_computation.81 | convolution fusion | flops 339740352 | bytes 6291744 | tf_op jit(solution)/shard_map/psc,pskd->ckd/dot_general | solution.py:77
  173.5 5.4 %fusion.56 = f32[24,128,128]{2,0,1:T(8,128)S(1)} fusion(f32[8,9,128,128]{3,2,1,0:T(8,128)S(1)} %fusion.93, s32[8,9]{1,0:T(8,128)S(1)} %copy.239), kind=kOutput, calls=%fused_computation.86 | convolution fusion | flops 339740352 | bytes 6291744 | tf_op jit(solution)/shard_map/psc,pskd->ckd/dot_general | solution.py:78
  179.1 5.2 %fusion.53 = f32[24,128,128]{2,0,1:T(8,128)S(1)} fusion(f32[8,9,128,128]{3,2,1,0:T(8,128)S(1)} %fusion.96, s32[8,9]{1,0:T(8,128)S(1)} %copy.239), kind=kOutput, calls=%fused_computation.85 | convolution fusion | flops 339740352 | bytes 6291744 | tf_op jit(solution)/shard_map/psc,pskd->ckd/dot_general | solution.py:78
  184.6 5.2 %fusion.50 = f32[24,128,128]{2,0,1:T(8,128)S(1)} fusion(f32[8,9,128,128]{3,2,1,0:T(8,128)S(1)} %fusion.99, s32[8,9]{1,0:T(8,128)S(1)} %copy.239), kind=kOutput, calls=%fused_computation.84 | convolution fusion | flops 339740352 | bytes 6291744 | tf_op jit(solution)/shard_map/psc,pskd->ckd/dot_general | solution.py:78
  199.0 6.0 %collective-permute-start.2 = (bf16[2,1024,384]{2,1,0:T(8,128)(2,1)}, bf16[2,1024,384]{2,1,0:T(8,128)(2,1)}, u32[]{:S(2)}, u32[]{:S(2)}) collective-permute-start(bf16[2,1024,384]{2,1,0:T(8,128)(2,1)} %get-tuple-element.36), channel_id=1, source_target_pairs={{1,0},{2,1},{3,2},{4,3},{5,4},{6,5},{7,6},{8,7},{9,8},{10,9},{11,1... | collective-permute-start | bytes 4718600 | tf_op jit(solution)/shard_map/ppermute | solution.py:28
  206.0 4.4 %all-to-all-start.3 = ((bf16[8,128,384]{1,2,0:T(8,128)(2,1)}), bf16[8,128,384]{1,2,0:T(8,128)(2,1)S(1)}, u32[]{:S(2)}, u32[]{:S(2)}) async-start(bf16[8,128,384]{1,2,0:T(8,128)(2,1)} %pad_maximum_fusion.3), calls=%async_computation.3 | async-start | bytes 1572864 | tf_op jit(solution)/shard_map/all_to_all | solution.py:133
  217.6 5.9 %all-to-all-done.3 = bf16[8,128,384]{1,2,0:T(8,128)(2,1)S(1)} async-done(((bf16[8,128,384]{1,2,0:T(8,128)(2,1)}), bf16[8,128,384]{1,2,0:T(8,128)(2,1)S(1)}, u32[]{:S(2)}, u32[]{:S(2)}) %all-to-all-start.3) | async-done | bytes 786464 | tf_op jit(solution)/shard_map/all_to_all | solution.py:133
  227.1 9.9 %collective-permute-done.3 = bf16[2,1024,384]{2,1,0:T(8,128)(2,1)} collective-permute-done((bf16[2,1024,384]{2,1,0:T(8,128)(2,1)}, bf16[2,1024,384]{2,1,0:T(8,128)(2,1)}, u32[]{:S(2)}, u32[]{:S(2)}) %collective-permute-start.3) | collective-permute-done | bytes 1572896 | tf_op jit(solution)/shard_map/ppermute | solution.py:28
  242.5 17.1 %all_to_all.134 = bf16[8,128,384]{2,1,0:T(8,128)(2,1)S(1)} all-to-all(bf16[8,128,384]{2,1,0:T(8,128)(2,1)S(1)} %bitcast.263), channel_id=1, replica_groups=mesh['head'=8,'tile'=32] {'head'}, dimensions={0} | all-to-all | bytes 1572864 | tf_op jit(solution)/shard_map/all_to_all | solution.py:135
  267.0 9.2 %all-to-all-done.7 = bf16[8,128,384]{2,1,0:T(8,128)(2,1)S(1)} async-done(((bf16[8,128,384]{2,1,0:T(8,128)(2,1)}), bf16[8,128,384]{2,1,0:T(8,128)(2,1)S(1)}, u32[]{:S(2)}, u32[]{:S(2)}) %all-to-all-start.7) | async-done | bytes 786464 | tf_op jit(solution)/shard_map/all_to_all | solution.py:136
  (159 shorter events, 116.9 us)
Async XLA Ops:
  0.6 27.0 %copy-start = (s32[256,256]{1,0:T(8,128)S(1)}, s32[256,256]{1,0:T(8,128)}, u32[]{:S(2)}) copy-start(s32[256,256]{1,0:T(8,128)} %param.12) | copy-start | bytes 786436
  0.6 7.0 %copy-start.26 = (bf16[128,3072]{1,0:T(8,128)(2,1)S(1)}, bf16[128,3072]{1,0:T(8,128)(2,1)}, u32[]{:S(2)}) copy-start(bf16[128,3072]{1,0:T(8,128)(2,1)} %param.9) | copy-start | bytes 2359300
  3.0 23.6 %copy-start.2 = (s32[256]{0:T(256)S(1)}, s32[256]{0:T(256)}, u32[]{:S(2)}) copy-start(s32[256]{0:T(256)} %param.13) | copy-start | bytes 3076
  3.0 17.7 %all-to-all-start.1 = ((bf16[128,8,384]{0,2,1:T(8,128)(2,1)}), bf16[128,8,384]{0,2,1:T(8,128)(2,1)S(1)}, u32[]{:S(2)}, u32[]{:S(2)}) async-start(bf16[128,8,384]{0,2,1:T(8,128)(2,1)} %bitcast.5), calls=%async_computation.1 | async-start | bytes 1572864 | tf_op jit(solution)/shard_map/all_to_all | solution.py:93
  20.8 16.6 %all-to-all-start = ((bf16[128,8,384]{0,2,1:T(8,128)(2,1)}), bf16[128,8,384]{0,2,1:T(8,128)(2,1)S(1)}, u32[]{:S(2)}, u32[]{:S(2)}) async-start(bf16[128,8,384]{0,2,1:T(8,128)(2,1)} %bitcast.2), calls=%async_computation | async-start | bytes 1572864 | tf_op jit(solution)/shard_map/all_to_all | solution.py:92
  37.4 18.9 %all-to-all-start.4 = ((bf16[128,8,384]{0,2,1:T(8,128)(2,1)}), bf16[128,8,384]{0,2,1:T(8,128)(2,1)S(1)}, u32[]{:S(2)}, u32[]{:S(2)}) async-start(bf16[128,8,384]{0,2,1:T(8,128)(2,1)} %bitcast.44), calls=%async_computation.4 | async-start | bytes 1572864 | tf_op jit(solution)/shard_map/all_to_all | solution.py:94
  42.6 42.5 %collective-permute-start.1 = (bf16[2,1024,384]{2,1,0:T(8,128)(2,1)}, bf16[2,1024,384]{2,1,0:T(8,128)(2,1)}, u32[]{:S(2)}, u32[]{:S(2)}) collective-permute-start(bf16[2,1024,384]{2,1,0:T(8,128)(2,1)} %pad_maximum_fusion.2), channel_id=1, source_target_pairs={{1,0},{2,1},{3,2},{4,3},{5,4},{6,5},{7,6},{8,7},{9,8},{10,9},{11,1... | collective-permute-start | bytes 4718600 | tf_op jit(solution)/shard_map/ppermute | solution.py:20
  50.7 40.7 %collective-permute-start = (bf16[2,1024,384]{2,1,0:T(8,128)(2,1)}, bf16[2,1024,384]{2,1,0:T(8,128)(2,1)}, u32[]{:S(2)}, u32[]{:S(2)}) collective-permute-start(bf16[2,1024,384]{2,1,0:T(8,128)(2,1)} %pad_maximum_fusion.2), channel_id=1, source_target_pairs={{0,1},{1,2},{2,3},{3,4},{4,5},{5,6},{6,7},{7,8},{8,9},{9,10},{10,1... | collective-permute-start | bytes 4718600 | tf_op jit(solution)/shard_map/ppermute | solution.py:19
  56.3 18.0 %all-to-all-start.2 = ((bf16[128,8,384]{2,0,1:T(8,128)(2,1)}), bf16[128,8,384]{2,0,1:T(8,128)(2,1)S(1)}, u32[]{:S(2)}, u32[]{:S(2)}) async-start(bf16[128,8,384]{2,0,1:T(8,128)(2,1)} %copy.209), calls=%async_computation.2 | async-start | bytes 1572864 | tf_op jit(solution)/shard_map/all_to_all | solution.py:91
  65.5 8.7 %copy-start.15 = (bf16[1024,128]{1,0:T(8,128)(2,1)}, bf16[1024,128]{1,0:T(8,128)(2,1)S(1)}, u32[]{:S(2)}) copy-start(bf16[1024,128]{1,0:T(8,128)(2,1)S(1)} %get-tuple-element.46) | copy-start | bytes 786436
  65.6 25.9 %copy-start.17 = (bf16[1024,128]{1,0:T(8,128)(2,1)}, bf16[1024,128]{1,0:T(8,128)(2,1)S(1)}, u32[]{:S(2)}) copy-start(bf16[1024,128]{1,0:T(8,128)(2,1)S(1)} %get-tuple-element.48) | copy-start | bytes 786436
  65.6 25.9 %copy-start.19 = (bf16[1024,128]{1,0:T(8,128)(2,1)}, bf16[1024,128]{1,0:T(8,128)(2,1)S(1)}, u32[]{:S(2)}) copy-start(bf16[1024,128]{1,0:T(8,128)(2,1)S(1)} %get-tuple-element.47) | copy-start | bytes 786436
  141.2 13.4 %copy-start.6 = (bf16[8,128,9,128]{1,3,2,0:T(8,128)(2,1)}, bf16[8,128,9,128]{1,3,2,0:T(8,128)(2,1)S(1)}, u32[]{:S(2)}) copy-start(bf16[8,128,9,128]{1,3,2,0:T(8,128)(2,1)S(1)} %fusion.13) | copy-start | bytes 7077892
  141.2 2.5 copy-start.23
  147.7 13.1 %copy-start.7 = (bf16[8,128,9,128]{1,3,2,0:T(8,128)(2,1)}, bf16[8,128,9,128]{1,3,2,0:T(8,128)(2,1)S(1)}, u32[]{:S(2)}) copy-start(bf16[8,128,9,128]{1,3,2,0:T(8,128)(2,1)S(1)} %fusion.14) | copy-start | bytes 7077892
  154.6 12.7 %copy-start.9 = (bf16[8,128,9,128]{1,3,2,0:T(8,128)(2,1)}, bf16[8,128,9,128]{1,3,2,0:T(8,128)(2,1)S(1)}, u32[]{:S(2)}) copy-start(bf16[8,128,9,128]{1,3,2,0:T(8,128)(2,1)S(1)} %fusion.15) | copy-start | bytes 7077892
  197.1 39.9 %collective-permute-start.3 = (bf16[2,1024,384]{2,1,0:T(8,128)(2,1)}, bf16[2,1024,384]{2,1,0:T(8,128)(2,1)}, u32[]{:S(2)}, u32[]{:S(2)}) collective-permute-start(bf16[2,1024,384]{2,1,0:T(8,128)(2,1)} %get-tuple-element.37), channel_id=1, source_target_pairs={{0,1},{1,2},{2,3},{3,4},{4,5},{5,6},{6,7},{7,8},{8,9},{9,10},{10,1... | collective-permute-start | bytes 4718600 | tf_op jit(solution)/shard_map/ppermute | solution.py:28
  199.0 39.1 %collective-permute-start.2 = (bf16[2,1024,384]{2,1,0:T(8,128)(2,1)}, bf16[2,1024,384]{2,1,0:T(8,128)(2,1)}, u32[]{:S(2)}, u32[]{:S(2)}) collective-permute-start(bf16[2,1024,384]{2,1,0:T(8,128)(2,1)} %get-tuple-element.36), channel_id=1, source_target_pairs={{1,0},{2,1},{3,2},{4,3},{5,4},{6,5},{7,6},{8,7},{9,8},{10,9},{11,1... | collective-permute-start | bytes 4718600 | tf_op jit(solution)/shard_map/ppermute | solution.py:28
  206.0 17.6 %all-to-all-start.3 = ((bf16[8,128,384]{1,2,0:T(8,128)(2,1)}), bf16[8,128,384]{1,2,0:T(8,128)(2,1)S(1)}, u32[]{:S(2)}, u32[]{:S(2)}) async-start(bf16[8,128,384]{1,2,0:T(8,128)(2,1)} %pad_maximum_fusion.3), calls=%async_computation.3 | async-start | bytes 1572864 | tf_op jit(solution)/shard_map/all_to_all | solution.py:133
  210.4 2.7 copy-start.8
  210.4 3.1 %copy-start.14 = (bf16[8,9,128,128]{2,3,1,0:T(8,128)(2,1)S(1)}, bf16[8,9,128,128]{2,3,1,0:T(8,128)(2,1)}, u32[]{:S(2)}) copy-start(bf16[8,9,128,128]{2,3,1,0:T(8,128)(2,1)} %copy.217) | copy-start | bytes 7077892
  223.5 19.0 %all-to-all-start.5 = ((bf16[8,128,384]{1,2,0:T(8,128)(2,1)}), bf16[8,128,384]{1,2,0:T(8,128)(2,1)S(1)}, u32[]{:S(2)}, u32[]{:S(2)}) async-start(bf16[8,128,384]{1,2,0:T(8,128)(2,1)} %pad_maximum_fusion.4), calls=%async_computation.5 | async-start | bytes 1572864 | tf_op jit(solution)/shard_map/all_to_all | solution.py:134
  259.6 16.6 %all-to-all-start.7 = ((bf16[8,128,384]{2,1,0:T(8,128)(2,1)}), bf16[8,128,384]{2,1,0:T(8,128)(2,1)S(1)}, u32[]{:S(2)}, u32[]{:S(2)}) async-start(bf16[8,128,384]{2,1,0:T(8,128)(2,1)} %bitcast.262), calls=%async_computation.7 | async-start | bytes 1572864 | tf_op jit(solution)/shard_map/all_to_all | solution.py:136
  265.5 12.3 %copy-start.1 = (s32[256,256]{1,0:T(8,128)S(1)}, s32[256,256]{1,0:T(8,128)}, u32[]{:S(2)}) copy-start(s32[256,256]{1,0:T(8,128)} %param.12) | copy-start | bytes 786436
  (17 other events, 34.5 us)
where the time goes:
time: 283 us; the launch traced here: 278 us
  local copies, waits for them, and re-layouts  71.8 us (25%)
  waiting for transfers between devices  67.7 us (24%)
  matrix products  59.6 us (21%)
  starting transfers between devices  46 us (16%)
  blocking collectives  17.1 us (6%)
  other arithmetic  14.2 us (5%)
    gather x6, local copies, waits for them, and re-layouts, head_pass(): key_blocks = jnp.take(key_win, slot_key, axis=0)  21.5 us
    unnamed x68, local copies, waits for them, and re-layouts  21.4 us
    all_to_all x1, blocking collectives, local(): lax.all_to_all(key_out, 'head', split_axis=0, concat_axis=1, tiled=True)  17.1 us
    dot_general x3, matrix products, head_pass(): jnp.einsum('psc,pskd->ckd', onehot, value_terms, precision=lax.Precision....  15.7 us
    dot_general x3, matrix products, head_pass(): jnp.einsum('psc,pskd->ckd', onehot, key_terms, precision=lax.Precision.HI...  15.6 us
    all_to_all x1, waiting for transfers between devices, local(): lax.all_to_all(value, 'head', split_axis=1, concat_axis=0, tiled=True)  12 us
    ppermute x2, waiting for transfers between devices, passed_along(): lax.ppermute(value, axis, [(source, source + steps) for source in range(i...  11 us
    ppermute x1, waiting for transfers between devices, with_halo(): after = lax.ppermute(initial, axis, down)  9.97 us
  transfers between devices with their start and end apart: 11, of which 9 were waited for; matrix products, arithmetic and copies ran while one was open for 12% of the time, Pallas kernels for 0%

commit v1 on v0

--- a/solution.py
+++ b/solution.py
@@ -2,6 +2,8 @@
 import jax.numpy as jnp
 from jax import lax
 from jax.sharding import PartitionSpec as P
+from jax.experimental import pallas as pl
+from jax.experimental.pallas import tpu as pltpu
 
 HD = 128
 
@@ -45,40 +47,98 @@
     return (slot_key, live_slot)
 
 
-def head_pass(query_h, key_win, value_win, grad_h, slot_key, live_slot, scaling):
-    key_blocks = jnp.take(key_win, slot_key, axis=0)
-    value_blocks = jnp.take(value_win, slot_key, axis=0)
-    scores = (
-        jnp.einsum("pqd,pskd->pqsk", query_h, key_blocks, preferred_element_type=jnp.float32)
-        * scaling
-    )
-    scores = jnp.where(live_slot[:, None, :, None], scores, NEG)
-    top = jnp.max(scores, axis=(2, 3), keepdims=True)
-    log_total = top + jnp.log(jnp.sum(jnp.exp(scores - top), axis=(2, 3), keepdims=True))
-    attn_prob = jnp.exp(scores - log_total)
-    prob_bf = attn_prob.astype(jnp.bfloat16)
-    output_h = jnp.einsum(
-        "pqsk,pskd->pqd", prob_bf, value_blocks, preferred_element_type=jnp.float32
-    ).astype(jnp.bfloat16)
-    delta_h = jnp.sum(grad_h.astype(jnp.float32) * output_h.astype(jnp.float32), axis=2)
-    dprob = jnp.einsum("pqd,pskd->pqsk", grad_h, value_blocks, preferred_element_type=jnp.float32)
-    dscore = (attn_prob * (dprob - delta_h[:, :, None, None])).astype(jnp.bfloat16)
-    grad_q = (
-        jnp.einsum("pqsk,pskd->pqd", dscore, key_blocks, preferred_element_type=jnp.float32)
-        * scaling
-    )
-    key_terms = (
-        jnp.einsum("pqsk,pqd->pskd", dscore, query_h, preferred_element_type=jnp.float32) * scaling
-    )
-    value_terms = jnp.einsum("pqsk,pqd->pskd", prob_bf, grad_h, preferred_element_type=jnp.float32)
-    onehot = (
-        slot_key[:, :, None] == jnp.arange(key_win.shape[0], dtype=jnp.int32)[None, None, :]
-    ).astype(jnp.float32)
-    key_win_grad = jnp.einsum("psc,pskd->ckd", onehot, key_terms, precision=lax.Precision.HIGHEST)
-    value_win_grad = jnp.einsum(
-        "psc,pskd->ckd", onehot, value_terms, precision=lax.Precision.HIGHEST
-    )
-    return (output_h, grad_q, key_win_grad, value_win_grad, log_total[:, :, 0, 0], delta_h)
+def attn_kernel(slot_ref, live_ref, q_ref, g_ref, k_ref, v_ref, o_ref, dq_ref, dk_ref, dv_ref, s_scr, p_scr):
+    tile_rows = HD
+    query_tiles, max_keys = slot_ref.shape
+    scaling = HD ** (-0.5)
+    dk_ref[...] = jnp.zeros(dk_ref.shape, dk_ref.dtype)
+    dv_ref[...] = jnp.zeros(dv_ref.shape, dv_ref.dtype)
+    nt = (((1,), (1,)), ((), ()))
+    tn = (((0,), (0,)), ((), ()))
+
+    def key_rows(p, s):
+        return pl.ds(pl.multiple_of(slot_ref[p, s] * tile_rows, tile_rows), tile_rows)
+
+    def body(p, carry):
+        rows = pl.ds(pl.multiple_of(p * tile_rows, tile_rows), tile_rows)
+        q = q_ref[rows, :]
+        g = g_ref[rows, :]
+        top = jnp.full((tile_rows, 1), NEG, jnp.float32)
+        for s in range(max_keys):
+            k = k_ref[key_rows(p, s), :]
+            sc = lax.dot_general(q, k, nt, preferred_element_type=jnp.float32) * scaling
+            sc = jnp.where(live_ref[p, s] > 0, sc, NEG)
+            s_scr[s] = sc
+            top = jnp.maximum(top, jnp.max(sc, axis=1, keepdims=True))
+        total = jnp.zeros((tile_rows, 1), jnp.float32)
+        for s in range(max_keys):
+            total = total + jnp.sum(jnp.exp(s_scr[s] - top), axis=1, keepdims=True)
+        log_total = top + jnp.log(total)
+        out_acc = jnp.zeros((tile_rows, HD), jnp.float32)
+        for s in range(max_keys):
+            prob = jnp.exp(s_scr[s] - log_total)
+            p_scr[s] = prob
+            v = v_ref[key_rows(p, s), :]
+            out_acc = out_acc + jnp.dot(
+                prob.astype(jnp.bfloat16), v, preferred_element_type=jnp.float32
+            )
+        out = out_acc.astype(jnp.bfloat16)
+        o_ref[rows, :] = out
+        delta = jnp.sum(g.astype(jnp.float32) * out.astype(jnp.float32), axis=1, keepdims=True)
+        dq_acc = jnp.zeros((tile_rows, HD), jnp.float32)
+        for s in range(max_keys):
+            krows = key_rows(p, s)
+            k = k_ref[krows, :]
+            v = v_ref[krows, :]
+            prob = p_scr[s]
+            dprob = lax.dot_general(g, v, nt, preferred_element_type=jnp.float32)
+            dscore = (prob * (dprob - delta)).astype(jnp.bfloat16)
+            dq_acc = dq_acc + jnp.dot(dscore, k, preferred_element_type=jnp.float32)
+            dk_ref[krows, :] += (
+                lax.dot_general(dscore, q, tn, preferred_element_type=jnp.float32) * scaling
+            )
+            dv_ref[krows, :] += lax.dot_general(
+                prob.astype(jnp.bfloat16), g, tn, preferred_element_type=jnp.float32
+            )
+        dq_ref[rows, :] = (dq_acc * scaling).astype(dq_ref.dtype)
+        return carry
+
+    lax.fori_loop(0, query_tiles, body, 0)
+
+
+def attention_heads(q_loc, g_loc, k_win, v_win, slot_key, live_slot):
+    rows_frame, width = q_loc.shape
+    window_rows = k_win.shape[0]
+    query_tiles, max_keys = slot_key.shape
+    head_count = width // HD
+    row_spec = pl.BlockSpec((rows_frame, HD), lambda h, *_: (0, h))
+    win_spec = pl.BlockSpec((window_rows, HD), lambda h, *_: (0, h))
+    flops = 12 * query_tiles * max_keys * HD * HD * HD * head_count
+    grid_spec = pltpu.PrefetchScalarGridSpec(
+        num_scalar_prefetch=2,
+        grid=(head_count,),
+        in_specs=[row_spec, row_spec, win_spec, win_spec],
+        out_specs=[row_spec, row_spec, win_spec, win_spec],
+        scratch_shapes=[
+            pltpu.VMEM((max_keys, HD, HD), jnp.float32),
+            pltpu.VMEM((max_keys, HD, HD), jnp.float32),
+        ],
+    )
+    return pl.pallas_call(
+        attn_kernel,
+        grid_spec=grid_spec,
+        out_shape=[
+            jax.ShapeDtypeStruct((rows_frame, width), jnp.bfloat16),
+            jax.ShapeDtypeStruct((rows_frame, width), jnp.bfloat16),
+            jax.ShapeDtypeStruct((window_rows, width), jnp.float32),
+            jax.ShapeDtypeStruct((window_rows, width), jnp.float32),
+        ],
+        cost_estimate=pl.CostEstimate(
+            flops=flops,
+            transcendentals=2 * query_tiles * max_keys * HD * HD * head_count,
+            bytes_accessed=2 * (4 * rows_frame + 2 * window_rows) * width + 8 * window_rows * width,
+        ),
+    )(slot_key, live_slot.astype(jnp.int32), q_loc, g_loc, k_win, v_win)
 
 
 def local(query, key, value, grad_out, block_mask, tile_order):
@@ -102,25 +162,10 @@
         block_mask, tile_order, frame_idx, frames, per_frame
     )
     slot_key, live_slot = compact_slots(forward_active, max_keys)
-    out_list, dq_list, dk_list, dv_list, lse_list, delta_list = ([], [], [], [], [], [])
-    for head_idx in range(head_count):
-        lo_col = head_idx * HD
-        query_h = q_loc[:, lo_col : lo_col + HD].reshape(per_frame, tile_rows, HD)
-        grad_h = g_loc[:, lo_col : lo_col + HD].reshape(per_frame, tile_rows, HD)
-        key_win = kv_rims[0, :, lo_col : lo_col + HD].reshape(3 * per_frame, tile_rows, HD)
-        value_win = kv_rims[1, :, lo_col : lo_col + HD].reshape(3 * per_frame, tile_rows, HD)
-        output_h, grad_q, key_wg, value_wg, lse_h, delta_h = head_pass(
-            query_h, key_win, value_win, grad_h, slot_key, live_slot, scaling
-        )
-        out_list.append(output_h.reshape(rows_frame, HD))
-        dq_list.append(grad_q.reshape(rows_frame, HD))
-        dk_list.append(key_wg.reshape(3 * rows_frame, HD))
-        dv_list.append(value_wg.reshape(3 * rows_frame, HD))
-        lse_list.append(lse_h.reshape(rows_frame))
-        delta_list.append(delta_h.reshape(rows_frame))
-    out_rows = jnp.concatenate(out_list, axis=1)
-    dq_rows = jnp.concatenate(dq_list, axis=1).astype(jnp.bfloat16)
-    grads_win = jnp.stack([jnp.concatenate(dk_list, axis=1), jnp.concatenate(dv_list, axis=1)])
+    out_rows, dq_rows, key_grad_win, value_grad_win = attention_heads(
+        q_loc, g_loc, kv_rims[0], kv_rims[1], slot_key, live_slot
+    )
+    grads_win = jnp.stack([key_grad_win, value_grad_win])
     middle = grads_win[:, rows_frame : 2 * rows_frame]
     lower_part = grads_win[:, :rows_frame]
     upper_part = grads_win[:, 2 * rows_frame :]

time: 283 us -> 268 us (0.947); the launches traced: 278 us -> 267 us
  Pallas kernels: 0 us -> 75.1 us
  matrix products: 59.6 us -> 0 us
  local copies, waits for them, and re-layouts: 71.8 us -> 24 us
  blocking collectives: 17.1 us -> 46.7 us
  starting transfers between devices: 46 us -> 35.1 us
  waiting for transfers between devices: 67.7 us -> 71.5 us
    pallas_call x0 -> x1, Pallas kernels: none -> 75.1 us  [attention_heads(): pl.pallas_call(attn_kernel, grid_spec=grid_spec, out_shape=[jax.ShapeDtyp...]
    dot_general x24 -> x0, matrix products: 59.6 us -> none  [the longest x3 15.7 us: head_pass(): jnp.einsum('psc,pskd->ckd', onehot, value_terms, precision=lax.Precision....]
    all_to_all x0 -> x2, blocking collectives: none -> 31.2 us  [the longest x1 15.6 us: local(): lax.all_to_all(dq_rows, 'head', split_axis=0, concat_axis=1, tiled=True)]
    gather x9 -> x0, local copies, waits for them, and re-layouts: 30 us -> none  [the longest x6 21.5 us: head_pass(): key_blocks = jnp.take(key_win, slot_key, axis=0)]
    unnamed x68 -> x12, local copies, waits for them, and re-layouts: 21.4 us -> 0.91 us
    all_to_all x2 -> x0, waiting for transfers between devices: 12 us -> none  [the longest x1 12 us: local(): lax.all_to_all(value, 'head', split_axis=1, concat_axis=0, tiled=True)]
    all_to_all x2 -> x0, starting transfers between devices: 8.15 us -> none  [the longest x1 4.6 us: local(): lax.all_to_all(value, 'head', split_axis=1, concat_axis=0, tiled=True)]
    all_to_all x1, waiting for transfers between devices: 0.01 us -> 7.96 us  [local(): lax.all_to_all(grad_out, 'head', split_axis=1, concat_axis=0, tiled=True)]
  transfers between devices with their start and end apart: 11 -> 9, of which waited for: 9 -> 7; matrix products, arithmetic and copies ran while one was open for 12% -> 10% of each run, Pallas kernels for 0% -> 0%
where the time goes in v1:
time: 268 us; the launch traced here: 267 us
  Pallas kernels  75.1 us (28%)
  waiting for transfers between devices  71.5 us (27%)
  blocking collectives  46.7 us (17%)
  starting transfers between devices  35.1 us (13%)
  local copies, waits for them, and re-layouts  24 us (9%)
  other arithmetic  14.1 us (5%)
    pallas_call x1, Pallas kernels, attention_heads(): pl.pallas_call(attn_kernel, grid_spec=grid_spec, out_shape=[jax.ShapeDtyp...  75.1 us
    ppermute x1, waiting for transfers between devices, with_halo(): after = lax.ppermute(initial, axis, down)  17.2 us
    ppermute x2, waiting for transfers between devices, passed_along(): lax.ppermute(value, axis, [(source, source + steps) for source in range(i...  17.1 us
    all_to_all x1, blocking collectives, local(): lax.all_to_all(dq_rows, 'head', split_axis=0, concat_axis=1, tiled=True)  15.6 us
    all_to_all x1, blocking collectives, local(): lax.all_to_all(key_out, 'head', split_axis=0, concat_axis=1, tiled=True)  15.6 us
    all_to_all x1, blocking collectives, local(): lax.all_to_all(value, 'head', split_axis=1, concat_axis=0, tiled=True)  15.6 us
    all_to_all x1, waiting for transfers between devices, local(): lax.all_to_all(key, 'head', split_axis=1, concat_axis=0, tiled=True)  13 us
    all_to_all x1, waiting for transfers between devices, local(): lax.all_to_all(value_out, 'head', split_axis=0, concat_axis=1, tiled=True)  10 us
  transfers between devices with their start and end apart: 9, of which 7 were waited for; matrix products, arithmetic and copies ran while one was open for 10% of the time, Pallas kernels for 0%

profile of v1, /device:TPU:6, one launch (start us, length us, event | category | flops | bytes accessed | tf_op | source)
XLA Modules:
  0.0 267.3 jit_solution(302930744341741490)
XLA Ops:
  0.7 2.2 copy.41
  2.8 4.5 %all-to-all-start.2 = ((bf16[128,8,384]{2,0,1:T(8,128)(2,1)}), bf16[128,8,384]{2,0,1:T(8,128)(2,1)S(1)}, u32[]{:S(2)}, u32[]{:S(2)}) async-start(bf16[128,8,384]{2,0,1:T(8,128)(2,1)} %bitcast.55), calls=%async_computation.2 | async-start | bytes 1572864 | tf_op jit(solution)/shard_map/all_to_all | solution.py:152
  7.4 13.0 %all-to-all-done.2 = bf16[128,8,384]{2,0,1:T(8,128)(2,1)S(1)} async-done(((bf16[128,8,384]{2,0,1:T(8,128)(2,1)}), bf16[128,8,384]{2,0,1:T(8,128)(2,1)S(1)}, u32[]{:S(2)}, u32[]{:S(2)}) %all-to-all-start.2) | async-done | bytes 786464 | tf_op jit(solution)/shard_map/all_to_all | solution.py:152
  20.4 15.6 %all_to_all.140 = bf16[128,8,384]{2,0,1:T(8,128)(2,1)S(1)} all-to-all(bf16[128,8,384]{2,0,1:T(8,128)(2,1)S(1)} %bitcast.71), channel_id=1, replica_groups=mesh['head'=8,'tile'=32] {'head'}, dimensions={1} | all-to-all | bytes 1572864 | tf_op jit(solution)/shard_map/all_to_all | solution.py:153
  37.4 8.0 %collective-permute-start.1 = (bf16[2,1024,384]{2,1,0:T(8,128)(2,1)}, bf16[2,1024,384]{2,1,0:T(8,128)(2,1)S(1)}, u32[]{:S(2)}, u32[]{:S(2)}) collective-permute-start(bf16[2,1024,384]{2,1,0:T(8,128)(2,1)} %pad_maximum_fusion.2), channel_id=1, source_target_pairs={{1,0},{2,1},{3,2},{4,3},{5,4},{6,5},{7,6},{8,7},{9,8},{10,9},{11,1... | collective-permute-start | bytes 4718600 | tf_op jit(solution)/shard_map/ppermute | solution.py:22
  49.4 4.2 %all-to-all-start = ((bf16[128,8,384]{2,0,1:T(8,128)(2,1)}), bf16[128,8,384]{2,0,1:T(8,128)(2,1)}, u32[]{:S(2)}, u32[]{:S(2)}) async-start(bf16[128,8,384]{2,0,1:T(8,128)(2,1)} %bitcast.57), calls=%async_computation | async-start | bytes 1572864 | tf_op jit(solution)/shard_map/all_to_all | solution.py:151
  59.1 2.1 copy.42
  61.8 17.2 %collective-permute-done.1 = bf16[2,1024,384]{2,1,0:T(8,128)(2,1)S(1)} collective-permute-done((bf16[2,1024,384]{2,1,0:T(8,128)(2,1)}, bf16[2,1024,384]{2,1,0:T(8,128)(2,1)S(1)}, u32[]{:S(2)}, u32[]{:S(2)}) %collective-permute-start.1) | collective-permute-done | bytes 1572896 | tf_op jit(solution)/shard_map/ppermute | solution.py:22
  79.0 6.2 %collective-permute-done = bf16[2,1024,384]{2,1,0:T(8,128)(2,1)} collective-permute-done((bf16[2,1024,384]{2,1,0:T(8,128)(2,1)}, bf16[2,1024,384]{2,1,0:T(8,128)(2,1)}, u32[]{:S(2)}, u32[]{:S(2)}) %collective-permute-start) | collective-permute-done | bytes 1572896 | tf_op jit(solution)/shard_map/ppermute | solution.py:21
  85.2 3.9 %pad_maximum_fusion.1 = bf16[2,3072,384]{2,1,0:T(8,128)(2,1)} fusion(bf16[2,1024,384]{2,1,0:T(8,128)(2,1)S(1)} %collective-permute-done.1, bf16[1,1024,384]{2,1,0:T(8,128)(2,1)S(1)} %bitcast.66, bf16[1,1024,384]{2,1,0:T(8,128)(2,1)S(1)} %bitcast.64, bf16[2,1024,384]{2,1,0:T(8,128)(2,1)} %collective-permute-done), kind=kLoop, calls=%fused_computation.7 | loop fusion | flops 18874368 | bytes 9437184 | tf_op jit(solution)/shard_map/concatenate | solution.py:23
  89.1 3.5 %all-to-all-start.1 = ((bf16[128,8,384]{2,0,1:T(8,128)(2,1)}), bf16[128,8,384]{2,0,1:T(8,128)(2,1)S(1)}, u32[]{:S(2)}, u32[]{:S(2)}) async-start(bf16[128,8,384]{2,0,1:T(8,128)(2,1)} %bitcast.56), calls=%async_computation.1 | async-start | bytes 1572864 | tf_op jit(solution)/shard_map/all_to_all | solution.py:154
  92.6 5.1 %slice_bitcast_fusion = (bf16[3072,384]{1,0:T(8,128)(2,1)}, bf16[3072,384]{1,0:T(8,128)(2,1)}) fusion(bf16[2,3072,384]{2,1,0:T(8,128)(2,1)} %pad_maximum_fusion.1), kind=kLoop, calls=%fused_computation.12 | loop fusion | bytes 9437184 | tf_op jit(solution)/shard_map/squeeze | solution.py:166
  97.7 8.0 %all-to-all-done.1 = bf16[128,8,384]{2,0,1:T(8,128)(2,1)S(1)} async-done(((bf16[128,8,384]{2,0,1:T(8,128)(2,1)}), bf16[128,8,384]{2,0,1:T(8,128)(2,1)S(1)}, u32[]{:S(2)}, u32[]{:S(2)}) %all-to-all-start.1) | async-done | bytes 786464 | tf_op jit(solution)/shard_map/all_to_all | solution.py:154
  106.6 75.1 %shard_map.93 = (bf16[1024,384]{1,0:T(8,128)(2,1)}, bf16[1024,384]{1,0:T(8,128)(2,1)}, f32[3072,384]{1,0:T(8,128)}, f32[3072,384]{1,0:T(8,128)}) custom-call(s32[8,9]{1,0:T(8,128)} %bitcast.85, s32[8,9]{1,0:T(8,128)} %fusion.5.live_ref, bf16[1024,384]{1,0:T(8,128)(2,1)} %bitcast.3.q_ref, bf16[1024,384]{1,0:T(8,128)(2,1)} %bitcast.80, ...), custom_call_target="tpu_custom_call" | custom-call | flops 5435817984 | bytes 17301504 | tf_op jit(solution)/shard_map/pallas_call | solution.py:127
  181.7 4.4 %fusion = bf16[2,3072,384]{2,1,0:T(8,128)(2,1)S(1)} fusion(f32[1,3072,384]{2,1,0:T(8,128)} %bitcast.61, f32[1,3072,384]{2,1,0:T(8,128)} %bitcast.59), kind=kLoop, calls=%fused_computation.6 | loop fusion | flops 2359296 | bytes 14155776 | tf_op jit(solution)/shard_map/convert.3
  190.1 3.9 %collective-permute-start.3 = (bf16[2,1024,384]{2,1,0:T(8,128)(2,1)}, bf16[2,1024,384]{2,1,0:T(8,128)(2,1)}, u32[]{:S(2)}, u32[]{:S(2)}) collective-permute-start(bf16[2,1024,384]{2,1,0:T(8,128)(2,1)} %get-tuple-element.17), channel_id=1, source_target_pairs={{0,1},{1,2},{2,3},{3,4},{4,5},{5,6},{6,7},{7,8},{8,9},{9,10},{10,1... | collective-permute-start | bytes 4718600 | tf_op jit(solution)/shard_map/ppermute | solution.py:30
  194.0 15.6 %all_to_all.141 = bf16[8,128,384]{2,1,0:T(8,128)(2,1)S(1)} all-to-all(bf16[8,128,384]{2,1,0:T(8,128)(2,1)S(1)} %bitcast.79), channel_id=1, replica_groups=mesh['head'=8,'tile'=32] {'head'}, dimensions={0} | all-to-all | bytes 1572864 | tf_op jit(solution)/shard_map/all_to_all | solution.py:179
  209.6 3.5 %all-to-all-start.4 = ((bf16[8,128,384]{2,1,0:T(8,128)(2,1)}), bf16[8,128,384]{2,1,0:T(8,128)(2,1)S(1)}, u32[]{:S(2)}, u32[]{:S(2)}) async-start(bf16[8,128,384]{2,1,0:T(8,128)(2,1)} %bitcast.78), calls=%async_computation.4 | async-start | bytes 1572864 | tf_op jit(solution)/shard_map/all_to_all | solution.py:178
  213.2 12.9 %collective-permute-done.2 = bf16[2,1024,384]{2,1,0:T(8,128)(2,1)S(1)} collective-permute-done((bf16[2,1024,384]{2,1,0:T(8,128)(2,1)}, bf16[2,1024,384]{2,1,0:T(8,128)(2,1)S(1)}, u32[]{:S(2)}, u32[]{:S(2)}) %collective-permute-start.2) | collective-permute-done | bytes 1572896 | tf_op jit(solution)/shard_map/ppermute | solution.py:30
  226.1 4.1 %collective-permute-done.3 = bf16[2,1024,384]{2,1,0:T(8,128)(2,1)} collective-permute-done((bf16[2,1024,384]{2,1,0:T(8,128)(2,1)}, bf16[2,1024,384]{2,1,0:T(8,128)(2,1)}, u32[]{:S(2)}, u32[]{:S(2)}) %collective-permute-start.3) | collective-permute-done | bytes 1572896 | tf_op jit(solution)/shard_map/ppermute | solution.py:30
  230.3 2.8 %fusion.4 = bf16[2,1024,384]{2,1,0:T(8,128)(2,1)S(1)} fusion(f32[1,3072,384]{2,1,0:T(8,128)} %bitcast.60, f32[1,3072,384]{2,1,0:T(8,128)} %bitcast.62, bf16[2,1024,384]{2,1,0:T(8,128)(2,1)} %collective-permute-done.3, bf16[2,1024,384]{2,1,0:T(8,128)(2,1)S(1)} %collective-permute-done.2), kind=kLoop, calls=%fused_computation.11 | loop fusion | flops 4718592 | bytes 14155776 | tf_op jit(solution)/shard_map/convert.1
  234.1 15.6 %all_to_all.142 = bf16[8,128,384]{2,1,0:T(8,128)(2,1)S(1)} all-to-all(bf16[8,128,384]{2,1,0:T(8,128)(2,1)S(1)} %bitcast.73), channel_id=1, replica_groups=mesh['head'=8,'tile'=32] {'head'}, dimensions={0} | all-to-all | bytes 1572864 | tf_op jit(solution)/shard_map/all_to_all | solution.py:180
  249.7 3.5 %all-to-all-start.7 = ((bf16[8,128,384]{2,1,0:T(8,128)(2,1)}), bf16[8,128,384]{2,1,0:T(8,128)(2,1)S(1)}, u32[]{:S(2)}, u32[]{:S(2)}) async-start(bf16[8,128,384]{2,1,0:T(8,128)(2,1)} %bitcast.72), calls=%async_computation.7 | async-start | bytes 1572864 | tf_op jit(solution)/shard_map/all_to_all | solution.py:181
  256.3 10.0 %all-to-all-done.7 = bf16[8,128,384]{2,1,0:T(8,128)(2,1)S(1)} async-done(((bf16[8,128,384]{2,1,0:T(8,128)(2,1)}), bf16[8,128,384]{2,1,0:T(8,128)(2,1)S(1)}, u32[]{:S(2)}, u32[]{:S(2)}) %all-to-all-start.7) | async-done | bytes 786464 | tf_op jit(solution)/shard_map/all_to_all | solution.py:181
  (45 shorter events, 21.4 us)
Async XLA Ops:
  0.6 54.0 %copy-start = (s32[256,256]{1,0:T(8,128)S(1)}, s32[256,256]{1,0:T(8,128)}, u32[]{:S(2)}) copy-start(s32[256,256]{1,0:T(8,128)} %param.10) | copy-start | bytes 786436
  0.6 6.7 %copy-start.2 = (bf16[128,3072]{1,0:T(8,128)(2,1)S(1)}, bf16[128,3072]{1,0:T(8,128)(2,1)}, u32[]{:S(2)}) copy-start(bf16[128,3072]{1,0:T(8,128)(2,1)} %param.8) | copy-start | bytes 2359300
  2.8 17.6 %all-to-all-start.2 = ((bf16[128,8,384]{2,0,1:T(8,128)(2,1)}), bf16[128,8,384]{2,0,1:T(8,128)(2,1)S(1)}, u32[]{:S(2)}, u32[]{:S(2)}) async-start(bf16[128,8,384]{2,0,1:T(8,128)(2,1)} %bitcast.55), calls=%async_computation.2 | async-start | bytes 1572864 | tf_op jit(solution)/shard_map/all_to_all | solution.py:152
  36.0 17.7 %copy-start.1 = (s32[256]{0:T(256)S(1)}, s32[256]{0:T(256)}, u32[]{:S(2)}) copy-start(s32[256]{0:T(256)} %param.11) | copy-start | bytes 3076
  37.4 41.6 %collective-permute-start.1 = (bf16[2,1024,384]{2,1,0:T(8,128)(2,1)}, bf16[2,1024,384]{2,1,0:T(8,128)(2,1)S(1)}, u32[]{:S(2)}, u32[]{:S(2)}) collective-permute-start(bf16[2,1024,384]{2,1,0:T(8,128)(2,1)} %pad_maximum_fusion.2), channel_id=1, source_target_pairs={{1,0},{2,1},{3,2},{4,3},{5,4},{6,5},{7,6},{8,7},{9,8},{10,9},{11,1... | collective-permute-start | bytes 4718600 | tf_op jit(solution)/shard_map/ppermute | solution.py:22
  45.4 39.8 %collective-permute-start = (bf16[2,1024,384]{2,1,0:T(8,128)(2,1)}, bf16[2,1024,384]{2,1,0:T(8,128)(2,1)}, u32[]{:S(2)}, u32[]{:S(2)}) collective-permute-start(bf16[2,1024,384]{2,1,0:T(8,128)(2,1)} %pad_maximum_fusion.2), channel_id=1, source_target_pairs={{0,1},{1,2},{2,3},{3,4},{4,5},{5,6},{6,7},{7,8},{8,9},{9,10},{10,1... | collective-permute-start | bytes 4718600 | tf_op jit(solution)/shard_map/ppermute | solution.py:21
  49.4 39.7 %all-to-all-start = ((bf16[128,8,384]{2,0,1:T(8,128)(2,1)}), bf16[128,8,384]{2,0,1:T(8,128)(2,1)}, u32[]{:S(2)}, u32[]{:S(2)}) async-start(bf16[128,8,384]{2,0,1:T(8,128)(2,1)} %bitcast.57), calls=%async_computation | async-start | bytes 1572864 | tf_op jit(solution)/shard_map/all_to_all | solution.py:151
  57.6 31.5 %copy-start.5 = (s32[8,24]{1,0:T(8,128)}, s32[8,24]{1,0:T(8,128)S(1)}, u32[]{:S(2)}) copy-start(s32[8,24]{1,0:T(8,128)S(1)} %copy.19) | copy-start | bytes 2308
  89.1 16.6 %all-to-all-start.1 = ((bf16[128,8,384]{2,0,1:T(8,128)(2,1)}), bf16[128,8,384]{2,0,1:T(8,128)(2,1)S(1)}, u32[]{:S(2)}, u32[]{:S(2)}) async-start(bf16[128,8,384]{2,0,1:T(8,128)(2,1)} %bitcast.56), calls=%async_computation.1 | async-start | bytes 1572864 | tf_op jit(solution)/shard_map/all_to_all | solution.py:154
  105.7 0.9 copy-start.4
  186.1 7.9 %copy-start.3 = (bf16[1024,384]{1,0:T(8,128)(2,1)S(1)}, bf16[1024,384]{1,0:T(8,128)(2,1)}, u32[]{:S(2)}) copy-start(bf16[1024,384]{1,0:T(8,128)(2,1)} %get-tuple-element.11) | copy-start | bytes 2359300
  188.2 37.9 %collective-permute-start.2 = (bf16[2,1024,384]{2,1,0:T(8,128)(2,1)}, bf16[2,1024,384]{2,1,0:T(8,128)(2,1)S(1)}, u32[]{:S(2)}, u32[]{:S(2)}) collective-permute-start(bf16[2,1024,384]{2,1,0:T(8,128)(2,1)} %get-tuple-element.16), channel_id=1, source_target_pairs={{1,0},{2,1},{3,2},{4,3},{5,4},{6,5},{7,6},{8,7},{9,8},{10,9},{11,1... | collective-permute-start | bytes 4718600 | tf_op jit(solution)/shard_map/ppermute | solution.py:30
  190.1 40.2 %collective-permute-start.3 = (bf16[2,1024,384]{2,1,0:T(8,128)(2,1)}, bf16[2,1024,384]{2,1,0:T(8,128)(2,1)}, u32[]{:S(2)}, u32[]{:S(2)}) collective-permute-start(bf16[2,1024,384]{2,1,0:T(8,128)(2,1)} %get-tuple-element.17), channel_id=1, source_target_pairs={{0,1},{1,2},{2,3},{3,4},{4,5},{5,6},{6,7},{7,8},{8,9},{9,10},{10,1... | collective-permute-start | bytes 4718600 | tf_op jit(solution)/shard_map/ppermute | solution.py:30
  209.6 24.5 %all-to-all-start.4 = ((bf16[8,128,384]{2,1,0:T(8,128)(2,1)}), bf16[8,128,384]{2,1,0:T(8,128)(2,1)S(1)}, u32[]{:S(2)}, u32[]{:S(2)}) async-start(bf16[8,128,384]{2,1,0:T(8,128)(2,1)} %bitcast.78), calls=%async_computation.4 | async-start | bytes 1572864 | tf_op jit(solution)/shard_map/all_to_all | solution.py:178
  249.7 16.6 %all-to-all-start.7 = ((bf16[8,128,384]{2,1,0:T(8,128)(2,1)}), bf16[8,128,384]{2,1,0:T(8,128)(2,1)S(1)}, u32[]{:S(2)}, u32[]{:S(2)}) async-start(bf16[8,128,384]{2,1,0:T(8,128)(2,1)} %bitcast.72), calls=%async_computation.7 | async-start | bytes 1572864 | tf_op jit(solution)/shard_map/all_to_all | solution.py:181

commit v2 on v1

--- a/solution.py
+++ b/solution.py
@@ -47,7 +47,7 @@
     return (slot_key, live_slot)
 
 
-def attn_kernel(slot_ref, live_ref, q_ref, g_ref, k_ref, v_ref, o_ref, dq_ref, dk_ref, dv_ref, s_scr, p_scr):
+def attn_kernel(slot_ref, live_ref, q_ref, g_ref, k_ref, v_ref, o_ref, dq_ref, dk_ref, dv_ref, kg_scr, vg_scr):
     tile_rows = HD
     query_tiles, max_keys = slot_ref.shape
     scaling = HD ** (-0.5)
@@ -55,52 +55,42 @@
     dv_ref[...] = jnp.zeros(dv_ref.shape, dv_ref.dtype)
     nt = (((1,), (1,)), ((), ()))
     tn = (((0,), (0,)), ((), ()))
+    lane_slot = lax.broadcasted_iota(jnp.int32, (1, max_keys * tile_rows), 1) // tile_rows
 
     def key_rows(p, s):
         return pl.ds(pl.multiple_of(slot_ref[p, s] * tile_rows, tile_rows), tile_rows)
 
     def body(p, carry):
         rows = pl.ds(pl.multiple_of(p * tile_rows, tile_rows), tile_rows)
+        live_lane = jnp.zeros((1, max_keys * tile_rows), jnp.int32)
+        for s in range(max_keys):
+            krows = key_rows(p, s)
+            kg_scr[s * tile_rows : (s + 1) * tile_rows, :] = k_ref[krows, :]
+            vg_scr[s * tile_rows : (s + 1) * tile_rows, :] = v_ref[krows, :]
+            live_lane = jnp.where(lane_slot == s, live_ref[p, s], live_lane)
         q = q_ref[rows, :]
         g = g_ref[rows, :]
-        top = jnp.full((tile_rows, 1), NEG, jnp.float32)
-        for s in range(max_keys):
-            k = k_ref[key_rows(p, s), :]
-            sc = lax.dot_general(q, k, nt, preferred_element_type=jnp.float32) * scaling
-            sc = jnp.where(live_ref[p, s] > 0, sc, NEG)
-            s_scr[s] = sc
-            top = jnp.maximum(top, jnp.max(sc, axis=1, keepdims=True))
-        total = jnp.zeros((tile_rows, 1), jnp.float32)
-        for s in range(max_keys):
-            total = total + jnp.sum(jnp.exp(s_scr[s] - top), axis=1, keepdims=True)
-        log_total = top + jnp.log(total)
-        out_acc = jnp.zeros((tile_rows, HD), jnp.float32)
-        for s in range(max_keys):
-            prob = jnp.exp(s_scr[s] - log_total)
-            p_scr[s] = prob
-            v = v_ref[key_rows(p, s), :]
-            out_acc = out_acc + jnp.dot(
-                prob.astype(jnp.bfloat16), v, preferred_element_type=jnp.float32
-            )
-        out = out_acc.astype(jnp.bfloat16)
+        kg = kg_scr[...]
+        vg = vg_scr[...]
+        sc = lax.dot_general(q, kg, nt, preferred_element_type=jnp.float32) * scaling
+        sc = jnp.where(live_lane > 0, sc, NEG)
+        top = jnp.max(sc, axis=1, keepdims=True)
+        log_total = top + jnp.log(jnp.sum(jnp.exp(sc - top), axis=1, keepdims=True))
+        prob = jnp.exp(sc - log_total)
+        prob_bf = prob.astype(jnp.bfloat16)
+        out = jnp.dot(prob_bf, vg, preferred_element_type=jnp.float32).astype(jnp.bfloat16)
         o_ref[rows, :] = out
         delta = jnp.sum(g.astype(jnp.float32) * out.astype(jnp.float32), axis=1, keepdims=True)
-        dq_acc = jnp.zeros((tile_rows, HD), jnp.float32)
+        dprob = lax.dot_general(g, vg, nt, preferred_element_type=jnp.float32)
+        dscore = (prob * (dprob - delta)).astype(jnp.bfloat16)
+        dq = jnp.dot(dscore, kg, preferred_element_type=jnp.float32) * scaling
+        dq_ref[rows, :] = dq.astype(dq_ref.dtype)
+        dk_g = lax.dot_general(dscore, q, tn, preferred_element_type=jnp.float32) * scaling
+        dv_g = lax.dot_general(prob_bf, g, tn, preferred_element_type=jnp.float32)
         for s in range(max_keys):
             krows = key_rows(p, s)
-            k = k_ref[krows, :]
-            v = v_ref[krows, :]
-            prob = p_scr[s]
-            dprob = lax.dot_general(g, v, nt, preferred_element_type=jnp.float32)
-            dscore = (prob * (dprob - delta)).astype(jnp.bfloat16)
-            dq_acc = dq_acc + jnp.dot(dscore, k, preferred_element_type=jnp.float32)
-            dk_ref[krows, :] += (
-                lax.dot_general(dscore, q, tn, preferred_element_type=jnp.float32) * scaling
-            )
-            dv_ref[krows, :] += lax.dot_general(
-                prob.astype(jnp.bfloat16), g, tn, preferred_element_type=jnp.float32
-            )
-        dq_ref[rows, :] = (dq_acc * scaling).astype(dq_ref.dtype)
+            dk_ref[krows, :] += dk_g[s * tile_rows : (s + 1) * tile_rows, :]
+            dv_ref[krows, :] += dv_g[s * tile_rows : (s + 1) * tile_rows, :]
         return carry
 
     lax.fori_loop(0, query_tiles, body, 0)
@@ -120,8 +110,8 @@
         in_specs=[row_spec, row_spec, win_spec, win_spec],
         out_specs=[row_spec, row_spec, win_spec, win_spec],
         scratch_shapes=[
-            pltpu.VMEM((max_keys, HD, HD), jnp.float32),
-            pltpu.VMEM((max_keys, HD, HD), jnp.float32),
+            pltpu.VMEM((max_keys * HD, HD), jnp.bfloat16),
+            pltpu.VMEM((max_keys * HD, HD), jnp.bfloat16),
         ],
     )
     return pl.pallas_call(

time: 268 us -> 226 us (0.84)
  Pallas kernels: 75.1 us -> 32.6 us
    pallas_call x1, Pallas kernels: 75.1 us -> 32.6 us  [attention_heads(): pl.pallas_call(attn_kernel, grid_spec=grid_spec, out_shape=[jax.ShapeDtyp...]
  transfers between devices with their start and end apart: 9 -> 9, of which waited for: 7 -> 7; matrix products, arithmetic and copies ran while one was open for 10% -> 12% of each run, Pallas kernels for 0% -> 0%
where the time goes in v2:
time: 226 us; the launch traced here: 225 us
  waiting for transfers between devices  71.5 us (32%)
  blocking collectives  46.7 us (21%)
  starting transfers between devices  35.1 us (16%)
  Pallas kernels  32.6 us (14%)
  local copies, waits for them, and re-layouts  24 us (11%)
  other arithmetic  14.1 us (6%)
    pallas_call x1, Pallas kernels, attention_heads(): pl.pallas_call(attn_kernel, grid_spec=grid_spec, out_shape=[jax.ShapeDtyp...  32.6 us
    ppermute x1, waiting for transfers between devices, with_halo(): after = lax.ppermute(initial, axis, down)  17.2 us
    ppermute x2, waiting for transfers between devices, passed_along(): lax.ppermute(value, axis, [(source, source + steps) for source in range(i...  17.1 us
    all_to_all x1, blocking collectives, local(): lax.all_to_all(dq_rows, 'head', split_axis=0, concat_axis=1, tiled=True)  15.6 us
    all_to_all x1, blocking collectives, local(): lax.all_to_all(key_out, 'head', split_axis=0, concat_axis=1, tiled=True)  15.6 us
    all_to_all x1, blocking collectives, local(): lax.all_to_all(value, 'head', split_axis=1, concat_axis=0, tiled=True)  15.6 us
    all_to_all x1, waiting for transfers between devices, local(): lax.all_to_all(key, 'head', split_axis=1, concat_axis=0, tiled=True)  13 us
    all_to_all x1, waiting for transfers between devices, local(): lax.all_to_all(value_out, 'head', split_axis=0, concat_axis=1, tiled=True)  10 us
  transfers between devices with their start and end apart: 9, of which 7 were waited for; matrix products, arithmetic and copies ran while one was open for 12% of the time, Pallas kernels for 0%

profile of v2, /device:TPU:6, one launch (start us, length us, event | category | flops | bytes accessed | tf_op | source)
XLA Modules:
  0.0 224.8 jit_solution(14250488718737531801)
XLA Ops:
  0.7 2.2 copy.41
  2.8 4.5 %all-to-all-start.2 = ((bf16[128,8,384]{2,0,1:T(8,128)(2,1)}), bf16[128,8,384]{2,0,1:T(8,128)(2,1)S(1)}, u32[]{:S(2)}, u32[]{:S(2)}) async-start(bf16[128,8,384]{2,0,1:T(8,128)(2,1)} %bitcast.55), calls=%async_computation.2 | async-start | bytes 1572864 | tf_op jit(solution)/shard_map/all_to_all | solution.py:142
  7.4 13.0 %all-to-all-done.2 = bf16[128,8,384]{2,0,1:T(8,128)(2,1)S(1)} async-done(((bf16[128,8,384]{2,0,1:T(8,128)(2,1)}), bf16[128,8,384]{2,0,1:T(8,128)(2,1)S(1)}, u32[]{:S(2)}, u32[]{:S(2)}) %all-to-all-start.2) | async-done | bytes 786464 | tf_op jit(solution)/shard_map/all_to_all | solution.py:142
  20.4 15.6 %all_to_all.140 = bf16[128,8,384]{2,0,1:T(8,128)(2,1)S(1)} all-to-all(bf16[128,8,384]{2,0,1:T(8,128)(2,1)S(1)} %bitcast.71), channel_id=1, replica_groups=mesh['head'=8,'tile'=32] {'head'}, dimensions={1} | all-to-all | bytes 1572864 | tf_op jit(solution)/shard_map/all_to_all | solution.py:143
  37.4 8.0 %collective-permute-start.1 = (bf16[2,1024,384]{2,1,0:T(8,128)(2,1)}, bf16[2,1024,384]{2,1,0:T(8,128)(2,1)S(1)}, u32[]{:S(2)}, u32[]{:S(2)}) collective-permute-start(bf16[2,1024,384]{2,1,0:T(8,128)(2,1)} %pad_maximum_fusion.2), channel_id=1, source_target_pairs={{1,0},{2,1},{3,2},{4,3},{5,4},{6,5},{7,6},{8,7},{9,8},{10,9},{11,1... | collective-permute-start | bytes 4718600 | tf_op jit(solution)/shard_map/ppermute | solution.py:22
  49.4 4.2 %all-to-all-start = ((bf16[128,8,384]{2,0,1:T(8,128)(2,1)}), bf16[128,8,384]{2,0,1:T(8,128)(2,1)}, u32[]{:S(2)}, u32[]{:S(2)}) async-start(bf16[128,8,384]{2,0,1:T(8,128)(2,1)} %bitcast.57), calls=%async_computation | async-start | bytes 1572864 | tf_op jit(solution)/shard_map/all_to_all | solution.py:141
  59.1 2.1 copy.42
  61.8 17.2 %collective-permute-done.1 = bf16[2,1024,384]{2,1,0:T(8,128)(2,1)S(1)} collective-permute-done((bf16[2,1024,384]{2,1,0:T(8,128)(2,1)}, bf16[2,1024,384]{2,1,0:T(8,128)(2,1)S(1)}, u32[]{:S(2)}, u32[]{:S(2)}) %collective-permute-start.1) | collective-permute-done | bytes 1572896 | tf_op jit(solution)/shard_map/ppermute | solution.py:22
  79.0 6.2 %collective-permute-done = bf16[2,1024,384]{2,1,0:T(8,128)(2,1)} collective-permute-done((bf16[2,1024,384]{2,1,0:T(8,128)(2,1)}, bf16[2,1024,384]{2,1,0:T(8,128)(2,1)}, u32[]{:S(2)}, u32[]{:S(2)}) %collective-permute-start) | collective-permute-done | bytes 1572896 | tf_op jit(solution)/shard_map/ppermute | solution.py:21
  85.2 3.9 %pad_maximum_fusion.1 = bf16[2,3072,384]{2,1,0:T(8,128)(2,1)} fusion(bf16[2,1024,384]{2,1,0:T(8,128)(2,1)S(1)} %collective-permute-done.1, bf16[1,1024,384]{2,1,0:T(8,128)(2,1)S(1)} %bitcast.66, bf16[1,1024,384]{2,1,0:T(8,128)(2,1)S(1)} %bitcast.64, bf16[2,1024,384]{2,1,0:T(8,128)(2,1)} %collective-permute-done), kind=kLoop, calls=%fused_computation.7 | loop fusion | flops 18874368 | bytes 9437184 | tf_op jit(solution)/shard_map/concatenate | solution.py:23
  89.1 3.5 %all-to-all-start.1 = ((bf16[128,8,384]{2,0,1:T(8,128)(2,1)}), bf16[128,8,384]{2,0,1:T(8,128)(2,1)S(1)}, u32[]{:S(2)}, u32[]{:S(2)}) async-start(bf16[128,8,384]{2,0,1:T(8,128)(2,1)} %bitcast.56), calls=%async_computation.1 | async-start | bytes 1572864 | tf_op jit(solution)/shard_map/all_to_all | solution.py:144
  92.6 5.1 %slice_bitcast_fusion = (bf16[3072,384]{1,0:T(8,128)(2,1)}, bf16[3072,384]{1,0:T(8,128)(2,1)}) fusion(bf16[2,3072,384]{2,1,0:T(8,128)(2,1)} %pad_maximum_fusion.1), kind=kLoop, calls=%fused_computation.12 | loop fusion | bytes 9437184 | tf_op jit(solution)/shard_map/squeeze | solution.py:156
  97.7 8.0 %all-to-all-done.1 = bf16[128,8,384]{2,0,1:T(8,128)(2,1)S(1)} async-done(((bf16[128,8,384]{2,0,1:T(8,128)(2,1)}), bf16[128,8,384]{2,0,1:T(8,128)(2,1)S(1)}, u32[]{:S(2)}, u32[]{:S(2)}) %all-to-all-start.1) | async-done | bytes 786464 | tf_op jit(solution)/shard_map/all_to_all | solution.py:144
  106.6 32.6 %shard_map.93 = (bf16[1024,384]{1,0:T(8,128)(2,1)}, bf16[1024,384]{1,0:T(8,128)(2,1)}, f32[3072,384]{1,0:T(8,128)}, f32[3072,384]{1,0:T(8,128)}) custom-call(s32[8,9]{1,0:T(8,128)} %bitcast.85, s32[8,9]{1,0:T(8,128)} %fusion.5.live_ref, bf16[1024,384]{1,0:T(8,128)(2,1)} %bitcast.3.q_ref, bf16[1024,384]{1,0:T(8,128)(2,1)} %bitcast.80, ...), custom_call_target="tpu_custom_call" | custom-call | flops 5435817984 | bytes 17301504 | tf_op jit(solution)/shard_map/pallas_call | solution.py:117
  139.1 4.4 %fusion = bf16[2,3072,384]{2,1,0:T(8,128)(2,1)S(1)} fusion(f32[1,3072,384]{2,1,0:T(8,128)} %bitcast.61, f32[1,3072,384]{2,1,0:T(8,128)} %bitcast.59), kind=kLoop, calls=%fused_computation.6 | loop fusion | flops 2359296 | bytes 14155776 | tf_op jit(solution)/shard_map/convert.3
  147.6 3.9 %collective-permute-start.3 = (bf16[2,1024,384]{2,1,0:T(8,128)(2,1)}, bf16[2,1024,384]{2,1,0:T(8,128)(2,1)}, u32[]{:S(2)}, u32[]{:S(2)}) collective-permute-start(bf16[2,1024,384]{2,1,0:T(8,128)(2,1)} %get-tuple-element.17), channel_id=1, source_target_pairs={{0,1},{1,2},{2,3},{3,4},{4,5},{5,6},{6,7},{7,8},{8,9},{9,10},{10,1... | collective-permute-start | bytes 4718600 | tf_op jit(solution)/shard_map/ppermute | solution.py:30
  151.5 15.6 %all_to_all.141 = bf16[8,128,384]{2,1,0:T(8,128)(2,1)S(1)} all-to-all(bf16[8,128,384]{2,1,0:T(8,128)(2,1)S(1)} %bitcast.79), channel_id=1, replica_groups=mesh['head'=8,'tile'=32] {'head'}, dimensions={0} | all-to-all | bytes 1572864 | tf_op jit(solution)/shard_map/all_to_all | solution.py:169
  167.1 3.5 %all-to-all-start.4 = ((bf16[8,128,384]{2,1,0:T(8,128)(2,1)}), bf16[8,128,384]{2,1,0:T(8,128)(2,1)S(1)}, u32[]{:S(2)}, u32[]{:S(2)}) async-start(bf16[8,128,384]{2,1,0:T(8,128)(2,1)} %bitcast.78), calls=%async_computation.4 | async-start | bytes 1572864 | tf_op jit(solution)/shard_map/all_to_all | solution.py:168
  170.7 12.9 %collective-permute-done.2 = bf16[2,1024,384]{2,1,0:T(8,128)(2,1)S(1)} collective-permute-done((bf16[2,1024,384]{2,1,0:T(8,128)(2,1)}, bf16[2,1024,384]{2,1,0:T(8,128)(2,1)S(1)}, u32[]{:S(2)}, u32[]{:S(2)}) %collective-permute-start.2) | collective-permute-done | bytes 1572896 | tf_op jit(solution)/shard_map/ppermute | solution.py:30
  183.6 4.1 %collective-permute-done.3 = bf16[2,1024,384]{2,1,0:T(8,128)(2,1)} collective-permute-done((bf16[2,1024,384]{2,1,0:T(8,128)(2,1)}, bf16[2,1024,384]{2,1,0:T(8,128)(2,1)}, u32[]{:S(2)}, u32[]{:S(2)}) %collective-permute-start.3) | collective-permute-done | bytes 1572896 | tf_op jit(solution)/shard_map/ppermute | solution.py:30
  187.8 2.8 %fusion.4 = bf16[2,1024,384]{2,1,0:T(8,128)(2,1)S(1)} fusion(f32[1,3072,384]{2,1,0:T(8,128)} %bitcast.60, f32[1,3072,384]{2,1,0:T(8,128)} %bitcast.62, bf16[2,1024,384]{2,1,0:T(8,128)(2,1)} %collective-permute-done.3, bf16[2,1024,384]{2,1,0:T(8,128)(2,1)S(1)} %collective-permute-done.2), kind=kLoop, calls=%fused_computation.11 | loop fusion | flops 4718592 | bytes 14155776 | tf_op jit(solution)/shard_map/convert.1
  191.6 15.6 %all_to_all.142 = bf16[8,128,384]{2,1,0:T(8,128)(2,1)S(1)} all-to-all(bf16[8,128,384]{2,1,0:T(8,128)(2,1)S(1)} %bitcast.73), channel_id=1, replica_groups=mesh['head'=8,'tile'=32] {'head'}, dimensions={0} | all-to-all | bytes 1572864 | tf_op jit(solution)/shard_map/all_to_all | solution.py:170
  207.2 3.5 %all-to-all-start.7 = ((bf16[8,128,384]{2,1,0:T(8,128)(2,1)}), bf16[8,128,384]{2,1,0:T(8,128)(2,1)S(1)}, u32[]{:S(2)}, u32[]{:S(2)}) async-start(bf16[8,128,384]{2,1,0:T(8,128)(2,1)} %bitcast.72), calls=%async_computation.7 | async-start | bytes 1572864 | tf_op jit(solution)/shard_map/all_to_all | solution.py:171
  213.8 10.0 %all-to-all-done.7 = bf16[8,128,384]{2,1,0:T(8,128)(2,1)S(1)} async-done(((bf16[8,128,384]{2,1,0:T(8,128)(2,1)}), bf16[8,128,384]{2,1,0:T(8,128)(2,1)S(1)}, u32[]{:S(2)}, u32[]{:S(2)}) %all-to-all-start.7) | async-done | bytes 786464 | tf_op jit(solution)/shard_map/all_to_all | solution.py:171
  (45 shorter events, 21.4 us)
Async XLA Ops:
  0.6 54.0 %copy-start = (s32[256,256]{1,0:T(8,128)S(1)}, s32[256,256]{1,0:T(8,128)}, u32[]{:S(2)}) copy-start(s32[256,256]{1,0:T(8,128)} %param.10) | copy-start | bytes 786436
  0.6 6.7 %copy-start.2 = (bf16[128,3072]{1,0:T(8,128)(2,1)S(1)}, bf16[128,3072]{1,0:T(8,128)(2,1)}, u32[]{:S(2)}) copy-start(bf16[128,3072]{1,0:T(8,128)(2,1)} %param.8) | copy-start | bytes 2359300
  2.8 17.6 %all-to-all-start.2 = ((bf16[128,8,384]{2,0,1:T(8,128)(2,1)}), bf16[128,8,384]{2,0,1:T(8,128)(2,1)S(1)}, u32[]{:S(2)}, u32[]{:S(2)}) async-start(bf16[128,8,384]{2,0,1:T(8,128)(2,1)} %bitcast.55), calls=%async_computation.2 | async-start | bytes 1572864 | tf_op jit(solution)/shard_map/all_to_all | solution.py:142
  36.0 17.7 %copy-start.1 = (s32[256]{0:T(256)S(1)}, s32[256]{0:T(256)}, u32[]{:S(2)}) copy-start(s32[256]{0:T(256)} %param.11) | copy-start | bytes 3076
  37.4 41.6 %collective-permute-start.1 = (bf16[2,1024,384]{2,1,0:T(8,128)(2,1)}, bf16[2,1024,384]{2,1,0:T(8,128)(2,1)S(1)}, u32[]{:S(2)}, u32[]{:S(2)}) collective-permute-start(bf16[2,1024,384]{2,1,0:T(8,128)(2,1)} %pad_maximum_fusion.2), channel_id=1, source_target_pairs={{1,0},{2,1},{3,2},{4,3},{5,4},{6,5},{7,6},{8,7},{9,8},{10,9},{11,1... | collective-permute-start | bytes 4718600 | tf_op jit(solution)/shard_map/ppermute | solution.py:22
  45.4 39.8 %collective-permute-start = (bf16[2,1024,384]{2,1,0:T(8,128)(2,1)}, bf16[2,1024,384]{2,1,0:T(8,128)(2,1)}, u32[]{:S(2)}, u32[]{:S(2)}) collective-permute-start(bf16[2,1024,384]{2,1,0:T(8,128)(2,1)} %pad_maximum_fusion.2), channel_id=1, source_target_pairs={{0,1},{1,2},{2,3},{3,4},{4,5},{5,6},{6,7},{7,8},{8,9},{9,10},{10,1... | collective-permute-start | bytes 4718600 | tf_op jit(solution)/shard_map/ppermute | solution.py:21
  49.4 39.7 %all-to-all-start = ((bf16[128,8,384]{2,0,1:T(8,128)(2,1)}), bf16[128,8,384]{2,0,1:T(8,128)(2,1)}, u32[]{:S(2)}, u32[]{:S(2)}) async-start(bf16[128,8,384]{2,0,1:T(8,128)(2,1)} %bitcast.57), calls=%async_computation | async-start | bytes 1572864 | tf_op jit(solution)/shard_map/all_to_all | solution.py:141
  57.6 31.5 %copy-start.5 = (s32[8,24]{1,0:T(8,128)}, s32[8,24]{1,0:T(8,128)S(1)}, u32[]{:S(2)}) copy-start(s32[8,24]{1,0:T(8,128)S(1)} %copy.19) | copy-start | bytes 2308
  89.1 16.6 %all-to-all-start.1 = ((bf16[128,8,384]{2,0,1:T(8,128)(2,1)}), bf16[128,8,384]{2,0,1:T(8,128)(2,1)S(1)}, u32[]{:S(2)}, u32[]{:S(2)}) async-start(bf16[128,8,384]{2,0,1:T(8,128)(2,1)} %bitcast.56), calls=%async_computation.1 | async-start | bytes 1572864 | tf_op jit(solution)/shard_map/all_to_all | solution.py:144
  105.7 0.9 copy-start.4
  143.6 7.9 %copy-start.3 = (bf16[1024,384]{1,0:T(8,128)(2,1)S(1)}, bf16[1024,384]{1,0:T(8,128)(2,1)}, u32[]{:S(2)}) copy-start(bf16[1024,384]{1,0:T(8,128)(2,1)} %get-tuple-element.11) | copy-start | bytes 2359300
  145.7 37.9 %collective-permute-start.2 = (bf16[2,1024,384]{2,1,0:T(8,128)(2,1)}, bf16[2,1024,384]{2,1,0:T(8,128)(2,1)S(1)}, u32[]{:S(2)}, u32[]{:S(2)}) collective-permute-start(bf16[2,1024,384]{2,1,0:T(8,128)(2,1)} %get-tuple-element.16), channel_id=1, source_target_pairs={{1,0},{2,1},{3,2},{4,3},{5,4},{6,5},{7,6},{8,7},{9,8},{10,9},{11,1... | collective-permute-start | bytes 4718600 | tf_op jit(solution)/shard_map/ppermute | solution.py:30
  147.6 40.2 %collective-permute-start.3 = (bf16[2,1024,384]{2,1,0:T(8,128)(2,1)}, bf16[2,1024,384]{2,1,0:T(8,128)(2,1)}, u32[]{:S(2)}, u32[]{:S(2)}) collective-permute-start(bf16[2,1024,384]{2,1,0:T(8,128)(2,1)} %get-tuple-element.17), channel_id=1, source_target_pairs={{0,1},{1,2},{2,3},{3,4},{4,5},{5,6},{6,7},{7,8},{8,9},{9,10},{10,1... | collective-permute-start | bytes 4718600 | tf_op jit(solution)/shard_map/ppermute | solution.py:30
  167.1 24.5 %all-to-all-start.4 = ((bf16[8,128,384]{2,1,0:T(8,128)(2,1)}), bf16[8,128,384]{2,1,0:T(8,128)(2,1)S(1)}, u32[]{:S(2)}, u32[]{:S(2)}) async-start(bf16[8,128,384]{2,1,0:T(8,128)(2,1)} %bitcast.78), calls=%async_computation.4 | async-start | bytes 1572864 | tf_op jit(solution)/shard_map/all_to_all | solution.py:168
  207.2 16.6 %all-to-all-start.7 = ((bf16[8,128,384]{2,1,0:T(8,128)(2,1)}), bf16[8,128,384]{2,1,0:T(8,128)(2,1)S(1)}, u32[]{:S(2)}, u32[]{:S(2)}) async-start(bf16[8,128,384]{2,1,0:T(8,128)(2,1)} %bitcast.72), calls=%async_computation.7 | async-start | bytes 1572864 | tf_op jit(solution)/shard_map/all_to_all | solution.py:171

commit v3 on v2

--- a/solution.py
+++ b/solution.py
@@ -131,46 +131,62 @@
     )(slot_key, live_slot.astype(jnp.int32), q_loc, g_loc, k_win, v_win)
 
 
+def head_columns(array, head, groups):
+    rows, width = array.shape
+    per_group = width // (groups * HD)
+    block = array.reshape(rows, groups, per_group, HD)[:, :, head, :]
+    return jnp.transpose(block, (1, 0, 2))
+
+
+def gather_heads(arrays, head, groups):
+    stacked = jnp.stack([head_columns(x, head, groups) for x in arrays])
+    moved = lax.all_to_all(stacked, "head", split_axis=1, concat_axis=1, tiled=True)
+    return moved.reshape(len(arrays), groups * stacked.shape[2], HD)
+
+
+def scatter_heads(arrays, groups):
+    stacked = jnp.stack(arrays)
+    count, rows_frame, _ = stacked.shape
+    stacked = stacked.reshape(count, groups, rows_frame // groups, HD)
+    return lax.all_to_all(stacked, "head", split_axis=1, concat_axis=1, tiled=True)
+
+
 def local(query, key, value, grad_out, block_mask, tile_order):
     per_frame = lax.axis_size("head")
     frames = lax.axis_size("tile")
     frame_idx = lax.axis_index("tile")
     max_keys = 3 * min(3, per_frame // 2)
-    tile_rows = query.shape[0]
-    q_loc, k_loc, v_loc, g_loc = (
-        lax.all_to_all(query, "head", split_axis=1, concat_axis=0, tiled=True),
-        lax.all_to_all(key, "head", split_axis=1, concat_axis=0, tiled=True),
-        lax.all_to_all(value, "head", split_axis=1, concat_axis=0, tiled=True),
-        lax.all_to_all(grad_out, "head", split_axis=1, concat_axis=0, tiled=True),
-    )
-    width_dev = q_loc.shape[1]
-    head_count = width_dev // HD
+    tile_rows, width = query.shape
+    head_count = width // (per_frame * HD)
     rows_frame = per_frame * tile_rows
-    scaling = HD ** (-0.5)
-    kv_rims = with_halo(jnp.stack([k_loc, v_loc]), (("tile", 1),), rows_frame)
-    forward_active, backward_active = window_lists(
-        block_mask, tile_order, frame_idx, frames, per_frame
-    )
+    forward_active, _ = window_lists(block_mask, tile_order, frame_idx, frames, per_frame)
     slot_key, live_slot = compact_slots(forward_active, max_keys)
-    out_rows, dq_rows, key_grad_win, value_grad_win = attention_heads(
-        q_loc, g_loc, kv_rims[0], kv_rims[1], slot_key, live_slot
-    )
-    grads_win = jnp.stack([key_grad_win, value_grad_win])
-    middle = grads_win[:, rows_frame : 2 * rows_frame]
-    lower_part = grads_win[:, :rows_frame]
-    upper_part = grads_win[:, 2 * rows_frame :]
-    from_above = passed_along(lower_part.astype(jnp.bfloat16), "tile", -1).astype(lower_part.dtype)
-    from_below = passed_along(upper_part.astype(jnp.bfloat16), "tile", 1).astype(upper_part.dtype)
-    summed = middle + from_above + from_below
-    key_out = summed[0].astype(jnp.bfloat16)
-    value_out = summed[1].astype(jnp.bfloat16)
-    attn_out, grad_query, grad_key, grad_value = (
-        lax.all_to_all(out_rows, "head", split_axis=0, concat_axis=1, tiled=True),
-        lax.all_to_all(dq_rows, "head", split_axis=0, concat_axis=1, tiled=True),
-        lax.all_to_all(key_out, "head", split_axis=0, concat_axis=1, tiled=True),
-        lax.all_to_all(value_out, "head", split_axis=0, concat_axis=1, tiled=True),
-    )
-    return (attn_out, grad_query, grad_key, grad_value)
+    fwd_parts, grad_parts = [], []
+    for head in range(head_count):
+        kv = gather_heads([key, value], head, per_frame)
+        qg = gather_heads([query, grad_out], head, per_frame)
+        kv_rims = with_halo(kv, (("tile", 1),), rows_frame)
+        out_h, dq_h, dk_win, dv_win = attention_heads(
+            qg[0], qg[1], kv_rims[0], kv_rims[1], slot_key, live_slot
+        )
+        fwd_parts.append(scatter_heads([out_h, dq_h], per_frame))
+        grads_win = jnp.stack([dk_win, dv_win])
+        middle = grads_win[:, rows_frame : 2 * rows_frame]
+        lower_part = grads_win[:, :rows_frame]
+        upper_part = grads_win[:, 2 * rows_frame :]
+        from_above = passed_along(lower_part.astype(jnp.bfloat16), "tile", -1).astype(jnp.float32)
+        from_below = passed_along(upper_part.astype(jnp.bfloat16), "tile", 1).astype(jnp.float32)
+        summed = (middle + from_above + from_below).astype(jnp.bfloat16)
+        grad_parts.append(scatter_heads([summed[0], summed[1]], per_frame))
+
+    def assemble(parts):
+        stacked = jnp.stack(parts, axis=2)
+        count = stacked.shape[0]
+        return jnp.transpose(stacked, (0, 3, 1, 2, 4)).reshape(count, tile_rows, width)
+
+    fwd = assemble(fwd_parts)
+    grads = assemble(grad_parts)
+    return (fwd[0], fwd[1], grads[0], grads[1])
 
 
 def solution(mesh):

time: 226 us -> 259 us (1.15)
  starting transfers between devices: 35.1 us -> 88 us
  blocking collectives: 46.7 us -> 0 us
  local copies, waits for them, and re-layouts: 24 us -> 48.2 us
  waiting for transfers between devices: 71.5 us -> 56.7 us
  other arithmetic: 14.1 us -> 22.5 us
  Pallas kernels: 32.6 us -> 40.5 us
    all_to_all x3 -> x0, blocking collectives: 46.7 us -> none  [the longest x1 15.6 us: local(): lax.all_to_all(dq_rows, 'head', split_axis=0, concat_axis=1, tiled=True)]
    all_to_all x5 -> x12, starting transfers between devices: 19.3 us -> 47.9 us  [the longest x6 24.7 us: scatter_heads(): lax.all_to_all(stacked, 'head', split_axis=1, concat_axis=1, tiled=True)]
    all_to_all x5 -> x12, waiting for transfers between devices: 31 us -> 51.2 us  [the longest x6 33.3 us: gather_heads(): lax.all_to_all(stacked, 'head', split_axis=1, concat_axis=1, tiled=True)]
    ppermute x1 -> x3, waiting for transfers between devices: 17.2 us -> 0.01 us  [with_halo(): after = lax.ppermute(initial, axis, down)]
    ppermute x2 -> x6, starting transfers between devices: 5.83 us -> 18.5 us  [passed_along(): lax.ppermute(value, axis, [(source, source + steps) for source in range(i...]
    ppermute x2 -> x6, waiting for transfers between devices: 17.1 us -> 5.5 us  [passed_along(): lax.ppermute(value, axis, [(source, source + steps) for source in range(i...]
    another operation x0 -> x14, local copies, waits for them, and re-layouts: none -> 10.7 us  [the longest x8 6.88 us: gather_heads(): stacked = jnp.stack([head_columns(x, head, groups) for x in arrays])]
    unnamed x12 -> x48, local copies, waits for them, and re-layouts: 0.91 us -> 9.61 us
  transfers between devices with their start and end apart: 9 -> 24, of which waited for: 7 -> 11; matrix products, arithmetic and copies ran while one was open for 12% -> 25% of each run, Pallas kernels for 0% -> 16%
where the time goes in v3:
time: 259 us; the launch traced here: 257 us
  starting transfers between devices  88 us (34%)
  waiting for transfers between devices  56.7 us (22%)
  local copies, waits for them, and re-layouts  48.2 us (19%)
  Pallas kernels  40.5 us (16%)
  other arithmetic  22.5 us (9%)
    pallas_call x3, Pallas kernels, attention_heads(): pl.pallas_call(attn_kernel, grid_spec=grid_spec, out_shape=[jax.ShapeDtyp...  40.5 us
    all_to_all x6, waiting for transfers between devices, gather_heads(): lax.all_to_all(stacked, 'head', split_axis=1, concat_axis=1, tiled=True)  33.3 us
    all_to_all x6, starting transfers between devices, scatter_heads(): lax.all_to_all(stacked, 'head', split_axis=1, concat_axis=1, tiled=True)  24.7 us
    all_to_all x6, starting transfers between devices, gather_heads(): lax.all_to_all(stacked, 'head', split_axis=1, concat_axis=1, tiled=True)  23.2 us
    ppermute x6, starting transfers between devices, passed_along(): lax.ppermute(value, axis, [(source, source + steps) for source in range(i...  18.5 us
    all_to_all x6, waiting for transfers between devices, scatter_heads(): lax.all_to_all(stacked, 'head', split_axis=1, concat_axis=1, tiled=True)  18 us
    ppermute x3, starting transfers between devices, with_halo(): after = lax.ppermute(initial, axis, down)  14.1 us
    unnamed x48, local copies, waits for them, and re-layouts  9.61 us
  transfers between devices with their start and end apart: 24, of which 11 were waited for; matrix products, arithmetic and copies ran while one was open for 25% of the time, Pallas kernels for 16%

profile of v3, /device:TPU:6, one launch (start us, length us, event | category | flops | bytes accessed | tf_op | source)
XLA Modules:
  0.0 257.3 jit_solution(7417827482430668081)
XLA Ops:
  4.5 4.5 %all-to-all-start.1 = ((bf16[2,8,128,128]{2,3,0,1:T(8,128)(2,1)}), bf16[2,8,128,128]{2,3,0,1:T(8,128)(2,1)S(1)}, u32[]{:S(2)}, u32[]{:S(2)}) async-start(bf16[2,8,128,128]{2,3,0,1:T(8,128)(2,1)} %copy.71), calls=%async_computation.1 | async-start | bytes 1048576 | tf_op jit(solution)/shard_map/all_to_all | solution.py:143
  12.7 6.6 %all-to-all-done.1 = bf16[2,8,128,128]{2,3,0,1:T(8,128)(2,1)S(1)} async-done(((bf16[2,8,128,128]{2,3,0,1:T(8,128)(2,1)}), bf16[2,8,128,128]{2,3,0,1:T(8,128)(2,1)S(1)}, u32[]{:S(2)}, u32[]{:S(2)}) %all-to-all-start.1) | async-done | bytes 524320 | tf_op jit(solution)/shard_map/all_to_all | solution.py:143
  19.3 3.5 %all-to-all-start = ((bf16[2,8,128,128]{2,3,0,1:T(8,128)(2,1)}), bf16[2,8,128,128]{2,3,0,1:T(8,128)(2,1)S(1)}, u32[]{:S(2)}, u32[]{:S(2)}) async-start(bf16[2,8,128,128]{2,3,0,1:T(8,128)(2,1)} %copy.65), calls=%async_computation | async-start | bytes 1048576 | tf_op jit(solution)/shard_map/all_to_all | solution.py:143
  25.4 7.6 %all-to-all-done = bf16[2,8,128,128]{2,3,0,1:T(8,128)(2,1)S(1)} async-done(((bf16[2,8,128,128]{2,3,0,1:T(8,128)(2,1)}), bf16[2,8,128,128]{2,3,0,1:T(8,128)(2,1)S(1)}, u32[]{:S(2)}, u32[]{:S(2)}) %all-to-all-start) | async-done | bytes 524320 | tf_op jit(solution)/shard_map/all_to_all | solution.py:143
  40.7 6.1 %all-to-all-done.4 = bf16[2,8,128,128]{2,3,0,1:T(8,128)(2,1)S(1)} async-done(((bf16[2,8,128,128]{2,3,0,1:T(8,128)(2,1)}), bf16[2,8,128,128]{2,3,0,1:T(8,128)(2,1)S(1)}, u32[]{:S(2)}, u32[]{:S(2)}) %all-to-all-start.4) | async-done | bytes 524320 | tf_op jit(solution)/shard_map/all_to_all | solution.py:143
  52.1 8.4 %all-to-all-done.3 = bf16[2,8,128,128]{2,3,0,1:T(8,128)(2,1)S(1)} async-done(((bf16[2,8,128,128]{2,3,0,1:T(8,128)(2,1)}), bf16[2,8,128,128]{2,3,0,1:T(8,128)(2,1)S(1)}, u32[]{:S(2)}, u32[]{:S(2)}) %all-to-all-start.3) | async-done | bytes 524320 | tf_op jit(solution)/shard_map/all_to_all | solution.py:143
  68.0 3.8 %collective-permute-start = (bf16[2,1024,128]{2,1,0:T(8,128)(2,1)}, bf16[2,1024,128]{2,1,0:T(8,128)(2,1)}, u32[]{:S(2)}, u32[]{:S(2)}) collective-permute-start(bf16[2,1024,128]{2,1,0:T(8,128)(2,1)} %bitcast.20), channel_id=1, source_target_pairs={{0,1},{1,2},{2,3},{3,4},{4,5},{5,6},{6,7},{7,8},{8,9},{9,10},{10,1... | collective-permute-start | bytes 1572872 | tf_op jit(solution)/shard_map/ppermute | solution.py:21
  71.8 6.1 %collective-permute-start.1 = (bf16[2,1024,128]{2,1,0:T(8,128)(2,1)}, bf16[2,1024,128]{2,1,0:T(8,128)(2,1)}, u32[]{:S(2)}, u32[]{:S(2)}) collective-permute-start(bf16[2,1024,128]{2,1,0:T(8,128)(2,1)} %bitcast.20), channel_id=1, source_target_pairs={{1,0},{2,1},{3,2},{4,3},{5,4},{6,5},{7,6},{8,7},{9,8},{10,9},{11,1... | collective-permute-start | bytes 1572872 | tf_op jit(solution)/shard_map/ppermute | solution.py:22
  80.9 6.0 %collective-permute-start.3 = (bf16[2,1024,128]{2,1,0:T(8,128)(2,1)}, bf16[2,1024,128]{2,1,0:T(8,128)(2,1)}, u32[]{:S(2)}, u32[]{:S(2)}) collective-permute-start(bf16[2,1024,128]{2,1,0:T(8,128)(2,1)} %bitcast.40), channel_id=1, source_target_pairs={{1,0},{2,1},{3,2},{4,3},{5,4},{6,5},{7,6},{8,7},{9,8},{10,9},{11,1... | collective-permute-start | bytes 1572872 | tf_op jit(solution)/shard_map/ppermute | solution.py:22
  86.9 4.7 %all-to-all-start.6 = ((bf16[2,8,128,128]{2,3,0,1:T(8,128)(2,1)}), bf16[2,8,128,128]{2,3,0,1:T(8,128)(2,1)S(1)}, u32[]{:S(2)}, u32[]{:S(2)}) async-start(bf16[2,8,128,128]{2,3,0,1:T(8,128)(2,1)} %copy.87), calls=%async_computation.6 | async-start | bytes 1048576 | tf_op jit(solution)/shard_map/all_to_all | solution.py:143
  97.4 4.6 %all-to-all-done.6 = bf16[2,8,128,128]{2,3,0,1:T(8,128)(2,1)S(1)} async-done(((bf16[2,8,128,128]{2,3,0,1:T(8,128)(2,1)}), bf16[2,8,128,128]{2,3,0,1:T(8,128)(2,1)S(1)}, u32[]{:S(2)}, u32[]{:S(2)}) %all-to-all-start.6) | async-done | bytes 524320 | tf_op jit(solution)/shard_map/all_to_all | solution.py:143
  108.4 13.5 %shard_map.93 = (bf16[1024,128]{1,0:T(8,128)(2,1)}, bf16[1024,128]{1,0:T(8,128)(2,1)}, f32[3072,128]{1,0:T(8,128)}, f32[3072,128]{1,0:T(8,128)}) custom-call(s32[8,9]{1,0:T(8,128)} %bitcast.203, s32[8,9]{1,0:T(8,128)} %fusion.15.live_ref, bf16[1024,128]{1,0:T(8,128)(2,1)} %bitcast.195, bf16[1024,128]{1,0:T(8,128)(2,1)} %bitcast.198, ...), custom_call_target="tpu_custom_call" | custom-call | flops 1811939328 | bytes 5767168 | tf_op jit(solution)/shard_map/pallas_call | solution.py:117
  133.7 13.5 %shard_map.94 = (bf16[1024,128]{1,0:T(8,128)(2,1)}, bf16[1024,128]{1,0:T(8,128)(2,1)}, f32[3072,128]{1,0:T(8,128)}, f32[3072,128]{1,0:T(8,128)}) custom-call(s32[8,9]{1,0:T(8,128)} %bitcast.204, s32[8,9]{1,0:T(8,128)} %fusion.15.live_ref, bf16[1024,128]{1,0:T(8,128)(2,1)} %bitcast.193, bf16[1024,128]{1,0:T(8,128)(2,1)} %bitcast.194, ...), custom_call_target="tpu_custom_call" | custom-call | flops 1811939328 | bytes 5767168 | tf_op jit(solution)/shard_map/pallas_call | solution.py:117
  150.3 4.9 %collective-permute-start.8 = (bf16[2,1024,128]{2,1,0:T(8,128)(2,1)}, bf16[2,1024,128]{2,1,0:T(8,128)(2,1)}, u32[]{:S(2)}, u32[]{:S(2)}) collective-permute-start(bf16[2,1024,128]{2,1,0:T(8,128)(2,1)} %get-tuple-element.44), channel_id=1, source_target_pairs={{1,0},{2,1},{3,2},{4,3},{5,4},{6,5},{7,6},{8,7},{9,8},{10,9},{11,1... | collective-permute-start | bytes 1572872 | tf_op jit(solution)/shard_map/ppermute | solution.py:30
  164.3 6.0 %all-to-all-done.2 = bf16[2,8,128,128]{2,3,0,1:T(8,128)(2,1)S(1)} async-done(((bf16[2,8,128,128]{2,3,0,1:T(8,128)(2,1)}), bf16[2,8,128,128]{2,3,0,1:T(8,128)(2,1)S(1)}, u32[]{:S(2)}, u32[]{:S(2)}) %all-to-all-start.2) | async-done | bytes 524320 | tf_op jit(solution)/shard_map/all_to_all | solution.py:151
  170.3 4.3 %all-to-all-start.5 = ((bf16[2,8,128,128]{2,3,0,1:T(8,128)(2,1)}), bf16[2,8,128,128]{2,3,0,1:T(8,128)(2,1)}, u32[]{:S(2)}, u32[]{:S(2)}) async-start(bf16[2,8,128,128]{2,3,0,1:T(8,128)(2,1)} %pad_maximum_fusion.11), calls=%async_computation.5 | async-start | bytes 1048576 | tf_op jit(solution)/shard_map/all_to_all | solution.py:151
  175.9 13.5 %shard_map.95 = (bf16[1024,128]{1,0:T(8,128)(2,1)}, bf16[1024,128]{1,0:T(8,128)(2,1)}, f32[3072,128]{1,0:T(8,128)}, f32[3072,128]{1,0:T(8,128)}) custom-call(s32[8,9]{1,0:T(8,128)} %bitcast.205, s32[8,9]{1,0:T(8,128)} %fusion.15.live_ref, bf16[1024,128]{1,0:T(8,128)(2,1)} %bitcast.191, bf16[1024,128]{1,0:T(8,128)(2,1)} %bitcast.192, ...), custom_call_target="tpu_custom_call" | custom-call | flops 1811939328 | bytes 5767168 | tf_op jit(solution)/shard_map/pallas_call | solution.py:117
  194.3 4.5 %all-to-all-start.8 = ((bf16[2,8,128,128]{2,3,0,1:T(8,128)(2,1)}), bf16[2,8,128,128]{2,3,0,1:T(8,128)(2,1)}, u32[]{:S(2)}, u32[]{:S(2)}) async-start(bf16[2,8,128,128]{2,3,0,1:T(8,128)(2,1)} %pad_maximum_fusion.14), calls=%async_computation.8 | async-start | bytes 1048576 | tf_op jit(solution)/shard_map/all_to_all | solution.py:151
  203.7 5.5 %all-to-all-done.8 = bf16[2,8,128,128]{2,3,0,1:T(8,128)(2,1)} async-done(((bf16[2,8,128,128]{2,3,0,1:T(8,128)(2,1)}), bf16[2,8,128,128]{2,3,0,1:T(8,128)(2,1)}, u32[]{:S(2)}, u32[]{:S(2)}) %all-to-all-start.8) | async-done | bytes 524320 | tf_op jit(solution)/shard_map/all_to_all | solution.py:151
  209.2 4.1 %all-to-all-start.9 = ((bf16[2,8,128,128]{2,3,0,1:T(8,128)(2,1)}), bf16[2,8,128,128]{2,3,0,1:T(8,128)(2,1)}, u32[]{:S(2)}, u32[]{:S(2)}) async-start(bf16[2,8,128,128]{2,3,0,1:T(8,128)(2,1)} %copy.96), calls=%async_computation.9 | async-start | bytes 1048576 | tf_op jit(solution)/shard_map/all_to_all | solution.py:151
  217.7 3.7 %collective-permute-start.11 = (bf16[2,1024,128]{2,1,0:T(8,128)(2,1)}, bf16[2,1024,128]{2,1,0:T(8,128)(2,1)}, u32[]{:S(2)}, u32[]{:S(2)}) collective-permute-start(bf16[2,1024,128]{2,1,0:T(8,128)(2,1)} %get-tuple-element.47), channel_id=1, source_target_pairs={{0,1},{1,2},{2,3},{3,4},{4,5},{5,6},{6,7},{7,8},{8,9},{9,10},{10,1... | collective-permute-start | bytes 1572872 | tf_op jit(solution)/shard_map/ppermute | solution.py:30
  225.8 4.7 %all-to-all-start.10 = ((bf16[2,8,128,128]{2,3,0,1:T(8,128)(2,1)}), bf16[2,8,128,128]{2,3,0,1:T(8,128)(2,1)S(1)}, u32[]{:S(2)}, u32[]{:S(2)}) async-start(bf16[2,8,128,128]{2,3,0,1:T(8,128)(2,1)} %copy.98), calls=%async_computation.10 | async-start | bytes 1048576 | tf_op jit(solution)/shard_map/all_to_all | solution.py:151
  232.0 4.0 %collective-permute-done.11 = bf16[2,1024,128]{2,1,0:T(8,128)(2,1)} collective-permute-done((bf16[2,1024,128]{2,1,0:T(8,128)(2,1)}, bf16[2,1024,128]{2,1,0:T(8,128)(2,1)}, u32[]{:S(2)}, u32[]{:S(2)}) %collective-permute-start.11) | collective-permute-done | bytes 524320 | tf_op jit(solution)/shard_map/ppermute | solution.py:30
  250.4 4.2 %all-to-all-done.11 = bf16[2,8,128,128]{2,3,0,1:T(8,128)(2,1)S(1)} async-done(((bf16[2,8,128,128]{2,3,0,1:T(8,128)(2,1)}), bf16[2,8,128,128]{2,3,0,1:T(8,128)(2,1)S(1)}, u32[]{:S(2)}, u32[]{:S(2)}) %all-to-all-start.11) | async-done | bytes 524320 | tf_op jit(solution)/shard_map/all_to_all | solution.py:151
  (158 shorter events, 107.6 us)
Async XLA Ops:
  4.5 14.8 %all-to-all-start.1 = ((bf16[2,8,128,128]{2,3,0,1:T(8,128)(2,1)}), bf16[2,8,128,128]{2,3,0,1:T(8,128)(2,1)S(1)}, u32[]{:S(2)}, u32[]{:S(2)}) async-start(bf16[2,8,128,128]{2,3,0,1:T(8,128)(2,1)} %copy.71), calls=%async_computation.1 | async-start | bytes 1048576 | tf_op jit(solution)/shard_map/all_to_all | solution.py:143
  19.3 13.7 %all-to-all-start = ((bf16[2,8,128,128]{2,3,0,1:T(8,128)(2,1)}), bf16[2,8,128,128]{2,3,0,1:T(8,128)(2,1)S(1)}, u32[]{:S(2)}, u32[]{:S(2)}) async-start(bf16[2,8,128,128]{2,3,0,1:T(8,128)(2,1)} %copy.65), calls=%async_computation | async-start | bytes 1048576 | tf_op jit(solution)/shard_map/all_to_all | solution.py:143
  33.0 13.7 %all-to-all-start.4 = ((bf16[2,8,128,128]{2,3,0,1:T(8,128)(2,1)}), bf16[2,8,128,128]{2,3,0,1:T(8,128)(2,1)S(1)}, u32[]{:S(2)}, u32[]{:S(2)}) async-start(bf16[2,8,128,128]{2,3,0,1:T(8,128)(2,1)} %copy.81), calls=%async_computation.4 | async-start | bytes 1048576 | tf_op jit(solution)/shard_map/all_to_all | solution.py:143
  46.8 13.7 %all-to-all-start.3 = ((bf16[2,8,128,128]{2,3,0,1:T(8,128)(2,1)}), bf16[2,8,128,128]{2,3,0,1:T(8,128)(2,1)S(1)}, u32[]{:S(2)}, u32[]{:S(2)}) async-start(bf16[2,8,128,128]{2,3,0,1:T(8,128)(2,1)} %copy.77), calls=%async_computation.3 | async-start | bytes 1048576 | tf_op jit(solution)/shard_map/all_to_all | solution.py:143
  60.5 26.4 %all-to-all-start.7 = ((bf16[2,8,128,128]{2,3,0,1:T(8,128)(2,1)}), bf16[2,8,128,128]{2,3,0,1:T(8,128)(2,1)S(1)}, u32[]{:S(2)}, u32[]{:S(2)}) async-start(bf16[2,8,128,128]{2,3,0,1:T(8,128)(2,1)} %copy.91), calls=%async_computation.7 | async-start | bytes 1048576 | tf_op jit(solution)/shard_map/all_to_all | solution.py:143
  68.0 35.8 %collective-permute-start = (bf16[2,1024,128]{2,1,0:T(8,128)(2,1)}, bf16[2,1024,128]{2,1,0:T(8,128)(2,1)}, u32[]{:S(2)}, u32[]{:S(2)}) collective-permute-start(bf16[2,1024,128]{2,1,0:T(8,128)(2,1)} %bitcast.20), channel_id=1, source_target_pairs={{0,1},{1,2},{2,3},{3,4},{4,5},{5,6},{6,7},{7,8},{8,9},{9,10},{10,1... | collective-permute-start | bytes 1572872 | tf_op jit(solution)/shard_map/ppermute | solution.py:21
  71.8 33.9 %collective-permute-start.1 = (bf16[2,1024,128]{2,1,0:T(8,128)(2,1)}, bf16[2,1024,128]{2,1,0:T(8,128)(2,1)}, u32[]{:S(2)}, u32[]{:S(2)}) collective-permute-start(bf16[2,1024,128]{2,1,0:T(8,128)(2,1)} %bitcast.20), channel_id=1, source_target_pairs={{1,0},{2,1},{3,2},{4,3},{5,4},{6,5},{7,6},{8,7},{9,8},{10,9},{11,1... | collective-permute-start | bytes 1572872 | tf_op jit(solution)/shard_map/ppermute | solution.py:22
  79.0 48.9 %collective-permute-start.2 = (bf16[2,1024,128]{2,1,0:T(8,128)(2,1)}, bf16[2,1024,128]{2,1,0:T(8,128)(2,1)}, u32[]{:S(2)}, u32[]{:S(2)}) collective-permute-start(bf16[2,1024,128]{2,1,0:T(8,128)(2,1)} %bitcast.40), channel_id=1, source_target_pairs={{0,1},{1,2},{2,3},{3,4},{4,5},{5,6},{6,7},{7,8},{8,9},{9,10},{10,1... | collective-permute-start | bytes 1572872 | tf_op jit(solution)/shard_map/ppermute | solution.py:21
  80.9 50.0 %collective-permute-start.3 = (bf16[2,1024,128]{2,1,0:T(8,128)(2,1)}, bf16[2,1024,128]{2,1,0:T(8,128)(2,1)}, u32[]{:S(2)}, u32[]{:S(2)}) collective-permute-start(bf16[2,1024,128]{2,1,0:T(8,128)(2,1)} %bitcast.40), channel_id=1, source_target_pairs={{1,0},{2,1},{3,2},{4,3},{5,4},{6,5},{7,6},{8,7},{9,8},{10,9},{11,1... | collective-permute-start | bytes 1572872 | tf_op jit(solution)/shard_map/ppermute | solution.py:22
  86.9 15.0 %all-to-all-start.6 = ((bf16[2,8,128,128]{2,3,0,1:T(8,128)(2,1)}), bf16[2,8,128,128]{2,3,0,1:T(8,128)(2,1)S(1)}, u32[]{:S(2)}, u32[]{:S(2)}) async-start(bf16[2,8,128,128]{2,3,0,1:T(8,128)(2,1)} %copy.87), calls=%async_computation.6 | async-start | bytes 1048576 | tf_op jit(solution)/shard_map/all_to_all | solution.py:143
  95.5 65.7 %collective-permute-start.4 = (bf16[2,1024,128]{2,1,0:T(8,128)(2,1)S(1)}, bf16[2,1024,128]{2,1,0:T(8,128)(2,1)S(1)}, u32[]{:S(2)}, u32[]{:S(2)}) collective-permute-start(bf16[2,1024,128]{2,1,0:T(8,128)(2,1)S(1)} %bitcast.182), channel_id=1, source_target_pairs={{0,1},{1,2},{2,3},{3,4},{4,5},{5,6},{6,7},{7,8},{8,9},{9,10},{10,1... | collective-permute-start | bytes 1572872 | tf_op jit(solution)/shard_map/ppermute | solution.py:21
  103.8 59.4 %collective-permute-start.5 = (bf16[2,1024,128]{2,1,0:T(8,128)(2,1)S(1)}, bf16[2,1024,128]{2,1,0:T(8,128)(2,1)}, u32[]{:S(2)}, u32[]{:S(2)}) collective-permute-start(bf16[2,1024,128]{2,1,0:T(8,128)(2,1)S(1)} %bitcast.183), channel_id=1, source_target_pairs={{1,0},{2,1},{3,2},{4,3},{5,4},{6,5},{7,6},{8,7},{9,8},{10,9},{11,1... | collective-permute-start | bytes 1572872 | tf_op jit(solution)/shard_map/ppermute | solution.py:22
  125.1 75.1 %collective-permute-start.6 = (bf16[2,1024,128]{2,1,0:T(8,128)(2,1)}, bf16[2,1024,128]{2,1,0:T(8,128)(2,1)}, u32[]{:S(2)}, u32[]{:S(2)}) collective-permute-start(bf16[2,1024,128]{2,1,0:T(8,128)(2,1)} %get-tuple-element.42), channel_id=1, source_target_pairs={{1,0},{2,1},{3,2},{4,3},{5,4},{6,5},{7,6},{8,7},{9,8},{10,9},{11,1... | collective-permute-start | bytes 1572872 | tf_op jit(solution)/shard_map/ppermute | solution.py:30
  127.9 72.3 %collective-permute-start.7 = (bf16[2,1024,128]{2,1,0:T(8,128)(2,1)}, bf16[2,1024,128]{2,1,0:T(8,128)(2,1)}, u32[]{:S(2)}, u32[]{:S(2)}) collective-permute-start(bf16[2,1024,128]{2,1,0:T(8,128)(2,1)} %get-tuple-element.43), channel_id=1, source_target_pairs={{0,1},{1,2},{2,3},{3,4},{4,5},{5,6},{6,7},{7,8},{8,9},{9,10},{10,1... | collective-permute-start | bytes 1572872 | tf_op jit(solution)/shard_map/ppermute | solution.py:30
  150.3 71.1 %collective-permute-start.8 = (bf16[2,1024,128]{2,1,0:T(8,128)(2,1)}, bf16[2,1024,128]{2,1,0:T(8,128)(2,1)}, u32[]{:S(2)}, u32[]{:S(2)}) collective-permute-start(bf16[2,1024,128]{2,1,0:T(8,128)(2,1)} %get-tuple-element.44), channel_id=1, source_target_pairs={{1,0},{2,1},{3,2},{4,3},{5,4},{6,5},{7,6},{8,7},{9,8},{10,9},{11,1... | collective-permute-start | bytes 1572872 | tf_op jit(solution)/shard_map/ppermute | solution.py:30
  156.5 13.8 %all-to-all-start.2 = ((bf16[2,8,128,128]{2,3,0,1:T(8,128)(2,1)}), bf16[2,8,128,128]{2,3,0,1:T(8,128)(2,1)S(1)}, u32[]{:S(2)}, u32[]{:S(2)}) async-start(bf16[2,8,128,128]{2,3,0,1:T(8,128)(2,1)} %pad_maximum_fusion.8), calls=%async_computation.2 | async-start | bytes 1048576 | tf_op jit(solution)/shard_map/all_to_all | solution.py:151
  161.2 60.2 %collective-permute-start.9 = (bf16[2,1024,128]{2,1,0:T(8,128)(2,1)}, bf16[2,1024,128]{2,1,0:T(8,128)(2,1)}, u32[]{:S(2)}, u32[]{:S(2)}) collective-permute-start(bf16[2,1024,128]{2,1,0:T(8,128)(2,1)} %get-tuple-element.45), channel_id=1, source_target_pairs={{0,1},{1,2},{2,3},{3,4},{4,5},{5,6},{6,7},{7,8},{8,9},{9,10},{10,1... | collective-permute-start | bytes 1572872 | tf_op jit(solution)/shard_map/ppermute | solution.py:30
  170.3 24.0 %all-to-all-start.5 = ((bf16[2,8,128,128]{2,3,0,1:T(8,128)(2,1)}), bf16[2,8,128,128]{2,3,0,1:T(8,128)(2,1)}, u32[]{:S(2)}, u32[]{:S(2)}) async-start(bf16[2,8,128,128]{2,3,0,1:T(8,128)(2,1)} %pad_maximum_fusion.11), calls=%async_computation.5 | async-start | bytes 1048576 | tf_op jit(solution)/shard_map/all_to_all | solution.py:151
  194.3 14.9 %all-to-all-start.8 = ((bf16[2,8,128,128]{2,3,0,1:T(8,128)(2,1)}), bf16[2,8,128,128]{2,3,0,1:T(8,128)(2,1)}, u32[]{:S(2)}, u32[]{:S(2)}) async-start(bf16[2,8,128,128]{2,3,0,1:T(8,128)(2,1)} %pad_maximum_fusion.14), calls=%async_computation.8 | async-start | bytes 1048576 | tf_op jit(solution)/shard_map/all_to_all | solution.py:151
  209.2 16.7 %all-to-all-start.9 = ((bf16[2,8,128,128]{2,3,0,1:T(8,128)(2,1)}), bf16[2,8,128,128]{2,3,0,1:T(8,128)(2,1)}, u32[]{:S(2)}, u32[]{:S(2)}) async-start(bf16[2,8,128,128]{2,3,0,1:T(8,128)(2,1)} %copy.96), calls=%async_computation.9 | async-start | bytes 1048576 | tf_op jit(solution)/shard_map/all_to_all | solution.py:151
  215.6 16.4 %collective-permute-start.10 = (bf16[2,1024,128]{2,1,0:T(8,128)(2,1)}, bf16[2,1024,128]{2,1,0:T(8,128)(2,1)}, u32[]{:S(2)}, u32[]{:S(2)}) collective-permute-start(bf16[2,1024,128]{2,1,0:T(8,128)(2,1)} %get-tuple-element.46), channel_id=1, source_target_pairs={{1,0},{2,1},{3,2},{4,3},{5,4},{6,5},{7,6},{8,7},{9,8},{10,9},{11,1... | collective-permute-start | bytes 1572872 | tf_op jit(solution)/shard_map/ppermute | solution.py:30
  217.7 18.3 %collective-permute-start.11 = (bf16[2,1024,128]{2,1,0:T(8,128)(2,1)}, bf16[2,1024,128]{2,1,0:T(8,128)(2,1)}, u32[]{:S(2)}, u32[]{:S(2)}) collective-permute-start(bf16[2,1024,128]{2,1,0:T(8,128)(2,1)} %get-tuple-element.47), channel_id=1, source_target_pairs={{0,1},{1,2},{2,3},{3,4},{4,5},{5,6},{6,7},{7,8},{8,9},{9,10},{10,1... | collective-permute-start | bytes 1572872 | tf_op jit(solution)/shard_map/ppermute | solution.py:30
  225.8 15.0 %all-to-all-start.10 = ((bf16[2,8,128,128]{2,3,0,1:T(8,128)(2,1)}), bf16[2,8,128,128]{2,3,0,1:T(8,128)(2,1)S(1)}, u32[]{:S(2)}, u32[]{:S(2)}) async-start(bf16[2,8,128,128]{2,3,0,1:T(8,128)(2,1)} %copy.98), calls=%async_computation.10 | async-start | bytes 1048576 | tf_op jit(solution)/shard_map/all_to_all | solution.py:151
  240.9 13.7 %all-to-all-start.11 = ((bf16[2,8,128,128]{2,3,0,1:T(8,128)(2,1)}), bf16[2,8,128,128]{2,3,0,1:T(8,128)(2,1)S(1)}, u32[]{:S(2)}, u32[]{:S(2)}) async-start(bf16[2,8,128,128]{2,3,0,1:T(8,128)(2,1)} %copy.100), calls=%async_computation.11 | async-start | bytes 1048576 | tf_op jit(solution)/shard_map/all_to_all | solution.py:151
  (20 other events, 188.6 us)

commit v4 on v2

v4 whole, which is shorter than its diff:
```python
import jax
import jax.numpy as jnp
from jax import lax
from jax.sharding import PartitionSpec as P
from jax.experimental import pallas as pl
from jax.experimental.pallas import tpu as pltpu

HD = 128


NEG = -1e30


def with_halo(array, sides, width):
    for axis, dim in sides:
        size, length = (lax.axis_size(axis), array.shape[dim])
        up = [(i, (i + 1) % size) for i in range(size - 1)]
        down = [(j, i) for i, j in up]
        last = lax.slice_in_dim(array, length - width, length, axis=dim)
        initial = lax.slice_in_dim(array, 0, width, axis=dim)
        before = lax.ppermute(last, axis, up)
        after = lax.ppermute(initial, axis, down)
        array = jnp.concatenate([before, array, after], axis=dim)
    return array


def passed_along(value, axis, steps):
    count = lax.axis_size(axis)
    initial, last = (max(0, -steps), min(count, count - steps))
    return lax.ppermute(value, axis, [(source, source + steps) for source in range(initial, last)])


def window_lists(block_mask, tile_order, frame_idx, frames, per_frame):
    tile_count = per_frame * frames
    query_clip = lax.dynamic_slice_in_dim(tile_order, frame_idx * per_frame, per_frame)
    cand_slot = (frame_idx - 1) * per_frame + jnp.arange(3 * per_frame, dtype=jnp.int32)
    valid_slot = ((cand_slot >= 0) & (cand_slot < tile_count)).astype(jnp.int32)
    cand_clip = jnp.take(tile_order, jnp.clip(cand_slot, 0, tile_count - 1))
    forward_active = block_mask[query_clip[:, None], cand_clip[None, :]] * valid_slot[None, :]
    backward_active = block_mask[cand_clip[:, None], query_clip[None, :]] * valid_slot[:, None]
    return (forward_active, backward_active)


def compact_slots(forward_active, max_keys):
    slot_key = jnp.argsort(1 - forward_active, axis=1, stable=True)[:, :max_keys]
    live_slot = jnp.take_along_axis(forward_active, slot_key, axis=1) > 0
    return (slot_key, live_slot)


def attn_kernel(
    slot_ref, live_ref, qg_ref, prev_ref, own_ref, next_ref,
    og_ref, gown_ref, gprev_ref, gnext_ref, kg_scr, vg_scr, acc_scr,
):
    tile_rows = HD
    query_tiles, max_keys = slot_ref.shape
    scaling = HD ** (-0.5)
    window = (prev_ref, own_ref, next_ref)
    acc_scr[...] = jnp.zeros(acc_scr.shape, acc_scr.dtype)
    nt = (((1,), (1,)), ((), ()))
    tn = (((0,), (0,)), ((), ()))
    lane_slot = lax.broadcasted_iota(jnp.int32, (1, max_keys * tile_rows), 1) // tile_rows

    def acc_rows(p, s):
        return pl.ds(pl.multiple_of(slot_ref[p, s] * tile_rows, tile_rows), tile_rows)

    def body(p, carry):
        rows = pl.ds(pl.multiple_of(p * tile_rows, tile_rows), tile_rows)
        live_lane = jnp.zeros((1, max_keys * tile_rows), jnp.int32)
        for s in range(max_keys):
            slot = slot_ref[p, s]
            side = slot // query_tiles
            src = pl.ds(pl.multiple_of((slot % query_tiles) * tile_rows, tile_rows), tile_rows)
            dst = slice(s * tile_rows, (s + 1) * tile_rows)
            for w in range(3):

                @pl.when(side == w)
                def _():
                    kg_scr[dst, :] = window[w][0, src, :]
                    vg_scr[dst, :] = window[w][1, src, :]

            live_lane = jnp.where(lane_slot == s, live_ref[p, s], live_lane)
        q = qg_ref[0, rows, :]
        g = qg_ref[1, rows, :]
        kg = kg_scr[...]
        vg = vg_scr[...]
        sc = lax.dot_general(q, kg, nt, preferred_element_type=jnp.float32) * scaling
        sc = jnp.where(live_lane > 0, sc, NEG)
        top = jnp.max(sc, axis=1, keepdims=True)
        log_total = top + jnp.log(jnp.sum(jnp.exp(sc - top), axis=1, keepdims=True))
        prob = jnp.exp(sc - log_total)
        prob_bf = prob.astype(jnp.bfloat16)
        out = jnp.dot(prob_bf, vg, preferred_element_type=jnp.float32).astype(jnp.bfloat16)
        og_ref[0, rows, :] = out
        delta = jnp.sum(g.astype(jnp.float32) * out.astype(jnp.float32), axis=1, keepdims=True)
        dprob = lax.dot_general(g, vg, nt, preferred_element_type=jnp.float32)
        dscore = (prob * (dprob - delta)).astype(jnp.bfloat16)
        dq = jnp.dot(dscore, kg, preferred_element_type=jnp.float32) * scaling
        og_ref[1, rows, :] = dq.astype(og_ref.dtype)
        dk_g = lax.dot_general(dscore, q, tn, preferred_element_type=jnp.float32) * scaling
        dv_g = lax.dot_general(prob_bf, g, tn, preferred_element_type=jnp.float32)
        for s in range(max_keys):
            arows = acc_rows(p, s)
            acc_scr[0, arows, :] += dk_g[s * tile_rows : (s + 1) * tile_rows, :]
            acc_scr[1, arows, :] += dv_g[s * tile_rows : (s + 1) * tile_rows, :]
        return carry

    lax.fori_loop(0, query_tiles, body, 0)
    rows_frame = query_tiles * tile_rows
    gprev_ref[...] = acc_scr[:, :rows_frame, :].astype(gprev_ref.dtype)
    gown_ref[...] = acc_scr[:, rows_frame : 2 * rows_frame, :]
    gnext_ref[...] = acc_scr[:, 2 * rows_frame :, :].astype(gnext_ref.dtype)


def attention_heads(qg, kv_prev, kv_own, kv_next, slot_key, live_slot):
    _, rows_frame, width = qg.shape
    query_tiles, max_keys = slot_key.shape
    head_count = width // HD
    spec = pl.BlockSpec((2, rows_frame, HD), lambda h, *_: (0, 0, h))
    flops = 12 * query_tiles * max_keys * HD * HD * HD * head_count
    grid_spec = pltpu.PrefetchScalarGridSpec(
        num_scalar_prefetch=2,
        grid=(head_count,),
        in_specs=[spec, spec, spec, spec],
        out_specs=[spec, spec, spec, spec],
        scratch_shapes=[
            pltpu.VMEM((max_keys * HD, HD), jnp.bfloat16),
            pltpu.VMEM((max_keys * HD, HD), jnp.bfloat16),
            pltpu.VMEM((2, 3 * rows_frame, HD), jnp.float32),
        ],
    )
    block = (2, rows_frame, width)
    return pl.pallas_call(
        attn_kernel,
        grid_spec=grid_spec,
        out_shape=[
            jax.ShapeDtypeStruct(block, jnp.bfloat16),
            jax.ShapeDtypeStruct(block, jnp.float32),
            jax.ShapeDtypeStruct(block, jnp.bfloat16),
            jax.ShapeDtypeStruct(block, jnp.bfloat16),
        ],
        cost_estimate=pl.CostEstimate(
            flops=flops,
            transcendentals=query_tiles * max_keys * HD * HD * head_count,
            bytes_accessed=2 * rows_frame * width * 2 * 8,
        ),
    )(slot_key, live_slot.astype(jnp.int32), qg, kv_prev, kv_own, kv_next)


def to_heads(arrays):
    return lax.all_to_all(jnp.stack(arrays), "head", split_axis=2, concat_axis=1, tiled=True)


def to_tokens(stacked):
    return lax.all_to_all(stacked, "head", split_axis=1, concat_axis=2, tiled=True)


def local(query, key, value, grad_out, block_mask, tile_order):
    per_frame = lax.axis_size("head")
    frames = lax.axis_size("tile")
    frame_idx = lax.axis_index("tile")
    max_keys = 3 * min(3, per_frame // 2)
    forward_active, _ = window_lists(block_mask, tile_order, frame_idx, frames, per_frame)
    slot_key, live_slot = compact_slots(forward_active, max_keys)
    kv = to_heads([key, value])
    kv_prev = passed_along(kv, "tile", 1)
    kv_next = passed_along(kv, "tile", -1)
    qg = to_heads([query, grad_out])
    og, grad_own, grad_prev, grad_next = attention_heads(
        qg, kv_prev, kv, kv_next, slot_key, live_slot
    )
    og_tok = to_tokens(og)
    from_above = passed_along(grad_prev, "tile", -1).astype(jnp.float32)
    from_below = passed_along(grad_next, "tile", 1).astype(jnp.float32)
    summed = (grad_own + from_above + from_below).astype(jnp.bfloat16)
    grads_tok = to_tokens(summed)
    return (og_tok[0], og_tok[1], grads_tok[0], grads_tok[1])


def solution(mesh):
    in_specs = (
        P(("tile", "head"), None),
        P(("tile", "head"), None),
        P(("tile", "head"), None),
        P(("tile", "head"), None),
        P(),
        P(),
    )
    out_specs = (
        P(("tile", "head"), None),
        P(("tile", "head"), None),
        P(("tile", "head"), None),
        P(("tile", "head"), None),
    )
    return jax.shard_map(local, mesh=mesh, in_specs=in_specs, out_specs=out_specs, check_vma=False)
```

time: 226 us -> 197 us (0.87)
  blocking collectives: 46.7 us -> 25.9 us
  local copies, waits for them, and re-layouts: 24 us -> 34.7 us
  starting transfers between devices: 35.1 us -> 26.8 us
  waiting for transfers between devices: 71.5 us -> 63.9 us
  other arithmetic: 14.1 us -> 6.61 us
  Pallas kernels: 32.6 us -> 38 us
    ppermute x2 -> x0, waiting for transfers between devices: 23.4 us -> none  [the longest x1 17.2 us: with_halo(): after = lax.ppermute(initial, axis, down)]
    all_to_all x3 -> x1, blocking collectives: 46.7 us -> 25.9 us  [to_heads(): lax.all_to_all(jnp.stack(arrays), 'head', split_axis=2, concat_axis=1, ti...]
    ppermute x2 -> x4, waiting for transfers between devices: 17.1 us -> 33.8 us  [passed_along(): lax.ppermute(value, axis, [(source, source + steps) for source in range(i...]
    ppermute x2 -> x4, starting transfers between devices: 5.83 us -> 15.8 us  [passed_along(): lax.ppermute(value, axis, [(source, source + steps) for source in range(i...]
    ppermute x2 -> x0, starting transfers between devices: 9.94 us -> none  [the longest x1 8.02 us: with_halo(): after = lax.ppermute(initial, axis, down)]
    all_to_all x5 -> x3, starting transfers between devices: 19.3 us -> 11.1 us  [the longest x2 7.34 us: to_tokens(): lax.all_to_all(stacked, 'head', split_axis=1, concat_axis=2, tiled=True)]
    another operation x3 -> x2, other arithmetic: 8.63 us -> 1.7 us  [to_heads(): jnp.stack(arrays)]
    slice x2 -> x6, local copies, waits for them, and re-layouts: 3.11 us -> 9.2 us  [local(): return (og_tok[0], og_tok[1], grads_tok[0], grads_tok[1])]
  transfers between devices with their start and end apart: 9 -> 7, of which waited for: 7 -> 6; matrix products, arithmetic and copies ran while one was open for 12% -> 15% of each run, Pallas kernels for 0% -> 0%
where the time goes in v4:
time: 197 us
  waiting for transfers between devices  63.9 us (32%)
  Pallas kernels  38 us (19%)
  local copies, waits for them, and re-layouts  34.7 us (18%)
  starting transfers between devices  26.8 us (14%)
  blocking collectives  25.9 us (13%)
  other arithmetic  6.61 us (3%)
    pallas_call x1, Pallas kernels, attention_heads(): pl.pallas_call(attn_kernel, grid_spec=grid_spec, out_shape=[jax.ShapeDtyp...  38 us
    ppermute x4, waiting for transfers between devices, passed_along(): lax.ppermute(value, axis, [(source, source + steps) for source in range(i...  33.8 us
    all_to_all x1, blocking collectives, to_heads(): lax.all_to_all(jnp.stack(arrays), 'head', split_axis=2, concat_axis=1, ti...  25.9 us
    ppermute x4, starting transfers between devices, passed_along(): lax.ppermute(value, axis, [(source, source + steps) for source in range(i...  15.8 us
    all_to_all x1, waiting for transfers between devices, to_heads(): lax.all_to_all(jnp.stack(arrays), 'head', split_axis=2, concat_axis=1, ti...  15.4 us
    all_to_all x2, waiting for transfers between devices, to_tokens(): lax.all_to_all(stacked, 'head', split_axis=1, concat_axis=2, tiled=True)  14.6 us
    slice x6, local copies, waits for them, and re-layouts, local(): return (og_tok[0], og_tok[1], grads_tok[0], grads_tok[1])  9.2 us
    all_to_all x2, starting transfers between devices, to_tokens(): lax.all_to_all(stacked, 'head', split_axis=1, concat_axis=2, tiled=True)  7.34 us
  transfers between devices with their start and end apart: 7, of which 6 were waited for; matrix products, arithmetic and copies ran while one was open for 15% of the time, Pallas kernels for 0%

profile of v4, /device:TPU:6, one launch (start us, length us, event | category | flops | bytes accessed | tf_op | source)
XLA Modules:
  0.0 196.8 jit_solution(3931579383718459010)
XLA Ops:
  0.6 1.6 pad_maximum_fusion.1
  3.4 25.9 %all_to_all.66 = bf16[2,128,3072]{1,0,2:T(2,128)(2,1)S(1)} all-to-all(bf16[2,128,3072]{1,0,2:T(2,128)(2,1)S(1)} %copy.42), channel_id=1, replica_groups=mesh['head'=8,'tile'=32] {'head'}, dimensions={2} | all-to-all | bytes 3145728 | tf_op jit(solution)/shard_map/all_to_all | solution.py:150
  29.2 3.0 %copy.43 = bf16[2,128,8,384]{3,1,2,0:T(8,128)(2,1)} copy(bf16[2,128,8,384]{1,0,3,2:T(2,128)(2,1)S(1)} %bitcast.42) | data formatting | bytes 3145728 | tf_op jit(solution)/shard_map/all_to_all | solution.py:150
  32.2 8.0 %collective-permute-start.1 = (bf16[2,1024,384]{2,1,0:T(8,128)(2,1)}, bf16[2,1024,384]{2,1,0:T(8,128)(2,1)}, u32[]{:S(2)}, u32[]{:S(2)}) collective-permute-start(bf16[2,1024,384]{2,1,0:T(8,128)(2,1)} %bitcast.11.own_ref), channel_id=1, source_target_pairs={{1,0},{2,1},{3,2},{4,3},{5,4},{6,5},{7,6},{8,7},{9,8},{10,9},{11,1... | collective-permute-start | bytes 4718600 | tf_op jit(solution)/shard_map/ppermute | solution.py:30
  40.3 1.9 collective-permute-start
  42.4 2.9 %copy.40 = bf16[2,128,3072]{1,0,2:T(2,128)(2,1)} copy(bf16[2,128,3072]{2,1,0:T(8,128)(2,1)S(1)} %pad_maximum_fusion) | data formatting | bytes 3145728 | tf_op jit(solution)/shard_map/stack | solution.py:150
  45.3 3.7 %all-to-all-start = ((bf16[2,128,3072]{1,0,2:T(2,128)(2,1)}), bf16[2,128,3072]{1,0,2:T(2,128)(2,1)S(1)}, u32[]{:S(2)}, u32[]{:S(2)}) async-start(bf16[2,128,3072]{1,0,2:T(2,128)(2,1)} %copy.40), calls=%async_computation | async-start | bytes 3145728 | tf_op jit(solution)/shard_map/all_to_all | solution.py:150
  50.0 1.9 gather_fusion.1
  55.1 15.4 %all-to-all-done = bf16[2,128,3072]{1,0,2:T(2,128)(2,1)S(1)} async-done(((bf16[2,128,3072]{1,0,2:T(2,128)(2,1)}), bf16[2,128,3072]{1,0,2:T(2,128)(2,1)S(1)}, u32[]{:S(2)}, u32[]{:S(2)}) %all-to-all-start) | async-done | bytes 1572896 | tf_op jit(solution)/shard_map/all_to_all | solution.py:150
  70.5 3.0 %copy.41 = bf16[2,128,8,384]{3,1,2,0:T(8,128)(2,1)} copy(bf16[2,128,8,384]{1,0,3,2:T(2,128)(2,1)S(1)} %bitcast.41) | data formatting | bytes 3145728 | tf_op jit(solution)/shard_map/all_to_all | solution.py:150
  73.9 6.2 %collective-permute-done.prev_ref = bf16[2,1024,384]{2,1,0:T(8,128)(2,1)} collective-permute-done((bf16[2,1024,384]{2,1,0:T(8,128)(2,1)}, bf16[2,1024,384]{2,1,0:T(8,128)(2,1)}, u32[]{:S(2)}, u32[]{:S(2)}) %collective-permute-start) | collective-permute-done | bytes 1572896 | tf_op jit(solution)/shard_map/ppermute | solution.py:30
  80.1 38.0 %shard_map.93 = (bf16[2,1024,384]{2,1,0:T(8,128)(2,1)}, f32[2,1024,384]{2,1,0:T(8,128)}, bf16[2,1024,384]{2,1,0:T(8,128)(2,1)}, bf16[2,1024,384]{2,1,0:T(8,128)(2,1)}) custom-call(s32[8,9]{1,0:T(8,128)} %bitcast.56, s32[8,9]{1,0:T(8,128)} %fusion.live_ref, bf16[2,1024,384]{2,1,0:T(8,128)(2,1)} %bitcast.47, ...), custom_call_target="tpu_custom_call" | custom-call | flops 5435817984 | bytes 12582912 | tf_op jit(solution)/shard_map/pallas_call | solution.py:132
  118.1 1.9 collective-permute-start.2
  120.1 3.9 %collective-permute-start.3 = (bf16[2,1024,384]{2,1,0:T(8,128)(2,1)}, bf16[2,1024,384]{2,1,0:T(8,128)(2,1)}, u32[]{:S(2)}, u32[]{:S(2)}) collective-permute-start(bf16[2,1024,384]{2,1,0:T(8,128)(2,1)} %get-tuple-element.13), channel_id=1, source_target_pairs={{0,1},{1,2},{2,3},{3,4},{4,5},{5,6},{6,7},{7,8},{8,9},{9,10},{10,1... | collective-permute-start | bytes 4718600 | tf_op jit(solution)/shard_map/ppermute | solution.py:30
  124.0 4.2 %copy.44 = bf16[2,1024,384]{2,0,1:T(2,128)(2,1)} copy(bf16[2,1024,384]{2,1,0:T(8,128)(2,1)} %get-tuple-element.10) | data formatting | bytes 3145728 | tf_op jit(solution)/shard_map/pallas_call | solution.py:132
  128.2 3.6 %all-to-all-start.2 = ((bf16[2,1024,384]{2,0,1:T(2,128)(2,1)}), bf16[2,1024,384]{2,0,1:T(2,128)(2,1)S(1)}, u32[]{:S(2)}, u32[]{:S(2)}) async-start(bf16[2,1024,384]{2,0,1:T(2,128)(2,1)} %copy.44), calls=%async_computation.2 | async-start | bytes 3145728 | tf_op jit(solution)/shard_map/all_to_all | solution.py:154
  131.8 23.1 %collective-permute-done.2 = bf16[2,1024,384]{2,1,0:T(8,128)(2,1)S(1)} collective-permute-done((bf16[2,1024,384]{2,1,0:T(8,128)(2,1)}, bf16[2,1024,384]{2,1,0:T(8,128)(2,1)S(1)}, u32[]{:S(2)}, u32[]{:S(2)}) %collective-permute-start.2) | collective-permute-done | bytes 1572896 | tf_op jit(solution)/shard_map/ppermute | solution.py:30
  154.9 4.1 %collective-permute-done.3 = bf16[2,1024,384]{2,1,0:T(8,128)(2,1)} collective-permute-done((bf16[2,1024,384]{2,1,0:T(8,128)(2,1)}, bf16[2,1024,384]{2,1,0:T(8,128)(2,1)}, u32[]{:S(2)}, u32[]{:S(2)}) %collective-permute-start.3) | collective-permute-done | bytes 1572896 | tf_op jit(solution)/shard_map/ppermute | solution.py:30
  159.0 3.3 %add_convert_fusion = bf16[2,1024,384]{2,1,0:T(8,128)(2,1)S(1)} fusion(bf16[2,1024,384]{2,1,0:T(8,128)(2,1)} %collective-permute-done.3, f32[2,1024,384]{2,1,0:T(8,128)} %get-tuple-element.11, bf16[2,1024,384]{2,1,0:T(8,128)(2,1)} %copy-done.2), kind=kLoop, calls=%fused_computation.3 | loop fusion | flops 3932160 | bytes 7864320 | tf_op jit(solution)/shard_map/convert_element_type | solution.py:174
  162.3 2.8 %copy.47 = bf16[2,1024,384]{2,0,1:T(2,128)(2,1)} copy(bf16[2,1024,384]{2,1,0:T(8,128)(2,1)S(1)} %add_convert_fusion) | data formatting | bytes 3145728 | tf_op jit(solution)/shard_map/convert_element_type | solution.py:174
  165.1 3.8 %all-to-all-start.3 = ((bf16[2,1024,384]{2,0,1:T(2,128)(2,1)}), bf16[2,1024,384]{2,0,1:T(2,128)(2,1)S(1)}, u32[]{:S(2)}, u32[]{:S(2)}) async-start(bf16[2,1024,384]{2,0,1:T(2,128)(2,1)} %copy.47), calls=%async_computation.3 | async-start | bytes 3145728 | tf_op jit(solution)/shard_map/all_to_all | solution.py:154
  168.9 2.9 %fusion.7 = (bf16[1,128,8,384]{3,0,1,2:T(2,128)(2,1)S(1)}, bf16[1,128,8,384]{3,0,1,2:T(2,128)(2,1)S(1)}) fusion(bf16[2,128,8,384]{3,0,1,2:T(2,128)(2,1)S(1)} %bitcast.39), kind=kLoop, calls=%fused_computation.27 | loop fusion | bytes 3145728 | tf_op jit(solution)/shard_map/slice | solution.py:176
  175.5 14.6 %all-to-all-done.3 = bf16[2,1024,384]{2,0,1:T(2,128)(2,1)S(1)} async-done(((bf16[2,1024,384]{2,0,1:T(2,128)(2,1)}), bf16[2,1024,384]{2,0,1:T(2,128)(2,1)S(1)}, u32[]{:S(2)}, u32[]{:S(2)}) %all-to-all-start.3) | async-done | bytes 1572896 | tf_op jit(solution)/shard_map/all_to_all | solution.py:154
  190.2 2.9 %fusion.6 = (bf16[1,128,8,384]{3,0,1,2:T(2,128)(2,1)S(1)}, bf16[1,128,8,384]{3,0,1,2:T(2,128)(2,1)S(1)}) fusion(bf16[2,128,8,384]{3,0,1,2:T(2,128)(2,1)S(1)} %bitcast.40), kind=kLoop, calls=%fused_computation.26 | loop fusion | bytes 3145728 | tf_op jit(solution)/shard_map/slice | solution.py:176
  (43 shorter events, 13.3 us)
Async XLA Ops:
  0.6 49.4 %copy-start = (s32[256,256]{1,0:T(8,128)S(1)}, s32[256,256]{1,0:T(8,128)}, u32[]{:S(2)}) copy-start(s32[256,256]{1,0:T(8,128)} %param.10) | copy-start | bytes 786436
  29.2 13.0 %copy-start.3 = (bf16[128,3072]{1,0:T(8,128)(2,1)S(1)}, bf16[128,3072]{1,0:T(8,128)(2,1)}, u32[]{:S(2)}) copy-start(bf16[128,3072]{1,0:T(8,128)(2,1)} %param.9) | copy-start | bytes 2359300
  29.2 13.0 %copy-start.4 = (bf16[128,3072]{1,0:T(8,128)(2,1)S(1)}, bf16[128,3072]{1,0:T(8,128)(2,1)}, u32[]{:S(2)}) copy-start(bf16[128,3072]{1,0:T(8,128)(2,1)} %param.6) | copy-start | bytes 2359300
  32.2 41.6 %collective-permute-start.1 = (bf16[2,1024,384]{2,1,0:T(8,128)(2,1)}, bf16[2,1024,384]{2,1,0:T(8,128)(2,1)}, u32[]{:S(2)}, u32[]{:S(2)}) collective-permute-start(bf16[2,1024,384]{2,1,0:T(8,128)(2,1)} %bitcast.11.own_ref), channel_id=1, source_target_pairs={{1,0},{2,1},{3,2},{4,3},{5,4},{6,5},{7,6},{8,7},{9,8},{10,9},{11,1... | collective-permute-start | bytes 4718600 | tf_op jit(solution)/shard_map/ppermute | solution.py:30
  40.3 39.8 %collective-permute-start = (bf16[2,1024,384]{2,1,0:T(8,128)(2,1)}, bf16[2,1024,384]{2,1,0:T(8,128)(2,1)}, u32[]{:S(2)}, u32[]{:S(2)}) collective-permute-start(bf16[2,1024,384]{2,1,0:T(8,128)(2,1)} %bitcast.11.own_ref), channel_id=1, source_target_pairs={{0,1},{1,2},{2,3},{3,4},{4,5},{5,6},{6,7},{7,8},{8,9},{9,10},{10,1... | collective-permute-start | bytes 4718600 | tf_op jit(solution)/shard_map/ppermute | solution.py:30
  45.3 3.8 %copy-start.1 = (s32[256]{0:T(256)S(1)}, s32[256]{0:T(256)}, u32[]{:S(2)}) copy-start(s32[256]{0:T(256)} %param.11) | copy-start | bytes 3076
  45.3 25.2 %all-to-all-start = ((bf16[2,128,3072]{1,0,2:T(2,128)(2,1)}), bf16[2,128,3072]{1,0,2:T(2,128)(2,1)S(1)}, u32[]{:S(2)}, u32[]{:S(2)}) async-start(bf16[2,128,3072]{1,0,2:T(2,128)(2,1)} %copy.40), calls=%async_computation | async-start | bytes 3145728 | tf_op jit(solution)/shard_map/all_to_all | solution.py:150
  53.0 1.5 copy-start.5
  118.1 36.7 %collective-permute-start.2 = (bf16[2,1024,384]{2,1,0:T(8,128)(2,1)}, bf16[2,1024,384]{2,1,0:T(8,128)(2,1)S(1)}, u32[]{:S(2)}, u32[]{:S(2)}) collective-permute-start(bf16[2,1024,384]{2,1,0:T(8,128)(2,1)} %get-tuple-element.12), channel_id=1, source_target_pairs={{1,0},{2,1},{3,2},{4,3},{5,4},{6,5},{7,6},{8,7},{9,8},{10,9},{11,1... | collective-permute-start | bytes 4718600 | tf_op jit(solution)/shard_map/ppermute | solution.py:30
  120.1 38.9 %collective-permute-start.3 = (bf16[2,1024,384]{2,1,0:T(8,128)(2,1)}, bf16[2,1024,384]{2,1,0:T(8,128)(2,1)}, u32[]{:S(2)}, u32[]{:S(2)}) collective-permute-start(bf16[2,1024,384]{2,1,0:T(8,128)(2,1)} %get-tuple-element.13), channel_id=1, source_target_pairs={{0,1},{1,2},{2,3},{3,4},{4,5},{5,6},{6,7},{7,8},{8,9},{9,10},{10,1... | collective-permute-start | bytes 4718600 | tf_op jit(solution)/shard_map/ppermute | solution.py:30
  128.2 36.9 %all-to-all-start.2 = ((bf16[2,1024,384]{2,0,1:T(2,128)(2,1)}), bf16[2,1024,384]{2,0,1:T(2,128)(2,1)S(1)}, u32[]{:S(2)}, u32[]{:S(2)}) async-start(bf16[2,1024,384]{2,0,1:T(2,128)(2,1)} %copy.44), calls=%async_computation.2 | async-start | bytes 3145728 | tf_op jit(solution)/shard_map/all_to_all | solution.py:154
  154.9 4.1 %copy-start.2 = (bf16[2,1024,384]{2,1,0:T(8,128)(2,1)}, bf16[2,1024,384]{2,1,0:T(8,128)(2,1)S(1)}, u32[]{:S(2)}) copy-start(bf16[2,1024,384]{2,1,0:T(8,128)(2,1)S(1)} %collective-permute-done.2) | copy-start | bytes 4718596
  165.1 25.1 %all-to-all-start.3 = ((bf16[2,1024,384]{2,0,1:T(2,128)(2,1)}), bf16[2,1024,384]{2,0,1:T(2,128)(2,1)S(1)}, u32[]{:S(2)}, u32[]{:S(2)}) async-start(bf16[2,1024,384]{2,0,1:T(2,128)(2,1)} %copy.47), calls=%async_computation.3 | async-start | bytes 3145728 | tf_op jit(solution)/shard_map/all_to_all | solution.py:154

commit v5 on v4

--- a/solution.py
+++ b/solution.py
@@ -60,75 +60,70 @@
     tn = (((0,), (0,)), ((), ()))
     lane_slot = lax.broadcasted_iota(jnp.int32, (1, max_keys * tile_rows), 1) // tile_rows
 
-    def acc_rows(p, s):
-        return pl.ds(pl.multiple_of(slot_ref[p, s] * tile_rows, tile_rows), tile_rows)
-
     def body(p, carry):
-        rows = pl.ds(pl.multiple_of(p * tile_rows, tile_rows), tile_rows)
         live_lane = jnp.zeros((1, max_keys * tile_rows), jnp.int32)
         for s in range(max_keys):
             slot = slot_ref[p, s]
             side = slot // query_tiles
-            src = pl.ds(pl.multiple_of((slot % query_tiles) * tile_rows, tile_rows), tile_rows)
+            tile = slot % query_tiles
             dst = slice(s * tile_rows, (s + 1) * tile_rows)
             for w in range(3):
 
                 @pl.when(side == w)
                 def _():
-                    kg_scr[dst, :] = window[w][0, src, :]
-                    vg_scr[dst, :] = window[w][1, src, :]
+                    kg_scr[dst, :] = window[w][tile, 0]
+                    vg_scr[dst, :] = window[w][tile, 1]
 
             live_lane = jnp.where(lane_slot == s, live_ref[p, s], live_lane)
-        q = qg_ref[0, rows, :]
-        g = qg_ref[1, rows, :]
+        q = qg_ref[p, 0]
+        g = qg_ref[p, 1]
         kg = kg_scr[...]
         vg = vg_scr[...]
         sc = lax.dot_general(q, kg, nt, preferred_element_type=jnp.float32) * scaling
         sc = jnp.where(live_lane > 0, sc, NEG)
         top = jnp.max(sc, axis=1, keepdims=True)
-        log_total = top + jnp.log(jnp.sum(jnp.exp(sc - top), axis=1, keepdims=True))
-        prob = jnp.exp(sc - log_total)
+        expd = jnp.exp(sc - top)
+        prob = expd * (1.0 / jnp.sum(expd, axis=1, keepdims=True))
         prob_bf = prob.astype(jnp.bfloat16)
         out = jnp.dot(prob_bf, vg, preferred_element_type=jnp.float32).astype(jnp.bfloat16)
-        og_ref[0, rows, :] = out
+        og_ref[p, 0] = out
         delta = jnp.sum(g.astype(jnp.float32) * out.astype(jnp.float32), axis=1, keepdims=True)
         dprob = lax.dot_general(g, vg, nt, preferred_element_type=jnp.float32)
         dscore = (prob * (dprob - delta)).astype(jnp.bfloat16)
         dq = jnp.dot(dscore, kg, preferred_element_type=jnp.float32) * scaling
-        og_ref[1, rows, :] = dq.astype(og_ref.dtype)
+        og_ref[p, 1] = dq.astype(og_ref.dtype)
         dk_g = lax.dot_general(dscore, q, tn, preferred_element_type=jnp.float32) * scaling
         dv_g = lax.dot_general(prob_bf, g, tn, preferred_element_type=jnp.float32)
         for s in range(max_keys):
-            arows = acc_rows(p, s)
-            acc_scr[0, arows, :] += dk_g[s * tile_rows : (s + 1) * tile_rows, :]
-            acc_scr[1, arows, :] += dv_g[s * tile_rows : (s + 1) * tile_rows, :]
+            slot = slot_ref[p, s]
+            acc_scr[slot, 0] += dk_g[s * tile_rows : (s + 1) * tile_rows, :]
+            acc_scr[slot, 1] += dv_g[s * tile_rows : (s + 1) * tile_rows, :]
         return carry
 
     lax.fori_loop(0, query_tiles, body, 0)
-    rows_frame = query_tiles * tile_rows
-    gprev_ref[...] = acc_scr[:, :rows_frame, :].astype(gprev_ref.dtype)
-    gown_ref[...] = acc_scr[:, rows_frame : 2 * rows_frame, :]
-    gnext_ref[...] = acc_scr[:, 2 * rows_frame :, :].astype(gnext_ref.dtype)
+    gprev_ref[...] = acc_scr[:query_tiles].astype(gprev_ref.dtype)
+    gown_ref[...] = acc_scr[query_tiles : 2 * query_tiles]
+    gnext_ref[...] = acc_scr[2 * query_tiles :].astype(gnext_ref.dtype)
 
 
 def attention_heads(qg, kv_prev, kv_own, kv_next, slot_key, live_slot):
-    _, rows_frame, width = qg.shape
-    query_tiles, max_keys = slot_key.shape
+    query_tiles, count, tile_rows, width = qg.shape
+    max_keys = slot_key.shape[1]
     head_count = width // HD
-    spec = pl.BlockSpec((2, rows_frame, HD), lambda h, *_: (0, 0, h))
-    flops = 12 * query_tiles * max_keys * HD * HD * HD * head_count
+    spec = pl.BlockSpec((query_tiles, count, tile_rows, HD), lambda h, *_: (0, 0, 0, h))
+    flops = 12 * query_tiles * max_keys * tile_rows * tile_rows * HD * head_count
     grid_spec = pltpu.PrefetchScalarGridSpec(
         num_scalar_prefetch=2,
         grid=(head_count,),
         in_specs=[spec, spec, spec, spec],
         out_specs=[spec, spec, spec, spec],
         scratch_shapes=[
-            pltpu.VMEM((max_keys * HD, HD), jnp.bfloat16),
-            pltpu.VMEM((max_keys * HD, HD), jnp.bfloat16),
-            pltpu.VMEM((2, 3 * rows_frame, HD), jnp.float32),
+            pltpu.VMEM((max_keys * tile_rows, HD), jnp.bfloat16),
+            pltpu.VMEM((max_keys * tile_rows, HD), jnp.bfloat16),
+            pltpu.VMEM((3 * query_tiles, count, tile_rows, HD), jnp.float32),
         ],
     )
-    block = (2, rows_frame, width)
+    block = qg.shape
     return pl.pallas_call(
         attn_kernel,
         grid_spec=grid_spec,
@@ -140,18 +135,56 @@
         ],
         cost_estimate=pl.CostEstimate(
             flops=flops,
-            transcendentals=query_tiles * max_keys * HD * HD * head_count,
-            bytes_accessed=2 * rows_frame * width * 2 * 8,
+            transcendentals=query_tiles * max_keys * tile_rows * tile_rows * head_count,
+            bytes_accessed=query_tiles * count * tile_rows * width * 2 * 8,
         ),
     )(slot_key, live_slot.astype(jnp.int32), qg, kv_prev, kv_own, kv_next)
 
 
-def to_heads(arrays):
-    return lax.all_to_all(jnp.stack(arrays), "head", split_axis=2, concat_axis=1, tiled=True)
+def split_kernel(*refs):
+    count = len(refs) - 1
+    for i in range(count):
+        refs[-1][0, i] = refs[i][...]
+
+
+def join_kernel(*refs):
+    count = len(refs) - 1
+    for i in range(count):
+        refs[1 + i][...] = refs[0][0, i]
+
+
+def split_columns(arrays, groups):
+    rows, width = arrays[0].shape
+    part = width // groups
+    count = len(arrays)
+    return pl.pallas_call(
+        split_kernel,
+        grid=(groups,),
+        in_specs=[pl.BlockSpec((rows, part), lambda j: (0, j))] * count,
+        out_specs=pl.BlockSpec((1, count, rows, part), lambda j: (j, 0, 0, 0)),
+        out_shape=jax.ShapeDtypeStruct((groups, count, rows, part), arrays[0].dtype),
+    )(*arrays)
+
+
+def join_columns(stacked):
+    groups, count, rows, part = stacked.shape
+    return pl.pallas_call(
+        join_kernel,
+        grid=(groups,),
+        in_specs=[pl.BlockSpec((1, count, rows, part), lambda j: (j, 0, 0, 0))],
+        out_specs=[pl.BlockSpec((rows, part), lambda j: (0, j))] * count,
+        out_shape=[jax.ShapeDtypeStruct((rows, groups * part), stacked.dtype)] * count,
+    )(stacked)
+
+
+def to_heads(arrays, groups):
+    stacked = split_columns(arrays, groups)
+    return lax.all_to_all(stacked, "head", split_axis=0, concat_axis=0, tiled=True)
 
 
 def to_tokens(stacked):
-    return lax.all_to_all(stacked, "head", split_axis=1, concat_axis=2, tiled=True)
+    moved = lax.all_to_all(stacked, "head", split_axis=0, concat_axis=0, tiled=True)
+    return join_columns(moved)
 
 
 def local(query, key, value, grad_out, block_mask, tile_order):
@@ -161,19 +194,19 @@
     max_keys = 3 * min(3, per_frame // 2)
     forward_active, _ = window_lists(block_mask, tile_order, frame_idx, frames, per_frame)
     slot_key, live_slot = compact_slots(forward_active, max_keys)
-    kv = to_heads([key, value])
+    kv = to_heads([key, value], per_frame)
     kv_prev = passed_along(kv, "tile", 1)
     kv_next = passed_along(kv, "tile", -1)
-    qg = to_heads([query, grad_out])
+    qg = to_heads([query, grad_out], per_frame)
     og, grad_own, grad_prev, grad_next = attention_heads(
         qg, kv_prev, kv, kv_next, slot_key, live_slot
     )
-    og_tok = to_tokens(og)
+    attn_out, grad_query = to_tokens(og)
     from_above = passed_along(grad_prev, "tile", -1).astype(jnp.float32)
     from_below = passed_along(grad_next, "tile", 1).astype(jnp.float32)
     summed = (grad_own + from_above + from_below).astype(jnp.bfloat16)
-    grads_tok = to_tokens(summed)
-    return (og_tok[0], og_tok[1], grads_tok[0], grads_tok[1])
+    grad_key, grad_value = to_tokens(summed)
+    return (attn_out, grad_query, grad_key, grad_value)
 
 
 def solution(mesh):

time: 197 us -> 197 us (level)
  local copies, waits for them, and re-layouts: 34.7 us -> 6.73 us
  Pallas kernels: 38 us -> 59.8 us
  waiting for transfers between devices: 63.9 us -> 69.9 us
    pallas_call x0 -> x4, Pallas kernels: none -> 21.9 us  [the longest x2 11 us: split_columns(): pl.pallas_call(split_kernel, grid=(groups,), in_specs=[pl.BlockSpec((rows...]
    slice x6 -> x0, local copies, waits for them, and re-layouts: 9.2 us -> none  [local(): return (og_tok[0], og_tok[1], grads_tok[0], grads_tok[1])]
    all_to_all x2 -> x0, local copies, waits for them, and re-layouts: 6.03 us -> none  [to_heads(): lax.all_to_all(jnp.stack(arrays), 'head', split_axis=2, concat_axis=1, ti...]
    ppermute x4, waiting for transfers between devices: 33.8 us -> 38.4 us  [passed_along(): lax.ppermute(value, axis, [(source, source + steps) for source in range(i...]
    pallas_call x1 -> x0, local copies, waits for them, and re-layouts: 4.19 us -> none  [attention_heads(): pl.pallas_call(attn_kernel, grid_spec=grid_spec, out_shape=[jax.ShapeDtyp...]
    another operation x2 -> x0, local copies, waits for them, and re-layouts: 4.07 us -> none  [to_heads(): jnp.stack(arrays)]
    convert_element_type x1 -> x0, local copies, waits for them, and re-layouts: 2.79 us -> none  [local(): summed = (grad_own + from_above + from_below).astype(jnp.bfloat16)]
    unnamed x16 -> x14, local copies, waits for them, and re-layouts: 4.09 us -> 2.34 us
  transfers between devices with their start and end apart: 7 -> 7, of which waited for: 6 -> 6; matrix products, arithmetic and copies ran while one was open for 15% -> 5% of each run, Pallas kernels for 0% -> 6%
where the time goes in v5:
time: 197 us; the launch traced here: 196 us
  waiting for transfers between devices  69.9 us (35%)
  Pallas kernels  59.8 us (30%)
  starting transfers between devices  26.7 us (14%)
  blocking collectives  26.1 us (13%)
  local copies, waits for them, and re-layouts  6.73 us (3%)
  other arithmetic  5.79 us (3%)
    ppermute x4, waiting for transfers between devices, passed_along(): lax.ppermute(value, axis, [(source, source + steps) for source in range(i...  38.4 us
    pallas_call x1, Pallas kernels, attention_heads(): pl.pallas_call(attn_kernel, grid_spec=grid_spec, out_shape=[jax.ShapeDtyp...  37.9 us
    all_to_all x1, blocking collectives, to_heads(): lax.all_to_all(stacked, 'head', split_axis=0, concat_axis=0, tiled=True)  26.1 us
    all_to_all x2, waiting for transfers between devices, to_tokens(): lax.all_to_all(stacked, 'head', split_axis=0, concat_axis=0, tiled=True)  16 us
    ppermute x4, starting transfers between devices, passed_along(): lax.ppermute(value, axis, [(source, source + steps) for source in range(i...  15.8 us
    all_to_all x1, waiting for transfers between devices, to_heads(): lax.all_to_all(stacked, 'head', split_axis=0, concat_axis=0, tiled=True)  15.4 us
    pallas_call x2, Pallas kernels, split_columns(): pl.pallas_call(split_kernel, grid=(groups,), in_specs=[pl.BlockSpec((rows...  11 us
    pallas_call x2, Pallas kernels, join_columns(): pl.pallas_call(join_kernel, grid=(groups,), in_specs=[pl.BlockSpec((1, co...  10.9 us
  transfers between devices with their start and end apart: 7, of which 6 were waited for; matrix products, arithmetic and copies ran while one was open for 5% of the time, Pallas kernels for 6%

profile of v5, /device:TPU:6, one launch (start us, length us, event | category | flops | bytes accessed | tf_op | source)
XLA Modules:
  0.0 195.6 jit_solution(3206853865491674703)
XLA Ops:
  0.6 5.5 %shard_map.94 = bf16[8,2,128,384]{3,2,1,0:T(8,128)(2,1)} custom-call(bf16[128,3072]{1,0:T(8,128)(2,1)} %refs_0_.3, bf16[128,3072]{1,0:T(8,128)(2,1)} %refs_1_.3), custom_call_target="tpu_custom_call" | custom-call | tf_op jit(solution)/shard_map/pallas_call | solution.py:160
  6.2 26.1 %all_to_all.20.own_ref = bf16[8,2,128,384]{3,2,1,0:T(8,128)(2,1)S(1)} all-to-all(bf16[8,2,128,384]{3,2,1,0:T(8,128)(2,1)} %shard_map.94), channel_id=1, replica_groups=mesh['head'=8,'tile'=32] {'head'}, dimensions={0} | all-to-all | bytes 3145728 | tf_op jit(solution)/shard_map/all_to_all | solution.py:182
  32.2 8.0 %collective-permute-start.1 = (bf16[8,2,128,384]{3,2,1,0:T(8,128)(2,1)S(1)}, bf16[8,2,128,384]{3,2,1,0:T(8,128)(2,1)}, u32[]{:S(2)}, u32[]{:S(2)}) collective-permute-start(bf16[8,2,128,384]{3,2,1,0:T(8,128)(2,1)S(1)} %all_to_all.20.own_ref), channel_id=1, source_target_pairs={{1,0},{2,1},{3,2},{4,3},{5,4},{6,5},{7,6},{8,7},{9,8},{10,9},{11,1... | collective-permute-start | bytes 4718600 | tf_op jit(solution)/shard_map/ppermute | solution.py:30
  40.3 1.9 collective-permute-start
  42.2 5.5 %shard_map.93 = bf16[8,2,128,384]{3,2,1,0:T(8,128)(2,1)} custom-call(bf16[128,3072]{1,0:T(8,128)(2,1)} %refs_0_.2, bf16[128,3072]{1,0:T(8,128)(2,1)} %refs_1_.2), custom_call_target="tpu_custom_call" | custom-call | tf_op jit(solution)/shard_map/pallas_call | solution.py:160
  47.7 3.7 %all-to-all-start = ((bf16[8,2,128,384]{3,2,1,0:T(8,128)(2,1)}), bf16[8,2,128,384]{3,2,1,0:T(8,128)(2,1)S(1)}, u32[]{:S(2)}, u32[]{:S(2)}) async-start(bf16[8,2,128,384]{3,2,1,0:T(8,128)(2,1)} %shard_map.93), calls=%async_computation | async-start | bytes 3145728 | tf_op jit(solution)/shard_map/all_to_all | solution.py:182
  52.4 1.9 gather_fusion.1
  54.5 0.8 sort.17
  55.5 1.3 gather_fusion.2
  57.5 15.4 %all-to-all-done.qg_ref = bf16[8,2,128,384]{3,2,1,0:T(8,128)(2,1)S(1)} async-done(((bf16[8,2,128,384]{3,2,1,0:T(8,128)(2,1)}), bf16[8,2,128,384]{3,2,1,0:T(8,128)(2,1)S(1)}, u32[]{:S(2)}, u32[]{:S(2)}) %all-to-all-start) | async-done | bytes 1572896 | tf_op jit(solution)/shard_map/all_to_all | solution.py:182
  73.5 6.3 %collective-permute-done.prev_ref = bf16[8,2,128,384]{3,2,1,0:T(8,128)(2,1)} collective-permute-done((bf16[8,2,128,384]{3,2,1,0:T(8,128)(2,1)S(1)}, bf16[8,2,128,384]{3,2,1,0:T(8,128)(2,1)}, u32[]{:S(2)}, u32[]{:S(2)}) %collective-permute-start) | collective-permute-done | bytes 1572896 | tf_op jit(solution)/shard_map/ppermute | solution.py:30
  79.9 37.9 %shard_map.95 = (bf16[8,2,128,384]{3,2,1,0:T(8,128)(2,1)}, f32[8,2,128,384]{3,2,1,0:T(8,128)}, bf16[8,2,128,384]{3,2,1,0:T(8,128)(2,1)}, bf16[8,2,128,384]{3,2,1,0:T(8,128)(2,1)}) custom-call(s32[8,9]{1,0:T(8,128)} %bitcast.9, s32[8,9]{1,0:T(8,128)} %fusion.live_ref, bf16[8,2,128,384]{3,2,1,0:T(8,128)(2,1)} %copy-done.5, ...), custom_call_target="tpu_custom_call" | custom-call | flops 5435817984 | bytes 12582912 | tf_op jit(solution)/shard_map/pallas_call | solution.py:127
  117.8 1.9 collective-permute-start.2
  119.7 3.9 %collective-permute-start.3 = (bf16[8,2,128,384]{3,2,1,0:T(8,128)(2,1)}, bf16[8,2,128,384]{3,2,1,0:T(8,128)(2,1)}, u32[]{:S(2)}, u32[]{:S(2)}) collective-permute-start(bf16[8,2,128,384]{3,2,1,0:T(8,128)(2,1)} %get-tuple-element.19), channel_id=1, source_target_pairs={{0,1},{1,2},{2,3},{3,4},{4,5},{5,6},{6,7},{7,8},{8,9},{9,10},{10,1... | collective-permute-start | bytes 4718600 | tf_op jit(solution)/shard_map/ppermute | solution.py:30
  123.6 3.6 %all-to-all-start.2 = ((bf16[8,2,128,384]{3,2,1,0:T(8,128)(2,1)}), bf16[8,2,128,384]{3,2,1,0:T(8,128)(2,1)S(1)}, u32[]{:S(2)}, u32[]{:S(2)}) async-start(bf16[8,2,128,384]{3,2,1,0:T(8,128)(2,1)} %get-tuple-element.14), calls=%async_computation.2 | async-start | bytes 3145728 | tf_op jit(solution)/shard_map/all_to_all | solution.py:186
  127.2 27.3 %collective-permute-done.2 = bf16[8,2,128,384]{3,2,1,0:T(8,128)(2,1)S(1)} collective-permute-done((bf16[8,2,128,384]{3,2,1,0:T(8,128)(2,1)}, bf16[8,2,128,384]{3,2,1,0:T(8,128)(2,1)S(1)}, u32[]{:S(2)}, u32[]{:S(2)}) %collective-permute-start.2) | collective-permute-done | bytes 1572896 | tf_op jit(solution)/shard_map/ppermute | solution.py:30
  154.5 4.1 %collective-permute-done.3 = bf16[8,2,128,384]{3,2,1,0:T(8,128)(2,1)} collective-permute-done((bf16[8,2,128,384]{3,2,1,0:T(8,128)(2,1)}, bf16[8,2,128,384]{3,2,1,0:T(8,128)(2,1)}, u32[]{:S(2)}, u32[]{:S(2)}) %collective-permute-start.3) | collective-permute-done | bytes 1572896 | tf_op jit(solution)/shard_map/ppermute | solution.py:30
  158.6 4.2 %add_convert_fusion = bf16[8,2,128,384]{3,2,1,0:T(8,128)(2,1)} fusion(bf16[8,2,128,384]{3,2,1,0:T(8,128)(2,1)} %collective-permute-done.3, f32[8,2,128,384]{3,2,1,0:T(8,128)} %get-tuple-element.17, bf16[8,2,128,384]{3,2,1,0:T(8,128)(2,1)S(1)} %collective-permute-done.2), kind=kLoop, calls=%fused_computation.3 | loop fusion | flops 3932160 | bytes 7864320 | tf_op jit(solution)/shard_map/convert_element_type | solution.py:207
  162.8 1.2 copy-done.2
  164.0 3.6 %all-to-all-start.3 = ((bf16[8,2,128,384]{3,2,1,0:T(8,128)(2,1)}), bf16[8,2,128,384]{3,2,1,0:T(8,128)(2,1)S(1)}, u32[]{:S(2)}, u32[]{:S(2)}) async-start(bf16[8,2,128,384]{3,2,1,0:T(8,128)(2,1)} %add_convert_fusion), calls=%async_computation.3 | async-start | bytes 3145728 | tf_op jit(solution)/shard_map/all_to_all | solution.py:186
  167.6 5.4 %shard_map.96 = (bf16[128,3072]{1,0:T(8,128)(2,1)}, bf16[128,3072]{1,0:T(8,128)(2,1)}) custom-call(bf16[8,2,128,384]{3,2,1,0:T(8,128)(2,1)} %copy-done.2), custom_call_target="tpu_custom_call" | custom-call | tf_op jit(solution)/shard_map/pallas_call | solution.py:171
  173.0 16.0 %all-to-all-done.3.refs_0_ = bf16[8,2,128,384]{3,2,1,0:T(8,128)(2,1)S(1)} async-done(((bf16[8,2,128,384]{3,2,1,0:T(8,128)(2,1)}), bf16[8,2,128,384]{3,2,1,0:T(8,128)(2,1)S(1)}, u32[]{:S(2)}, u32[]{:S(2)}) %all-to-all-start.3) | async-done | bytes 1572896 | tf_op jit(solution)/shard_map/all_to_all | solution.py:186
  189.0 1.2 copy-done.3
  190.2 5.4 %shard_map.97 = (bf16[128,3072]{1,0:T(8,128)(2,1)}, bf16[128,3072]{1,0:T(8,128)(2,1)}) custom-call(bf16[8,2,128,384]{3,2,1,0:T(8,128)(2,1)} %copy-done.3), custom_call_target="tpu_custom_call" | custom-call | tf_op jit(solution)/shard_map/pallas_call | solution.py:171
  (31 shorter events, 2.6 us)
Async XLA Ops:
  0.6 51.8 %copy-start = (s32[256,256]{1,0:T(8,128)S(1)}, s32[256,256]{1,0:T(8,128)}, u32[]{:S(2)}) copy-start(s32[256,256]{1,0:T(8,128)} %param.10) | copy-start | bytes 786436
  32.2 15.5 %copy-start.4 = (bf16[8,2,128,384]{3,2,1,0:T(8,128)(2,1)}, bf16[8,2,128,384]{3,2,1,0:T(8,128)(2,1)S(1)}, u32[]{:S(2)}) copy-start(bf16[8,2,128,384]{3,2,1,0:T(8,128)(2,1)S(1)} %all_to_all.20.own_ref) | copy-start | bytes 4718596
  32.2 41.3 %collective-permute-start.1 = (bf16[8,2,128,384]{3,2,1,0:T(8,128)(2,1)S(1)}, bf16[8,2,128,384]{3,2,1,0:T(8,128)(2,1)}, u32[]{:S(2)}, u32[]{:S(2)}) collective-permute-start(bf16[8,2,128,384]{3,2,1,0:T(8,128)(2,1)S(1)} %all_to_all.20.own_ref), channel_id=1, source_target_pairs={{1,0},{2,1},{3,2},{4,3},{5,4},{6,5},{7,6},{8,7},{9,8},{10,9},{11,1... | collective-permute-start | bytes 4718600 | tf_op jit(solution)/shard_map/ppermute | solution.py:30
  40.3 39.6 %collective-permute-start = (bf16[8,2,128,384]{3,2,1,0:T(8,128)(2,1)S(1)}, bf16[8,2,128,384]{3,2,1,0:T(8,128)(2,1)}, u32[]{:S(2)}, u32[]{:S(2)}) collective-permute-start(bf16[8,2,128,384]{3,2,1,0:T(8,128)(2,1)S(1)} %all_to_all.20.own_ref), channel_id=1, source_target_pairs={{0,1},{1,2},{2,3},{3,4},{4,5},{5,6},{6,7},{7,8},{8,9},{9,10},{10,1... | collective-permute-start | bytes 4718600 | tf_op jit(solution)/shard_map/ppermute | solution.py:30
  47.7 3.8 %copy-start.1 = (s32[256]{0:T(256)S(1)}, s32[256]{0:T(256)}, u32[]{:S(2)}) copy-start(s32[256]{0:T(256)} %param.11) | copy-start | bytes 3076
  47.7 25.2 %all-to-all-start = ((bf16[8,2,128,384]{3,2,1,0:T(8,128)(2,1)}), bf16[8,2,128,384]{3,2,1,0:T(8,128)(2,1)S(1)}, u32[]{:S(2)}, u32[]{:S(2)}) async-start(bf16[8,2,128,384]{3,2,1,0:T(8,128)(2,1)} %shard_map.93), calls=%async_computation | async-start | bytes 3145728 | tf_op jit(solution)/shard_map/all_to_all | solution.py:182
  55.4 1.5 copy-start.6
  72.9 7.0 %copy-start.5 = (bf16[8,2,128,384]{3,2,1,0:T(8,128)(2,1)}, bf16[8,2,128,384]{3,2,1,0:T(8,128)(2,1)S(1)}, u32[]{:S(2)}) copy-start(bf16[8,2,128,384]{3,2,1,0:T(8,128)(2,1)S(1)} %all-to-all-done.qg_ref) | copy-start | bytes 4718596
  117.8 36.7 %collective-permute-start.2 = (bf16[8,2,128,384]{3,2,1,0:T(8,128)(2,1)}, bf16[8,2,128,384]{3,2,1,0:T(8,128)(2,1)S(1)}, u32[]{:S(2)}, u32[]{:S(2)}) collective-permute-start(bf16[8,2,128,384]{3,2,1,0:T(8,128)(2,1)} %get-tuple-element.18), channel_id=1, source_target_pairs={{1,0},{2,1},{3,2},{4,3},{5,4},{6,5},{7,6},{8,7},{9,8},{10,9},{11,1... | collective-permute-start | bytes 4718600 | tf_op jit(solution)/shard_map/ppermute | solution.py:30
  119.7 38.9 %collective-permute-start.3 = (bf16[8,2,128,384]{3,2,1,0:T(8,128)(2,1)}, bf16[8,2,128,384]{3,2,1,0:T(8,128)(2,1)}, u32[]{:S(2)}, u32[]{:S(2)}) collective-permute-start(bf16[8,2,128,384]{3,2,1,0:T(8,128)(2,1)} %get-tuple-element.19), channel_id=1, source_target_pairs={{0,1},{1,2},{2,3},{3,4},{4,5},{5,6},{6,7},{7,8},{8,9},{9,10},{10,1... | collective-permute-start | bytes 4718600 | tf_op jit(solution)/shard_map/ppermute | solution.py:30
  123.6 39.2 %all-to-all-start.2 = ((bf16[8,2,128,384]{3,2,1,0:T(8,128)(2,1)}), bf16[8,2,128,384]{3,2,1,0:T(8,128)(2,1)S(1)}, u32[]{:S(2)}, u32[]{:S(2)}) async-start(bf16[8,2,128,384]{3,2,1,0:T(8,128)(2,1)} %get-tuple-element.14), calls=%async_computation.2 | async-start | bytes 3145728 | tf_op jit(solution)/shard_map/all_to_all | solution.py:186
  162.8 1.2 copy-start.2
  164.0 25.1 %all-to-all-start.3 = ((bf16[8,2,128,384]{3,2,1,0:T(8,128)(2,1)}), bf16[8,2,128,384]{3,2,1,0:T(8,128)(2,1)S(1)}, u32[]{:S(2)}, u32[]{:S(2)}) async-start(bf16[8,2,128,384]{3,2,1,0:T(8,128)(2,1)} %add_convert_fusion), calls=%async_computation.3 | async-start | bytes 3145728 | tf_op jit(solution)/shard_map/all_to_all | solution.py:186
  189.0 1.2 copy-start.3

commit v6 on v5

--- a/solution.py
+++ b/solution.py
@@ -100,7 +100,7 @@
             acc_scr[slot, 1] += dv_g[s * tile_rows : (s + 1) * tile_rows, :]
         return carry
 
-    lax.fori_loop(0, query_tiles, body, 0)
+    lax.fori_loop(0, query_tiles, body, 0, unroll=2)
     gprev_ref[...] = acc_scr[:query_tiles].astype(gprev_ref.dtype)
     gown_ref[...] = acc_scr[query_tiles : 2 * query_tiles]
     gnext_ref[...] = acc_scr[2 * query_tiles :].astype(gnext_ref.dtype)
@@ -143,14 +143,17 @@
 
 def split_kernel(*refs):
     count = len(refs) - 1
-    for i in range(count):
-        refs[-1][0, i] = refs[i][...]
+    groups, _, _, part = refs[-1].shape
+    for j in range(groups):
+        for i in range(count):
+            refs[-1][j, i] = refs[i][:, j * part : (j + 1) * part]
 
 
 def join_kernel(*refs):
-    count = len(refs) - 1
-    for i in range(count):
-        refs[1 + i][...] = refs[0][0, i]
+    groups, count, _, part = refs[0].shape
+    for j in range(groups):
+        for i in range(count):
+            refs[1 + i][:, j * part : (j + 1) * part] = refs[0][j, i]
 
 
 def split_columns(arrays, groups):
@@ -159,9 +162,8 @@
     count = len(arrays)
     return pl.pallas_call(
         split_kernel,
-        grid=(groups,),
-        in_specs=[pl.BlockSpec((rows, part), lambda j: (0, j))] * count,
-        out_specs=pl.BlockSpec((1, count, rows, part), lambda j: (j, 0, 0, 0)),
+        in_specs=[pl.BlockSpec(memory_space=pltpu.VMEM)] * count,
+        out_specs=pl.BlockSpec(memory_space=pltpu.VMEM),
         out_shape=jax.ShapeDtypeStruct((groups, count, rows, part), arrays[0].dtype),
     )(*arrays)
 
@@ -170,9 +172,8 @@
     groups, count, rows, part = stacked.shape
     return pl.pallas_call(
         join_kernel,
-        grid=(groups,),
-        in_specs=[pl.BlockSpec((1, count, rows, part), lambda j: (j, 0, 0, 0))],
-        out_specs=[pl.BlockSpec((rows, part), lambda j: (0, j))] * count,
+        in_specs=[pl.BlockSpec(memory_space=pltpu.VMEM)],
+        out_specs=[pl.BlockSpec(memory_space=pltpu.VMEM)] * count,
         out_shape=[jax.ShapeDtypeStruct((rows, groups * part), stacked.dtype)] * count,
     )(stacked)
 

time: 197 us -> 191 us (0.970)
  Pallas kernels: 59.8 us -> 48.5 us
  waiting for transfers between devices: 69.9 us -> 75.4 us
    pallas_call x4, Pallas kernels: 21.9 us -> 10.7 us  [the longest x2 5.38 us: split_columns(): pl.pallas_call(split_kernel, in_specs=[pl.BlockSpec(memory_space=pltpu.VM...]
    ppermute x4, waiting for transfers between devices: 38.4 us -> 41.2 us  [passed_along(): lax.ppermute(value, axis, [(source, source + steps) for source in range(i...]
    all_to_all x2, waiting for transfers between devices: 16 us -> 18.8 us  [to_tokens(): lax.all_to_all(stacked, 'head', split_axis=0, concat_axis=0, tiled=True)]
  transfers between devices with their start and end apart: 7 -> 7, of which waited for: 6 -> 6; matrix products, arithmetic and copies ran while one was open for 5% -> 5% of each run, Pallas kernels for 6% -> 3%
where the time goes in v6:
time: 191 us; the launch traced here: 190 us
  waiting for transfers between devices  75.4 us (39%)
  Pallas kernels  48.5 us (25%)
  starting transfers between devices  26.7 us (14%)
  blocking collectives  26.1 us (14%)
  local copies, waits for them, and re-layouts  6.73 us (4%)
  other arithmetic  5.79 us (3%)
    ppermute x4, waiting for transfers between devices, passed_along(): lax.ppermute(value, axis, [(source, source + steps) for source in range(i...  41.2 us
    pallas_call x1, Pallas kernels, attention_heads(): pl.pallas_call(attn_kernel, grid_spec=grid_spec, out_shape=[jax.ShapeDtyp...  37.7 us
    all_to_all x1, blocking collectives, to_heads(): lax.all_to_all(stacked, 'head', split_axis=0, concat_axis=0, tiled=True)  26.1 us
    all_to_all x2, waiting for transfers between devices, to_tokens(): lax.all_to_all(stacked, 'head', split_axis=0, concat_axis=0, tiled=True)  18.8 us
    ppermute x4, starting transfers between devices, passed_along(): lax.ppermute(value, axis, [(source, source + steps) for source in range(i...  15.8 us
    all_to_all x1, waiting for transfers between devices, to_heads(): lax.all_to_all(stacked, 'head', split_axis=0, concat_axis=0, tiled=True)  15.4 us
    all_to_all x2, starting transfers between devices, to_tokens(): lax.all_to_all(stacked, 'head', split_axis=0, concat_axis=0, tiled=True)  7.17 us
    pallas_call x2, Pallas kernels, split_columns(): pl.pallas_call(split_kernel, in_specs=[pl.BlockSpec(memory_space=pltpu.VM...  5.38 us
  transfers between devices with their start and end apart: 7, of which 6 were waited for; matrix products, arithmetic and copies ran while one was open for 5% of the time, Pallas kernels for 3%

profile of v6, /device:TPU:6, one launch (start us, length us, event | category | flops | bytes accessed | tf_op | source)
XLA Modules:
  0.0 189.9 jit_solution(4977823121223940559)
XLA Ops:
  0.6 2.7 %shard_map.94 = bf16[8,2,128,384]{3,2,1,0:T(8,128)(2,1)} custom-call(bf16[128,3072]{1,0:T(8,128)(2,1)} %refs_0_.3, bf16[128,3072]{1,0:T(8,128)(2,1)} %refs_1_.3), custom_call_target="tpu_custom_call" | custom-call | tf_op jit(solution)/shard_map/pallas_call | solution.py:163
  3.4 26.1 %all_to_all.20.own_ref = bf16[8,2,128,384]{3,2,1,0:T(8,128)(2,1)S(1)} all-to-all(bf16[8,2,128,384]{3,2,1,0:T(8,128)(2,1)} %shard_map.94), channel_id=1, replica_groups=mesh['head'=8,'tile'=32] {'head'}, dimensions={0} | all-to-all | bytes 3145728 | tf_op jit(solution)/shard_map/all_to_all | solution.py:183
  29.4 8.0 %collective-permute-start.1 = (bf16[8,2,128,384]{3,2,1,0:T(8,128)(2,1)S(1)}, bf16[8,2,128,384]{3,2,1,0:T(8,128)(2,1)}, u32[]{:S(2)}, u32[]{:S(2)}) collective-permute-start(bf16[8,2,128,384]{3,2,1,0:T(8,128)(2,1)S(1)} %all_to_all.20.own_ref), channel_id=1, source_target_pairs={{1,0},{2,1},{3,2},{4,3},{5,4},{6,5},{7,6},{8,7},{9,8},{10,9},{11,1... | collective-permute-start | bytes 4718600 | tf_op jit(solution)/shard_map/ppermute | solution.py:30
  37.4 1.9 %collective-permute-start = (bf16[8,2,128,384]{3,2,1,0:T(8,128)(2,1)S(1)}, bf16[8,2,128,384]{3,2,1,0:T(8,128)(2,1)}, u32[]{:S(2)}, u32[]{:S(2)}) collective-permute-start(bf16[8,2,128,384]{3,2,1,0:T(8,128)(2,1)S(1)} %all_to_all.20.own_ref), channel_id=1, source_target_pairs={{0,1},{1,2},{2,3},{3,4},{4,5},{5,6},{6,7},{7,8},{8,9},{9,10},{10,1... | collective-permute-start | bytes 4718600 | tf_op jit(solution)/shard_map/ppermute | solution.py:30
  39.4 2.7 %shard_map.93 = bf16[8,2,128,384]{3,2,1,0:T(8,128)(2,1)} custom-call(bf16[128,3072]{1,0:T(8,128)(2,1)} %refs_0_.2, bf16[128,3072]{1,0:T(8,128)(2,1)} %refs_1_.2), custom_call_target="tpu_custom_call" | custom-call | tf_op jit(solution)/shard_map/pallas_call | solution.py:163
  42.0 3.7 %all-to-all-start = ((bf16[8,2,128,384]{3,2,1,0:T(8,128)(2,1)}), bf16[8,2,128,384]{3,2,1,0:T(8,128)(2,1)S(1)}, u32[]{:S(2)}, u32[]{:S(2)}) async-start(bf16[8,2,128,384]{3,2,1,0:T(8,128)(2,1)} %shard_map.93), calls=%async_computation | async-start | bytes 3145728 | tf_op jit(solution)/shard_map/all_to_all | solution.py:183
  46.8 1.9 %gather_fusion.1 = s32[192]{0:T(256)S(1)} fusion(s32[256,256]{1,0:T(8,128)S(1)} %copy-done, s32[192]{0:T(256)S(1)} %reshape.73), kind=kCustom, calls=%fused_computation.1 | custom fusion | bytes 3072 | tf_op jit(solution)/shard_map/gather | solution.py:39
  49.8 1.3 gather_fusion.2
  51.8 15.4 %all-to-all-done.qg_ref = bf16[8,2,128,384]{3,2,1,0:T(8,128)(2,1)S(1)} async-done(((bf16[8,2,128,384]{3,2,1,0:T(8,128)(2,1)}), bf16[8,2,128,384]{3,2,1,0:T(8,128)(2,1)S(1)}, u32[]{:S(2)}, u32[]{:S(2)}) %all-to-all-start) | async-done | bytes 1572896 | tf_op jit(solution)/shard_map/all_to_all | solution.py:183
  67.2 3.5 %collective-permute-done.1.next_ref = bf16[8,2,128,384]{3,2,1,0:T(8,128)(2,1)} collective-permute-done((bf16[8,2,128,384]{3,2,1,0:T(8,128)(2,1)S(1)}, bf16[8,2,128,384]{3,2,1,0:T(8,128)(2,1)}, u32[]{:S(2)}, u32[]{:S(2)}) %collective-permute-start.1) | collective-permute-done | bytes 1572896 | tf_op jit(solution)/shard_map/ppermute | solution.py:30
  70.7 6.3 %collective-permute-done.prev_ref = bf16[8,2,128,384]{3,2,1,0:T(8,128)(2,1)} collective-permute-done((bf16[8,2,128,384]{3,2,1,0:T(8,128)(2,1)S(1)}, bf16[8,2,128,384]{3,2,1,0:T(8,128)(2,1)}, u32[]{:S(2)}, u32[]{:S(2)}) %collective-permute-start) | collective-permute-done | bytes 1572896 | tf_op jit(solution)/shard_map/ppermute | solution.py:30
  77.0 37.7 %shard_map.95 = (bf16[8,2,128,384]{3,2,1,0:T(8,128)(2,1)}, f32[8,2,128,384]{3,2,1,0:T(8,128)}, bf16[8,2,128,384]{3,2,1,0:T(8,128)(2,1)}, bf16[8,2,128,384]{3,2,1,0:T(8,128)(2,1)}) custom-call(s32[8,9]{1,0:T(8,128)} %bitcast.9, s32[8,9]{1,0:T(8,128)} %fusion.live_ref, bf16[8,2,128,384]{3,2,1,0:T(8,128)(2,1)} %copy-done.5, ...), custom_call_target="tpu_custom_call" | custom-call | flops 5435817984 | bytes 12582912 | tf_op jit(solution)/shard_map/pallas_call | solution.py:127
  114.8 1.9 %collective-permute-start.2 = (bf16[8,2,128,384]{3,2,1,0:T(8,128)(2,1)}, bf16[8,2,128,384]{3,2,1,0:T(8,128)(2,1)S(1)}, u32[]{:S(2)}, u32[]{:S(2)}) collective-permute-start(bf16[8,2,128,384]{3,2,1,0:T(8,128)(2,1)} %get-tuple-element.18), channel_id=1, source_target_pairs={{1,0},{2,1},{3,2},{4,3},{5,4},{6,5},{7,6},{8,7},{9,8},{10,9},{11,1... | collective-permute-start | bytes 4718600 | tf_op jit(solution)/shard_map/ppermute | solution.py:30
  116.7 3.9 %collective-permute-start.3 = (bf16[8,2,128,384]{3,2,1,0:T(8,128)(2,1)}, bf16[8,2,128,384]{3,2,1,0:T(8,128)(2,1)}, u32[]{:S(2)}, u32[]{:S(2)}) collective-permute-start(bf16[8,2,128,384]{3,2,1,0:T(8,128)(2,1)} %get-tuple-element.19), channel_id=1, source_target_pairs={{0,1},{1,2},{2,3},{3,4},{4,5},{5,6},{6,7},{7,8},{8,9},{9,10},{10,1... | collective-permute-start | bytes 4718600 | tf_op jit(solution)/shard_map/ppermute | solution.py:30
  120.6 3.6 %all-to-all-start.2 = ((bf16[8,2,128,384]{3,2,1,0:T(8,128)(2,1)}), bf16[8,2,128,384]{3,2,1,0:T(8,128)(2,1)S(1)}, u32[]{:S(2)}, u32[]{:S(2)}) async-start(bf16[8,2,128,384]{3,2,1,0:T(8,128)(2,1)} %get-tuple-element.14), calls=%async_computation.2 | async-start | bytes 3145728 | tf_op jit(solution)/shard_map/all_to_all | solution.py:187
  124.2 27.3 %collective-permute-done.2 = bf16[8,2,128,384]{3,2,1,0:T(8,128)(2,1)S(1)} collective-permute-done((bf16[8,2,128,384]{3,2,1,0:T(8,128)(2,1)}, bf16[8,2,128,384]{3,2,1,0:T(8,128)(2,1)S(1)}, u32[]{:S(2)}, u32[]{:S(2)}) %collective-permute-start.2) | collective-permute-done | bytes 1572896 | tf_op jit(solution)/shard_map/ppermute | solution.py:30
  151.5 4.1 %collective-permute-done.3 = bf16[8,2,128,384]{3,2,1,0:T(8,128)(2,1)} collective-permute-done((bf16[8,2,128,384]{3,2,1,0:T(8,128)(2,1)}, bf16[8,2,128,384]{3,2,1,0:T(8,128)(2,1)}, u32[]{:S(2)}, u32[]{:S(2)}) %collective-permute-start.3) | collective-permute-done | bytes 1572896 | tf_op jit(solution)/shard_map/ppermute | solution.py:30
  155.7 4.2 %add_convert_fusion = bf16[8,2,128,384]{3,2,1,0:T(8,128)(2,1)} fusion(bf16[8,2,128,384]{3,2,1,0:T(8,128)(2,1)} %collective-permute-done.3, f32[8,2,128,384]{3,2,1,0:T(8,128)} %get-tuple-element.17, bf16[8,2,128,384]{3,2,1,0:T(8,128)(2,1)S(1)} %collective-permute-done.2), kind=kLoop, calls=%fused_computation.3 | loop fusion | flops 3932160 | bytes 7864320 | tf_op jit(solution)/shard_map/convert_element_type | solution.py:208
  159.9 1.2 copy-done.2
  161.0 3.6 %all-to-all-start.3 = ((bf16[8,2,128,384]{3,2,1,0:T(8,128)(2,1)}), bf16[8,2,128,384]{3,2,1,0:T(8,128)(2,1)S(1)}, u32[]{:S(2)}, u32[]{:S(2)}) async-start(bf16[8,2,128,384]{3,2,1,0:T(8,128)(2,1)} %add_convert_fusion), calls=%async_computation.3 | async-start | bytes 3145728 | tf_op jit(solution)/shard_map/all_to_all | solution.py:187
  164.6 2.7 %shard_map.96 = (bf16[128,3072]{1,0:T(8,128)(2,1)}, bf16[128,3072]{1,0:T(8,128)(2,1)}) custom-call(bf16[8,2,128,384]{3,2,1,0:T(8,128)(2,1)} %copy-done.2), custom_call_target="tpu_custom_call" | custom-call | tf_op jit(solution)/shard_map/pallas_call | solution.py:173
  167.3 18.8 %all-to-all-done.3.refs_0_ = bf16[8,2,128,384]{3,2,1,0:T(8,128)(2,1)S(1)} async-done(((bf16[8,2,128,384]{3,2,1,0:T(8,128)(2,1)}), bf16[8,2,128,384]{3,2,1,0:T(8,128)(2,1)S(1)}, u32[]{:S(2)}, u32[]{:S(2)}) %all-to-all-start.3) | async-done | bytes 1572896 | tf_op jit(solution)/shard_map/all_to_all | solution.py:187
  186.1 1.2 copy-done.3
  187.2 2.7 %shard_map.97 = (bf16[128,3072]{1,0:T(8,128)(2,1)}, bf16[128,3072]{1,0:T(8,128)(2,1)}) custom-call(bf16[8,2,128,384]{3,2,1,0:T(8,128)(2,1)} %copy-done.3), custom_call_target="tpu_custom_call" | custom-call | tf_op jit(solution)/shard_map/pallas_call | solution.py:173
  (31 shorter events, 2.8 us)
Async XLA Ops:
  0.6 46.1 %copy-start = (s32[256,256]{1,0:T(8,128)S(1)}, s32[256,256]{1,0:T(8,128)}, u32[]{:S(2)}) copy-start(s32[256,256]{1,0:T(8,128)} %param.10) | copy-start | bytes 786436
  29.4 12.6 %copy-start.4 = (bf16[8,2,128,384]{3,2,1,0:T(8,128)(2,1)}, bf16[8,2,128,384]{3,2,1,0:T(8,128)(2,1)S(1)}, u32[]{:S(2)}) copy-start(bf16[8,2,128,384]{3,2,1,0:T(8,128)(2,1)S(1)} %all_to_all.20.own_ref) | copy-start | bytes 4718596
  29.4 41.3 %collective-permute-start.1 = (bf16[8,2,128,384]{3,2,1,0:T(8,128)(2,1)S(1)}, bf16[8,2,128,384]{3,2,1,0:T(8,128)(2,1)}, u32[]{:S(2)}, u32[]{:S(2)}) collective-permute-start(bf16[8,2,128,384]{3,2,1,0:T(8,128)(2,1)S(1)} %all_to_all.20.own_ref), channel_id=1, source_target_pairs={{1,0},{2,1},{3,2},{4,3},{5,4},{6,5},{7,6},{8,7},{9,8},{10,9},{11,1... | collective-permute-start | bytes 4718600 | tf_op jit(solution)/shard_map/ppermute | solution.py:30
  37.4 39.6 %collective-permute-start = (bf16[8,2,128,384]{3,2,1,0:T(8,128)(2,1)S(1)}, bf16[8,2,128,384]{3,2,1,0:T(8,128)(2,1)}, u32[]{:S(2)}, u32[]{:S(2)}) collective-permute-start(bf16[8,2,128,384]{3,2,1,0:T(8,128)(2,1)S(1)} %all_to_all.20.own_ref), channel_id=1, source_target_pairs={{0,1},{1,2},{2,3},{3,4},{4,5},{5,6},{6,7},{7,8},{8,9},{9,10},{10,1... | collective-permute-start | bytes 4718600 | tf_op jit(solution)/shard_map/ppermute | solution.py:30
  42.0 3.8 %copy-start.1 = (s32[256]{0:T(256)S(1)}, s32[256]{0:T(256)}, u32[]{:S(2)}) copy-start(s32[256]{0:T(256)} %param.11) | copy-start | bytes 3076
  42.0 25.2 %all-to-all-start = ((bf16[8,2,128,384]{3,2,1,0:T(8,128)(2,1)}), bf16[8,2,128,384]{3,2,1,0:T(8,128)(2,1)S(1)}, u32[]{:S(2)}, u32[]{:S(2)}) async-start(bf16[8,2,128,384]{3,2,1,0:T(8,128)(2,1)} %shard_map.93), calls=%async_computation | async-start | bytes 3145728 | tf_op jit(solution)/shard_map/all_to_all | solution.py:183
  49.7 1.5 copy-start.6
  67.2 9.8 %copy-start.5 = (bf16[8,2,128,384]{3,2,1,0:T(8,128)(2,1)}, bf16[8,2,128,384]{3,2,1,0:T(8,128)(2,1)S(1)}, u32[]{:S(2)}) copy-start(bf16[8,2,128,384]{3,2,1,0:T(8,128)(2,1)S(1)} %all-to-all-done.qg_ref) | copy-start | bytes 4718596
  114.8 36.7 %collective-permute-start.2 = (bf16[8,2,128,384]{3,2,1,0:T(8,128)(2,1)}, bf16[8,2,128,384]{3,2,1,0:T(8,128)(2,1)S(1)}, u32[]{:S(2)}, u32[]{:S(2)}) collective-permute-start(bf16[8,2,128,384]{3,2,1,0:T(8,128)(2,1)} %get-tuple-element.18), channel_id=1, source_target_pairs={{1,0},{2,1},{3,2},{4,3},{5,4},{6,5},{7,6},{8,7},{9,8},{10,9},{11,1... | collective-permute-start | bytes 4718600 | tf_op jit(solution)/shard_map/ppermute | solution.py:30
  116.7 38.9 %collective-permute-start.3 = (bf16[8,2,128,384]{3,2,1,0:T(8,128)(2,1)}, bf16[8,2,128,384]{3,2,1,0:T(8,128)(2,1)}, u32[]{:S(2)}, u32[]{:S(2)}) collective-permute-start(bf16[8,2,128,384]{3,2,1,0:T(8,128)(2,1)} %get-tuple-element.19), channel_id=1, source_target_pairs={{0,1},{1,2},{2,3},{3,4},{4,5},{5,6},{6,7},{7,8},{8,9},{9,10},{10,1... | collective-permute-start | bytes 4718600 | tf_op jit(solution)/shard_map/ppermute | solution.py:30
  120.6 39.2 %all-to-all-start.2 = ((bf16[8,2,128,384]{3,2,1,0:T(8,128)(2,1)}), bf16[8,2,128,384]{3,2,1,0:T(8,128)(2,1)S(1)}, u32[]{:S(2)}, u32[]{:S(2)}) async-start(bf16[8,2,128,384]{3,2,1,0:T(8,128)(2,1)} %get-tuple-element.14), calls=%async_computation.2 | async-start | bytes 3145728 | tf_op jit(solution)/shard_map/all_to_all | solution.py:187
  159.9 1.2 copy-start.2
  161.0 25.1 %all-to-all-start.3 = ((bf16[8,2,128,384]{3,2,1,0:T(8,128)(2,1)}), bf16[8,2,128,384]{3,2,1,0:T(8,128)(2,1)S(1)}, u32[]{:S(2)}, u32[]{:S(2)}) async-start(bf16[8,2,128,384]{3,2,1,0:T(8,128)(2,1)} %add_convert_fusion), calls=%async_computation.3 | async-start | bytes 3145728 | tf_op jit(solution)/shard_map/all_to_all | solution.py:187
  186.1 1.2 copy-start.3

commit v7 on v6

--- a/solution.py
+++ b/solution.py
@@ -49,7 +49,7 @@
 
 def attn_kernel(
     slot_ref, live_ref, qg_ref, prev_ref, own_ref, next_ref,
-    og_ref, gown_ref, gprev_ref, gnext_ref, kg_scr, vg_scr, acc_scr,
+    og_ref, gown_ref, gprev_ref, gnext_ref, kg_scr, vg_scr, acc_scr, e_scr, pbf_scr, ds_scr,
 ):
     tile_rows = HD
     query_tiles, max_keys = slot_ref.shape
@@ -58,10 +58,8 @@
     acc_scr[...] = jnp.zeros(acc_scr.shape, acc_scr.dtype)
     nt = (((1,), (1,)), ((), ()))
     tn = (((0,), (0,)), ((), ()))
-    lane_slot = lax.broadcasted_iota(jnp.int32, (1, max_keys * tile_rows), 1) // tile_rows
 
     def body(p, carry):
-        live_lane = jnp.zeros((1, max_keys * tile_rows), jnp.int32)
         for s in range(max_keys):
             slot = slot_ref[p, s]
             side = slot // query_tiles
@@ -74,22 +72,39 @@
                     kg_scr[dst, :] = window[w][tile, 0]
                     vg_scr[dst, :] = window[w][tile, 1]
 
-            live_lane = jnp.where(lane_slot == s, live_ref[p, s], live_lane)
         q = qg_ref[p, 0]
         g = qg_ref[p, 1]
         kg = kg_scr[...]
         vg = vg_scr[...]
-        sc = lax.dot_general(q, kg, nt, preferred_element_type=jnp.float32) * scaling
-        sc = jnp.where(live_lane > 0, sc, NEG)
-        top = jnp.max(sc, axis=1, keepdims=True)
-        expd = jnp.exp(sc - top)
-        prob = expd * (1.0 / jnp.sum(expd, axis=1, keepdims=True))
-        prob_bf = prob.astype(jnp.bfloat16)
+        sc = lax.dot_general(q, kg, nt, preferred_element_type=jnp.float32)
+
+        def masked(s):
+            chunk = sc[:, s * tile_rows : (s + 1) * tile_rows] * scaling
+            return jnp.where(live_ref[p, s] > 0, chunk, NEG)
+
+        run_max = masked(0)
+        for s in range(1, max_keys):
+            run_max = jnp.maximum(run_max, masked(s))
+        top = jnp.max(run_max, axis=1, keepdims=True)
+        run_sum = jnp.zeros((tile_rows, tile_rows), jnp.float32)
+        for s in range(max_keys):
+            expd = jnp.exp(masked(s) - top)
+            e_scr[:, s * tile_rows : (s + 1) * tile_rows] = expd
+            run_sum = run_sum + expd
+        inv = 1.0 / jnp.sum(run_sum, axis=1, keepdims=True)
+        for s in range(max_keys):
+            cols = slice(s * tile_rows, (s + 1) * tile_rows)
+            pbf_scr[:, cols] = (e_scr[:, cols] * inv).astype(jnp.bfloat16)
+        prob_bf = pbf_scr[...]
         out = jnp.dot(prob_bf, vg, preferred_element_type=jnp.float32).astype(jnp.bfloat16)
         og_ref[p, 0] = out
         delta = jnp.sum(g.astype(jnp.float32) * out.astype(jnp.float32), axis=1, keepdims=True)
         dprob = lax.dot_general(g, vg, nt, preferred_element_type=jnp.float32)
-        dscore = (prob * (dprob - delta)).astype(jnp.bfloat16)
+        for s in range(max_keys):
+            cols = slice(s * tile_rows, (s + 1) * tile_rows)
+            prob = e_scr[:, cols] * inv
+            ds_scr[:, cols] = (prob * (dprob[:, cols] - delta)).astype(jnp.bfloat16)
+        dscore = ds_scr[...]
         dq = jnp.dot(dscore, kg, preferred_element_type=jnp.float32) * scaling
         og_ref[p, 1] = dq.astype(og_ref.dtype)
         dk_g = lax.dot_general(dscore, q, tn, preferred_element_type=jnp.float32) * scaling
@@ -100,7 +115,7 @@
             acc_scr[slot, 1] += dv_g[s * tile_rows : (s + 1) * tile_rows, :]
         return carry
 
-    lax.fori_loop(0, query_tiles, body, 0, unroll=2)
+    lax.fori_loop(0, query_tiles, body, 0)
     gprev_ref[...] = acc_scr[:query_tiles].astype(gprev_ref.dtype)
     gown_ref[...] = acc_scr[query_tiles : 2 * query_tiles]
     gnext_ref[...] = acc_scr[2 * query_tiles :].astype(gnext_ref.dtype)
@@ -121,6 +136,9 @@
             pltpu.VMEM((max_keys * tile_rows, HD), jnp.bfloat16),
             pltpu.VMEM((max_keys * tile_rows, HD), jnp.bfloat16),
             pltpu.VMEM((3 * query_tiles, count, tile_rows, HD), jnp.float32),
+            pltpu.VMEM((tile_rows, max_keys * tile_rows), jnp.float32),
+            pltpu.VMEM((tile_rows, max_keys * tile_rows), jnp.bfloat16),
+            pltpu.VMEM((tile_rows, max_keys * tile_rows), jnp.bfloat16),
         ],
     )
     block = qg.shape

time: 191 us -> 192 us (level)
  no operation moved by 1% of the time
where the time goes in v7:
time: 192 us; the launch traced here: 191 us
  waiting for transfers between devices  75.4 us (39%)
  Pallas kernels  49.9 us (26%)
  starting transfers between devices  26.7 us (14%)
  blocking collectives  26.1 us (14%)
  local copies, waits for them, and re-layouts  6.73 us (4%)
  other arithmetic  5.79 us (3%)
    ppermute x4, waiting for transfers between devices, passed_along(): lax.ppermute(value, axis, [(source, source + steps) for source in range(i...  41.2 us
    pallas_call x1, Pallas kernels, attention_heads(): pl.pallas_call(attn_kernel, grid_spec=grid_spec, out_shape=[jax.ShapeDtyp...  39.2 us
    all_to_all x1, blocking collectives, to_heads(): lax.all_to_all(stacked, 'head', split_axis=0, concat_axis=0, tiled=True)  26.1 us
    all_to_all x2, waiting for transfers between devices, to_tokens(): lax.all_to_all(stacked, 'head', split_axis=0, concat_axis=0, tiled=True)  18.8 us
    ppermute x4, starting transfers between devices, passed_along(): lax.ppermute(value, axis, [(source, source + steps) for source in range(i...  15.8 us
    all_to_all x1, waiting for transfers between devices, to_heads(): lax.all_to_all(stacked, 'head', split_axis=0, concat_axis=0, tiled=True)  15.4 us
    all_to_all x2, starting transfers between devices, to_tokens(): lax.all_to_all(stacked, 'head', split_axis=0, concat_axis=0, tiled=True)  7.17 us
    pallas_call x2, Pallas kernels, split_columns(): pl.pallas_call(split_kernel, in_specs=[pl.BlockSpec(memory_space=pltpu.VM...  5.38 us
  transfers between devices with their start and end apart: 7, of which 6 were waited for; matrix products, arithmetic and copies ran while one was open for 5% of the time, Pallas kernels for 3%

profile of v7, /device:TPU:6, one launch (start us, length us, event | category | flops | bytes accessed | tf_op | source)
XLA Modules:
  0.0 191.4 jit_solution(8810860628385065819)
XLA Ops:
  0.6 2.7 %shard_map.94 = bf16[8,2,128,384]{3,2,1,0:T(8,128)(2,1)} custom-call(bf16[128,3072]{1,0:T(8,128)(2,1)} %refs_0_.3, bf16[128,3072]{1,0:T(8,128)(2,1)} %refs_1_.3), custom_call_target="tpu_custom_call" | custom-call | tf_op jit(solution)/shard_map/pallas_call | solution.py:181
  3.4 26.1 %all_to_all.20.own_ref = bf16[8,2,128,384]{3,2,1,0:T(8,128)(2,1)S(1)} all-to-all(bf16[8,2,128,384]{3,2,1,0:T(8,128)(2,1)} %shard_map.94), channel_id=1, replica_groups=mesh['head'=8,'tile'=32] {'head'}, dimensions={0} | all-to-all | bytes 3145728 | tf_op jit(solution)/shard_map/all_to_all | solution.py:201
  29.4 8.0 %collective-permute-start.1 = (bf16[8,2,128,384]{3,2,1,0:T(8,128)(2,1)S(1)}, bf16[8,2,128,384]{3,2,1,0:T(8,128)(2,1)}, u32[]{:S(2)}, u32[]{:S(2)}) collective-permute-start(bf16[8,2,128,384]{3,2,1,0:T(8,128)(2,1)S(1)} %all_to_all.20.own_ref), channel_id=1, source_target_pairs={{1,0},{2,1},{3,2},{4,3},{5,4},{6,5},{7,6},{8,7},{9,8},{10,9},{11,1... | collective-permute-start | bytes 4718600 | tf_op jit(solution)/shard_map/ppermute | solution.py:30
  37.4 1.9 %collective-permute-start = (bf16[8,2,128,384]{3,2,1,0:T(8,128)(2,1)S(1)}, bf16[8,2,128,384]{3,2,1,0:T(8,128)(2,1)}, u32[]{:S(2)}, u32[]{:S(2)}) collective-permute-start(bf16[8,2,128,384]{3,2,1,0:T(8,128)(2,1)S(1)} %all_to_all.20.own_ref), channel_id=1, source_target_pairs={{0,1},{1,2},{2,3},{3,4},{4,5},{5,6},{6,7},{7,8},{8,9},{9,10},{10,1... | collective-permute-start | bytes 4718600 | tf_op jit(solution)/shard_map/ppermute | solution.py:30
  39.4 2.7 %shard_map.93 = bf16[8,2,128,384]{3,2,1,0:T(8,128)(2,1)} custom-call(bf16[128,3072]{1,0:T(8,128)(2,1)} %refs_0_.2, bf16[128,3072]{1,0:T(8,128)(2,1)} %refs_1_.2), custom_call_target="tpu_custom_call" | custom-call | tf_op jit(solution)/shard_map/pallas_call | solution.py:181
  42.0 3.7 %all-to-all-start = ((bf16[8,2,128,384]{3,2,1,0:T(8,128)(2,1)}), bf16[8,2,128,384]{3,2,1,0:T(8,128)(2,1)S(1)}, u32[]{:S(2)}, u32[]{:S(2)}) async-start(bf16[8,2,128,384]{3,2,1,0:T(8,128)(2,1)} %shard_map.93), calls=%async_computation | async-start | bytes 3145728 | tf_op jit(solution)/shard_map/all_to_all | solution.py:201
  46.8 1.9 gather_fusion.1
  49.8 1.3 gather_fusion.2
  51.8 15.4 %all-to-all-done.qg_ref = bf16[8,2,128,384]{3,2,1,0:T(8,128)(2,1)S(1)} async-done(((bf16[8,2,128,384]{3,2,1,0:T(8,128)(2,1)}), bf16[8,2,128,384]{3,2,1,0:T(8,128)(2,1)S(1)}, u32[]{:S(2)}, u32[]{:S(2)}) %all-to-all-start) | async-done | bytes 1572896 | tf_op jit(solution)/shard_map/all_to_all | solution.py:201
  67.2 3.5 %collective-permute-done.1.next_ref = bf16[8,2,128,384]{3,2,1,0:T(8,128)(2,1)} collective-permute-done((bf16[8,2,128,384]{3,2,1,0:T(8,128)(2,1)S(1)}, bf16[8,2,128,384]{3,2,1,0:T(8,128)(2,1)}, u32[]{:S(2)}, u32[]{:S(2)}) %collective-permute-start.1) | collective-permute-done | bytes 1572896 | tf_op jit(solution)/shard_map/ppermute | solution.py:30
  70.7 6.3 %collective-permute-done.prev_ref = bf16[8,2,128,384]{3,2,1,0:T(8,128)(2,1)} collective-permute-done((bf16[8,2,128,384]{3,2,1,0:T(8,128)(2,1)S(1)}, bf16[8,2,128,384]{3,2,1,0:T(8,128)(2,1)}, u32[]{:S(2)}, u32[]{:S(2)}) %collective-permute-start) | collective-permute-done | bytes 1572896 | tf_op jit(solution)/shard_map/ppermute | solution.py:30
  77.0 39.2 %shard_map.95 = (bf16[8,2,128,384]{3,2,1,0:T(8,128)(2,1)}, f32[8,2,128,384]{3,2,1,0:T(8,128)}, bf16[8,2,128,384]{3,2,1,0:T(8,128)(2,1)}, bf16[8,2,128,384]{3,2,1,0:T(8,128)(2,1)}) custom-call(s32[8,9]{1,0:T(8,128)} %bitcast.9, s32[8,9]{1,0:T(8,128)} %fusion.live_ref, bf16[8,2,128,384]{3,2,1,0:T(8,128)(2,1)} %copy-done.5, ...), custom_call_target="tpu_custom_call" | custom-call | flops 5435817984 | bytes 12582912 | tf_op jit(solution)/shard_map/pallas_call | solution.py:145
  116.3 1.9 collective-permute-start.2
  118.2 3.9 %collective-permute-start.3 = (bf16[8,2,128,384]{3,2,1,0:T(8,128)(2,1)}, bf16[8,2,128,384]{3,2,1,0:T(8,128)(2,1)}, u32[]{:S(2)}, u32[]{:S(2)}) collective-permute-start(bf16[8,2,128,384]{3,2,1,0:T(8,128)(2,1)} %get-tuple-element.19), channel_id=1, source_target_pairs={{0,1},{1,2},{2,3},{3,4},{4,5},{5,6},{6,7},{7,8},{8,9},{9,10},{10,1... | collective-permute-start | bytes 4718600 | tf_op jit(solution)/shard_map/ppermute | solution.py:30
  122.1 3.6 %all-to-all-start.2 = ((bf16[8,2,128,384]{3,2,1,0:T(8,128)(2,1)}), bf16[8,2,128,384]{3,2,1,0:T(8,128)(2,1)S(1)}, u32[]{:S(2)}, u32[]{:S(2)}) async-start(bf16[8,2,128,384]{3,2,1,0:T(8,128)(2,1)} %get-tuple-element.14), calls=%async_computation.2 | async-start | bytes 3145728 | tf_op jit(solution)/shard_map/all_to_all | solution.py:205
  125.7 27.3 %collective-permute-done.2 = bf16[8,2,128,384]{3,2,1,0:T(8,128)(2,1)S(1)} collective-permute-done((bf16[8,2,128,384]{3,2,1,0:T(8,128)(2,1)}, bf16[8,2,128,384]{3,2,1,0:T(8,128)(2,1)S(1)}, u32[]{:S(2)}, u32[]{:S(2)}) %collective-permute-start.2) | collective-permute-done | bytes 1572896 | tf_op jit(solution)/shard_map/ppermute | solution.py:30
  153.0 4.1 %collective-permute-done.3 = bf16[8,2,128,384]{3,2,1,0:T(8,128)(2,1)} collective-permute-done((bf16[8,2,128,384]{3,2,1,0:T(8,128)(2,1)}, bf16[8,2,128,384]{3,2,1,0:T(8,128)(2,1)}, u32[]{:S(2)}, u32[]{:S(2)}) %collective-permute-start.3) | collective-permute-done | bytes 1572896 | tf_op jit(solution)/shard_map/ppermute | solution.py:30
  157.1 4.2 %add_convert_fusion = bf16[8,2,128,384]{3,2,1,0:T(8,128)(2,1)} fusion(bf16[8,2,128,384]{3,2,1,0:T(8,128)(2,1)} %collective-permute-done.3, f32[8,2,128,384]{3,2,1,0:T(8,128)} %get-tuple-element.17, bf16[8,2,128,384]{3,2,1,0:T(8,128)(2,1)S(1)} %collective-permute-done.2), kind=kLoop, calls=%fused_computation.3 | loop fusion | flops 3932160 | bytes 7864320 | tf_op jit(solution)/shard_map/convert_element_type | solution.py:226
  161.3 1.2 copy-done.2
  162.5 3.6 %all-to-all-start.3 = ((bf16[8,2,128,384]{3,2,1,0:T(8,128)(2,1)}), bf16[8,2,128,384]{3,2,1,0:T(8,128)(2,1)S(1)}, u32[]{:S(2)}, u32[]{:S(2)}) async-start(bf16[8,2,128,384]{3,2,1,0:T(8,128)(2,1)} %add_convert_fusion), calls=%async_computation.3 | async-start | bytes 3145728 | tf_op jit(solution)/shard_map/all_to_all | solution.py:205
  166.1 2.7 %shard_map.96 = (bf16[128,3072]{1,0:T(8,128)(2,1)}, bf16[128,3072]{1,0:T(8,128)(2,1)}) custom-call(bf16[8,2,128,384]{3,2,1,0:T(8,128)(2,1)} %copy-done.2), custom_call_target="tpu_custom_call" | custom-call | tf_op jit(solution)/shard_map/pallas_call | solution.py:191
  168.8 18.8 %all-to-all-done.3.refs_0_ = bf16[8,2,128,384]{3,2,1,0:T(8,128)(2,1)S(1)} async-done(((bf16[8,2,128,384]{3,2,1,0:T(8,128)(2,1)}), bf16[8,2,128,384]{3,2,1,0:T(8,128)(2,1)S(1)}, u32[]{:S(2)}, u32[]{:S(2)}) %all-to-all-start.3) | async-done | bytes 1572896 | tf_op jit(solution)/shard_map/all_to_all | solution.py:205
  187.6 1.2 copy-done.3
  188.7 2.7 %shard_map.97 = (bf16[128,3072]{1,0:T(8,128)(2,1)}, bf16[128,3072]{1,0:T(8,128)(2,1)}) custom-call(bf16[8,2,128,384]{3,2,1,0:T(8,128)(2,1)} %copy-done.3), custom_call_target="tpu_custom_call" | custom-call | tf_op jit(solution)/shard_map/pallas_call | solution.py:191
  (31 shorter events, 2.8 us)
Async XLA Ops:
  0.6 46.1 %copy-start = (s32[256,256]{1,0:T(8,128)S(1)}, s32[256,256]{1,0:T(8,128)}, u32[]{:S(2)}) copy-start(s32[256,256]{1,0:T(8,128)} %param.10) | copy-start | bytes 786436
  29.4 12.6 %copy-start.4 = (bf16[8,2,128,384]{3,2,1,0:T(8,128)(2,1)}, bf16[8,2,128,384]{3,2,1,0:T(8,128)(2,1)S(1)}, u32[]{:S(2)}) copy-start(bf16[8,2,128,384]{3,2,1,0:T(8,128)(2,1)S(1)} %all_to_all.20.own_ref) | copy-start | bytes 4718596
  29.4 41.3 %collective-permute-start.1 = (bf16[8,2,128,384]{3,2,1,0:T(8,128)(2,1)S(1)}, bf16[8,2,128,384]{3,2,1,0:T(8,128)(2,1)}, u32[]{:S(2)}, u32[]{:S(2)}) collective-permute-start(bf16[8,2,128,384]{3,2,1,0:T(8,128)(2,1)S(1)} %all_to_all.20.own_ref), channel_id=1, source_target_pairs={{1,0},{2,1},{3,2},{4,3},{5,4},{6,5},{7,6},{8,7},{9,8},{10,9},{11,1... | collective-permute-start | bytes 4718600 | tf_op jit(solution)/shard_map/ppermute | solution.py:30
  37.4 39.6 %collective-permute-start = (bf16[8,2,128,384]{3,2,1,0:T(8,128)(2,1)S(1)}, bf16[8,2,128,384]{3,2,1,0:T(8,128)(2,1)}, u32[]{:S(2)}, u32[]{:S(2)}) collective-permute-start(bf16[8,2,128,384]{3,2,1,0:T(8,128)(2,1)S(1)} %all_to_all.20.own_ref), channel_id=1, source_target_pairs={{0,1},{1,2},{2,3},{3,4},{4,5},{5,6},{6,7},{7,8},{8,9},{9,10},{10,1... | collective-permute-start | bytes 4718600 | tf_op jit(solution)/shard_map/ppermute | solution.py:30
  42.0 3.8 %copy-start.1 = (s32[256]{0:T(256)S(1)}, s32[256]{0:T(256)}, u32[]{:S(2)}) copy-start(s32[256]{0:T(256)} %param.11) | copy-start | bytes 3076
  42.0 25.2 %all-to-all-start = ((bf16[8,2,128,384]{3,2,1,0:T(8,128)(2,1)}), bf16[8,2,128,384]{3,2,1,0:T(8,128)(2,1)S(1)}, u32[]{:S(2)}, u32[]{:S(2)}) async-start(bf16[8,2,128,384]{3,2,1,0:T(8,128)(2,1)} %shard_map.93), calls=%async_computation | async-start | bytes 3145728 | tf_op jit(solution)/shard_map/all_to_all | solution.py:201
  49.7 1.5 copy-start.6
  67.2 9.8 %copy-start.5 = (bf16[8,2,128,384]{3,2,1,0:T(8,128)(2,1)}, bf16[8,2,128,384]{3,2,1,0:T(8,128)(2,1)S(1)}, u32[]{:S(2)}) copy-start(bf16[8,2,128,384]{3,2,1,0:T(8,128)(2,1)S(1)} %all-to-all-done.qg_ref) | copy-start | bytes 4718596
  116.3 36.7 %collective-permute-start.2 = (bf16[8,2,128,384]{3,2,1,0:T(8,128)(2,1)}, bf16[8,2,128,384]{3,2,1,0:T(8,128)(2,1)S(1)}, u32[]{:S(2)}, u32[]{:S(2)}) collective-permute-start(bf16[8,2,128,384]{3,2,1,0:T(8,128)(2,1)} %get-tuple-element.18), channel_id=1, source_target_pairs={{1,0},{2,1},{3,2},{4,3},{5,4},{6,5},{7,6},{8,7},{9,8},{10,9},{11,1... | collective-permute-start | bytes 4718600 | tf_op jit(solution)/shard_map/ppermute | solution.py:30
  118.2 39.0 %collective-permute-start.3 = (bf16[8,2,128,384]{3,2,1,0:T(8,128)(2,1)}, bf16[8,2,128,384]{3,2,1,0:T(8,128)(2,1)}, u32[]{:S(2)}, u32[]{:S(2)}) collective-permute-start(bf16[8,2,128,384]{3,2,1,0:T(8,128)(2,1)} %get-tuple-element.19), channel_id=1, source_target_pairs={{0,1},{1,2},{2,3},{3,4},{4,5},{5,6},{6,7},{7,8},{8,9},{9,10},{10,1... | collective-permute-start | bytes 4718600 | tf_op jit(solution)/shard_map/ppermute | solution.py:30
  122.1 39.2 %all-to-all-start.2 = ((bf16[8,2,128,384]{3,2,1,0:T(8,128)(2,1)}), bf16[8,2,128,384]{3,2,1,0:T(8,128)(2,1)S(1)}, u32[]{:S(2)}, u32[]{:S(2)}) async-start(bf16[8,2,128,384]{3,2,1,0:T(8,128)(2,1)} %get-tuple-element.14), calls=%async_computation.2 | async-start | bytes 3145728 | tf_op jit(solution)/shard_map/all_to_all | solution.py:205
  161.3 1.2 copy-start.2
  162.5 25.1 %all-to-all-start.3 = ((bf16[8,2,128,384]{3,2,1,0:T(8,128)(2,1)}), bf16[8,2,128,384]{3,2,1,0:T(8,128)(2,1)S(1)}, u32[]{:S(2)}, u32[]{:S(2)}) async-start(bf16[8,2,128,384]{3,2,1,0:T(8,128)(2,1)} %add_convert_fusion), calls=%async_computation.3 | async-start | bytes 3145728 | tf_op jit(solution)/shard_map/all_to_all | solution.py:205
  187.5 1.2 copy-start.3

commit v8 on v6

--- a/solution.py
+++ b/solution.py
@@ -67,12 +67,11 @@
             side = slot // query_tiles
             tile = slot % query_tiles
             dst = slice(s * tile_rows, (s + 1) * tile_rows)
-            for w in range(3):
-
-                @pl.when(side == w)
-                def _():
-                    kg_scr[dst, :] = window[w][tile, 0]
-                    vg_scr[dst, :] = window[w][tile, 1]
+            for i, buf in ((0, kg_scr), (1, vg_scr)):
+                picked = window[0][tile, i]
+                for w in (1, 2):
+                    picked = jnp.where(side == w, window[w][tile, i], picked)
+                buf[dst, :] = picked
 
             live_lane = jnp.where(lane_slot == s, live_ref[p, s], live_lane)
         q = qg_ref[p, 0]

time: 191 us -> 188 us (0.984)
  Pallas kernels: 48.5 us -> 45.8 us
    pallas_call x1, Pallas kernels: 37.7 us -> 35.1 us  [attention_heads(): pl.pallas_call(attn_kernel, grid_spec=grid_spec, out_shape=[jax.ShapeDtyp...]
where the time goes in v8:
time: 188 us; the launch traced here: 187 us
  waiting for transfers between devices  75.4 us (40%)
  Pallas kernels  45.8 us (24%)
  starting transfers between devices  26.7 us (14%)
  blocking collectives  26.1 us (14%)
  local copies, waits for them, and re-layouts  6.73 us (4%)
  other arithmetic  5.79 us (3%)
    ppermute x4, waiting for transfers between devices, passed_along(): lax.ppermute(value, axis, [(source, source + steps) for source in range(i...  41.2 us
    pallas_call x1, Pallas kernels, attention_heads(): pl.pallas_call(attn_kernel, grid_spec=grid_spec, out_shape=[jax.ShapeDtyp...  35.1 us
    all_to_all x1, blocking collectives, to_heads(): lax.all_to_all(stacked, 'head', split_axis=0, concat_axis=0, tiled=True)  26.1 us
    all_to_all x2, waiting for transfers between devices, to_tokens(): lax.all_to_all(stacked, 'head', split_axis=0, concat_axis=0, tiled=True)  18.8 us
    ppermute x4, starting transfers between devices, passed_along(): lax.ppermute(value, axis, [(source, source + steps) for source in range(i...  15.8 us
    all_to_all x1, waiting for transfers between devices, to_heads(): lax.all_to_all(stacked, 'head', split_axis=0, concat_axis=0, tiled=True)  15.4 us
    all_to_all x2, starting transfers between devices, to_tokens(): lax.all_to_all(stacked, 'head', split_axis=0, concat_axis=0, tiled=True)  7.17 us
    pallas_call x2, Pallas kernels, split_columns(): pl.pallas_call(split_kernel, in_specs=[pl.BlockSpec(memory_space=pltpu.VM...  5.38 us
  transfers between devices with their start and end apart: 7, of which 6 were waited for; matrix products, arithmetic and copies ran while one was open for 5% of the time, Pallas kernels for 3%

profile of v8, /device:TPU:6, one launch (start us, length us, event | category | flops | bytes accessed | tf_op | source)
XLA Modules:
  0.0 187.3 jit_solution(15710149194382176391)
XLA Ops:
  0.6 2.7 %shard_map.94 = bf16[8,2,128,384]{3,2,1,0:T(8,128)(2,1)} custom-call(bf16[128,3072]{1,0:T(8,128)(2,1)} %refs_0_.3, bf16[128,3072]{1,0:T(8,128)(2,1)} %refs_1_.3), custom_call_target="tpu_custom_call" | custom-call | tf_op jit(solution)/shard_map/pallas_call | solution.py:162
  3.4 26.1 %all_to_all.20.own_ref = bf16[8,2,128,384]{3,2,1,0:T(8,128)(2,1)S(1)} all-to-all(bf16[8,2,128,384]{3,2,1,0:T(8,128)(2,1)} %shard_map.94), channel_id=1, replica_groups=mesh['head'=8,'tile'=32] {'head'}, dimensions={0} | all-to-all | bytes 3145728 | tf_op jit(solution)/shard_map/all_to_all | solution.py:182
  29.4 8.0 %collective-permute-start.1 = (bf16[8,2,128,384]{3,2,1,0:T(8,128)(2,1)S(1)}, bf16[8,2,128,384]{3,2,1,0:T(8,128)(2,1)}, u32[]{:S(2)}, u32[]{:S(2)}) collective-permute-start(bf16[8,2,128,384]{3,2,1,0:T(8,128)(2,1)S(1)} %all_to_all.20.own_ref), channel_id=1, source_target_pairs={{1,0},{2,1},{3,2},{4,3},{5,4},{6,5},{7,6},{8,7},{9,8},{10,9},{11,1... | collective-permute-start | bytes 4718600 | tf_op jit(solution)/shard_map/ppermute | solution.py:30
  37.4 1.9 %collective-permute-start = (bf16[8,2,128,384]{3,2,1,0:T(8,128)(2,1)S(1)}, bf16[8,2,128,384]{3,2,1,0:T(8,128)(2,1)}, u32[]{:S(2)}, u32[]{:S(2)}) collective-permute-start(bf16[8,2,128,384]{3,2,1,0:T(8,128)(2,1)S(1)} %all_to_all.20.own_ref), channel_id=1, source_target_pairs={{0,1},{1,2},{2,3},{3,4},{4,5},{5,6},{6,7},{7,8},{8,9},{9,10},{10,1... | collective-permute-start | bytes 4718600 | tf_op jit(solution)/shard_map/ppermute | solution.py:30
  39.4 2.7 %shard_map.93 = bf16[8,2,128,384]{3,2,1,0:T(8,128)(2,1)} custom-call(bf16[128,3072]{1,0:T(8,128)(2,1)} %refs_0_.2, bf16[128,3072]{1,0:T(8,128)(2,1)} %refs_1_.2), custom_call_target="tpu_custom_call" | custom-call | tf_op jit(solution)/shard_map/pallas_call | solution.py:162
  42.0 3.7 %all-to-all-start = ((bf16[8,2,128,384]{3,2,1,0:T(8,128)(2,1)}), bf16[8,2,128,384]{3,2,1,0:T(8,128)(2,1)S(1)}, u32[]{:S(2)}, u32[]{:S(2)}) async-start(bf16[8,2,128,384]{3,2,1,0:T(8,128)(2,1)} %shard_map.93), calls=%async_computation | async-start | bytes 3145728 | tf_op jit(solution)/shard_map/all_to_all | solution.py:182
  46.8 1.9 %gather_fusion.1 = s32[192]{0:T(256)S(1)} fusion(s32[256,256]{1,0:T(8,128)S(1)} %copy-done, s32[192]{0:T(256)S(1)} %reshape.73), kind=kCustom, calls=%fused_computation.1 | custom fusion | bytes 3072 | tf_op jit(solution)/shard_map/gather | solution.py:39
  49.8 1.3 gather_fusion.2
  51.8 15.4 %all-to-all-done.qg_ref = bf16[8,2,128,384]{3,2,1,0:T(8,128)(2,1)S(1)} async-done(((bf16[8,2,128,384]{3,2,1,0:T(8,128)(2,1)}), bf16[8,2,128,384]{3,2,1,0:T(8,128)(2,1)S(1)}, u32[]{:S(2)}, u32[]{:S(2)}) %all-to-all-start) | async-done | bytes 1572896 | tf_op jit(solution)/shard_map/all_to_all | solution.py:182
  67.2 3.5 %collective-permute-done.1.next_ref = bf16[8,2,128,384]{3,2,1,0:T(8,128)(2,1)} collective-permute-done((bf16[8,2,128,384]{3,2,1,0:T(8,128)(2,1)S(1)}, bf16[8,2,128,384]{3,2,1,0:T(8,128)(2,1)}, u32[]{:S(2)}, u32[]{:S(2)}) %collective-permute-start.1) | collective-permute-done | bytes 1572896 | tf_op jit(solution)/shard_map/ppermute | solution.py:30
  70.7 6.3 %collective-permute-done.prev_ref = bf16[8,2,128,384]{3,2,1,0:T(8,128)(2,1)} collective-permute-done((bf16[8,2,128,384]{3,2,1,0:T(8,128)(2,1)S(1)}, bf16[8,2,128,384]{3,2,1,0:T(8,128)(2,1)}, u32[]{:S(2)}, u32[]{:S(2)}) %collective-permute-start) | collective-permute-done | bytes 1572896 | tf_op jit(solution)/shard_map/ppermute | solution.py:30
  77.0 35.1 %shard_map.95 = (bf16[8,2,128,384]{3,2,1,0:T(8,128)(2,1)}, f32[8,2,128,384]{3,2,1,0:T(8,128)}, bf16[8,2,128,384]{3,2,1,0:T(8,128)(2,1)}, bf16[8,2,128,384]{3,2,1,0:T(8,128)(2,1)}) custom-call(s32[8,9]{1,0:T(8,128)} %bitcast.9, s32[8,9]{1,0:T(8,128)} %fusion.live_ref, bf16[8,2,128,384]{3,2,1,0:T(8,128)(2,1)} %copy-done.5, ...), custom_call_target="tpu_custom_call" | custom-call | flops 5435817984 | bytes 12582912 | tf_op jit(solution)/shard_map/pallas_call | solution.py:126
  112.2 1.9 %collective-permute-start.2 = (bf16[8,2,128,384]{3,2,1,0:T(8,128)(2,1)}, bf16[8,2,128,384]{3,2,1,0:T(8,128)(2,1)S(1)}, u32[]{:S(2)}, u32[]{:S(2)}) collective-permute-start(bf16[8,2,128,384]{3,2,1,0:T(8,128)(2,1)} %get-tuple-element.18), channel_id=1, source_target_pairs={{1,0},{2,1},{3,2},{4,3},{5,4},{6,5},{7,6},{8,7},{9,8},{10,9},{11,1... | collective-permute-start | bytes 4718600 | tf_op jit(solution)/shard_map/ppermute | solution.py:30
  114.1 3.9 %collective-permute-start.3 = (bf16[8,2,128,384]{3,2,1,0:T(8,128)(2,1)}, bf16[8,2,128,384]{3,2,1,0:T(8,128)(2,1)}, u32[]{:S(2)}, u32[]{:S(2)}) collective-permute-start(bf16[8,2,128,384]{3,2,1,0:T(8,128)(2,1)} %get-tuple-element.19), channel_id=1, source_target_pairs={{0,1},{1,2},{2,3},{3,4},{4,5},{5,6},{6,7},{7,8},{8,9},{9,10},{10,1... | collective-permute-start | bytes 4718600 | tf_op jit(solution)/shard_map/ppermute | solution.py:30
  118.0 3.6 %all-to-all-start.2 = ((bf16[8,2,128,384]{3,2,1,0:T(8,128)(2,1)}), bf16[8,2,128,384]{3,2,1,0:T(8,128)(2,1)S(1)}, u32[]{:S(2)}, u32[]{:S(2)}) async-start(bf16[8,2,128,384]{3,2,1,0:T(8,128)(2,1)} %get-tuple-element.14), calls=%async_computation.2 | async-start | bytes 3145728 | tf_op jit(solution)/shard_map/all_to_all | solution.py:186
  121.6 27.3 %collective-permute-done.2 = bf16[8,2,128,384]{3,2,1,0:T(8,128)(2,1)S(1)} collective-permute-done((bf16[8,2,128,384]{3,2,1,0:T(8,128)(2,1)}, bf16[8,2,128,384]{3,2,1,0:T(8,128)(2,1)S(1)}, u32[]{:S(2)}, u32[]{:S(2)}) %collective-permute-start.2) | collective-permute-done | bytes 1572896 | tf_op jit(solution)/shard_map/ppermute | solution.py:30
  148.9 4.1 %collective-permute-done.3 = bf16[8,2,128,384]{3,2,1,0:T(8,128)(2,1)} collective-permute-done((bf16[8,2,128,384]{3,2,1,0:T(8,128)(2,1)}, bf16[8,2,128,384]{3,2,1,0:T(8,128)(2,1)}, u32[]{:S(2)}, u32[]{:S(2)}) %collective-permute-start.3) | collective-permute-done | bytes 1572896 | tf_op jit(solution)/shard_map/ppermute | solution.py:30
  153.0 4.2 %add_convert_fusion = bf16[8,2,128,384]{3,2,1,0:T(8,128)(2,1)} fusion(bf16[8,2,128,384]{3,2,1,0:T(8,128)(2,1)} %collective-permute-done.3, f32[8,2,128,384]{3,2,1,0:T(8,128)} %get-tuple-element.17, bf16[8,2,128,384]{3,2,1,0:T(8,128)(2,1)S(1)} %collective-permute-done.2), kind=kLoop, calls=%fused_computation.3 | loop fusion | flops 3932160 | bytes 7864320 | tf_op jit(solution)/shard_map/convert_element_type | solution.py:207
  157.2 1.2 copy-done.2
  158.4 3.6 %all-to-all-start.3 = ((bf16[8,2,128,384]{3,2,1,0:T(8,128)(2,1)}), bf16[8,2,128,384]{3,2,1,0:T(8,128)(2,1)S(1)}, u32[]{:S(2)}, u32[]{:S(2)}) async-start(bf16[8,2,128,384]{3,2,1,0:T(8,128)(2,1)} %add_convert_fusion), calls=%async_computation.3 | async-start | bytes 3145728 | tf_op jit(solution)/shard_map/all_to_all | solution.py:186
  162.0 2.7 %shard_map.96 = (bf16[128,3072]{1,0:T(8,128)(2,1)}, bf16[128,3072]{1,0:T(8,128)(2,1)}) custom-call(bf16[8,2,128,384]{3,2,1,0:T(8,128)(2,1)} %copy-done.2), custom_call_target="tpu_custom_call" | custom-call | tf_op jit(solution)/shard_map/pallas_call | solution.py:172
  164.6 18.8 %all-to-all-done.3.refs_0_ = bf16[8,2,128,384]{3,2,1,0:T(8,128)(2,1)S(1)} async-done(((bf16[8,2,128,384]{3,2,1,0:T(8,128)(2,1)}), bf16[8,2,128,384]{3,2,1,0:T(8,128)(2,1)S(1)}, u32[]{:S(2)}, u32[]{:S(2)}) %all-to-all-start.3) | async-done | bytes 1572896 | tf_op jit(solution)/shard_map/all_to_all | solution.py:186
  183.4 1.2 copy-done.3
  184.6 2.7 %shard_map.97 = (bf16[128,3072]{1,0:T(8,128)(2,1)}, bf16[128,3072]{1,0:T(8,128)(2,1)}) custom-call(bf16[8,2,128,384]{3,2,1,0:T(8,128)(2,1)} %copy-done.3), custom_call_target="tpu_custom_call" | custom-call | tf_op jit(solution)/shard_map/pallas_call | solution.py:172
  (31 shorter events, 2.8 us)
Async XLA Ops:
  0.6 46.1 %copy-start = (s32[256,256]{1,0:T(8,128)S(1)}, s32[256,256]{1,0:T(8,128)}, u32[]{:S(2)}) copy-start(s32[256,256]{1,0:T(8,128)} %param.10) | copy-start | bytes 786436
  29.4 12.6 %copy-start.4 = (bf16[8,2,128,384]{3,2,1,0:T(8,128)(2,1)}, bf16[8,2,128,384]{3,2,1,0:T(8,128)(2,1)S(1)}, u32[]{:S(2)}) copy-start(bf16[8,2,128,384]{3,2,1,0:T(8,128)(2,1)S(1)} %all_to_all.20.own_ref) | copy-start | bytes 4718596
  29.4 41.3 %collective-permute-start.1 = (bf16[8,2,128,384]{3,2,1,0:T(8,128)(2,1)S(1)}, bf16[8,2,128,384]{3,2,1,0:T(8,128)(2,1)}, u32[]{:S(2)}, u32[]{:S(2)}) collective-permute-start(bf16[8,2,128,384]{3,2,1,0:T(8,128)(2,1)S(1)} %all_to_all.20.own_ref), channel_id=1, source_target_pairs={{1,0},{2,1},{3,2},{4,3},{5,4},{6,5},{7,6},{8,7},{9,8},{10,9},{11,1... | collective-permute-start | bytes 4718600 | tf_op jit(solution)/shard_map/ppermute | solution.py:30
  37.4 39.6 %collective-permute-start = (bf16[8,2,128,384]{3,2,1,0:T(8,128)(2,1)S(1)}, bf16[8,2,128,384]{3,2,1,0:T(8,128)(2,1)}, u32[]{:S(2)}, u32[]{:S(2)}) collective-permute-start(bf16[8,2,128,384]{3,2,1,0:T(8,128)(2,1)S(1)} %all_to_all.20.own_ref), channel_id=1, source_target_pairs={{0,1},{1,2},{2,3},{3,4},{4,5},{5,6},{6,7},{7,8},{8,9},{9,10},{10,1... | collective-permute-start | bytes 4718600 | tf_op jit(solution)/shard_map/ppermute | solution.py:30
  42.0 3.8 %copy-start.1 = (s32[256]{0:T(256)S(1)}, s32[256]{0:T(256)}, u32[]{:S(2)}) copy-start(s32[256]{0:T(256)} %param.11) | copy-start | bytes 3076
  42.0 25.2 %all-to-all-start = ((bf16[8,2,128,384]{3,2,1,0:T(8,128)(2,1)}), bf16[8,2,128,384]{3,2,1,0:T(8,128)(2,1)S(1)}, u32[]{:S(2)}, u32[]{:S(2)}) async-start(bf16[8,2,128,384]{3,2,1,0:T(8,128)(2,1)} %shard_map.93), calls=%async_computation | async-start | bytes 3145728 | tf_op jit(solution)/shard_map/all_to_all | solution.py:182
  49.7 1.5 copy-start.6
  67.2 9.8 %copy-start.5 = (bf16[8,2,128,384]{3,2,1,0:T(8,128)(2,1)}, bf16[8,2,128,384]{3,2,1,0:T(8,128)(2,1)S(1)}, u32[]{:S(2)}) copy-start(bf16[8,2,128,384]{3,2,1,0:T(8,128)(2,1)S(1)} %all-to-all-done.qg_ref) | copy-start | bytes 4718596
  112.2 36.7 %collective-permute-start.2 = (bf16[8,2,128,384]{3,2,1,0:T(8,128)(2,1)}, bf16[8,2,128,384]{3,2,1,0:T(8,128)(2,1)S(1)}, u32[]{:S(2)}, u32[]{:S(2)}) collective-permute-start(bf16[8,2,128,384]{3,2,1,0:T(8,128)(2,1)} %get-tuple-element.18), channel_id=1, source_target_pairs={{1,0},{2,1},{3,2},{4,3},{5,4},{6,5},{7,6},{8,7},{9,8},{10,9},{11,1... | collective-permute-start | bytes 4718600 | tf_op jit(solution)/shard_map/ppermute | solution.py:30
  114.1 38.9 %collective-permute-start.3 = (bf16[8,2,128,384]{3,2,1,0:T(8,128)(2,1)}, bf16[8,2,128,384]{3,2,1,0:T(8,128)(2,1)}, u32[]{:S(2)}, u32[]{:S(2)}) collective-permute-start(bf16[8,2,128,384]{3,2,1,0:T(8,128)(2,1)} %get-tuple-element.19), channel_id=1, source_target_pairs={{0,1},{1,2},{2,3},{3,4},{4,5},{5,6},{6,7},{7,8},{8,9},{9,10},{10,1... | collective-permute-start | bytes 4718600 | tf_op jit(solution)/shard_map/ppermute | solution.py:30
  118.0 39.2 %all-to-all-start.2 = ((bf16[8,2,128,384]{3,2,1,0:T(8,128)(2,1)}), bf16[8,2,128,384]{3,2,1,0:T(8,128)(2,1)S(1)}, u32[]{:S(2)}, u32[]{:S(2)}) async-start(bf16[8,2,128,384]{3,2,1,0:T(8,128)(2,1)} %get-tuple-element.14), calls=%async_computation.2 | async-start | bytes 3145728 | tf_op jit(solution)/shard_map/all_to_all | solution.py:186
  157.2 1.2 copy-start.2
  158.4 25.1 %all-to-all-start.3 = ((bf16[8,2,128,384]{3,2,1,0:T(8,128)(2,1)}), bf16[8,2,128,384]{3,2,1,0:T(8,128)(2,1)S(1)}, u32[]{:S(2)}, u32[]{:S(2)}) async-start(bf16[8,2,128,384]{3,2,1,0:T(8,128)(2,1)} %add_convert_fusion), calls=%async_computation.3 | async-start | bytes 3145728 | tf_op jit(solution)/shard_map/all_to_all | solution.py:186
  183.4 1.2 copy-start.3

commit v9 on v8

--- a/solution.py
+++ b/solution.py
@@ -48,13 +48,13 @@
 
 
 def attn_kernel(
-    slot_ref, live_ref, qg_ref, prev_ref, own_ref, next_ref,
-    og_ref, gown_ref, gprev_ref, gnext_ref, kg_scr, vg_scr, acc_scr,
+    slot_ref, live_ref, qg_ref, kp_ref, ko_ref, kn_ref, vp_ref, vo_ref, vn_ref,
+    og_ref, gok_ref, gov_ref, gpk_ref, gpv_ref, gnk_ref, gnv_ref, kg_scr, vg_scr, acc_scr,
 ):
     tile_rows = HD
     query_tiles, max_keys = slot_ref.shape
     scaling = HD ** (-0.5)
-    window = (prev_ref, own_ref, next_ref)
+    windows = ((kp_ref, ko_ref, kn_ref), (vp_ref, vo_ref, vn_ref))
     acc_scr[...] = jnp.zeros(acc_scr.shape, acc_scr.dtype)
     nt = (((1,), (1,)), ((), ()))
     tn = (((0,), (0,)), ((), ()))
@@ -67,10 +67,10 @@
             side = slot // query_tiles
             tile = slot % query_tiles
             dst = slice(s * tile_rows, (s + 1) * tile_rows)
-            for i, buf in ((0, kg_scr), (1, vg_scr)):
-                picked = window[0][tile, i]
+            for window, buf in zip(windows, (kg_scr, vg_scr)):
+                picked = window[0][tile, 0]
                 for w in (1, 2):
-                    picked = jnp.where(side == w, window[w][tile, i], picked)
+                    picked = jnp.where(side == w, window[w][tile, 0], picked)
                 buf[dst, :] = picked
 
             live_lane = jnp.where(lane_slot == s, live_ref[p, s], live_lane)
@@ -100,44 +100,44 @@
         return carry
 
     lax.fori_loop(0, query_tiles, body, 0, unroll=2)
-    gprev_ref[...] = acc_scr[:query_tiles].astype(gprev_ref.dtype)
-    gown_ref[...] = acc_scr[query_tiles : 2 * query_tiles]
-    gnext_ref[...] = acc_scr[2 * query_tiles :].astype(gnext_ref.dtype)
-
-
-def attention_heads(qg, kv_prev, kv_own, kv_next, slot_key, live_slot):
+    for i, (own, before, after) in enumerate(((gok_ref, gpk_ref, gnk_ref), (gov_ref, gpv_ref, gnv_ref))):
+        before[...] = acc_scr[:query_tiles, i : i + 1].astype(before.dtype)
+        own[...] = acc_scr[query_tiles : 2 * query_tiles, i : i + 1]
+        after[...] = acc_scr[2 * query_tiles :, i : i + 1].astype(after.dtype)
+
+
+def attention_heads(qg, k_win, v_win, slot_key, live_slot):
     query_tiles, count, tile_rows, width = qg.shape
     max_keys = slot_key.shape[1]
     head_count = width // HD
     spec = pl.BlockSpec((query_tiles, count, tile_rows, HD), lambda h, *_: (0, 0, 0, h))
+    one = pl.BlockSpec((query_tiles, 1, tile_rows, HD), lambda h, *_: (0, 0, 0, h))
+    second = pl.BlockSpec((query_tiles, 1, tile_rows, HD), lambda h, *_: (0, 1, 0, h))
     flops = 12 * query_tiles * max_keys * tile_rows * tile_rows * HD * head_count
     grid_spec = pltpu.PrefetchScalarGridSpec(
         num_scalar_prefetch=2,
         grid=(head_count,),
-        in_specs=[spec, spec, spec, spec],
-        out_specs=[spec, spec, spec, spec],
+        in_specs=[spec] + [one] * 3 + [second] * 3,
+        out_specs=[spec] + [one] * 6,
         scratch_shapes=[
             pltpu.VMEM((max_keys * tile_rows, HD), jnp.bfloat16),
             pltpu.VMEM((max_keys * tile_rows, HD), jnp.bfloat16),
             pltpu.VMEM((3 * query_tiles, count, tile_rows, HD), jnp.float32),
         ],
     )
-    block = qg.shape
+    single = (query_tiles, 1, tile_rows, width)
     return pl.pallas_call(
         attn_kernel,
         grid_spec=grid_spec,
-        out_shape=[
-            jax.ShapeDtypeStruct(block, jnp.bfloat16),
-            jax.ShapeDtypeStruct(block, jnp.float32),
-            jax.ShapeDtypeStruct(block, jnp.bfloat16),
-            jax.ShapeDtypeStruct(block, jnp.bfloat16),
-        ],
+        out_shape=[jax.ShapeDtypeStruct(qg.shape, jnp.bfloat16)]
+        + [jax.ShapeDtypeStruct(single, jnp.float32)] * 2
+        + [jax.ShapeDtypeStruct(single, jnp.bfloat16)] * 4,
         cost_estimate=pl.CostEstimate(
             flops=flops,
             transcendentals=query_tiles * max_keys * tile_rows * tile_rows * head_count,
             bytes_accessed=query_tiles * count * tile_rows * width * 2 * 8,
         ),
-    )(slot_key, live_slot.astype(jnp.int32), qg, kv_prev, kv_own, kv_next)
+    )(slot_key, live_slot.astype(jnp.int32), qg, *k_win, *v_win)
 
 
 def split_kernel(*refs):
@@ -195,18 +195,17 @@
     forward_active, _ = window_lists(block_mask, tile_order, frame_idx, frames, per_frame)
     slot_key, live_slot = compact_slots(forward_active, max_keys)
     kv = to_heads([key, value], per_frame)
-    kv_prev = passed_along(kv, "tile", 1)
-    kv_next = passed_along(kv, "tile", -1)
+    k_win = (passed_along(kv, "tile", 1), kv, passed_along(kv, "tile", -1))
+    v_win = k_win
     qg = to_heads([query, grad_out], per_frame)
-    og, grad_own, grad_prev, grad_next = attention_heads(
-        qg, kv_prev, kv, kv_next, slot_key, live_slot
-    )
+    og, gok, gov, gpk, gpv, gnk, gnv = attention_heads(qg, k_win, v_win, slot_key, live_slot)
     attn_out, grad_query = to_tokens(og)
-    from_above = passed_along(grad_prev, "tile", -1).astype(jnp.float32)
-    from_below = passed_along(grad_next, "tile", 1).astype(jnp.float32)
-    summed = (grad_own + from_above + from_below).astype(jnp.bfloat16)
-    grad_key, grad_value = to_tokens(summed)
-    return (attn_out, grad_query, grad_key, grad_value)
+    grads = []
+    for own, before, after in ((gok, gpk, gnk), (gov, gpv, gnv)):
+        from_above = passed_along(before, "tile", -1).astype(jnp.float32)
+        from_below = passed_along(after, "tile", 1).astype(jnp.float32)
+        grads.append(to_tokens((own + from_above + from_below).astype(jnp.bfloat16))[0])
+    return (attn_out, grad_query, grads[0], grads[1])
 
 
 def solution(mesh):

time: 188 us -> 183 us (0.973)
  waiting for transfers between devices: 75.4 us -> 58.7 us
  starting transfers between devices: 26.7 us -> 38.3 us
    all_to_all x2 -> x3, waiting for transfers between devices: 18.8 us -> 8.37 us  [to_tokens(): lax.all_to_all(stacked, 'head', split_axis=0, concat_axis=0, tiled=True)]
    ppermute x4 -> x6, waiting for transfers between devices: 41.2 us -> 35 us  [passed_along(): lax.ppermute(value, axis, [(source, source + steps) for source in range(i...]
    ppermute x4 -> x6, starting transfers between devices: 15.8 us -> 21.7 us  [passed_along(): lax.ppermute(value, axis, [(source, source + steps) for source in range(i...]
    all_to_all x2 -> x3, starting transfers between devices: 7.17 us -> 12.9 us  [to_tokens(): lax.all_to_all(stacked, 'head', split_axis=0, concat_axis=0, tiled=True)]
    pallas_call x2 -> x3, Pallas kernels: 5.35 us -> 6.83 us  [join_columns(): pl.pallas_call(join_kernel, in_specs=[pl.BlockSpec(memory_space=pltpu.VME...]
    convert_element_type x1 -> x2, other arithmetic: 4.19 us -> 4.24 us  [local(): (own + from_above + from_below).astype(jnp.bfloat16)]
  transfers between devices with their start and end apart: 7 -> 10, of which waited for: 6 -> 8; matrix products, arithmetic and copies ran while one was open for 5% -> 6% of each run, Pallas kernels for 3% -> 4%
where the time goes in v9:
time: 183 us; the launch traced here: 182 us
  waiting for transfers between devices  58.7 us (32%)
  Pallas kernels  47.3 us (26%)
  starting transfers between devices  38.3 us (21%)
  blocking collectives  26.1 us (14%)
  other arithmetic  5.83 us (3%)
  local copies, waits for them, and re-layouts  5.31 us (3%)
    pallas_call x1, Pallas kernels, attention_heads(): pl.pallas_call(attn_kernel, grid_spec=grid_spec, out_shape=[jax.ShapeDtyp...  35.1 us
    ppermute x6, waiting for transfers between devices, passed_along(): lax.ppermute(value, axis, [(source, source + steps) for source in range(i...  35 us
    all_to_all x1, blocking collectives, to_heads(): lax.all_to_all(stacked, 'head', split_axis=0, concat_axis=0, tiled=True)  26.1 us
    ppermute x6, starting transfers between devices, passed_along(): lax.ppermute(value, axis, [(source, source + steps) for source in range(i...  21.7 us
    all_to_all x1, waiting for transfers between devices, to_heads(): lax.all_to_all(stacked, 'head', split_axis=0, concat_axis=0, tiled=True)  15.4 us
    all_to_all x3, starting transfers between devices, to_tokens(): lax.all_to_all(stacked, 'head', split_axis=0, concat_axis=0, tiled=True)  12.9 us
    all_to_all x3, waiting for transfers between devices, to_tokens(): lax.all_to_all(stacked, 'head', split_axis=0, concat_axis=0, tiled=True)  8.37 us
    pallas_call x3, Pallas kernels, join_columns(): pl.pallas_call(join_kernel, in_specs=[pl.BlockSpec(memory_space=pltpu.VME...  6.83 us
  transfers between devices with their start and end apart: 10, of which 8 were waited for; matrix products, arithmetic and copies ran while one was open for 6% of the time, Pallas kernels for 4%

profile of v9, /device:TPU:6, one launch (start us, length us, event | category | flops | bytes accessed | tf_op | source)
XLA Modules:
  0.0 182.4 jit_solution(12683052721639079759)
XLA Ops:
  0.6 2.7 %shard_map.94 = bf16[8,2,128,384]{3,2,1,0:T(8,128)(2,1)} custom-call(bf16[128,3072]{1,0:T(8,128)(2,1)} %refs_0_.3, bf16[128,3072]{1,0:T(8,128)(2,1)} %refs_1_.3), custom_call_target="tpu_custom_call" | custom-call | tf_op jit(solution)/shard_map/pallas_call | solution.py:162
  3.4 26.1 %all_to_all.25.ko_ref.vo_ref = bf16[8,2,128,384]{3,2,1,0:T(8,128)(2,1)S(1)} all-to-all(bf16[8,2,128,384]{3,2,1,0:T(8,128)(2,1)} %shard_map.94), channel_id=1, replica_groups=mesh['head'=8,'tile'=32] {'head'}, dimensions={0} | all-to-all | bytes 3145728 | tf_op jit(solution)/shard_map/all_to_all | solution.py:182
  29.4 8.0 %collective-permute-start.1 = (bf16[8,2,128,384]{3,2,1,0:T(8,128)(2,1)S(1)}, bf16[8,2,128,384]{3,2,1,0:T(8,128)(2,1)}, u32[]{:S(2)}, u32[]{:S(2)}) collective-permute-start(bf16[8,2,128,384]{3,2,1,0:T(8,128)(2,1)S(1)} %all_to_all.25.ko_ref.vo_ref), channel_id=1, source_target_pairs={{1,0},{2,1},{3,2},{4,3},{5,4},{6,5},{7,6},{8,7},{9,8},{10,9},{11,1... | collective-permute-start | bytes 4718600 | tf_op jit(solution)/shard_map/ppermute | solution.py:30
  39.4 2.7 %shard_map.93 = bf16[8,2,128,384]{3,2,1,0:T(8,128)(2,1)} custom-call(bf16[128,3072]{1,0:T(8,128)(2,1)} %refs_0_.2, bf16[128,3072]{1,0:T(8,128)(2,1)} %refs_1_.2), custom_call_target="tpu_custom_call" | custom-call | tf_op jit(solution)/shard_map/pallas_call | solution.py:162
  42.1 3.7 %all-to-all-start = ((bf16[8,2,128,384]{3,2,1,0:T(8,128)(2,1)}), bf16[8,2,128,384]{3,2,1,0:T(8,128)(2,1)S(1)}, u32[]{:S(2)}, u32[]{:S(2)}) async-start(bf16[8,2,128,384]{3,2,1,0:T(8,128)(2,1)} %shard_map.93), calls=%async_computation | async-start | bytes 3145728 | tf_op jit(solution)/shard_map/all_to_all | solution.py:182
  51.8 15.4 %all-to-all-done.qg_ref = bf16[8,2,128,384]{3,2,1,0:T(8,128)(2,1)S(1)} async-done(((bf16[8,2,128,384]{3,2,1,0:T(8,128)(2,1)}), bf16[8,2,128,384]{3,2,1,0:T(8,128)(2,1)S(1)}, u32[]{:S(2)}, u32[]{:S(2)}) %all-to-all-start) | async-done | bytes 1572896 | tf_op jit(solution)/shard_map/all_to_all | solution.py:182
  67.3 3.5 %collective-permute-done.1.kn_ref.vn_ref = bf16[8,2,128,384]{3,2,1,0:T(8,128)(2,1)} collective-permute-done((bf16[8,2,128,384]{3,2,1,0:T(8,128)(2,1)S(1)}, bf16[8,2,128,384]{3,2,1,0:T(8,128)(2,1)}, u32[]{:S(2)}, u32[]{:S(2)}) %collective-permute-start.1) | collective-permute-done | bytes 1572896 | tf_op jit(solution)/shard_map/ppermute | solution.py:30
  70.7 6.3 %collective-permute-done.kp_ref.vp_ref = bf16[8,2,128,384]{3,2,1,0:T(8,128)(2,1)} collective-permute-done((bf16[8,2,128,384]{3,2,1,0:T(8,128)(2,1)S(1)}, bf16[8,2,128,384]{3,2,1,0:T(8,128)(2,1)}, u32[]{:S(2)}, u32[]{:S(2)}) %collective-permute-start) | collective-permute-done | bytes 1572896 | tf_op jit(solution)/shard_map/ppermute | solution.py:30
  77.1 35.1 %shard_map.95 = (bf16[8,2,128,384]{3,2,1,0:T(8,128)(2,1)}, f32[8,1,128,384]{3,2,1,0:T(8,128)}, f32[8,1,128,384]{3,2,1,0:T(8,128)}, bf16[8,1,128,384]{3,2,1,0:T(8...) custom-call(s32[8,9]{1,0:T(8,128)} %bitcast.9, ...), custom_call_target="tpu_custom_call" | custom-call | flops 5435817984 | bytes 12582912 | tf_op jit(solution)/shard_map/pallas_call | solution.py:129
  112.1 3.7 %all-to-all-start.2 = ((bf16[8,2,128,384]{3,2,1,0:T(8,128)(2,1)}), bf16[8,2,128,384]{3,2,1,0:T(8,128)(2,1)S(1)}, u32[]{:S(2)}, u32[]{:S(2)}) async-start(bf16[8,2,128,384]{3,2,1,0:T(8,128)(2,1)} %get-tuple-element.15), calls=%async_computation.2 | async-start | bytes 3145728 | tf_op jit(solution)/shard_map/all_to_all | solution.py:186
  117.8 3.9 %collective-permute-start.3 = (bf16[8,1,128,384]{3,2,1,0:T(8,128)(2,1)}, bf16[8,1,128,384]{3,2,1,0:T(8,128)(2,1)S(1)}, u32[]{:S(2)}, u32[]{:S(2)}) collective-permute-start(bf16[8,1,128,384]{3,2,1,0:T(8,128)(2,1)} %get-tuple-element.20), channel_id=1, source_target_pairs={{0,1},{1,2},{2,3},{3,4},{4,5},{5,6},{6,7},{7,8},{8,9},{9,10},{10,1... | collective-permute-start | bytes 2359304 | tf_op jit(solution)/shard_map/ppermute | solution.py:30
  121.7 4.0 %collective-permute-start.4 = (bf16[8,1,128,384]{3,2,1,0:T(8,128)(2,1)}, bf16[8,1,128,384]{3,2,1,0:T(8,128)(2,1)}, u32[]{:S(2)}, u32[]{:S(2)}) collective-permute-start(bf16[8,1,128,384]{3,2,1,0:T(8,128)(2,1)} %get-tuple-element.22), channel_id=1, source_target_pairs={{1,0},{2,1},{3,2},{4,3},{5,4},{6,5},{7,6},{8,7},{9,8},{10,9},{11,1... | collective-permute-start | bytes 2359304 | tf_op jit(solution)/shard_map/ppermute | solution.py:30
  125.8 1.9 %collective-permute-start.5 = (bf16[8,1,128,384]{3,2,1,0:T(8,128)(2,1)}, bf16[8,1,128,384]{3,2,1,0:T(8,128)(2,1)}, u32[]{:S(2)}, u32[]{:S(2)}) collective-permute-start(bf16[8,1,128,384]{3,2,1,0:T(8,128)(2,1)} %get-tuple-element.23), channel_id=1, source_target_pairs={{0,1},{1,2},{2,3},{3,4},{4,5},{5,6},{6,7},{7,8},{8,9},{9,10},{10,1... | collective-permute-start | bytes 2359304 | tf_op jit(solution)/shard_map/ppermute | solution.py:30
  127.7 10.7 %collective-permute-done.2 = bf16[8,1,128,384]{3,2,1,0:T(8,128)(2,1)S(1)} collective-permute-done((bf16[8,1,128,384]{3,2,1,0:T(8,128)(2,1)}, bf16[8,1,128,384]{3,2,1,0:T(8,128)(2,1)S(1)}, u32[]{:S(2)}, u32[]{:S(2)}) %collective-permute-start.2) | collective-permute-done | bytes 786464 | tf_op jit(solution)/shard_map/ppermute | solution.py:30
  138.4 4.0 %collective-permute-done.3 = bf16[8,1,128,384]{3,2,1,0:T(8,128)(2,1)S(1)} collective-permute-done((bf16[8,1,128,384]{3,2,1,0:T(8,128)(2,1)}, bf16[8,1,128,384]{3,2,1,0:T(8,128)(2,1)S(1)}, u32[]{:S(2)}, u32[]{:S(2)}) %collective-permute-start.3) | collective-permute-done | bytes 786464 | tf_op jit(solution)/shard_map/ppermute | solution.py:30
  143.6 4.7 %all-to-all-start.3 = ((bf16[8,1,128,384]{3,2,1,0:T(8,128)(2,1)}), bf16[8,1,128,384]{3,2,1,0:T(8,128)(2,1)S(1)}, u32[]{:S(2)}, u32[]{:S(2)}) async-start(bf16[8,1,128,384]{3,2,1,0:T(8,128)(2,1)} %add_convert_fusion.1), calls=%async_computation.3 | async-start | bytes 1572864 | tf_op jit(solution)/shard_map/all_to_all | solution.py:186
  148.4 6.4 %collective-permute-done.4 = bf16[8,1,128,384]{3,2,1,0:T(8,128)(2,1)} collective-permute-done((bf16[8,1,128,384]{3,2,1,0:T(8,128)(2,1)}, bf16[8,1,128,384]{3,2,1,0:T(8,128)(2,1)}, u32[]{:S(2)}, u32[]{:S(2)}) %collective-permute-start.4) | collective-permute-done | bytes 786464 | tf_op jit(solution)/shard_map/ppermute | solution.py:30
  154.8 4.0 %collective-permute-done.5 = bf16[8,1,128,384]{3,2,1,0:T(8,128)(2,1)} collective-permute-done((bf16[8,1,128,384]{3,2,1,0:T(8,128)(2,1)}, bf16[8,1,128,384]{3,2,1,0:T(8,128)(2,1)}, u32[]{:S(2)}, u32[]{:S(2)}) %collective-permute-start.5) | collective-permute-done | bytes 786464 | tf_op jit(solution)/shard_map/ppermute | solution.py:30
  158.8 3.0 %add_convert_fusion = bf16[8,1,128,384]{3,2,1,0:T(8,128)(2,1)} fusion(bf16[8,1,128,384]{3,2,1,0:T(8,128)(2,1)} %collective-permute-done.5, f32[8,1,128,384]{3,2,1,0:T(8,128)} %get-tuple-element.21, bf16[8,1,128,384]{3,2,1,0:T(8,128)(2,1)} %collective-permute-done.4), kind=kLoop, calls=%fused_computation.3 | loop fusion | flops 1966080 | bytes 3932160 | tf_op jit(solution)/shard_map/convert_element_type | solution.py:207
  161.8 4.5 %all-to-all-start.4 = ((bf16[8,1,128,384]{3,2,1,0:T(8,128)(2,1)}), bf16[8,1,128,384]{3,2,1,0:T(8,128)(2,1)S(1)}, u32[]{:S(2)}, u32[]{:S(2)}) async-start(bf16[8,1,128,384]{3,2,1,0:T(8,128)(2,1)} %add_convert_fusion), calls=%async_computation.4 | async-start | bytes 1572864 | tf_op jit(solution)/shard_map/all_to_all | solution.py:186
  166.3 2.7 %shard_map.96 = (bf16[128,3072]{1,0:T(8,128)(2,1)}, bf16[128,3072]{1,0:T(8,128)(2,1)}) custom-call(bf16[8,2,128,384]{3,2,1,0:T(8,128)(2,1)} %copy-done.2), custom_call_target="tpu_custom_call" | custom-call | tf_op jit(solution)/shard_map/pallas_call | solution.py:172
  169.0 2.1 %shard_map.97 = bf16[128,3072]{1,0:T(8,128)(2,1)} custom-call(bf16[8,1,128,384]{3,2,1,0:T(8,128)(2,1)} %copy-done.3), custom_call_target="tpu_custom_call" | custom-call | tf_op jit(solution)/shard_map/pallas_call | solution.py:172
  171.0 8.4 %all-to-all-done.4.refs_0_ = bf16[8,1,128,384]{3,2,1,0:T(8,128)(2,1)S(1)} async-done(((bf16[8,1,128,384]{3,2,1,0:T(8,128)(2,1)}), bf16[8,1,128,384]{3,2,1,0:T(8,128)(2,1)S(1)}, u32[]{:S(2)}, u32[]{:S(2)}) %all-to-all-start.4) | async-done | bytes 786464 | tf_op jit(solution)/shard_map/all_to_all | solution.py:186
  180.3 2.1 %shard_map.98 = bf16[128,3072]{1,0:T(8,128)(2,1)} custom-call(bf16[8,1,128,384]{3,2,1,0:T(8,128)(2,1)} %copy-done.4), custom_call_target="tpu_custom_call" | custom-call | tf_op jit(solution)/shard_map/pallas_call | solution.py:172
  (43 shorter events, 12.0 us)
Async XLA Ops:
  0.6 46.2 %copy-start = (s32[256,256]{1,0:T(8,128)S(1)}, s32[256,256]{1,0:T(8,128)}, u32[]{:S(2)}) copy-start(s32[256,256]{1,0:T(8,128)} %param.10) | copy-start | bytes 786436
  29.4 12.6 %copy-start.5 = (bf16[8,2,128,384]{3,2,1,0:T(8,128)(2,1)}, bf16[8,2,128,384]{3,2,1,0:T(8,128)(2,1)S(1)}, u32[]{:S(2)}) copy-start(bf16[8,2,128,384]{3,2,1,0:T(8,128)(2,1)S(1)} %all_to_all.25.ko_ref.vo_ref) | copy-start | bytes 4718596
  29.4 41.3 %collective-permute-start.1 = (bf16[8,2,128,384]{3,2,1,0:T(8,128)(2,1)S(1)}, bf16[8,2,128,384]{3,2,1,0:T(8,128)(2,1)}, u32[]{:S(2)}, u32[]{:S(2)}) collective-permute-start(bf16[8,2,128,384]{3,2,1,0:T(8,128)(2,1)S(1)} %all_to_all.25.ko_ref.vo_ref), channel_id=1, source_target_pairs={{1,0},{2,1},{3,2},{4,3},{5,4},{6,5},{7,6},{8,7},{9,8},{10,9},{11,1... | collective-permute-start | bytes 4718600 | tf_op jit(solution)/shard_map/ppermute | solution.py:30
  37.5 39.6 %collective-permute-start = (bf16[8,2,128,384]{3,2,1,0:T(8,128)(2,1)S(1)}, bf16[8,2,128,384]{3,2,1,0:T(8,128)(2,1)}, u32[]{:S(2)}, u32[]{:S(2)}) collective-permute-start(bf16[8,2,128,384]{3,2,1,0:T(8,128)(2,1)S(1)} %all_to_all.25.ko_ref.vo_ref), channel_id=1, source_target_pairs={{0,1},{1,2},{2,3},{3,4},{4,5},{5,6},{6,7},{7,8},{8,9},{9,10},{10,1... | collective-permute-start | bytes 4718600 | tf_op jit(solution)/shard_map/ppermute | solution.py:30
  42.1 3.8 %copy-start.1 = (s32[256]{0:T(256)S(1)}, s32[256]{0:T(256)}, u32[]{:S(2)}) copy-start(s32[256]{0:T(256)} %param.11) | copy-start | bytes 3076
  42.1 25.2 %all-to-all-start = ((bf16[8,2,128,384]{3,2,1,0:T(8,128)(2,1)}), bf16[8,2,128,384]{3,2,1,0:T(8,128)(2,1)S(1)}, u32[]{:S(2)}, u32[]{:S(2)}) async-start(bf16[8,2,128,384]{3,2,1,0:T(8,128)(2,1)} %shard_map.93), calls=%async_computation | async-start | bytes 3145728 | tf_op jit(solution)/shard_map/all_to_all | solution.py:182
  49.8 1.5 copy-start.8
  67.3 9.8 %copy-start.6 = (bf16[8,2,128,384]{3,2,1,0:T(8,128)(2,1)}, bf16[8,2,128,384]{3,2,1,0:T(8,128)(2,1)S(1)}, u32[]{:S(2)}) copy-start(bf16[8,2,128,384]{3,2,1,0:T(8,128)(2,1)S(1)} %all-to-all-done.qg_ref) | copy-start | bytes 4718596
  112.1 30.3 %copy-start.7 = (f32[8,1,128,384]{3,2,1,0:T(8,128)S(1)}, f32[8,1,128,384]{3,2,1,0:T(8,128)}, u32[]{:S(2)}) copy-start(f32[8,1,128,384]{3,2,1,0:T(8,128)} %get-tuple-element.18) | copy-start | bytes 4718596
  112.1 31.5 %all-to-all-start.2 = ((bf16[8,2,128,384]{3,2,1,0:T(8,128)(2,1)}), bf16[8,2,128,384]{3,2,1,0:T(8,128)(2,1)S(1)}, u32[]{:S(2)}, u32[]{:S(2)}) async-start(bf16[8,2,128,384]{3,2,1,0:T(8,128)(2,1)} %get-tuple-element.15), calls=%async_computation.2 | async-start | bytes 3145728 | tf_op jit(solution)/shard_map/all_to_all | solution.py:186
  115.9 22.5 %collective-permute-start.2 = (bf16[8,1,128,384]{3,2,1,0:T(8,128)(2,1)}, bf16[8,1,128,384]{3,2,1,0:T(8,128)(2,1)S(1)}, u32[]{:S(2)}, u32[]{:S(2)}) collective-permute-start(bf16[8,1,128,384]{3,2,1,0:T(8,128)(2,1)} %get-tuple-element.19), channel_id=1, source_target_pairs={{1,0},{2,1},{3,2},{4,3},{5,4},{6,5},{7,6},{8,7},{9,8},{10,9},{11,1... | collective-permute-start | bytes 2359304 | tf_op jit(solution)/shard_map/ppermute | solution.py:30
  117.8 24.6 %collective-permute-start.3 = (bf16[8,1,128,384]{3,2,1,0:T(8,128)(2,1)}, bf16[8,1,128,384]{3,2,1,0:T(8,128)(2,1)S(1)}, u32[]{:S(2)}, u32[]{:S(2)}) collective-permute-start(bf16[8,1,128,384]{3,2,1,0:T(8,128)(2,1)} %get-tuple-element.20), channel_id=1, source_target_pairs={{0,1},{1,2},{2,3},{3,4},{4,5},{5,6},{6,7},{7,8},{8,9},{9,10},{10,1... | collective-permute-start | bytes 2359304 | tf_op jit(solution)/shard_map/ppermute | solution.py:30
  121.7 33.0 %collective-permute-start.4 = (bf16[8,1,128,384]{3,2,1,0:T(8,128)(2,1)}, bf16[8,1,128,384]{3,2,1,0:T(8,128)(2,1)}, u32[]{:S(2)}, u32[]{:S(2)}) collective-permute-start(bf16[8,1,128,384]{3,2,1,0:T(8,128)(2,1)} %get-tuple-element.22), channel_id=1, source_target_pairs={{1,0},{2,1},{3,2},{4,3},{5,4},{6,5},{7,6},{8,7},{9,8},{10,9},{11,1... | collective-permute-start | bytes 2359304 | tf_op jit(solution)/shard_map/ppermute | solution.py:30
  125.8 33.0 %collective-permute-start.5 = (bf16[8,1,128,384]{3,2,1,0:T(8,128)(2,1)}, bf16[8,1,128,384]{3,2,1,0:T(8,128)(2,1)}, u32[]{:S(2)}, u32[]{:S(2)}) collective-permute-start(bf16[8,1,128,384]{3,2,1,0:T(8,128)(2,1)} %get-tuple-element.23), channel_id=1, source_target_pairs={{0,1},{1,2},{2,3},{3,4},{4,5},{5,6},{6,7},{7,8},{8,9},{9,10},{10,1... | collective-permute-start | bytes 2359304 | tf_op jit(solution)/shard_map/ppermute | solution.py:30
  143.6 18.2 %copy-start.2 = (bf16[8,2,128,384]{3,2,1,0:T(8,128)(2,1)}, bf16[8,2,128,384]{3,2,1,0:T(8,128)(2,1)S(1)}, u32[]{:S(2)}) copy-start(bf16[8,2,128,384]{3,2,1,0:T(8,128)(2,1)S(1)} %all-to-all-done.2.refs_0_) | copy-start | bytes 4718596
  143.6 18.2 %all-to-all-start.3 = ((bf16[8,1,128,384]{3,2,1,0:T(8,128)(2,1)}), bf16[8,1,128,384]{3,2,1,0:T(8,128)(2,1)S(1)}, u32[]{:S(2)}, u32[]{:S(2)}) async-start(bf16[8,1,128,384]{3,2,1,0:T(8,128)(2,1)} %add_convert_fusion.1), calls=%async_computation.3 | async-start | bytes 1572864 | tf_op jit(solution)/shard_map/all_to_all | solution.py:186
  161.8 7.1 %copy-start.3 = (bf16[8,1,128,384]{3,2,1,0:T(8,128)(2,1)}, bf16[8,1,128,384]{3,2,1,0:T(8,128)(2,1)S(1)}, u32[]{:S(2)}) copy-start(bf16[8,1,128,384]{3,2,1,0:T(8,128)(2,1)S(1)} %all-to-all-done.3.refs_0_) | copy-start | bytes 2359300
  161.8 17.6 %all-to-all-start.4 = ((bf16[8,1,128,384]{3,2,1,0:T(8,128)(2,1)}), bf16[8,1,128,384]{3,2,1,0:T(8,128)(2,1)S(1)}, u32[]{:S(2)}, u32[]{:S(2)}) async-start(bf16[8,1,128,384]{3,2,1,0:T(8,128)(2,1)} %add_convert_fusion), calls=%async_computation.4 | async-start | bytes 1572864 | tf_op jit(solution)/shard_map/all_to_all | solution.py:186
  179.4 0.9 copy-start.4

commit v10 on v9

--- a/solution.py
+++ b/solution.py
@@ -102,7 +102,7 @@
     lax.fori_loop(0, query_tiles, body, 0, unroll=2)
     for i, (own, before, after) in enumerate(((gok_ref, gpk_ref, gnk_ref), (gov_ref, gpv_ref, gnv_ref))):
         before[...] = acc_scr[:query_tiles, i : i + 1].astype(before.dtype)
-        own[...] = acc_scr[query_tiles : 2 * query_tiles, i : i + 1]
+        own[...] = acc_scr[query_tiles : 2 * query_tiles, i : i + 1].astype(own.dtype)
         after[...] = acc_scr[2 * query_tiles :, i : i + 1].astype(after.dtype)
 
 
@@ -130,8 +130,7 @@
         attn_kernel,
         grid_spec=grid_spec,
         out_shape=[jax.ShapeDtypeStruct(qg.shape, jnp.bfloat16)]
-        + [jax.ShapeDtypeStruct(single, jnp.float32)] * 2
-        + [jax.ShapeDtypeStruct(single, jnp.bfloat16)] * 4,
+        + [jax.ShapeDtypeStruct(single, jnp.bfloat16)] * 6,
         cost_estimate=pl.CostEstimate(
             flops=flops,
             transcendentals=query_tiles * max_keys * tile_rows * tile_rows * head_count,
@@ -155,24 +154,28 @@
             refs[1 + i][:, j * part : (j + 1) * part] = refs[0][j, i]
 
 
-def split_columns(arrays, groups):
+def split_columns(arrays, groups, blocks=4):
     rows, width = arrays[0].shape
     part = width // groups
     count = len(arrays)
+    step = rows // blocks
     return pl.pallas_call(
         split_kernel,
-        in_specs=[pl.BlockSpec(memory_space=pltpu.VMEM)] * count,
-        out_specs=pl.BlockSpec(memory_space=pltpu.VMEM),
+        grid=(blocks,),
+        in_specs=[pl.BlockSpec((step, width), lambda r: (r, 0))] * count,
+        out_specs=pl.BlockSpec((groups, count, step, part), lambda r: (0, 0, r, 0)),
         out_shape=jax.ShapeDtypeStruct((groups, count, rows, part), arrays[0].dtype),
     )(*arrays)
 
 
-def join_columns(stacked):
+def join_columns(stacked, blocks=4):
     groups, count, rows, part = stacked.shape
+    step = rows // blocks
     return pl.pallas_call(
         join_kernel,
-        in_specs=[pl.BlockSpec(memory_space=pltpu.VMEM)],
-        out_specs=[pl.BlockSpec(memory_space=pltpu.VMEM)] * count,
+        grid=(blocks,),
+        in_specs=[pl.BlockSpec((groups, count, step, part), lambda r: (0, 0, r, 0))],
+        out_specs=[pl.BlockSpec((step, groups * part), lambda r: (r, 0))] * count,
         out_shape=[jax.ShapeDtypeStruct((rows, groups * part), stacked.dtype)] * count,
     )(stacked)
 
@@ -204,7 +207,8 @@
     for own, before, after in ((gok, gpk, gnk), (gov, gpv, gnv)):
         from_above = passed_along(before, "tile", -1).astype(jnp.float32)
         from_below = passed_along(after, "tile", 1).astype(jnp.float32)
-        grads.append(to_tokens((own + from_above + from_below).astype(jnp.bfloat16))[0])
+        summed = own.astype(jnp.float32) + from_above + from_below
+        grads.append(to_tokens(summed.astype(jnp.bfloat16))[0])
     return (attn_out, grad_query, grads[0], grads[1])
 
 

time: 183 us -> 185 us (1.011)
  Pallas kernels: 47.3 us -> 52.5 us
  waiting for transfers between devices: 58.7 us -> 55.5 us
    pallas_call x5, Pallas kernels: 12.2 us -> 17.6 us  [the longest x3 10.1 us: join_columns(): pl.pallas_call(join_kernel, grid=(blocks,), in_specs=[pl.BlockSpec((group...]
  transfers between devices with their start and end apart: 10 -> 10, of which waited for: 8 -> 9; matrix products, arithmetic and copies ran while one was open for 6% -> 5% of each run, Pallas kernels for 4% -> 6%
where the time goes in v10:
time: 185 us; the launch traced here: 184 us
  waiting for transfers between devices  55.5 us (30%)
  Pallas kernels  52.5 us (28%)
  starting transfers between devices  38.2 us (21%)
  blocking collectives  26.1 us (14%)
  other arithmetic  5.35 us (3%)
  local copies, waits for them, and re-layouts  5.31 us (3%)
    pallas_call x1, Pallas kernels, attention_heads(): pl.pallas_call(attn_kernel, grid_spec=grid_spec, out_shape=[jax.ShapeDtyp...  34.9 us
    ppermute x6, waiting for transfers between devices, passed_along(): lax.ppermute(value, axis, [(source, source + steps) for source in range(i...  33.6 us
    all_to_all x1, blocking collectives, to_heads(): lax.all_to_all(stacked, 'head', split_axis=0, concat_axis=0, tiled=True)  26.1 us
    ppermute x6, starting transfers between devices, passed_along(): lax.ppermute(value, axis, [(source, source + steps) for source in range(i...  21.7 us
    all_to_all x1, waiting for transfers between devices, to_heads(): lax.all_to_all(stacked, 'head', split_axis=0, concat_axis=0, tiled=True)  15.4 us
    all_to_all x3, starting transfers between devices, to_tokens(): lax.all_to_all(stacked, 'head', split_axis=0, concat_axis=0, tiled=True)  12.8 us
    pallas_call x3, Pallas kernels, join_columns(): pl.pallas_call(join_kernel, grid=(blocks,), in_specs=[pl.BlockSpec((group...  10.1 us
    pallas_call x2, Pallas kernels, split_columns(): pl.pallas_call(split_kernel, grid=(blocks,), in_specs=[pl.BlockSpec((step...  7.47 us
  transfers between devices with their start and end apart: 10, of which 9 were waited for; matrix products, arithmetic and copies ran while one was open for 5% of the time, Pallas kernels for 6%

profile of v10, /device:TPU:6, one launch (start us, length us, event | category | flops | bytes accessed | tf_op | source)
XLA Modules:
  0.0 183.7 jit_solution(8470322681289435499)
XLA Ops:
  0.6 3.7 %shard_map.94 = bf16[8,2,128,384]{3,2,1,0:T(8,128)(2,1)} custom-call(bf16[128,3072]{1,0:T(8,128)(2,1)} %refs_0_.3, bf16[128,3072]{1,0:T(8,128)(2,1)} %refs_1_.3), custom_call_target="tpu_custom_call" | custom-call | tf_op jit(solution)/shard_map/pallas_call | solution.py:162
  4.4 26.1 %all_to_all.25.ko_ref.vo_ref = bf16[8,2,128,384]{3,2,1,0:T(8,128)(2,1)S(1)} all-to-all(bf16[8,2,128,384]{3,2,1,0:T(8,128)(2,1)} %shard_map.94), channel_id=1, replica_groups=mesh['head'=8,'tile'=32] {'head'}, dimensions={0} | all-to-all | bytes 3145728 | tf_op jit(solution)/shard_map/all_to_all | solution.py:185
  30.5 8.0 %collective-permute-start.1 = (bf16[8,2,128,384]{3,2,1,0:T(8,128)(2,1)S(1)}, bf16[8,2,128,384]{3,2,1,0:T(8,128)(2,1)}, u32[]{:S(2)}, u32[]{:S(2)}) collective-permute-start(bf16[8,2,128,384]{3,2,1,0:T(8,128)(2,1)S(1)} %all_to_all.25.ko_ref.vo_ref), channel_id=1, source_target_pairs={{1,0},{2,1},{3,2},{4,3},{5,4},{6,5},{7,6},{8,7},{9,8},{10,9},{11,1... | collective-permute-start | bytes 4718600 | tf_op jit(solution)/shard_map/ppermute | solution.py:30
  38.5 1.9 %collective-permute-start = (bf16[8,2,128,384]{3,2,1,0:T(8,128)(2,1)S(1)}, bf16[8,2,128,384]{3,2,1,0:T(8,128)(2,1)}, u32[]{:S(2)}, u32[]{:S(2)}) collective-permute-start(bf16[8,2,128,384]{3,2,1,0:T(8,128)(2,1)S(1)} %all_to_all.25.ko_ref.vo_ref), channel_id=1, source_target_pairs={{0,1},{1,2},{2,3},{3,4},{4,5},{5,6},{6,7},{7,8},{8,9},{9,10},{10,1... | collective-permute-start | bytes 4718600 | tf_op jit(solution)/shard_map/ppermute | solution.py:30
  40.4 3.7 %shard_map.93 = bf16[8,2,128,384]{3,2,1,0:T(8,128)(2,1)} custom-call(bf16[128,3072]{1,0:T(8,128)(2,1)} %refs_0_.2, bf16[128,3072]{1,0:T(8,128)(2,1)} %refs_1_.2), custom_call_target="tpu_custom_call" | custom-call | tf_op jit(solution)/shard_map/pallas_call | solution.py:162
  44.1 3.7 %all-to-all-start = ((bf16[8,2,128,384]{3,2,1,0:T(8,128)(2,1)}), bf16[8,2,128,384]{3,2,1,0:T(8,128)(2,1)S(1)}, u32[]{:S(2)}, u32[]{:S(2)}) async-start(bf16[8,2,128,384]{3,2,1,0:T(8,128)(2,1)} %shard_map.93), calls=%async_computation | async-start | bytes 3145728 | tf_op jit(solution)/shard_map/all_to_all | solution.py:185
  53.9 15.4 %all-to-all-done.qg_ref = bf16[8,2,128,384]{3,2,1,0:T(8,128)(2,1)S(1)} async-done(((bf16[8,2,128,384]{3,2,1,0:T(8,128)(2,1)}), bf16[8,2,128,384]{3,2,1,0:T(8,128)(2,1)S(1)}, u32[]{:S(2)}, u32[]{:S(2)}) %all-to-all-start) | async-done | bytes 1572896 | tf_op jit(solution)/shard_map/all_to_all | solution.py:185
  69.3 2.4 %collective-permute-done.1.kn_ref.vn_ref = bf16[8,2,128,384]{3,2,1,0:T(8,128)(2,1)} collective-permute-done((bf16[8,2,128,384]{3,2,1,0:T(8,128)(2,1)S(1)}, bf16[8,2,128,384]{3,2,1,0:T(8,128)(2,1)}, u32[]{:S(2)}, u32[]{:S(2)}) %collective-permute-start.1) | collective-permute-done | bytes 1572896 | tf_op jit(solution)/shard_map/ppermute | solution.py:30
  71.7 6.3 %collective-permute-done.kp_ref.vp_ref = bf16[8,2,128,384]{3,2,1,0:T(8,128)(2,1)} collective-permute-done((bf16[8,2,128,384]{3,2,1,0:T(8,128)(2,1)S(1)}, bf16[8,2,128,384]{3,2,1,0:T(8,128)(2,1)}, u32[]{:S(2)}, u32[]{:S(2)}) %collective-permute-start) | collective-permute-done | bytes 1572896 | tf_op jit(solution)/shard_map/ppermute | solution.py:30
  78.1 34.9 %shard_map.95 = (bf16[8,2,128,384]{3,2,1,0:T(8,128)(2,1)}, bf16[8,1,128,384]{3,2,1,0:T(8,128)(2,1)}, bf16[8,1,128,384]{3,2,1,0:T(8,128)(2,1)}, bf16[8,1,128,384]...) custom-call(s32[8,9]{1,0:T(8,128)} %bitcast.9, ...), custom_call_target="tpu_custom_call" | custom-call | flops 5435817984 | bytes 12582912 | tf_op jit(solution)/shard_map/pallas_call | solution.py:129
  113.0 3.7 %all-to-all-start.2 = ((bf16[8,2,128,384]{3,2,1,0:T(8,128)(2,1)}), bf16[8,2,128,384]{3,2,1,0:T(8,128)(2,1)S(1)}, u32[]{:S(2)}, u32[]{:S(2)}) async-start(bf16[8,2,128,384]{3,2,1,0:T(8,128)(2,1)} %get-tuple-element.15), calls=%async_computation.2 | async-start | bytes 3145728 | tf_op jit(solution)/shard_map/all_to_all | solution.py:189
  118.6 3.9 %collective-permute-start.3 = (bf16[8,1,128,384]{3,2,1,0:T(8,128)(2,1)S(1)}, bf16[8,1,128,384]{3,2,1,0:T(8,128)(2,1)S(1)}, u32[]{:S(2)}, u32[]{:S(2)}) collective-permute-start(bf16[8,1,128,384]{3,2,1,0:T(8,128)(2,1)S(1)} %copy-done.10), channel_id=1, source_target_pairs={{0,1},{1,2},{2,3},{3,4},{4,5},{5,6},{6,7},{7,8},{8,9},{9,10},{10,1... | collective-permute-start | bytes 2359304 | tf_op jit(solution)/shard_map/ppermute | solution.py:30
  122.6 4.0 %collective-permute-start.4 = (bf16[8,1,128,384]{3,2,1,0:T(8,128)(2,1)}, bf16[8,1,128,384]{3,2,1,0:T(8,128)(2,1)}, u32[]{:S(2)}, u32[]{:S(2)}) collective-permute-start(bf16[8,1,128,384]{3,2,1,0:T(8,128)(2,1)} %get-tuple-element.22), channel_id=1, source_target_pairs={{1,0},{2,1},{3,2},{4,3},{5,4},{6,5},{7,6},{8,7},{9,8},{10,9},{11,1... | collective-permute-start | bytes 2359304 | tf_op jit(solution)/shard_map/ppermute | solution.py:30
  128.5 10.7 %collective-permute-done.2 = bf16[8,1,128,384]{3,2,1,0:T(8,128)(2,1)S(1)} collective-permute-done((bf16[8,1,128,384]{3,2,1,0:T(8,128)(2,1)}, bf16[8,1,128,384]{3,2,1,0:T(8,128)(2,1)S(1)}, u32[]{:S(2)}, u32[]{:S(2)}) %collective-permute-start.2) | collective-permute-done | bytes 786464 | tf_op jit(solution)/shard_map/ppermute | solution.py:30
  139.2 3.8 %collective-permute-done.3 = bf16[8,1,128,384]{3,2,1,0:T(8,128)(2,1)S(1)} collective-permute-done((bf16[8,1,128,384]{3,2,1,0:T(8,128)(2,1)S(1)}, bf16[8,1,128,384]{3,2,1,0:T(8,128)(2,1)S(1)}, u32[]{:S(2)}, u32[]{:S(2)}) %collective-permute-start.3) | collective-permute-done | bytes 786464 | tf_op jit(solution)/shard_map/ppermute | solution.py:30
  144.3 4.8 %all-to-all-start.3 = ((bf16[8,1,128,384]{3,2,1,0:T(8,128)(2,1)}), bf16[8,1,128,384]{3,2,1,0:T(8,128)(2,1)S(1)}, u32[]{:S(2)}, u32[]{:S(2)}) async-start(bf16[8,1,128,384]{3,2,1,0:T(8,128)(2,1)} %add_convert_fusion.1), calls=%async_computation.3 | async-start | bytes 1572864 | tf_op jit(solution)/shard_map/all_to_all | solution.py:189
  149.1 6.5 %collective-permute-done.4 = bf16[8,1,128,384]{3,2,1,0:T(8,128)(2,1)} collective-permute-done((bf16[8,1,128,384]{3,2,1,0:T(8,128)(2,1)}, bf16[8,1,128,384]{3,2,1,0:T(8,128)(2,1)}, u32[]{:S(2)}, u32[]{:S(2)}) %collective-permute-start.4) | collective-permute-done | bytes 786464 | tf_op jit(solution)/shard_map/ppermute | solution.py:30
  155.6 3.8 %collective-permute-done.5 = bf16[8,1,128,384]{3,2,1,0:T(8,128)(2,1)} collective-permute-done((bf16[8,1,128,384]{3,2,1,0:T(8,128)(2,1)}, bf16[8,1,128,384]{3,2,1,0:T(8,128)(2,1)}, u32[]{:S(2)}, u32[]{:S(2)}) %collective-permute-start.5) | collective-permute-done | bytes 786464 | tf_op jit(solution)/shard_map/ppermute | solution.py:30
  159.5 2.5 %add_convert_fusion = bf16[8,1,128,384]{3,2,1,0:T(8,128)(2,1)} fusion(bf16[8,1,128,384]{3,2,1,0:T(8,128)(2,1)} %collective-permute-done.5, bf16[8,1,128,384]{3,2,1,0:T(8,128)(2,1)} %collective-permute-done.4, bf16[8,1,128,384]{3,2,1,0:T(8,128)(2,1)S(1)} %copy-done.7), kind=kLoop, calls=%fused_computation.3 | loop fusion | flops 2359296 | bytes 3145728 | tf_op jit(solution)/shard_map/convert_element_type | solution.py:211
  162.3 4.2 %all-to-all-start.4 = ((bf16[8,1,128,384]{3,2,1,0:T(8,128)(2,1)}), bf16[8,1,128,384]{3,2,1,0:T(8,128)(2,1)S(1)}, u32[]{:S(2)}, u32[]{:S(2)}) async-start(bf16[8,1,128,384]{3,2,1,0:T(8,128)(2,1)} %add_convert_fusion), calls=%async_computation.4 | async-start | bytes 1572864 | tf_op jit(solution)/shard_map/all_to_all | solution.py:189
  166.5 3.6 %shard_map.96 = (bf16[128,3072]{1,0:T(8,128)(2,1)}, bf16[128,3072]{1,0:T(8,128)(2,1)}) custom-call(bf16[8,2,128,384]{3,2,1,0:T(8,128)(2,1)} %copy-done.2), custom_call_target="tpu_custom_call" | custom-call | tf_op jit(solution)/shard_map/pallas_call | solution.py:174
  170.1 3.3 %shard_map.97 = bf16[128,3072]{1,0:T(8,128)(2,1)} custom-call(bf16[8,1,128,384]{3,2,1,0:T(8,128)(2,1)} %copy-done.3), custom_call_target="tpu_custom_call" | custom-call | tf_op jit(solution)/shard_map/pallas_call | solution.py:174
  173.3 6.3 %all-to-all-done.4.refs_0_ = bf16[8,1,128,384]{3,2,1,0:T(8,128)(2,1)S(1)} async-done(((bf16[8,1,128,384]{3,2,1,0:T(8,128)(2,1)}), bf16[8,1,128,384]{3,2,1,0:T(8,128)(2,1)S(1)}, u32[]{:S(2)}, u32[]{:S(2)}) %all-to-all-start.4) | async-done | bytes 786464 | tf_op jit(solution)/shard_map/all_to_all | solution.py:189
  180.5 3.3 %shard_map.98 = bf16[128,3072]{1,0:T(8,128)(2,1)} custom-call(bf16[8,1,128,384]{3,2,1,0:T(8,128)(2,1)} %copy-done.4), custom_call_target="tpu_custom_call" | custom-call | tf_op jit(solution)/shard_map/pallas_call | solution.py:174
  (47 shorter events, 12.2 us)
Async XLA Ops:
  0.6 48.2 %copy-start = (s32[256,256]{1,0:T(8,128)S(1)}, s32[256,256]{1,0:T(8,128)}, u32[]{:S(2)}) copy-start(s32[256,256]{1,0:T(8,128)} %param.10) | copy-start | bytes 786436
  30.5 13.7 %copy-start.5 = (bf16[8,2,128,384]{3,2,1,0:T(8,128)(2,1)}, bf16[8,2,128,384]{3,2,1,0:T(8,128)(2,1)S(1)}, u32[]{:S(2)}) copy-start(bf16[8,2,128,384]{3,2,1,0:T(8,128)(2,1)S(1)} %all_to_all.25.ko_ref.vo_ref) | copy-start | bytes 4718596
  30.5 41.3 %collective-permute-start.1 = (bf16[8,2,128,384]{3,2,1,0:T(8,128)(2,1)S(1)}, bf16[8,2,128,384]{3,2,1,0:T(8,128)(2,1)}, u32[]{:S(2)}, u32[]{:S(2)}) collective-permute-start(bf16[8,2,128,384]{3,2,1,0:T(8,128)(2,1)S(1)} %all_to_all.25.ko_ref.vo_ref), channel_id=1, source_target_pairs={{1,0},{2,1},{3,2},{4,3},{5,4},{6,5},{7,6},{8,7},{9,8},{10,9},{11,1... | collective-permute-start | bytes 4718600 | tf_op jit(solution)/shard_map/ppermute | solution.py:30
  38.5 39.6 %collective-permute-start = (bf16[8,2,128,384]{3,2,1,0:T(8,128)(2,1)S(1)}, bf16[8,2,128,384]{3,2,1,0:T(8,128)(2,1)}, u32[]{:S(2)}, u32[]{:S(2)}) collective-permute-start(bf16[8,2,128,384]{3,2,1,0:T(8,128)(2,1)S(1)} %all_to_all.25.ko_ref.vo_ref), channel_id=1, source_target_pairs={{0,1},{1,2},{2,3},{3,4},{4,5},{5,6},{6,7},{7,8},{8,9},{9,10},{10,1... | collective-permute-start | bytes 4718600 | tf_op jit(solution)/shard_map/ppermute | solution.py:30
  44.1 3.8 %copy-start.1 = (s32[256]{0:T(256)S(1)}, s32[256]{0:T(256)}, u32[]{:S(2)}) copy-start(s32[256]{0:T(256)} %param.11) | copy-start | bytes 3076
  44.1 25.2 %all-to-all-start = ((bf16[8,2,128,384]{3,2,1,0:T(8,128)(2,1)}), bf16[8,2,128,384]{3,2,1,0:T(8,128)(2,1)S(1)}, u32[]{:S(2)}, u32[]{:S(2)}) async-start(bf16[8,2,128,384]{3,2,1,0:T(8,128)(2,1)} %shard_map.93), calls=%async_computation | async-start | bytes 3145728 | tf_op jit(solution)/shard_map/all_to_all | solution.py:185
  51.8 1.5 copy-start.9
  69.3 8.7 %copy-start.6 = (bf16[8,2,128,384]{3,2,1,0:T(8,128)(2,1)}, bf16[8,2,128,384]{3,2,1,0:T(8,128)(2,1)S(1)}, u32[]{:S(2)}) copy-start(bf16[8,2,128,384]{3,2,1,0:T(8,128)(2,1)S(1)} %all-to-all-done.qg_ref) | copy-start | bytes 4718596
  113.0 5.7 %copy-start.10 = (bf16[8,1,128,384]{3,2,1,0:T(8,128)(2,1)S(1)}, bf16[8,1,128,384]{3,2,1,0:T(8,128)(2,1)}, u32[]{:S(2)}) copy-start(bf16[8,1,128,384]{3,2,1,0:T(8,128)(2,1)} %get-tuple-element.20) | copy-start | bytes 2359300
  113.0 30.1 %copy-start.8 = (bf16[8,1,128,384]{3,2,1,0:T(8,128)(2,1)S(1)}, bf16[8,1,128,384]{3,2,1,0:T(8,128)(2,1)}, u32[]{:S(2)}) copy-start(bf16[8,1,128,384]{3,2,1,0:T(8,128)(2,1)} %get-tuple-element.18) | copy-start | bytes 2359300
  113.0 31.3 %all-to-all-start.2 = ((bf16[8,2,128,384]{3,2,1,0:T(8,128)(2,1)}), bf16[8,2,128,384]{3,2,1,0:T(8,128)(2,1)S(1)}, u32[]{:S(2)}, u32[]{:S(2)}) async-start(bf16[8,2,128,384]{3,2,1,0:T(8,128)(2,1)} %get-tuple-element.15), calls=%async_computation.2 | async-start | bytes 3145728 | tf_op jit(solution)/shard_map/all_to_all | solution.py:189
  116.7 22.5 %collective-permute-start.2 = (bf16[8,1,128,384]{3,2,1,0:T(8,128)(2,1)}, bf16[8,1,128,384]{3,2,1,0:T(8,128)(2,1)S(1)}, u32[]{:S(2)}, u32[]{:S(2)}) collective-permute-start(bf16[8,1,128,384]{3,2,1,0:T(8,128)(2,1)} %get-tuple-element.19), channel_id=1, source_target_pairs={{1,0},{2,1},{3,2},{4,3},{5,4},{6,5},{7,6},{8,7},{9,8},{10,9},{11,1... | collective-permute-start | bytes 2359304 | tf_op jit(solution)/shard_map/ppermute | solution.py:30
  118.6 24.4 %collective-permute-start.3 = (bf16[8,1,128,384]{3,2,1,0:T(8,128)(2,1)S(1)}, bf16[8,1,128,384]{3,2,1,0:T(8,128)(2,1)S(1)}, u32[]{:S(2)}, u32[]{:S(2)}) collective-permute-start(bf16[8,1,128,384]{3,2,1,0:T(8,128)(2,1)S(1)} %copy-done.10), channel_id=1, source_target_pairs={{0,1},{1,2},{2,3},{3,4},{4,5},{5,6},{6,7},{7,8},{8,9},{9,10},{10,1... | collective-permute-start | bytes 2359304 | tf_op jit(solution)/shard_map/ppermute | solution.py:30
  122.6 33.0 %collective-permute-start.4 = (bf16[8,1,128,384]{3,2,1,0:T(8,128)(2,1)}, bf16[8,1,128,384]{3,2,1,0:T(8,128)(2,1)}, u32[]{:S(2)}, u32[]{:S(2)}) collective-permute-start(bf16[8,1,128,384]{3,2,1,0:T(8,128)(2,1)} %get-tuple-element.22), channel_id=1, source_target_pairs={{1,0},{2,1},{3,2},{4,3},{5,4},{6,5},{7,6},{8,7},{9,8},{10,9},{11,1... | collective-permute-start | bytes 2359304 | tf_op jit(solution)/shard_map/ppermute | solution.py:30
  126.6 32.8 %collective-permute-start.5 = (bf16[8,1,128,384]{3,2,1,0:T(8,128)(2,1)}, bf16[8,1,128,384]{3,2,1,0:T(8,128)(2,1)}, u32[]{:S(2)}, u32[]{:S(2)}) collective-permute-start(bf16[8,1,128,384]{3,2,1,0:T(8,128)(2,1)} %get-tuple-element.23), channel_id=1, source_target_pairs={{0,1},{1,2},{2,3},{3,4},{4,5},{5,6},{6,7},{7,8},{8,9},{9,10},{10,1... | collective-permute-start | bytes 2359304 | tf_op jit(solution)/shard_map/ppermute | solution.py:30
  144.3 15.2 %copy-start.7 = (bf16[8,1,128,384]{3,2,1,0:T(8,128)(2,1)S(1)}, bf16[8,1,128,384]{3,2,1,0:T(8,128)(2,1)}, u32[]{:S(2)}) copy-start(bf16[8,1,128,384]{3,2,1,0:T(8,128)(2,1)} %get-tuple-element.21) | copy-start | bytes 2359300
  144.3 17.7 %copy-start.2 = (bf16[8,2,128,384]{3,2,1,0:T(8,128)(2,1)}, bf16[8,2,128,384]{3,2,1,0:T(8,128)(2,1)S(1)}, u32[]{:S(2)}) copy-start(bf16[8,2,128,384]{3,2,1,0:T(8,128)(2,1)S(1)} %all-to-all-done.2.refs_0_) | copy-start | bytes 4718596
  144.3 18.0 %all-to-all-start.3 = ((bf16[8,1,128,384]{3,2,1,0:T(8,128)(2,1)}), bf16[8,1,128,384]{3,2,1,0:T(8,128)(2,1)S(1)}, u32[]{:S(2)}, u32[]{:S(2)}) async-start(bf16[8,1,128,384]{3,2,1,0:T(8,128)(2,1)} %add_convert_fusion.1), calls=%async_computation.3 | async-start | bytes 1572864 | tf_op jit(solution)/shard_map/all_to_all | solution.py:189
  162.3 7.8 %copy-start.3 = (bf16[8,1,128,384]{3,2,1,0:T(8,128)(2,1)}, bf16[8,1,128,384]{3,2,1,0:T(8,128)(2,1)S(1)}, u32[]{:S(2)}) copy-start(bf16[8,1,128,384]{3,2,1,0:T(8,128)(2,1)S(1)} %all-to-all-done.3.refs_0_) | copy-start | bytes 2359300
  162.3 17.3 %all-to-all-start.4 = ((bf16[8,1,128,384]{3,2,1,0:T(8,128)(2,1)}), bf16[8,1,128,384]{3,2,1,0:T(8,128)(2,1)S(1)}, u32[]{:S(2)}, u32[]{:S(2)}) async-start(bf16[8,1,128,384]{3,2,1,0:T(8,128)(2,1)} %add_convert_fusion), calls=%async_computation.4 | async-start | bytes 1572864 | tf_op jit(solution)/shard_map/all_to_all | solution.py:189
  179.6 0.9 copy-start.4

commit v11 on v9

--- a/solution.py
+++ b/solution.py
@@ -48,7 +48,7 @@
 
 
 def attn_kernel(
-    slot_ref, live_ref, qg_ref, kp_ref, ko_ref, kn_ref, vp_ref, vo_ref, vn_ref,
+    slot_ref, live_ref, gather_ref, qg_ref, kp_ref, ko_ref, kn_ref, vp_ref, vo_ref, vn_ref,
     og_ref, gok_ref, gov_ref, gpk_ref, gpv_ref, gnk_ref, gnv_ref, kg_scr, vg_scr, acc_scr,
 ):
     tile_rows = HD
@@ -63,7 +63,7 @@
     def body(p, carry):
         live_lane = jnp.zeros((1, max_keys * tile_rows), jnp.int32)
         for s in range(max_keys):
-            slot = slot_ref[p, s]
+            slot = gather_ref[p, s]
             side = slot // query_tiles
             tile = slot % query_tiles
             dst = slice(s * tile_rows, (s + 1) * tile_rows)
@@ -106,7 +106,7 @@
         after[...] = acc_scr[2 * query_tiles :, i : i + 1].astype(after.dtype)
 
 
-def attention_heads(qg, k_win, v_win, slot_key, live_slot):
+def attention_heads(qg, k_win, v_win, slot_key, live_slot, gather_key):
     query_tiles, count, tile_rows, width = qg.shape
     max_keys = slot_key.shape[1]
     head_count = width // HD
@@ -115,7 +115,7 @@
     second = pl.BlockSpec((query_tiles, 1, tile_rows, HD), lambda h, *_: (0, 1, 0, h))
     flops = 12 * query_tiles * max_keys * tile_rows * tile_rows * HD * head_count
     grid_spec = pltpu.PrefetchScalarGridSpec(
-        num_scalar_prefetch=2,
+        num_scalar_prefetch=3,
         grid=(head_count,),
         in_specs=[spec] + [one] * 3 + [second] * 3,
         out_specs=[spec] + [one] * 6,
@@ -137,7 +137,7 @@
             transcendentals=query_tiles * max_keys * tile_rows * tile_rows * head_count,
             bytes_accessed=query_tiles * count * tile_rows * width * 2 * 8,
         ),
-    )(slot_key, live_slot.astype(jnp.int32), qg, *k_win, *v_win)
+    )(slot_key, live_slot.astype(jnp.int32), gather_key, qg, *k_win, *v_win)
 
 
 def split_kernel(*refs):
@@ -187,6 +187,17 @@
     return join_columns(moved)
 
 
+def exchange_heads(arrays, groups):
+    stacked = split_columns(arrays, groups)
+    me = lax.axis_index("head")
+    received = [lax.dynamic_index_in_dim(stacked, me, keepdims=False)]
+    for shift in range(1, groups):
+        block = lax.dynamic_index_in_dim(stacked, (me + shift) % groups, keepdims=False)
+        pairs = [(j, (j + shift) % groups) for j in range(groups)]
+        received.append(lax.ppermute(block, "head", pairs))
+    return jnp.stack(received)
+
+
 def local(query, key, value, grad_out, block_mask, tile_order):
     per_frame = lax.axis_size("head")
     frames = lax.axis_size("tile")
@@ -194,11 +205,15 @@
     max_keys = 3 * min(3, per_frame // 2)
     forward_active, _ = window_lists(block_mask, tile_order, frame_idx, frames, per_frame)
     slot_key, live_slot = compact_slots(forward_active, max_keys)
-    kv = to_heads([key, value], per_frame)
+    kv = exchange_heads([key, value], per_frame)
+    me = lax.axis_index("head")
+    side, tile = slot_key // per_frame, slot_key % per_frame
+    gather_key = (side * per_frame + (me - tile) % per_frame).astype(jnp.int32)
+    kv, query, grad_out = lax.optimization_barrier((kv, query, grad_out))
     k_win = (passed_along(kv, "tile", 1), kv, passed_along(kv, "tile", -1))
     v_win = k_win
     qg = to_heads([query, grad_out], per_frame)
-    og, gok, gov, gpk, gpv, gnk, gnv = attention_heads(qg, k_win, v_win, slot_key, live_slot)
+    og, gok, gov, gpk, gpv, gnk, gnv = attention_heads(qg, k_win, v_win, slot_key, live_slot, gather_key)
     attn_out, grad_query = to_tokens(og)
     grads = []
     for own, before, after in ((gok, gpk, gnk), (gov, gpv, gnv)):

time: 183 us -> 191 us (1.044)
  blocking collectives: 26.1 us -> 0 us
  waiting for transfers between devices: 58.7 us -> 77.9 us
  local copies, waits for them, and re-layouts: 5.31 us -> 12.6 us
  starting transfers between devices: 38.3 us -> 44.9 us
    all_to_all x1 -> x0, blocking collectives: 26.1 us -> none  [to_heads(): lax.all_to_all(stacked, 'head', split_axis=0, concat_axis=0, tiled=True)]
    ppermute x0 -> x7, waiting for transfers between devices: none -> 18.2 us  [exchange_heads(): received.append(lax.ppermute(block, 'head', pairs))]
    ppermute x0 -> x7, starting transfers between devices: none -> 6.66 us  [exchange_heads(): received.append(lax.ppermute(block, 'head', pairs))]
    unnamed x18 -> x22, local copies, waits for them, and re-layouts: 0.93 us -> 5.16 us
    squeeze x0 -> x1, local copies, waits for them, and re-layouts: none -> 2.29 us  [exchange_heads(): lax.dynamic_index_in_dim(stacked, (me + shift) % groups, keepdims=False)]
  transfers between devices with their start and end apart: 10 -> 17, of which waited for: 8 -> 10; matrix products, arithmetic and copies ran while one was open for 6% -> 8% of each run, Pallas kernels for 4% -> 4%
where the time goes in v11:
time: 191 us; the launch traced here: 190 us
  waiting for transfers between devices  77.9 us (41%)
  Pallas kernels  47.4 us (25%)
  starting transfers between devices  44.9 us (24%)
  local copies, waits for them, and re-layouts  12.6 us (7%)
  other arithmetic  6.4 us (3%)
    ppermute x6, waiting for transfers between devices, passed_along(): lax.ppermute(value, axis, [(source, source + steps) for source in range(i...  35.8 us
    pallas_call x1, Pallas kernels, attention_heads(): pl.pallas_call(attn_kernel, grid_spec=grid_spec, out_shape=[jax.ShapeDtyp...  35.2 us
    ppermute x6, starting transfers between devices, passed_along(): lax.ppermute(value, axis, [(source, source + steps) for source in range(i...  21.7 us
    ppermute x7, waiting for transfers between devices, exchange_heads(): received.append(lax.ppermute(block, 'head', pairs))  18.2 us
    all_to_all x1, waiting for transfers between devices, to_heads(): lax.all_to_all(stacked, 'head', split_axis=0, concat_axis=0, tiled=True)  15.6 us
    all_to_all x3, starting transfers between devices, to_tokens(): lax.all_to_all(stacked, 'head', split_axis=0, concat_axis=0, tiled=True)  12.9 us
    all_to_all x3, waiting for transfers between devices, to_tokens(): lax.all_to_all(stacked, 'head', split_axis=0, concat_axis=0, tiled=True)  8.37 us
    pallas_call x3, Pallas kernels, join_columns(): pl.pallas_call(join_kernel, in_specs=[pl.BlockSpec(memory_space=pltpu.VME...  6.83 us
  transfers between devices with their start and end apart: 17, of which 10 were waited for; matrix products, arithmetic and copies ran while one was open for 8% of the time, Pallas kernels for 4%

profile of v11, /device:TPU:6, one launch (start us, length us, event | category | flops | bytes accessed | tf_op | source)
XLA Modules:
  0.0 190.0 jit_solution(11850546448764390580)
XLA Ops:
  0.8 2.7 %shard_map.93 = bf16[8,2,128,384]{3,2,1,0:T(8,128)(2,1)} custom-call(bf16[128,3072]{1,0:T(8,128)(2,1)} %refs_0_.1, bf16[128,3072]{1,0:T(8,128)(2,1)} %refs_1_.1), custom_call_target="tpu_custom_call" | custom-call | tf_op jit(solution)/shard_map/pallas_call | solution.py:162
  3.4 2.3 %dynamic-slice_bitcast_fusion = (bf16[2,128,384]{2,1,0:T(8,128)(2,1)S(1)}, bf16[2,128,384]{2,1,0:T(8,128)(2,1)S(1)}, bf16[2,128,384]{2,1,0:T(8,128)(2,1)S(1)}, b...) fusion(bf16[8,2,128,384]{3,2,1,0:T(8,128)(2,1)} %shard_map.93, ...), kind=kLoop, calls=%fused_computation.12 | loop fusion | bytes 3145760 | tf_op jit(solution)/shard_map/jit(dynamic_index_in_dim)/squeeze | solution.py:195
  5.7 3.0 %collective-permute-start.6 = (bf16[2,128,384]{2,1,0:T(8,128)(2,1)S(1)}, bf16[2,128,384]{2,1,0:T(8,128)(2,1)S(1)}, u32[]{:S(2)}, u32[]{:S(2)}) collective-permute-start(bf16[2,128,384]{2,1,0:T(8,128)(2,1)S(1)} %get-tuple-element.32), channel_id=1, source_target_pairs={{0,224},{32,0},{64,32},{96,64},{128,96},{160,128},{192,160},{224,1... | collective-permute-start | bytes 589832 | tf_op jit(solution)/shard_map/ppermute | solution.py:197
  13.1 11.1 %collective-permute-done.1 = bf16[2,128,384]{2,1,0:T(8,128)(2,1)S(1)} collective-permute-done((bf16[2,128,384]{2,1,0:T(8,128)(2,1)S(1)}, bf16[2,128,384]{2,1,0:T(8,128)(2,1)S(1)}, u32[]{:S(2)}, u32[]{:S(2)}) %collective-permute-start.1) | collective-permute-done | bytes 196640 | tf_op jit(solution)/shard_map/ppermute | solution.py:197
  24.9 7.0 %collective-permute-done.2 = bf16[2,128,384]{2,1,0:T(8,128)(2,1)S(1)} collective-permute-done((bf16[2,128,384]{2,1,0:T(8,128)(2,1)S(1)}, bf16[2,128,384]{2,1,0:T(8,128)(2,1)S(1)}, u32[]{:S(2)}, u32[]{:S(2)}) %collective-permute-start.2) | collective-permute-done | bytes 196640 | tf_op jit(solution)/shard_map/ppermute | solution.py:197
  35.5 8.0 %collective-permute-start.8 = (bf16[8,2,128,384]{3,2,1,0:T(8,128)(2,1)}, bf16[8,2,128,384]{3,2,1,0:T(8,128)(2,1)S(1)}, u32[]{:S(2)}, u32[]{:S(2)}) collective-permute-start(bf16[8,2,128,384]{3,2,1,0:T(8,128)(2,1)} %bitcast_dynamic-update-slice_fusion.ko_ref.vo_ref), channel_id=1, source_target_pairs={{1,0},{2,1},{3,2},{4,3},{5,4},{6,5},{7,6},{8,7},{9,8},{10,9},{11,1... | collective-permute-start | bytes 4718600 | tf_op jit(solution)/shard_map/ppermute | solution.py:30
  46.2 2.7 %shard_map.94 = bf16[8,2,128,384]{3,2,1,0:T(8,128)(2,1)} custom-call(bf16[128,3072]{1,0:T(8,128)(2,1)} %refs_0_.2, bf16[128,3072]{1,0:T(8,128)(2,1)} %refs_1_.2), custom_call_target="tpu_custom_call" | custom-call | tf_op jit(solution)/shard_map/pallas_call | solution.py:162
  48.9 3.6 %all-to-all-start = ((bf16[8,2,128,384]{3,2,1,0:T(8,128)(2,1)}), bf16[8,2,128,384]{3,2,1,0:T(8,128)(2,1)S(1)}, u32[]{:S(2)}, u32[]{:S(2)}) async-start(bf16[8,2,128,384]{3,2,1,0:T(8,128)(2,1)} %shard_map.94), calls=%async_computation | async-start | bytes 3145728 | tf_op jit(solution)/shard_map/all_to_all | solution.py:182
  58.4 15.6 %all-to-all-done.qg_ref = bf16[8,2,128,384]{3,2,1,0:T(8,128)(2,1)S(1)} async-done(((bf16[8,2,128,384]{3,2,1,0:T(8,128)(2,1)}), bf16[8,2,128,384]{3,2,1,0:T(8,128)(2,1)S(1)}, u32[]{:S(2)}, u32[]{:S(2)}) %all-to-all-start) | async-done | bytes 1572896 | tf_op jit(solution)/shard_map/all_to_all | solution.py:182
  74.0 4.4 %collective-permute-done.8.kn_ref.vn_ref = bf16[8,2,128,384]{3,2,1,0:T(8,128)(2,1)S(1)} collective-permute-done((bf16[8,2,128,384]{3,2,1,0:T(8,128)(2,1)}, bf16[8,2,128,384]{3,2,1,0:T(8,128)(2,1)S(1)}, u32[]{:S(2)}, u32[]{:S(2)}) %collective-permute-start.8) | collective-permute-done | bytes 1572896 | tf_op jit(solution)/shard_map/ppermute | solution.py:30
  78.4 6.2 %collective-permute-done.7.kp_ref.vp_ref = bf16[8,2,128,384]{3,2,1,0:T(8,128)(2,1)} collective-permute-done((bf16[8,2,128,384]{3,2,1,0:T(8,128)(2,1)}, bf16[8,2,128,384]{3,2,1,0:T(8,128)(2,1)}, u32[]{:S(2)}, u32[]{:S(2)}) %collective-permute-start.7) | collective-permute-done | bytes 1572896 | tf_op jit(solution)/shard_map/ppermute | solution.py:30
  84.6 35.2 %shard_map.95 = (bf16[8,2,128,384]{3,2,1,0:T(8,128)(2,1)}, f32[8,1,128,384]{3,2,1,0:T(8,128)}, f32[8,1,128,384]{3,2,1,0:T(8,128)}, bf16[8,1,128,384]{3,2,1,0:T(8...) custom-call(s32[8,9]{1,0:T(8,128)} %get-tuple-element.41.slot_ref, ...), custom_call_target="tpu_custom_call" | custom-call | flops 5435817984 | bytes 12582912 | tf_op jit(solution)/shard_map/pallas_call | solution.py:129
  119.8 3.7 %all-to-all-start.1 = ((bf16[8,2,128,384]{3,2,1,0:T(8,128)(2,1)}), bf16[8,2,128,384]{3,2,1,0:T(8,128)(2,1)S(1)}, u32[]{:S(2)}, u32[]{:S(2)}) async-start(bf16[8,2,128,384]{3,2,1,0:T(8,128)(2,1)} %get-tuple-element.21), calls=%async_computation.1 | async-start | bytes 3145728 | tf_op jit(solution)/shard_map/all_to_all | solution.py:186
  125.5 3.9 %collective-permute-start.10 = (bf16[8,1,128,384]{3,2,1,0:T(8,128)(2,1)}, bf16[8,1,128,384]{3,2,1,0:T(8,128)(2,1)S(1)}, u32[]{:S(2)}, u32[]{:S(2)}) collective-permute-start(bf16[8,1,128,384]{3,2,1,0:T(8,128)(2,1)} %get-tuple-element.26), channel_id=1, source_target_pairs={{0,1},{1,2},{2,3},{3,4},{4,5},{5,6},{6,7},{7,8},{8,9},{9,10},{10,1... | collective-permute-start | bytes 2359304 | tf_op jit(solution)/shard_map/ppermute | solution.py:30
  129.4 4.0 %collective-permute-start.11 = (bf16[8,1,128,384]{3,2,1,0:T(8,128)(2,1)}, bf16[8,1,128,384]{3,2,1,0:T(8,128)(2,1)}, u32[]{:S(2)}, u32[]{:S(2)}) collective-permute-start(bf16[8,1,128,384]{3,2,1,0:T(8,128)(2,1)} %get-tuple-element.28), channel_id=1, source_target_pairs={{1,0},{2,1},{3,2},{4,3},{5,4},{6,5},{7,6},{8,7},{9,8},{10,9},{11,1... | collective-permute-start | bytes 2359304 | tf_op jit(solution)/shard_map/ppermute | solution.py:30
  135.4 10.7 %collective-permute-done.9 = bf16[8,1,128,384]{3,2,1,0:T(8,128)(2,1)S(1)} collective-permute-done((bf16[8,1,128,384]{3,2,1,0:T(8,128)(2,1)}, bf16[8,1,128,384]{3,2,1,0:T(8,128)(2,1)S(1)}, u32[]{:S(2)}, u32[]{:S(2)}) %collective-permute-start.9) | collective-permute-done | bytes 786464 | tf_op jit(solution)/shard_map/ppermute | solution.py:30
  146.1 4.0 %collective-permute-done.10 = bf16[8,1,128,384]{3,2,1,0:T(8,128)(2,1)S(1)} collective-permute-done((bf16[8,1,128,384]{3,2,1,0:T(8,128)(2,1)}, bf16[8,1,128,384]{3,2,1,0:T(8,128)(2,1)S(1)}, u32[]{:S(2)}, u32[]{:S(2)}) %collective-permute-start.10) | collective-permute-done | bytes 786464 | tf_op jit(solution)/shard_map/ppermute | solution.py:30
  151.3 4.7 %all-to-all-start.2 = ((bf16[8,1,128,384]{3,2,1,0:T(8,128)(2,1)}), bf16[8,1,128,384]{3,2,1,0:T(8,128)(2,1)S(1)}, u32[]{:S(2)}, u32[]{:S(2)}) async-start(bf16[8,1,128,384]{3,2,1,0:T(8,128)(2,1)} %add_convert_fusion.1), calls=%async_computation.2 | async-start | bytes 1572864 | tf_op jit(solution)/shard_map/all_to_all | solution.py:186
  156.0 6.4 %collective-permute-done.11 = bf16[8,1,128,384]{3,2,1,0:T(8,128)(2,1)} collective-permute-done((bf16[8,1,128,384]{3,2,1,0:T(8,128)(2,1)}, bf16[8,1,128,384]{3,2,1,0:T(8,128)(2,1)}, u32[]{:S(2)}, u32[]{:S(2)}) %collective-permute-start.11) | collective-permute-done | bytes 786464 | tf_op jit(solution)/shard_map/ppermute | solution.py:30
  162.4 4.0 %collective-permute-done.12 = bf16[8,1,128,384]{3,2,1,0:T(8,128)(2,1)} collective-permute-done((bf16[8,1,128,384]{3,2,1,0:T(8,128)(2,1)}, bf16[8,1,128,384]{3,2,1,0:T(8,128)(2,1)}, u32[]{:S(2)}, u32[]{:S(2)}) %collective-permute-start.12) | collective-permute-done | bytes 786464 | tf_op jit(solution)/shard_map/ppermute | solution.py:30
  166.5 3.0 %add_convert_fusion = bf16[8,1,128,384]{3,2,1,0:T(8,128)(2,1)} fusion(bf16[8,1,128,384]{3,2,1,0:T(8,128)(2,1)} %collective-permute-done.12, f32[8,1,128,384]{3,2,1,0:T(8,128)} %get-tuple-element.27, bf16[8,1,128,384]{3,2,1,0:T(8,128)(2,1)} %collective-permute-done.11), kind=kLoop, calls=%fused_computation.3 | loop fusion | flops 1966080 | bytes 3932160 | tf_op jit(solution)/shard_map/convert_element_type | solution.py:222
  169.5 4.5 %all-to-all-start.3 = ((bf16[8,1,128,384]{3,2,1,0:T(8,128)(2,1)}), bf16[8,1,128,384]{3,2,1,0:T(8,128)(2,1)S(1)}, u32[]{:S(2)}, u32[]{:S(2)}) async-start(bf16[8,1,128,384]{3,2,1,0:T(8,128)(2,1)} %add_convert_fusion), calls=%async_computation.3 | async-start | bytes 1572864 | tf_op jit(solution)/shard_map/all_to_all | solution.py:186
  173.9 2.7 %shard_map.96 = (bf16[128,3072]{1,0:T(8,128)(2,1)}, bf16[128,3072]{1,0:T(8,128)(2,1)}) custom-call(bf16[8,2,128,384]{3,2,1,0:T(8,128)(2,1)} %copy-done.2), custom_call_target="tpu_custom_call" | custom-call | tf_op jit(solution)/shard_map/pallas_call | solution.py:172
  178.7 8.4 %all-to-all-done.3.refs_0_ = bf16[8,1,128,384]{3,2,1,0:T(8,128)(2,1)S(1)} async-done(((bf16[8,1,128,384]{3,2,1,0:T(8,128)(2,1)}), bf16[8,1,128,384]{3,2,1,0:T(8,128)(2,1)S(1)}, u32[]{:S(2)}, u32[]{:S(2)}) %all-to-all-start.3) | async-done | bytes 786464 | tf_op jit(solution)/shard_map/all_to_all | solution.py:186
  (63 shorter events, 27.3 us)
Async XLA Ops:
  0.6 52.1 %copy-start = (s32[256,256]{1,0:T(8,128)S(1)}, s32[256,256]{1,0:T(8,128)}, u32[]{:S(2)}) copy-start(s32[256,256]{1,0:T(8,128)} %param.10) | copy-start | bytes 786436
  5.7 39.8 %copy-start.1 = (s32[256]{0:T(256)S(1)}, s32[256]{0:T(256)}, u32[]{:S(2)}) copy-start(s32[256]{0:T(256)} %param.11) | copy-start | bytes 3076
  5.7 6.4 %collective-permute-start = (bf16[2,128,384]{2,1,0:T(8,128)(2,1)S(1)}, bf16[2,128,384]{2,1,0:T(8,128)(2,1)S(1)}, u32[]{:S(2)}, u32[]{:S(2)}) collective-permute-start(bf16[2,128,384]{2,1,0:T(8,128)(2,1)S(1)} %get-tuple-element.38), channel_id=1, source_target_pairs={{0,32},{32,64},{64,96},{96,128},{128,160},{160,192},{192,224},{224... | collective-permute-start | bytes 589832 | tf_op jit(solution)/shard_map/ppermute | solution.py:197
  5.7 29.1 %collective-permute-start.6 = (bf16[2,128,384]{2,1,0:T(8,128)(2,1)S(1)}, bf16[2,128,384]{2,1,0:T(8,128)(2,1)S(1)}, u32[]{:S(2)}, u32[]{:S(2)}) collective-permute-start(bf16[2,128,384]{2,1,0:T(8,128)(2,1)S(1)} %get-tuple-element.32), channel_id=1, source_target_pairs={{0,224},{32,0},{64,32},{96,64},{128,96},{160,128},{192,160},{224,1... | collective-permute-start | bytes 589832 | tf_op jit(solution)/shard_map/ppermute | solution.py:197
  8.7 25.4 %collective-permute-start.5 = (bf16[2,128,384]{2,1,0:T(8,128)(2,1)S(1)}, bf16[2,128,384]{2,1,0:T(8,128)(2,1)S(1)}, u32[]{:S(2)}, u32[]{:S(2)}) collective-permute-start(bf16[2,128,384]{2,1,0:T(8,128)(2,1)S(1)} %get-tuple-element.33), channel_id=1, source_target_pairs={{0,192},{32,224},{64,0},{96,32},{128,64},{160,96},{192,128},{224,1... | collective-permute-start | bytes 589832 | tf_op jit(solution)/shard_map/ppermute | solution.py:197
  10.5 22.9 %collective-permute-start.4 = (bf16[2,128,384]{2,1,0:T(8,128)(2,1)S(1)}, bf16[2,128,384]{2,1,0:T(8,128)(2,1)S(1)}, u32[]{:S(2)}, u32[]{:S(2)}) collective-permute-start(bf16[2,128,384]{2,1,0:T(8,128)(2,1)S(1)} %get-tuple-element.34), channel_id=1, source_target_pairs={{0,160},{32,192},{64,224},{96,0},{128,32},{160,64},{192,96},{224,1... | collective-permute-start | bytes 589832 | tf_op jit(solution)/shard_map/ppermute | solution.py:197
  10.5 22.2 %collective-permute-start.3 = (bf16[2,128,384]{2,1,0:T(8,128)(2,1)S(1)}, bf16[2,128,384]{2,1,0:T(8,128)(2,1)S(1)}, u32[]{:S(2)}, u32[]{:S(2)}) collective-permute-start(bf16[2,128,384]{2,1,0:T(8,128)(2,1)S(1)} %get-tuple-element.35), channel_id=1, source_target_pairs={{0,128},{32,160},{64,192},{96,224},{128,0},{160,32},{192,64},{224,... | collective-permute-start | bytes 589832 | tf_op jit(solution)/shard_map/ppermute | solution.py:197
  12.1 12.1 %collective-permute-start.1 = (bf16[2,128,384]{2,1,0:T(8,128)(2,1)S(1)}, bf16[2,128,384]{2,1,0:T(8,128)(2,1)S(1)}, u32[]{:S(2)}, u32[]{:S(2)}) collective-permute-start(bf16[2,128,384]{2,1,0:T(8,128)(2,1)S(1)} %get-tuple-element.37), channel_id=1, source_target_pairs={{0,64},{32,96},{64,128},{96,160},{128,192},{160,224},{192,0},{224,... | collective-permute-start | bytes 589832 | tf_op jit(solution)/shard_map/ppermute | solution.py:197
  24.2 7.8 %collective-permute-start.2 = (bf16[2,128,384]{2,1,0:T(8,128)(2,1)S(1)}, bf16[2,128,384]{2,1,0:T(8,128)(2,1)S(1)}, u32[]{:S(2)}, u32[]{:S(2)}) collective-permute-start(bf16[2,128,384]{2,1,0:T(8,128)(2,1)S(1)} %get-tuple-element.36), channel_id=1, source_target_pairs={{0,96},{32,128},{64,160},{96,192},{128,224},{160,0},{192,32},{224,... | collective-permute-start | bytes 589832 | tf_op jit(solution)/shard_map/ppermute | solution.py:197
  35.5 42.9 %collective-permute-start.8 = (bf16[8,2,128,384]{3,2,1,0:T(8,128)(2,1)}, bf16[8,2,128,384]{3,2,1,0:T(8,128)(2,1)S(1)}, u32[]{:S(2)}, u32[]{:S(2)}) collective-permute-start(bf16[8,2,128,384]{3,2,1,0:T(8,128)(2,1)} %bitcast_dynamic-update-slice_fusion.ko_ref.vo_ref), channel_id=1, source_target_pairs={{1,0},{2,1},{3,2},{4,3},{5,4},{6,5},{7,6},{8,7},{9,8},{10,9},{11,1... | collective-permute-start | bytes 4718600 | tf_op jit(solution)/shard_map/ppermute | solution.py:30
  43.6 41.1 %collective-permute-start.7 = (bf16[8,2,128,384]{3,2,1,0:T(8,128)(2,1)}, bf16[8,2,128,384]{3,2,1,0:T(8,128)(2,1)}, u32[]{:S(2)}, u32[]{:S(2)}) collective-permute-start(bf16[8,2,128,384]{3,2,1,0:T(8,128)(2,1)} %bitcast_dynamic-update-slice_fusion.ko_ref.vo_ref), channel_id=1, source_target_pairs={{0,1},{1,2},{2,3},{3,4},{4,5},{5,6},{6,7},{7,8},{8,9},{9,10},{10,1... | collective-permute-start | bytes 4718600 | tf_op jit(solution)/shard_map/ppermute | solution.py:30
  48.9 25.1 %all-to-all-start = ((bf16[8,2,128,384]{3,2,1,0:T(8,128)(2,1)}), bf16[8,2,128,384]{3,2,1,0:T(8,128)(2,1)S(1)}, u32[]{:S(2)}, u32[]{:S(2)}) async-start(bf16[8,2,128,384]{3,2,1,0:T(8,128)(2,1)} %shard_map.94), calls=%async_computation | async-start | bytes 3145728 | tf_op jit(solution)/shard_map/all_to_all | solution.py:182
  74.0 10.7 %copy-start.5 = (bf16[8,2,128,384]{3,2,1,0:T(8,128)(2,1)}, bf16[8,2,128,384]{3,2,1,0:T(8,128)(2,1)S(1)}, u32[]{:S(2)}) copy-start(bf16[8,2,128,384]{3,2,1,0:T(8,128)(2,1)S(1)} %all-to-all-done.qg_ref) | copy-start | bytes 4718596
  78.4 6.2 %copy-start.7 = (bf16[8,2,128,384]{3,2,1,0:T(8,128)(2,1)}, bf16[8,2,128,384]{3,2,1,0:T(8,128)(2,1)S(1)}, u32[]{:S(2)}) copy-start(bf16[8,2,128,384]{3,2,1,0:T(8,128)(2,1)S(1)} %collective-permute-done.8.kn_ref.vn_ref) | copy-start | bytes 4718596
  119.8 30.3 %copy-start.6 = (f32[8,1,128,384]{3,2,1,0:T(8,128)S(1)}, f32[8,1,128,384]{3,2,1,0:T(8,128)}, u32[]{:S(2)}) copy-start(f32[8,1,128,384]{3,2,1,0:T(8,128)} %get-tuple-element.24) | copy-start | bytes 4718596
  119.8 31.5 %all-to-all-start.1 = ((bf16[8,2,128,384]{3,2,1,0:T(8,128)(2,1)}), bf16[8,2,128,384]{3,2,1,0:T(8,128)(2,1)S(1)}, u32[]{:S(2)}, u32[]{:S(2)}) async-start(bf16[8,2,128,384]{3,2,1,0:T(8,128)(2,1)} %get-tuple-element.21), calls=%async_computation.1 | async-start | bytes 3145728 | tf_op jit(solution)/shard_map/all_to_all | solution.py:186
  123.5 22.5 %collective-permute-start.9 = (bf16[8,1,128,384]{3,2,1,0:T(8,128)(2,1)}, bf16[8,1,128,384]{3,2,1,0:T(8,128)(2,1)S(1)}, u32[]{:S(2)}, u32[]{:S(2)}) collective-permute-start(bf16[8,1,128,384]{3,2,1,0:T(8,128)(2,1)} %get-tuple-element.25), channel_id=1, source_target_pairs={{1,0},{2,1},{3,2},{4,3},{5,4},{6,5},{7,6},{8,7},{9,8},{10,9},{11,1... | collective-permute-start | bytes 2359304 | tf_op jit(solution)/shard_map/ppermute | solution.py:30
  125.5 24.6 %collective-permute-start.10 = (bf16[8,1,128,384]{3,2,1,0:T(8,128)(2,1)}, bf16[8,1,128,384]{3,2,1,0:T(8,128)(2,1)S(1)}, u32[]{:S(2)}, u32[]{:S(2)}) collective-permute-start(bf16[8,1,128,384]{3,2,1,0:T(8,128)(2,1)} %get-tuple-element.26), channel_id=1, source_target_pairs={{0,1},{1,2},{2,3},{3,4},{4,5},{5,6},{6,7},{7,8},{8,9},{9,10},{10,1... | collective-permute-start | bytes 2359304 | tf_op jit(solution)/shard_map/ppermute | solution.py:30
  129.4 33.0 %collective-permute-start.11 = (bf16[8,1,128,384]{3,2,1,0:T(8,128)(2,1)}, bf16[8,1,128,384]{3,2,1,0:T(8,128)(2,1)}, u32[]{:S(2)}, u32[]{:S(2)}) collective-permute-start(bf16[8,1,128,384]{3,2,1,0:T(8,128)(2,1)} %get-tuple-element.28), channel_id=1, source_target_pairs={{1,0},{2,1},{3,2},{4,3},{5,4},{6,5},{7,6},{8,7},{9,8},{10,9},{11,1... | collective-permute-start | bytes 2359304 | tf_op jit(solution)/shard_map/ppermute | solution.py:30
  133.4 33.0 %collective-permute-start.12 = (bf16[8,1,128,384]{3,2,1,0:T(8,128)(2,1)}, bf16[8,1,128,384]{3,2,1,0:T(8,128)(2,1)}, u32[]{:S(2)}, u32[]{:S(2)}) collective-permute-start(bf16[8,1,128,384]{3,2,1,0:T(8,128)(2,1)} %get-tuple-element.29), channel_id=1, source_target_pairs={{0,1},{1,2},{2,3},{3,4},{4,5},{5,6},{6,7},{7,8},{8,9},{9,10},{10,1... | collective-permute-start | bytes 2359304 | tf_op jit(solution)/shard_map/ppermute | solution.py:30
  151.3 18.1 %copy-start.2 = (bf16[8,2,128,384]{3,2,1,0:T(8,128)(2,1)}, bf16[8,2,128,384]{3,2,1,0:T(8,128)(2,1)S(1)}, u32[]{:S(2)}) copy-start(bf16[8,2,128,384]{3,2,1,0:T(8,128)(2,1)S(1)} %all-to-all-done.1.refs_0_) | copy-start | bytes 4718596
  151.3 18.1 %all-to-all-start.2 = ((bf16[8,1,128,384]{3,2,1,0:T(8,128)(2,1)}), bf16[8,1,128,384]{3,2,1,0:T(8,128)(2,1)S(1)}, u32[]{:S(2)}, u32[]{:S(2)}) async-start(bf16[8,1,128,384]{3,2,1,0:T(8,128)(2,1)} %add_convert_fusion.1), calls=%async_computation.2 | async-start | bytes 1572864 | tf_op jit(solution)/shard_map/all_to_all | solution.py:186
  169.5 7.1 %copy-start.3 = (bf16[8,1,128,384]{3,2,1,0:T(8,128)(2,1)}, bf16[8,1,128,384]{3,2,1,0:T(8,128)(2,1)S(1)}, u32[]{:S(2)}) copy-start(bf16[8,1,128,384]{3,2,1,0:T(8,128)(2,1)S(1)} %all-to-all-done.2.refs_0_) | copy-start | bytes 2359300
  169.5 17.6 %all-to-all-start.3 = ((bf16[8,1,128,384]{3,2,1,0:T(8,128)(2,1)}), bf16[8,1,128,384]{3,2,1,0:T(8,128)(2,1)S(1)}, u32[]{:S(2)}, u32[]{:S(2)}) async-start(bf16[8,1,128,384]{3,2,1,0:T(8,128)(2,1)} %add_convert_fusion), calls=%async_computation.3 | async-start | bytes 1572864 | tf_op jit(solution)/shard_map/all_to_all | solution.py:186
  (1 other events, 0.9 us)

commit v12 on v9

--- a/solution.py
+++ b/solution.py
@@ -78,10 +78,10 @@
         g = qg_ref[p, 1]
         kg = kg_scr[...]
         vg = vg_scr[...]
-        sc = lax.dot_general(q, kg, nt, preferred_element_type=jnp.float32) * scaling
+        sc = lax.dot_general(q, kg, nt, preferred_element_type=jnp.float32)
         sc = jnp.where(live_lane > 0, sc, NEG)
         top = jnp.max(sc, axis=1, keepdims=True)
-        expd = jnp.exp(sc - top)
+        expd = jnp.exp((sc - top) * scaling)
         prob = expd * (1.0 / jnp.sum(expd, axis=1, keepdims=True))
         prob_bf = prob.astype(jnp.bfloat16)
         out = jnp.dot(prob_bf, vg, preferred_element_type=jnp.float32).astype(jnp.bfloat16)

time: 183 us -> 184 us (level)
  no operation moved by 1% of the time
where the time goes in v12:
time: 184 us; the launch traced here: 183 us
  waiting for transfers between devices  58.7 us (32%)
  Pallas kernels  47.7 us (26%)
  starting transfers between devices  38.3 us (21%)
  blocking collectives  26.1 us (14%)
  other arithmetic  5.83 us (3%)
  local copies, waits for them, and re-layouts  5.31 us (3%)
    pallas_call x1, Pallas kernels, attention_heads(): pl.pallas_call(attn_kernel, grid_spec=grid_spec, out_shape=[jax.ShapeDtyp...  35.5 us
    ppermute x6, waiting for transfers between devices, passed_along(): lax.ppermute(value, axis, [(source, source + steps) for source in range(i...  35 us
    all_to_all x1, blocking collectives, to_heads(): lax.all_to_all(stacked, 'head', split_axis=0, concat_axis=0, tiled=True)  26.1 us
    ppermute x6, starting transfers between devices, passed_along(): lax.ppermute(value, axis, [(source, source + steps) for source in range(i...  21.7 us
    all_to_all x1, waiting for transfers between devices, to_heads(): lax.all_to_all(stacked, 'head', split_axis=0, concat_axis=0, tiled=True)  15.4 us
    all_to_all x3, starting transfers between devices, to_tokens(): lax.all_to_all(stacked, 'head', split_axis=0, concat_axis=0, tiled=True)  12.9 us
    all_to_all x3, waiting for transfers between devices, to_tokens(): lax.all_to_all(stacked, 'head', split_axis=0, concat_axis=0, tiled=True)  8.37 us
    pallas_call x3, Pallas kernels, join_columns(): pl.pallas_call(join_kernel, in_specs=[pl.BlockSpec(memory_space=pltpu.VME...  6.83 us
  transfers between devices with their start and end apart: 10, of which 8 were waited for; matrix products, arithmetic and copies ran while one was open for 6% of the time, Pallas kernels for 4%

profile of v12, /device:TPU:6, one launch (start us, length us, event | category | flops | bytes accessed | tf_op | source)
XLA Modules:
  0.0 182.8 jit_solution(14365351038998543155)
XLA Ops:
  0.6 2.7 %shard_map.94 = bf16[8,2,128,384]{3,2,1,0:T(8,128)(2,1)} custom-call(bf16[128,3072]{1,0:T(8,128)(2,1)} %refs_0_.3, bf16[128,3072]{1,0:T(8,128)(2,1)} %refs_1_.3), custom_call_target="tpu_custom_call" | custom-call | tf_op jit(solution)/shard_map/pallas_call | solution.py:162
  3.4 26.1 %all_to_all.25.ko_ref.vo_ref = bf16[8,2,128,384]{3,2,1,0:T(8,128)(2,1)S(1)} all-to-all(bf16[8,2,128,384]{3,2,1,0:T(8,128)(2,1)} %shard_map.94), channel_id=1, replica_groups=mesh['head'=8,'tile'=32] {'head'}, dimensions={0} | all-to-all | bytes 3145728 | tf_op jit(solution)/shard_map/all_to_all | solution.py:182
  29.4 8.0 %collective-permute-start.1 = (bf16[8,2,128,384]{3,2,1,0:T(8,128)(2,1)S(1)}, bf16[8,2,128,384]{3,2,1,0:T(8,128)(2,1)}, u32[]{:S(2)}, u32[]{:S(2)}) collective-permute-start(bf16[8,2,128,384]{3,2,1,0:T(8,128)(2,1)S(1)} %all_to_all.25.ko_ref.vo_ref), channel_id=1, source_target_pairs={{1,0},{2,1},{3,2},{4,3},{5,4},{6,5},{7,6},{8,7},{9,8},{10,9},{11,1... | collective-permute-start | bytes 4718600 | tf_op jit(solution)/shard_map/ppermute | solution.py:30
  39.4 2.7 %shard_map.93 = bf16[8,2,128,384]{3,2,1,0:T(8,128)(2,1)} custom-call(bf16[128,3072]{1,0:T(8,128)(2,1)} %refs_0_.2, bf16[128,3072]{1,0:T(8,128)(2,1)} %refs_1_.2), custom_call_target="tpu_custom_call" | custom-call | tf_op jit(solution)/shard_map/pallas_call | solution.py:162
  42.1 3.7 %all-to-all-start = ((bf16[8,2,128,384]{3,2,1,0:T(8,128)(2,1)}), bf16[8,2,128,384]{3,2,1,0:T(8,128)(2,1)S(1)}, u32[]{:S(2)}, u32[]{:S(2)}) async-start(bf16[8,2,128,384]{3,2,1,0:T(8,128)(2,1)} %shard_map.93), calls=%async_computation | async-start | bytes 3145728 | tf_op jit(solution)/shard_map/all_to_all | solution.py:182
  51.8 15.4 %all-to-all-done.qg_ref = bf16[8,2,128,384]{3,2,1,0:T(8,128)(2,1)S(1)} async-done(((bf16[8,2,128,384]{3,2,1,0:T(8,128)(2,1)}), bf16[8,2,128,384]{3,2,1,0:T(8,128)(2,1)S(1)}, u32[]{:S(2)}, u32[]{:S(2)}) %all-to-all-start) | async-done | bytes 1572896 | tf_op jit(solution)/shard_map/all_to_all | solution.py:182
  67.3 3.5 %collective-permute-done.1.kn_ref.vn_ref = bf16[8,2,128,384]{3,2,1,0:T(8,128)(2,1)} collective-permute-done((bf16[8,2,128,384]{3,2,1,0:T(8,128)(2,1)S(1)}, bf16[8,2,128,384]{3,2,1,0:T(8,128)(2,1)}, u32[]{:S(2)}, u32[]{:S(2)}) %collective-permute-start.1) | collective-permute-done | bytes 1572896 | tf_op jit(solution)/shard_map/ppermute | solution.py:30
  70.7 6.3 %collective-permute-done.kp_ref.vp_ref = bf16[8,2,128,384]{3,2,1,0:T(8,128)(2,1)} collective-permute-done((bf16[8,2,128,384]{3,2,1,0:T(8,128)(2,1)S(1)}, bf16[8,2,128,384]{3,2,1,0:T(8,128)(2,1)}, u32[]{:S(2)}, u32[]{:S(2)}) %collective-permute-start) | collective-permute-done | bytes 1572896 | tf_op jit(solution)/shard_map/ppermute | solution.py:30
  77.1 35.5 %shard_map.95 = (bf16[8,2,128,384]{3,2,1,0:T(8,128)(2,1)}, f32[8,1,128,384]{3,2,1,0:T(8,128)}, f32[8,1,128,384]{3,2,1,0:T(8,128)}, bf16[8,1,128,384]{3,2,1,0:T(8...) custom-call(s32[8,9]{1,0:T(8,128)} %bitcast.9, ...), custom_call_target="tpu_custom_call" | custom-call | flops 5435817984 | bytes 12582912 | tf_op jit(solution)/shard_map/pallas_call | solution.py:129
  112.5 3.7 %all-to-all-start.2 = ((bf16[8,2,128,384]{3,2,1,0:T(8,128)(2,1)}), bf16[8,2,128,384]{3,2,1,0:T(8,128)(2,1)S(1)}, u32[]{:S(2)}, u32[]{:S(2)}) async-start(bf16[8,2,128,384]{3,2,1,0:T(8,128)(2,1)} %get-tuple-element.15), calls=%async_computation.2 | async-start | bytes 3145728 | tf_op jit(solution)/shard_map/all_to_all | solution.py:186
  118.2 3.9 %collective-permute-start.3 = (bf16[8,1,128,384]{3,2,1,0:T(8,128)(2,1)}, bf16[8,1,128,384]{3,2,1,0:T(8,128)(2,1)S(1)}, u32[]{:S(2)}, u32[]{:S(2)}) collective-permute-start(bf16[8,1,128,384]{3,2,1,0:T(8,128)(2,1)} %get-tuple-element.20), channel_id=1, source_target_pairs={{0,1},{1,2},{2,3},{3,4},{4,5},{5,6},{6,7},{7,8},{8,9},{9,10},{10,1... | collective-permute-start | bytes 2359304 | tf_op jit(solution)/shard_map/ppermute | solution.py:30
  122.1 4.0 %collective-permute-start.4 = (bf16[8,1,128,384]{3,2,1,0:T(8,128)(2,1)}, bf16[8,1,128,384]{3,2,1,0:T(8,128)(2,1)}, u32[]{:S(2)}, u32[]{:S(2)}) collective-permute-start(bf16[8,1,128,384]{3,2,1,0:T(8,128)(2,1)} %get-tuple-element.22), channel_id=1, source_target_pairs={{1,0},{2,1},{3,2},{4,3},{5,4},{6,5},{7,6},{8,7},{9,8},{10,9},{11,1... | collective-permute-start | bytes 2359304 | tf_op jit(solution)/shard_map/ppermute | solution.py:30
  126.1 1.9 %collective-permute-start.5 = (bf16[8,1,128,384]{3,2,1,0:T(8,128)(2,1)}, bf16[8,1,128,384]{3,2,1,0:T(8,128)(2,1)}, u32[]{:S(2)}, u32[]{:S(2)}) collective-permute-start(bf16[8,1,128,384]{3,2,1,0:T(8,128)(2,1)} %get-tuple-element.23), channel_id=1, source_target_pairs={{0,1},{1,2},{2,3},{3,4},{4,5},{5,6},{6,7},{7,8},{8,9},{9,10},{10,1... | collective-permute-start | bytes 2359304 | tf_op jit(solution)/shard_map/ppermute | solution.py:30
  128.1 10.7 %collective-permute-done.2 = bf16[8,1,128,384]{3,2,1,0:T(8,128)(2,1)S(1)} collective-permute-done((bf16[8,1,128,384]{3,2,1,0:T(8,128)(2,1)}, bf16[8,1,128,384]{3,2,1,0:T(8,128)(2,1)S(1)}, u32[]{:S(2)}, u32[]{:S(2)}) %collective-permute-start.2) | collective-permute-done | bytes 786464 | tf_op jit(solution)/shard_map/ppermute | solution.py:30
  138.8 4.0 %collective-permute-done.3 = bf16[8,1,128,384]{3,2,1,0:T(8,128)(2,1)S(1)} collective-permute-done((bf16[8,1,128,384]{3,2,1,0:T(8,128)(2,1)}, bf16[8,1,128,384]{3,2,1,0:T(8,128)(2,1)S(1)}, u32[]{:S(2)}, u32[]{:S(2)}) %collective-permute-start.3) | collective-permute-done | bytes 786464 | tf_op jit(solution)/shard_map/ppermute | solution.py:30
  144.0 4.7 %all-to-all-start.3 = ((bf16[8,1,128,384]{3,2,1,0:T(8,128)(2,1)}), bf16[8,1,128,384]{3,2,1,0:T(8,128)(2,1)S(1)}, u32[]{:S(2)}, u32[]{:S(2)}) async-start(bf16[8,1,128,384]{3,2,1,0:T(8,128)(2,1)} %add_convert_fusion.1), calls=%async_computation.3 | async-start | bytes 1572864 | tf_op jit(solution)/shard_map/all_to_all | solution.py:186
  148.7 6.4 %collective-permute-done.4 = bf16[8,1,128,384]{3,2,1,0:T(8,128)(2,1)} collective-permute-done((bf16[8,1,128,384]{3,2,1,0:T(8,128)(2,1)}, bf16[8,1,128,384]{3,2,1,0:T(8,128)(2,1)}, u32[]{:S(2)}, u32[]{:S(2)}) %collective-permute-start.4) | collective-permute-done | bytes 786464 | tf_op jit(solution)/shard_map/ppermute | solution.py:30
  155.1 4.0 %collective-permute-done.5 = bf16[8,1,128,384]{3,2,1,0:T(8,128)(2,1)} collective-permute-done((bf16[8,1,128,384]{3,2,1,0:T(8,128)(2,1)}, bf16[8,1,128,384]{3,2,1,0:T(8,128)(2,1)}, u32[]{:S(2)}, u32[]{:S(2)}) %collective-permute-start.5) | collective-permute-done | bytes 786464 | tf_op jit(solution)/shard_map/ppermute | solution.py:30
  159.2 3.0 %add_convert_fusion = bf16[8,1,128,384]{3,2,1,0:T(8,128)(2,1)} fusion(bf16[8,1,128,384]{3,2,1,0:T(8,128)(2,1)} %collective-permute-done.5, f32[8,1,128,384]{3,2,1,0:T(8,128)} %get-tuple-element.21, bf16[8,1,128,384]{3,2,1,0:T(8,128)(2,1)} %collective-permute-done.4), kind=kLoop, calls=%fused_computation.3 | loop fusion | flops 1966080 | bytes 3932160 | tf_op jit(solution)/shard_map/convert_element_type | solution.py:207
  162.2 4.5 %all-to-all-start.4 = ((bf16[8,1,128,384]{3,2,1,0:T(8,128)(2,1)}), bf16[8,1,128,384]{3,2,1,0:T(8,128)(2,1)S(1)}, u32[]{:S(2)}, u32[]{:S(2)}) async-start(bf16[8,1,128,384]{3,2,1,0:T(8,128)(2,1)} %add_convert_fusion), calls=%async_computation.4 | async-start | bytes 1572864 | tf_op jit(solution)/shard_map/all_to_all | solution.py:186
  166.7 2.7 %shard_map.96 = (bf16[128,3072]{1,0:T(8,128)(2,1)}, bf16[128,3072]{1,0:T(8,128)(2,1)}) custom-call(bf16[8,2,128,384]{3,2,1,0:T(8,128)(2,1)} %copy-done.2), custom_call_target="tpu_custom_call" | custom-call | tf_op jit(solution)/shard_map/pallas_call | solution.py:172
  169.4 2.1 %shard_map.97 = bf16[128,3072]{1,0:T(8,128)(2,1)} custom-call(bf16[8,1,128,384]{3,2,1,0:T(8,128)(2,1)} %copy-done.3), custom_call_target="tpu_custom_call" | custom-call | tf_op jit(solution)/shard_map/pallas_call | solution.py:172
  171.4 8.4 %all-to-all-done.4.refs_0_ = bf16[8,1,128,384]{3,2,1,0:T(8,128)(2,1)S(1)} async-done(((bf16[8,1,128,384]{3,2,1,0:T(8,128)(2,1)}), bf16[8,1,128,384]{3,2,1,0:T(8,128)(2,1)S(1)}, u32[]{:S(2)}, u32[]{:S(2)}) %all-to-all-start.4) | async-done | bytes 786464 | tf_op jit(solution)/shard_map/all_to_all | solution.py:186
  180.7 2.1 %shard_map.98 = bf16[128,3072]{1,0:T(8,128)(2,1)} custom-call(bf16[8,1,128,384]{3,2,1,0:T(8,128)(2,1)} %copy-done.4), custom_call_target="tpu_custom_call" | custom-call | tf_op jit(solution)/shard_map/pallas_call | solution.py:172
  (43 shorter events, 12.0 us)
Async XLA Ops:
  0.6 46.2 %copy-start = (s32[256,256]{1,0:T(8,128)S(1)}, s32[256,256]{1,0:T(8,128)}, u32[]{:S(2)}) copy-start(s32[256,256]{1,0:T(8,128)} %param.10) | copy-start | bytes 786436
  29.4 12.6 %copy-start.5 = (bf16[8,2,128,384]{3,2,1,0:T(8,128)(2,1)}, bf16[8,2,128,384]{3,2,1,0:T(8,128)(2,1)S(1)}, u32[]{:S(2)}) copy-start(bf16[8,2,128,384]{3,2,1,0:T(8,128)(2,1)S(1)} %all_to_all.25.ko_ref.vo_ref) | copy-start | bytes 4718596
  29.4 41.3 %collective-permute-start.1 = (bf16[8,2,128,384]{3,2,1,0:T(8,128)(2,1)S(1)}, bf16[8,2,128,384]{3,2,1,0:T(8,128)(2,1)}, u32[]{:S(2)}, u32[]{:S(2)}) collective-permute-start(bf16[8,2,128,384]{3,2,1,0:T(8,128)(2,1)S(1)} %all_to_all.25.ko_ref.vo_ref), channel_id=1, source_target_pairs={{1,0},{2,1},{3,2},{4,3},{5,4},{6,5},{7,6},{8,7},{9,8},{10,9},{11,1... | collective-permute-start | bytes 4718600 | tf_op jit(solution)/shard_map/ppermute | solution.py:30
  37.5 39.6 %collective-permute-start = (bf16[8,2,128,384]{3,2,1,0:T(8,128)(2,1)S(1)}, bf16[8,2,128,384]{3,2,1,0:T(8,128)(2,1)}, u32[]{:S(2)}, u32[]{:S(2)}) collective-permute-start(bf16[8,2,128,384]{3,2,1,0:T(8,128)(2,1)S(1)} %all_to_all.25.ko_ref.vo_ref), channel_id=1, source_target_pairs={{0,1},{1,2},{2,3},{3,4},{4,5},{5,6},{6,7},{7,8},{8,9},{9,10},{10,1... | collective-permute-start | bytes 4718600 | tf_op jit(solution)/shard_map/ppermute | solution.py:30
  42.1 3.8 %copy-start.1 = (s32[256]{0:T(256)S(1)}, s32[256]{0:T(256)}, u32[]{:S(2)}) copy-start(s32[256]{0:T(256)} %param.11) | copy-start | bytes 3076
  42.1 25.2 %all-to-all-start = ((bf16[8,2,128,384]{3,2,1,0:T(8,128)(2,1)}), bf16[8,2,128,384]{3,2,1,0:T(8,128)(2,1)S(1)}, u32[]{:S(2)}, u32[]{:S(2)}) async-start(bf16[8,2,128,384]{3,2,1,0:T(8,128)(2,1)} %shard_map.93), calls=%async_computation | async-start | bytes 3145728 | tf_op jit(solution)/shard_map/all_to_all | solution.py:182
  49.8 1.5 copy-start.8
  67.3 9.8 %copy-start.6 = (bf16[8,2,128,384]{3,2,1,0:T(8,128)(2,1)}, bf16[8,2,128,384]{3,2,1,0:T(8,128)(2,1)S(1)}, u32[]{:S(2)}) copy-start(bf16[8,2,128,384]{3,2,1,0:T(8,128)(2,1)S(1)} %all-to-all-done.qg_ref) | copy-start | bytes 4718596
  112.5 30.3 %copy-start.7 = (f32[8,1,128,384]{3,2,1,0:T(8,128)S(1)}, f32[8,1,128,384]{3,2,1,0:T(8,128)}, u32[]{:S(2)}) copy-start(f32[8,1,128,384]{3,2,1,0:T(8,128)} %get-tuple-element.18) | copy-start | bytes 4718596
  112.5 31.5 %all-to-all-start.2 = ((bf16[8,2,128,384]{3,2,1,0:T(8,128)(2,1)}), bf16[8,2,128,384]{3,2,1,0:T(8,128)(2,1)S(1)}, u32[]{:S(2)}, u32[]{:S(2)}) async-start(bf16[8,2,128,384]{3,2,1,0:T(8,128)(2,1)} %get-tuple-element.15), calls=%async_computation.2 | async-start | bytes 3145728 | tf_op jit(solution)/shard_map/all_to_all | solution.py:186
  116.2 22.5 %collective-permute-start.2 = (bf16[8,1,128,384]{3,2,1,0:T(8,128)(2,1)}, bf16[8,1,128,384]{3,2,1,0:T(8,128)(2,1)S(1)}, u32[]{:S(2)}, u32[]{:S(2)}) collective-permute-start(bf16[8,1,128,384]{3,2,1,0:T(8,128)(2,1)} %get-tuple-element.19), channel_id=1, source_target_pairs={{1,0},{2,1},{3,2},{4,3},{5,4},{6,5},{7,6},{8,7},{9,8},{10,9},{11,1... | collective-permute-start | bytes 2359304 | tf_op jit(solution)/shard_map/ppermute | solution.py:30
  118.2 24.6 %collective-permute-start.3 = (bf16[8,1,128,384]{3,2,1,0:T(8,128)(2,1)}, bf16[8,1,128,384]{3,2,1,0:T(8,128)(2,1)S(1)}, u32[]{:S(2)}, u32[]{:S(2)}) collective-permute-start(bf16[8,1,128,384]{3,2,1,0:T(8,128)(2,1)} %get-tuple-element.20), channel_id=1, source_target_pairs={{0,1},{1,2},{2,3},{3,4},{4,5},{5,6},{6,7},{7,8},{8,9},{9,10},{10,1... | collective-permute-start | bytes 2359304 | tf_op jit(solution)/shard_map/ppermute | solution.py:30
  122.1 33.0 %collective-permute-start.4 = (bf16[8,1,128,384]{3,2,1,0:T(8,128)(2,1)}, bf16[8,1,128,384]{3,2,1,0:T(8,128)(2,1)}, u32[]{:S(2)}, u32[]{:S(2)}) collective-permute-start(bf16[8,1,128,384]{3,2,1,0:T(8,128)(2,1)} %get-tuple-element.22), channel_id=1, source_target_pairs={{1,0},{2,1},{3,2},{4,3},{5,4},{6,5},{7,6},{8,7},{9,8},{10,9},{11,1... | collective-permute-start | bytes 2359304 | tf_op jit(solution)/shard_map/ppermute | solution.py:30
  126.1 33.0 %collective-permute-start.5 = (bf16[8,1,128,384]{3,2,1,0:T(8,128)(2,1)}, bf16[8,1,128,384]{3,2,1,0:T(8,128)(2,1)}, u32[]{:S(2)}, u32[]{:S(2)}) collective-permute-start(bf16[8,1,128,384]{3,2,1,0:T(8,128)(2,1)} %get-tuple-element.23), channel_id=1, source_target_pairs={{0,1},{1,2},{2,3},{3,4},{4,5},{5,6},{6,7},{7,8},{8,9},{9,10},{10,1... | collective-permute-start | bytes 2359304 | tf_op jit(solution)/shard_map/ppermute | solution.py:30
  144.0 18.2 %copy-start.2 = (bf16[8,2,128,384]{3,2,1,0:T(8,128)(2,1)}, bf16[8,2,128,384]{3,2,1,0:T(8,128)(2,1)S(1)}, u32[]{:S(2)}) copy-start(bf16[8,2,128,384]{3,2,1,0:T(8,128)(2,1)S(1)} %all-to-all-done.2.refs_0_) | copy-start | bytes 4718596
  144.0 18.2 %all-to-all-start.3 = ((bf16[8,1,128,384]{3,2,1,0:T(8,128)(2,1)}), bf16[8,1,128,384]{3,2,1,0:T(8,128)(2,1)S(1)}, u32[]{:S(2)}, u32[]{:S(2)}) async-start(bf16[8,1,128,384]{3,2,1,0:T(8,128)(2,1)} %add_convert_fusion.1), calls=%async_computation.3 | async-start | bytes 1572864 | tf_op jit(solution)/shard_map/all_to_all | solution.py:186
  162.2 7.1 %copy-start.3 = (bf16[8,1,128,384]{3,2,1,0:T(8,128)(2,1)}, bf16[8,1,128,384]{3,2,1,0:T(8,128)(2,1)S(1)}, u32[]{:S(2)}) copy-start(bf16[8,1,128,384]{3,2,1,0:T(8,128)(2,1)S(1)} %all-to-all-done.3.refs_0_) | copy-start | bytes 2359300
  162.2 17.6 %all-to-all-start.4 = ((bf16[8,1,128,384]{3,2,1,0:T(8,128)(2,1)}), bf16[8,1,128,384]{3,2,1,0:T(8,128)(2,1)S(1)}, u32[]{:S(2)}, u32[]{:S(2)}) async-start(bf16[8,1,128,384]{3,2,1,0:T(8,128)(2,1)} %add_convert_fusion), calls=%async_computation.4 | async-start | bytes 1572864 | tf_op jit(solution)/shard_map/all_to_all | solution.py:186
  179.8 0.9 copy-start.4

commit v13 on v9

--- a/solution.py
+++ b/solution.py
@@ -102,7 +102,7 @@
     lax.fori_loop(0, query_tiles, body, 0, unroll=2)
     for i, (own, before, after) in enumerate(((gok_ref, gpk_ref, gnk_ref), (gov_ref, gpv_ref, gnv_ref))):
         before[...] = acc_scr[:query_tiles, i : i + 1].astype(before.dtype)
-        own[...] = acc_scr[query_tiles : 2 * query_tiles, i : i + 1]
+        own[...] = acc_scr[query_tiles : 2 * query_tiles, i : i + 1].astype(own.dtype)
         after[...] = acc_scr[2 * query_tiles :, i : i + 1].astype(after.dtype)
 
 
@@ -130,8 +130,7 @@
         attn_kernel,
         grid_spec=grid_spec,
         out_shape=[jax.ShapeDtypeStruct(qg.shape, jnp.bfloat16)]
-        + [jax.ShapeDtypeStruct(single, jnp.float32)] * 2
-        + [jax.ShapeDtypeStruct(single, jnp.bfloat16)] * 4,
+        + [jax.ShapeDtypeStruct(single, jnp.bfloat16)] * 6,
         cost_estimate=pl.CostEstimate(
             flops=flops,
             transcendentals=query_tiles * max_keys * tile_rows * tile_rows * head_count,
@@ -204,7 +203,8 @@
     for own, before, after in ((gok, gpk, gnk), (gov, gpv, gnv)):
         from_above = passed_along(before, "tile", -1).astype(jnp.float32)
         from_below = passed_along(after, "tile", 1).astype(jnp.float32)
-        grads.append(to_tokens((own + from_above + from_below).astype(jnp.bfloat16))[0])
+        summed = own.astype(jnp.float32) + from_above + from_below
+        grads.append(to_tokens(summed.astype(jnp.bfloat16))[0])
     return (attn_out, grad_query, grads[0], grads[1])
 
 

time: 183 us -> 182 us (level)
  transfers between devices with their start and end apart: 10 -> 10, of which waited for: 8 -> 9; matrix products, arithmetic and copies ran while one was open for 6% -> 5% of each run, Pallas kernels for 4% -> 4%
where the time goes in v13:
time: 182 us
  waiting for transfers between devices  58.6 us (32%)
  Pallas kernels  47.1 us (26%)
  starting transfers between devices  38.2 us (21%)
  blocking collectives  26.1 us (14%)
  other arithmetic  5.35 us (3%)
  local copies, waits for them, and re-layouts  5.31 us (3%)
    pallas_call x1, Pallas kernels, attention_heads(): pl.pallas_call(attn_kernel, grid_spec=grid_spec, out_shape=[jax.ShapeDtyp...  34.9 us
    ppermute x6, waiting for transfers between devices, passed_along(): lax.ppermute(value, axis, [(source, source + steps) for source in range(i...  34.6 us
    all_to_all x1, blocking collectives, to_heads(): lax.all_to_all(stacked, 'head', split_axis=0, concat_axis=0, tiled=True)  26.1 us
    ppermute x6, starting transfers between devices, passed_along(): lax.ppermute(value, axis, [(source, source + steps) for source in range(i...  21.7 us
    all_to_all x1, waiting for transfers between devices, to_heads(): lax.all_to_all(stacked, 'head', split_axis=0, concat_axis=0, tiled=True)  15.4 us
    all_to_all x3, starting transfers between devices, to_tokens(): lax.all_to_all(stacked, 'head', split_axis=0, concat_axis=0, tiled=True)  12.8 us
    all_to_all x3, waiting for transfers between devices, to_tokens(): lax.all_to_all(stacked, 'head', split_axis=0, concat_axis=0, tiled=True)  8.62 us
    pallas_call x3, Pallas kernels, join_columns(): pl.pallas_call(join_kernel, in_specs=[pl.BlockSpec(memory_space=pltpu.VME...  6.83 us
  transfers between devices with their start and end apart: 10, of which 9 were waited for; matrix products, arithmetic and copies ran while one was open for 5% of the time, Pallas kernels for 4%

profile of v13, /device:TPU:6, one launch (start us, length us, event | category | flops | bytes accessed | tf_op | source)
XLA Modules:
  0.0 181.5 jit_solution(6714331051837132750)
XLA Ops:
  0.6 2.7 %shard_map.94 = bf16[8,2,128,384]{3,2,1,0:T(8,128)(2,1)} custom-call(bf16[128,3072]{1,0:T(8,128)(2,1)} %refs_0_.3, bf16[128,3072]{1,0:T(8,128)(2,1)} %refs_1_.3), custom_call_target="tpu_custom_call" | custom-call | tf_op jit(solution)/shard_map/pallas_call | solution.py:161
  3.4 26.1 %all_to_all.25.ko_ref.vo_ref = bf16[8,2,128,384]{3,2,1,0:T(8,128)(2,1)S(1)} all-to-all(bf16[8,2,128,384]{3,2,1,0:T(8,128)(2,1)} %shard_map.94), channel_id=1, replica_groups=mesh['head'=8,'tile'=32] {'head'}, dimensions={0} | all-to-all | bytes 3145728 | tf_op jit(solution)/shard_map/all_to_all | solution.py:181
  29.4 8.0 %collective-permute-start.1 = (bf16[8,2,128,384]{3,2,1,0:T(8,128)(2,1)S(1)}, bf16[8,2,128,384]{3,2,1,0:T(8,128)(2,1)}, u32[]{:S(2)}, u32[]{:S(2)}) collective-permute-start(bf16[8,2,128,384]{3,2,1,0:T(8,128)(2,1)S(1)} %all_to_all.25.ko_ref.vo_ref), channel_id=1, source_target_pairs={{1,0},{2,1},{3,2},{4,3},{5,4},{6,5},{7,6},{8,7},{9,8},{10,9},{11,1... | collective-permute-start | bytes 4718600 | tf_op jit(solution)/shard_map/ppermute | solution.py:30
  37.5 1.9 %collective-permute-start = (bf16[8,2,128,384]{3,2,1,0:T(8,128)(2,1)S(1)}, bf16[8,2,128,384]{3,2,1,0:T(8,128)(2,1)}, u32[]{:S(2)}, u32[]{:S(2)}) collective-permute-start(bf16[8,2,128,384]{3,2,1,0:T(8,128)(2,1)S(1)} %all_to_all.25.ko_ref.vo_ref), channel_id=1, source_target_pairs={{0,1},{1,2},{2,3},{3,4},{4,5},{5,6},{6,7},{7,8},{8,9},{9,10},{10,1... | collective-permute-start | bytes 4718600 | tf_op jit(solution)/shard_map/ppermute | solution.py:30
  39.4 2.7 %shard_map.93 = bf16[8,2,128,384]{3,2,1,0:T(8,128)(2,1)} custom-call(bf16[128,3072]{1,0:T(8,128)(2,1)} %refs_0_.2, bf16[128,3072]{1,0:T(8,128)(2,1)} %refs_1_.2), custom_call_target="tpu_custom_call" | custom-call | tf_op jit(solution)/shard_map/pallas_call | solution.py:161
  42.1 3.7 %all-to-all-start = ((bf16[8,2,128,384]{3,2,1,0:T(8,128)(2,1)}), bf16[8,2,128,384]{3,2,1,0:T(8,128)(2,1)S(1)}, u32[]{:S(2)}, u32[]{:S(2)}) async-start(bf16[8,2,128,384]{3,2,1,0:T(8,128)(2,1)} %shard_map.93), calls=%async_computation | async-start | bytes 3145728 | tf_op jit(solution)/shard_map/all_to_all | solution.py:181
  51.9 15.4 %all-to-all-done.qg_ref = bf16[8,2,128,384]{3,2,1,0:T(8,128)(2,1)S(1)} async-done(((bf16[8,2,128,384]{3,2,1,0:T(8,128)(2,1)}), bf16[8,2,128,384]{3,2,1,0:T(8,128)(2,1)S(1)}, u32[]{:S(2)}, u32[]{:S(2)}) %all-to-all-start) | async-done | bytes 1572896 | tf_op jit(solution)/shard_map/all_to_all | solution.py:181
  67.3 3.4 %collective-permute-done.1.kn_ref.vn_ref = bf16[8,2,128,384]{3,2,1,0:T(8,128)(2,1)} collective-permute-done((bf16[8,2,128,384]{3,2,1,0:T(8,128)(2,1)S(1)}, bf16[8,2,128,384]{3,2,1,0:T(8,128)(2,1)}, u32[]{:S(2)}, u32[]{:S(2)}) %collective-permute-start.1) | collective-permute-done | bytes 1572896 | tf_op jit(solution)/shard_map/ppermute | solution.py:30
  70.7 6.3 %collective-permute-done.kp_ref.vp_ref = bf16[8,2,128,384]{3,2,1,0:T(8,128)(2,1)} collective-permute-done((bf16[8,2,128,384]{3,2,1,0:T(8,128)(2,1)S(1)}, bf16[8,2,128,384]{3,2,1,0:T(8,128)(2,1)}, u32[]{:S(2)}, u32[]{:S(2)}) %collective-permute-start) | collective-permute-done | bytes 1572896 | tf_op jit(solution)/shard_map/ppermute | solution.py:30
  77.1 34.9 %shard_map.95 = (bf16[8,2,128,384]{3,2,1,0:T(8,128)(2,1)}, bf16[8,1,128,384]{3,2,1,0:T(8,128)(2,1)}, bf16[8,1,128,384]{3,2,1,0:T(8,128)(2,1)}, bf16[8,1,128,384]...) custom-call(s32[8,9]{1,0:T(8,128)} %bitcast.9, ...), custom_call_target="tpu_custom_call" | custom-call | flops 5435817984 | bytes 12582912 | tf_op jit(solution)/shard_map/pallas_call | solution.py:129
  111.9 3.7 %all-to-all-start.2 = ((bf16[8,2,128,384]{3,2,1,0:T(8,128)(2,1)}), bf16[8,2,128,384]{3,2,1,0:T(8,128)(2,1)S(1)}, u32[]{:S(2)}, u32[]{:S(2)}) async-start(bf16[8,2,128,384]{3,2,1,0:T(8,128)(2,1)} %get-tuple-element.15), calls=%async_computation.2 | async-start | bytes 3145728 | tf_op jit(solution)/shard_map/all_to_all | solution.py:185
  117.6 3.9 %collective-permute-start.3 = (bf16[8,1,128,384]{3,2,1,0:T(8,128)(2,1)S(1)}, bf16[8,1,128,384]{3,2,1,0:T(8,128)(2,1)S(1)}, u32[]{:S(2)}, u32[]{:S(2)}) collective-permute-start(bf16[8,1,128,384]{3,2,1,0:T(8,128)(2,1)S(1)} %copy-done.10), channel_id=1, source_target_pairs={{0,1},{1,2},{2,3},{3,4},{4,5},{5,6},{6,7},{7,8},{8,9},{9,10},{10,1... | collective-permute-start | bytes 2359304 | tf_op jit(solution)/shard_map/ppermute | solution.py:30
  121.5 4.0 %collective-permute-start.4 = (bf16[8,1,128,384]{3,2,1,0:T(8,128)(2,1)}, bf16[8,1,128,384]{3,2,1,0:T(8,128)(2,1)}, u32[]{:S(2)}, u32[]{:S(2)}) collective-permute-start(bf16[8,1,128,384]{3,2,1,0:T(8,128)(2,1)} %get-tuple-element.22), channel_id=1, source_target_pairs={{1,0},{2,1},{3,2},{4,3},{5,4},{6,5},{7,6},{8,7},{9,8},{10,9},{11,1... | collective-permute-start | bytes 2359304 | tf_op jit(solution)/shard_map/ppermute | solution.py:30
  127.5 10.7 %collective-permute-done.2 = bf16[8,1,128,384]{3,2,1,0:T(8,128)(2,1)S(1)} collective-permute-done((bf16[8,1,128,384]{3,2,1,0:T(8,128)(2,1)}, bf16[8,1,128,384]{3,2,1,0:T(8,128)(2,1)S(1)}, u32[]{:S(2)}, u32[]{:S(2)}) %collective-permute-start.2) | collective-permute-done | bytes 786464 | tf_op jit(solution)/shard_map/ppermute | solution.py:30
  138.2 3.8 %collective-permute-done.3 = bf16[8,1,128,384]{3,2,1,0:T(8,128)(2,1)S(1)} collective-permute-done((bf16[8,1,128,384]{3,2,1,0:T(8,128)(2,1)S(1)}, bf16[8,1,128,384]{3,2,1,0:T(8,128)(2,1)S(1)}, u32[]{:S(2)}, u32[]{:S(2)}) %collective-permute-start.3) | collective-permute-done | bytes 786464 | tf_op jit(solution)/shard_map/ppermute | solution.py:30
  143.3 4.8 %all-to-all-start.3 = ((bf16[8,1,128,384]{3,2,1,0:T(8,128)(2,1)}), bf16[8,1,128,384]{3,2,1,0:T(8,128)(2,1)S(1)}, u32[]{:S(2)}, u32[]{:S(2)}) async-start(bf16[8,1,128,384]{3,2,1,0:T(8,128)(2,1)} %add_convert_fusion.1), calls=%async_computation.3 | async-start | bytes 1572864 | tf_op jit(solution)/shard_map/all_to_all | solution.py:185
  148.1 6.5 %collective-permute-done.4 = bf16[8,1,128,384]{3,2,1,0:T(8,128)(2,1)} collective-permute-done((bf16[8,1,128,384]{3,2,1,0:T(8,128)(2,1)}, bf16[8,1,128,384]{3,2,1,0:T(8,128)(2,1)}, u32[]{:S(2)}, u32[]{:S(2)}) %collective-permute-start.4) | collective-permute-done | bytes 786464 | tf_op jit(solution)/shard_map/ppermute | solution.py:30
  154.6 3.8 %collective-permute-done.5 = bf16[8,1,128,384]{3,2,1,0:T(8,128)(2,1)} collective-permute-done((bf16[8,1,128,384]{3,2,1,0:T(8,128)(2,1)}, bf16[8,1,128,384]{3,2,1,0:T(8,128)(2,1)}, u32[]{:S(2)}, u32[]{:S(2)}) %collective-permute-start.5) | collective-permute-done | bytes 786464 | tf_op jit(solution)/shard_map/ppermute | solution.py:30
  158.4 2.5 %add_convert_fusion = bf16[8,1,128,384]{3,2,1,0:T(8,128)(2,1)} fusion(bf16[8,1,128,384]{3,2,1,0:T(8,128)(2,1)} %collective-permute-done.5, bf16[8,1,128,384]{3,2,1,0:T(8,128)(2,1)} %collective-permute-done.4, bf16[8,1,128,384]{3,2,1,0:T(8,128)(2,1)S(1)} %copy-done.7), kind=kLoop, calls=%fused_computation.3 | loop fusion | flops 2359296 | bytes 3145728 | tf_op jit(solution)/shard_map/convert_element_type | solution.py:207
  161.2 4.2 %all-to-all-start.4 = ((bf16[8,1,128,384]{3,2,1,0:T(8,128)(2,1)}), bf16[8,1,128,384]{3,2,1,0:T(8,128)(2,1)S(1)}, u32[]{:S(2)}, u32[]{:S(2)}) async-start(bf16[8,1,128,384]{3,2,1,0:T(8,128)(2,1)} %add_convert_fusion), calls=%async_computation.4 | async-start | bytes 1572864 | tf_op jit(solution)/shard_map/all_to_all | solution.py:185
  165.4 2.7 %shard_map.96 = (bf16[128,3072]{1,0:T(8,128)(2,1)}, bf16[128,3072]{1,0:T(8,128)(2,1)}) custom-call(bf16[8,2,128,384]{3,2,1,0:T(8,128)(2,1)} %copy-done.2), custom_call_target="tpu_custom_call" | custom-call | tf_op jit(solution)/shard_map/pallas_call | solution.py:171
  168.1 2.1 %shard_map.97 = bf16[128,3072]{1,0:T(8,128)(2,1)} custom-call(bf16[8,1,128,384]{3,2,1,0:T(8,128)(2,1)} %copy-done.3), custom_call_target="tpu_custom_call" | custom-call | tf_op jit(solution)/shard_map/pallas_call | solution.py:171
  170.2 8.4 %all-to-all-done.4.refs_0_ = bf16[8,1,128,384]{3,2,1,0:T(8,128)(2,1)S(1)} async-done(((bf16[8,1,128,384]{3,2,1,0:T(8,128)(2,1)}), bf16[8,1,128,384]{3,2,1,0:T(8,128)(2,1)S(1)}, u32[]{:S(2)}, u32[]{:S(2)}) %all-to-all-start.4) | async-done | bytes 786464 | tf_op jit(solution)/shard_map/all_to_all | solution.py:185
  179.4 2.1 %shard_map.98 = bf16[128,3072]{1,0:T(8,128)(2,1)} custom-call(bf16[8,1,128,384]{3,2,1,0:T(8,128)(2,1)} %copy-done.4), custom_call_target="tpu_custom_call" | custom-call | tf_op jit(solution)/shard_map/pallas_call | solution.py:171
  (47 shorter events, 12.2 us)
Async XLA Ops:
  0.6 46.2 %copy-start = (s32[256,256]{1,0:T(8,128)S(1)}, s32[256,256]{1,0:T(8,128)}, u32[]{:S(2)}) copy-start(s32[256,256]{1,0:T(8,128)} %param.10) | copy-start | bytes 786436
  29.4 12.7 %copy-start.5 = (bf16[8,2,128,384]{3,2,1,0:T(8,128)(2,1)}, bf16[8,2,128,384]{3,2,1,0:T(8,128)(2,1)S(1)}, u32[]{:S(2)}) copy-start(bf16[8,2,128,384]{3,2,1,0:T(8,128)(2,1)S(1)} %all_to_all.25.ko_ref.vo_ref) | copy-start | bytes 4718596
  29.4 41.3 %collective-permute-start.1 = (bf16[8,2,128,384]{3,2,1,0:T(8,128)(2,1)S(1)}, bf16[8,2,128,384]{3,2,1,0:T(8,128)(2,1)}, u32[]{:S(2)}, u32[]{:S(2)}) collective-permute-start(bf16[8,2,128,384]{3,2,1,0:T(8,128)(2,1)S(1)} %all_to_all.25.ko_ref.vo_ref), channel_id=1, source_target_pairs={{1,0},{2,1},{3,2},{4,3},{5,4},{6,5},{7,6},{8,7},{9,8},{10,9},{11,1... | collective-permute-start | bytes 4718600 | tf_op jit(solution)/shard_map/ppermute | solution.py:30
  37.5 39.6 %collective-permute-start = (bf16[8,2,128,384]{3,2,1,0:T(8,128)(2,1)S(1)}, bf16[8,2,128,384]{3,2,1,0:T(8,128)(2,1)}, u32[]{:S(2)}, u32[]{:S(2)}) collective-permute-start(bf16[8,2,128,384]{3,2,1,0:T(8,128)(2,1)S(1)} %all_to_all.25.ko_ref.vo_ref), channel_id=1, source_target_pairs={{0,1},{1,2},{2,3},{3,4},{4,5},{5,6},{6,7},{7,8},{8,9},{9,10},{10,1... | collective-permute-start | bytes 4718600 | tf_op jit(solution)/shard_map/ppermute | solution.py:30
  42.1 3.8 %copy-start.1 = (s32[256]{0:T(256)S(1)}, s32[256]{0:T(256)}, u32[]{:S(2)}) copy-start(s32[256]{0:T(256)} %param.11) | copy-start | bytes 3076
  42.1 25.2 %all-to-all-start = ((bf16[8,2,128,384]{3,2,1,0:T(8,128)(2,1)}), bf16[8,2,128,384]{3,2,1,0:T(8,128)(2,1)S(1)}, u32[]{:S(2)}, u32[]{:S(2)}) async-start(bf16[8,2,128,384]{3,2,1,0:T(8,128)(2,1)} %shard_map.93), calls=%async_computation | async-start | bytes 3145728 | tf_op jit(solution)/shard_map/all_to_all | solution.py:181
  49.8 1.5 copy-start.9
  67.3 9.8 %copy-start.6 = (bf16[8,2,128,384]{3,2,1,0:T(8,128)(2,1)}, bf16[8,2,128,384]{3,2,1,0:T(8,128)(2,1)S(1)}, u32[]{:S(2)}) copy-start(bf16[8,2,128,384]{3,2,1,0:T(8,128)(2,1)S(1)} %all-to-all-done.qg_ref) | copy-start | bytes 4718596
  111.9 5.7 %copy-start.10 = (bf16[8,1,128,384]{3,2,1,0:T(8,128)(2,1)S(1)}, bf16[8,1,128,384]{3,2,1,0:T(8,128)(2,1)}, u32[]{:S(2)}) copy-start(bf16[8,1,128,384]{3,2,1,0:T(8,128)(2,1)} %get-tuple-element.20) | copy-start | bytes 2359300
  111.9 30.1 %copy-start.8 = (bf16[8,1,128,384]{3,2,1,0:T(8,128)(2,1)S(1)}, bf16[8,1,128,384]{3,2,1,0:T(8,128)(2,1)}, u32[]{:S(2)}) copy-start(bf16[8,1,128,384]{3,2,1,0:T(8,128)(2,1)} %get-tuple-element.18) | copy-start | bytes 2359300
  111.9 31.3 %all-to-all-start.2 = ((bf16[8,2,128,384]{3,2,1,0:T(8,128)(2,1)}), bf16[8,2,128,384]{3,2,1,0:T(8,128)(2,1)S(1)}, u32[]{:S(2)}, u32[]{:S(2)}) async-start(bf16[8,2,128,384]{3,2,1,0:T(8,128)(2,1)} %get-tuple-element.15), calls=%async_computation.2 | async-start | bytes 3145728 | tf_op jit(solution)/shard_map/all_to_all | solution.py:185
  115.7 22.5 %collective-permute-start.2 = (bf16[8,1,128,384]{3,2,1,0:T(8,128)(2,1)}, bf16[8,1,128,384]{3,2,1,0:T(8,128)(2,1)S(1)}, u32[]{:S(2)}, u32[]{:S(2)}) collective-permute-start(bf16[8,1,128,384]{3,2,1,0:T(8,128)(2,1)} %get-tuple-element.19), channel_id=1, source_target_pairs={{1,0},{2,1},{3,2},{4,3},{5,4},{6,5},{7,6},{8,7},{9,8},{10,9},{11,1... | collective-permute-start | bytes 2359304 | tf_op jit(solution)/shard_map/ppermute | solution.py:30
  117.6 24.4 %collective-permute-start.3 = (bf16[8,1,128,384]{3,2,1,0:T(8,128)(2,1)S(1)}, bf16[8,1,128,384]{3,2,1,0:T(8,128)(2,1)S(1)}, u32[]{:S(2)}, u32[]{:S(2)}) collective-permute-start(bf16[8,1,128,384]{3,2,1,0:T(8,128)(2,1)S(1)} %copy-done.10), channel_id=1, source_target_pairs={{0,1},{1,2},{2,3},{3,4},{4,5},{5,6},{6,7},{7,8},{8,9},{9,10},{10,1... | collective-permute-start | bytes 2359304 | tf_op jit(solution)/shard_map/ppermute | solution.py:30
  121.5 33.0 %collective-permute-start.4 = (bf16[8,1,128,384]{3,2,1,0:T(8,128)(2,1)}, bf16[8,1,128,384]{3,2,1,0:T(8,128)(2,1)}, u32[]{:S(2)}, u32[]{:S(2)}) collective-permute-start(bf16[8,1,128,384]{3,2,1,0:T(8,128)(2,1)} %get-tuple-element.22), channel_id=1, source_target_pairs={{1,0},{2,1},{3,2},{4,3},{5,4},{6,5},{7,6},{8,7},{9,8},{10,9},{11,1... | collective-permute-start | bytes 2359304 | tf_op jit(solution)/shard_map/ppermute | solution.py:30
  125.6 32.8 %collective-permute-start.5 = (bf16[8,1,128,384]{3,2,1,0:T(8,128)(2,1)}, bf16[8,1,128,384]{3,2,1,0:T(8,128)(2,1)}, u32[]{:S(2)}, u32[]{:S(2)}) collective-permute-start(bf16[8,1,128,384]{3,2,1,0:T(8,128)(2,1)} %get-tuple-element.23), channel_id=1, source_target_pairs={{0,1},{1,2},{2,3},{3,4},{4,5},{5,6},{6,7},{7,8},{8,9},{9,10},{10,1... | collective-permute-start | bytes 2359304 | tf_op jit(solution)/shard_map/ppermute | solution.py:30
  143.2 15.2 %copy-start.7 = (bf16[8,1,128,384]{3,2,1,0:T(8,128)(2,1)S(1)}, bf16[8,1,128,384]{3,2,1,0:T(8,128)(2,1)}, u32[]{:S(2)}) copy-start(bf16[8,1,128,384]{3,2,1,0:T(8,128)(2,1)} %get-tuple-element.21) | copy-start | bytes 2359300
  143.2 17.7 %copy-start.2 = (bf16[8,2,128,384]{3,2,1,0:T(8,128)(2,1)}, bf16[8,2,128,384]{3,2,1,0:T(8,128)(2,1)S(1)}, u32[]{:S(2)}) copy-start(bf16[8,2,128,384]{3,2,1,0:T(8,128)(2,1)S(1)} %all-to-all-done.2.refs_0_) | copy-start | bytes 4718596
  143.3 18.0 %all-to-all-start.3 = ((bf16[8,1,128,384]{3,2,1,0:T(8,128)(2,1)}), bf16[8,1,128,384]{3,2,1,0:T(8,128)(2,1)S(1)}, u32[]{:S(2)}, u32[]{:S(2)}) async-start(bf16[8,1,128,384]{3,2,1,0:T(8,128)(2,1)} %add_convert_fusion.1), calls=%async_computation.3 | async-start | bytes 1572864 | tf_op jit(solution)/shard_map/all_to_all | solution.py:185
  161.2 6.9 %copy-start.3 = (bf16[8,1,128,384]{3,2,1,0:T(8,128)(2,1)}, bf16[8,1,128,384]{3,2,1,0:T(8,128)(2,1)S(1)}, u32[]{:S(2)}) copy-start(bf16[8,1,128,384]{3,2,1,0:T(8,128)(2,1)S(1)} %all-to-all-done.3.refs_0_) | copy-start | bytes 2359300
  161.2 17.3 %all-to-all-start.4 = ((bf16[8,1,128,384]{3,2,1,0:T(8,128)(2,1)}), bf16[8,1,128,384]{3,2,1,0:T(8,128)(2,1)S(1)}, u32[]{:S(2)}, u32[]{:S(2)}) async-start(bf16[8,1,128,384]{3,2,1,0:T(8,128)(2,1)} %add_convert_fusion), calls=%async_computation.4 | async-start | bytes 1572864 | tf_op jit(solution)/shard_map/all_to_all | solution.py:185
  178.6 0.9 copy-start.4

commit v14 on v13

--- a/solution.py
+++ b/solution.py
@@ -48,7 +48,7 @@
 
 
 def attn_kernel(
-    slot_ref, live_ref, qg_ref, kp_ref, ko_ref, kn_ref, vp_ref, vo_ref, vn_ref,
+    slot_ref, live_ref, bias_ref, qg_ref, kp_ref, ko_ref, kn_ref, vp_ref, vo_ref, vn_ref,
     og_ref, gok_ref, gov_ref, gpk_ref, gpv_ref, gnk_ref, gnv_ref, kg_scr, vg_scr, acc_scr,
 ):
     tile_rows = HD
@@ -58,10 +58,8 @@
     acc_scr[...] = jnp.zeros(acc_scr.shape, acc_scr.dtype)
     nt = (((1,), (1,)), ((), ()))
     tn = (((0,), (0,)), ((), ()))
-    lane_slot = lax.broadcasted_iota(jnp.int32, (1, max_keys * tile_rows), 1) // tile_rows
 
     def body(p, carry):
-        live_lane = jnp.zeros((1, max_keys * tile_rows), jnp.int32)
         for s in range(max_keys):
             slot = slot_ref[p, s]
             side = slot // query_tiles
@@ -73,13 +71,12 @@
                     picked = jnp.where(side == w, window[w][tile, 0], picked)
                 buf[dst, :] = picked
 
-            live_lane = jnp.where(lane_slot == s, live_ref[p, s], live_lane)
         q = qg_ref[p, 0]
         g = qg_ref[p, 1]
         kg = kg_scr[...]
         vg = vg_scr[...]
         sc = lax.dot_general(q, kg, nt, preferred_element_type=jnp.float32) * scaling
-        sc = jnp.where(live_lane > 0, sc, NEG)
+        sc = sc + bias_ref[p]
         top = jnp.max(sc, axis=1, keepdims=True)
         expd = jnp.exp(sc - top)
         prob = expd * (1.0 / jnp.sum(expd, axis=1, keepdims=True))
@@ -117,7 +114,8 @@
     grid_spec = pltpu.PrefetchScalarGridSpec(
         num_scalar_prefetch=2,
         grid=(head_count,),
-        in_specs=[spec] + [one] * 3 + [second] * 3,
+        in_specs=[pl.BlockSpec((query_tiles, 1, max_keys * tile_rows), lambda h, *_: (0, 0, 0))]
+        + [spec] + [one] * 3 + [second] * 3,
         out_specs=[spec] + [one] * 6,
         scratch_shapes=[
             pltpu.VMEM((max_keys * tile_rows, HD), jnp.bfloat16),
@@ -126,6 +124,8 @@
         ],
     )
     single = (query_tiles, 1, tile_rows, width)
+    bias = jnp.where(live_slot, 0.0, NEG).astype(jnp.float32)
+    bias = jnp.repeat(bias, tile_rows, axis=1).reshape(query_tiles, 1, max_keys * tile_rows)
     return pl.pallas_call(
         attn_kernel,
         grid_spec=grid_spec,
@@ -136,7 +136,7 @@
             transcendentals=query_tiles * max_keys * tile_rows * tile_rows * head_count,
             bytes_accessed=query_tiles * count * tile_rows * width * 2 * 8,
         ),
-    )(slot_key, live_slot.astype(jnp.int32), qg, *k_win, *v_win)
+    )(slot_key, live_slot.astype(jnp.int32), bias, qg, *k_win, *v_win)
 
 
 def split_kernel(*refs):

time: 182 us -> 188 us (1.033)
  blocking collectives: 26.1 us -> 0 us
  waiting for transfers between devices: 58.6 us -> 84 us
  starting transfers between devices: 38.2 us -> 43.7 us
    all_to_all x1 -> x0, blocking collectives: 26.1 us -> none  [to_heads(): lax.all_to_all(stacked, 'head', split_axis=0, concat_axis=0, tiled=True)]
    ppermute x6, waiting for transfers between devices: 34.6 us -> 51.9 us  [passed_along(): lax.ppermute(value, axis, [(source, source + steps) for source in range(i...]
    all_to_all x1 -> x2, waiting for transfers between devices: 15.4 us -> 23.5 us  [to_heads(): lax.all_to_all(stacked, 'head', split_axis=0, concat_axis=0, tiled=True)]
    all_to_all x1 -> x2, starting transfers between devices: 3.71 us -> 8.18 us  [to_heads(): lax.all_to_all(stacked, 'head', split_axis=0, concat_axis=0, tiled=True)]
  transfers between devices with their start and end apart: 10 -> 11, of which waited for: 9 -> 10; matrix products, arithmetic and copies ran while one was open for 5% -> 6% of each run, Pallas kernels for 4% -> 4%
where the time goes in v14:
time: 188 us; the launch traced here: 187 us
  waiting for transfers between devices  84 us (45%)
  Pallas kernels  47 us (25%)
  starting transfers between devices  43.7 us (23%)
  local copies, waits for them, and re-layouts  6.13 us (3%)
  other arithmetic  5.36 us (3%)
    ppermute x6, waiting for transfers between devices, passed_along(): lax.ppermute(value, axis, [(source, source + steps) for source in range(i...  51.9 us
    pallas_call x1, Pallas kernels, attention_heads(): pl.pallas_call(attn_kernel, grid_spec=grid_spec, out_shape=[jax.ShapeDtyp...  34.8 us
    all_to_all x2, waiting for transfers between devices, to_heads(): lax.all_to_all(stacked, 'head', split_axis=0, concat_axis=0, tiled=True)  23.5 us
    ppermute x6, starting transfers between devices, passed_along(): lax.ppermute(value, axis, [(source, source + steps) for source in range(i...  21.7 us
    all_to_all x3, starting transfers between devices, to_tokens(): lax.all_to_all(stacked, 'head', split_axis=0, concat_axis=0, tiled=True)  13.7 us
    all_to_all x3, waiting for transfers between devices, to_tokens(): lax.all_to_all(stacked, 'head', split_axis=0, concat_axis=0, tiled=True)  8.59 us
    all_to_all x2, starting transfers between devices, to_heads(): lax.all_to_all(stacked, 'head', split_axis=0, concat_axis=0, tiled=True)  8.18 us
    pallas_call x3, Pallas kernels, join_columns(): pl.pallas_call(join_kernel, in_specs=[pl.BlockSpec(memory_space=pltpu.VME...  6.83 us
  transfers between devices with their start and end apart: 11, of which 10 were waited for; matrix products, arithmetic and copies ran while one was open for 6% of the time, Pallas kernels for 4%

profile of v14, /device:TPU:6, one launch (start us, length us, event | category | flops | bytes accessed | tf_op | source)
XLA Modules:
  0.0 187.0 jit_solution(13166386642375297071)
XLA Ops:
  0.6 2.7 %shard_map.94 = bf16[8,2,128,384]{3,2,1,0:T(8,128)(2,1)} custom-call(bf16[128,3072]{1,0:T(8,128)(2,1)} %refs_0_.3, bf16[128,3072]{1,0:T(8,128)(2,1)} %refs_1_.3), custom_call_target="tpu_custom_call" | custom-call | tf_op jit(solution)/shard_map/pallas_call | solution.py:161
  3.3 4.6 %all-to-all-start.1 = ((bf16[8,2,128,384]{3,2,1,0:T(8,128)(2,1)}), bf16[8,2,128,384]{3,2,1,0:T(8,128)(2,1)S(1)}, u32[]{:S(2)}, u32[]{:S(2)}) async-start(bf16[8,2,128,384]{3,2,1,0:T(8,128)(2,1)} %shard_map.94), calls=%async_computation.1 | async-start | bytes 3145728 | tf_op jit(solution)/shard_map/all_to_all | solution.py:181
  8.7 2.7 %shard_map.93 = bf16[8,2,128,384]{3,2,1,0:T(8,128)(2,1)} custom-call(bf16[128,3072]{1,0:T(8,128)(2,1)} %refs_0_.2, bf16[128,3072]{1,0:T(8,128)(2,1)} %refs_1_.2), custom_call_target="tpu_custom_call" | custom-call | tf_op jit(solution)/shard_map/pallas_call | solution.py:161
  11.3 18.1 %all-to-all-done.1.ko_ref.vo_ref = bf16[8,2,128,384]{3,2,1,0:T(8,128)(2,1)S(1)} async-done(((bf16[8,2,128,384]{3,2,1,0:T(8,128)(2,1)}), bf16[8,2,128,384]{3,2,1,0:T(8,128)(2,1)S(1)}, u32[]{:S(2)}, u32[]{:S(2)}) %all-to-all-start.1) | async-done | bytes 1572896 | tf_op jit(solution)/shard_map/all_to_all | solution.py:181
  29.5 3.6 %all-to-all-start = ((bf16[8,2,128,384]{3,2,1,0:T(8,128)(2,1)}), bf16[8,2,128,384]{3,2,1,0:T(8,128)(2,1)S(1)}, u32[]{:S(2)}, u32[]{:S(2)}) async-start(bf16[8,2,128,384]{3,2,1,0:T(8,128)(2,1)} %shard_map.93), calls=%async_computation | async-start | bytes 3145728 | tf_op jit(solution)/shard_map/all_to_all | solution.py:181
  33.1 8.0 %collective-permute-start.1 = (bf16[8,2,128,384]{3,2,1,0:T(8,128)(2,1)S(1)}, bf16[8,2,128,384]{3,2,1,0:T(8,128)(2,1)}, u32[]{:S(2)}, u32[]{:S(2)}) collective-permute-start(bf16[8,2,128,384]{3,2,1,0:T(8,128)(2,1)S(1)} %all-to-all-done.1.ko_ref.vo_ref), channel_id=1, source_target_pairs={{1,0},{2,1},{3,2},{4,3},{5,4},{6,5},{7,6},{8,7},{9,8},{10,9},{11,1... | collective-permute-start | bytes 4718600 | tf_op jit(solution)/shard_map/ppermute | solution.py:30
  49.2 5.4 %all-to-all-done.qg_ref = bf16[8,2,128,384]{3,2,1,0:T(8,128)(2,1)S(1)} async-done(((bf16[8,2,128,384]{3,2,1,0:T(8,128)(2,1)}), bf16[8,2,128,384]{3,2,1,0:T(8,128)(2,1)S(1)}, u32[]{:S(2)}, u32[]{:S(2)}) %all-to-all-start) | async-done | bytes 1572896 | tf_op jit(solution)/shard_map/all_to_all | solution.py:181
  54.6 20.7 %collective-permute-done.1.kn_ref.vn_ref = bf16[8,2,128,384]{3,2,1,0:T(8,128)(2,1)} collective-permute-done((bf16[8,2,128,384]{3,2,1,0:T(8,128)(2,1)S(1)}, bf16[8,2,128,384]{3,2,1,0:T(8,128)(2,1)}, u32[]{:S(2)}, u32[]{:S(2)}) %collective-permute-start.1) | collective-permute-done | bytes 1572896 | tf_op jit(solution)/shard_map/ppermute | solution.py:30
  75.3 6.3 %collective-permute-done.kp_ref.vp_ref = bf16[8,2,128,384]{3,2,1,0:T(8,128)(2,1)} collective-permute-done((bf16[8,2,128,384]{3,2,1,0:T(8,128)(2,1)S(1)}, bf16[8,2,128,384]{3,2,1,0:T(8,128)(2,1)}, u32[]{:S(2)}, u32[]{:S(2)}) %collective-permute-start) | collective-permute-done | bytes 1572896 | tf_op jit(solution)/shard_map/ppermute | solution.py:30
  81.6 34.8 %shard_map.95 = (bf16[8,2,128,384]{3,2,1,0:T(8,128)(2,1)}, bf16[8,1,128,384]{3,2,1,0:T(8,128)(2,1)}, bf16[8,1,128,384]{3,2,1,0:T(8,128)(2,1)}, bf16[8,1,128,384]...) custom-call(s32[8,9]{1,0:T(8,128)} %bitcast.11, ...), custom_call_target="tpu_custom_call" | custom-call | flops 5435817984 | bytes 12582912 | tf_op jit(solution)/shard_map/pallas_call | solution.py:129
  116.5 4.6 %all-to-all-start.2 = ((bf16[8,2,128,384]{3,2,1,0:T(8,128)(2,1)}), bf16[8,2,128,384]{3,2,1,0:T(8,128)(2,1)S(1)}, u32[]{:S(2)}, u32[]{:S(2)}) async-start(bf16[8,2,128,384]{3,2,1,0:T(8,128)(2,1)} %get-tuple-element.15), calls=%async_computation.2 | async-start | bytes 3145728 | tf_op jit(solution)/shard_map/all_to_all | solution.py:185
  123.0 3.9 %collective-permute-start.3 = (bf16[8,1,128,384]{3,2,1,0:T(8,128)(2,1)S(1)}, bf16[8,1,128,384]{3,2,1,0:T(8,128)(2,1)S(1)}, u32[]{:S(2)}, u32[]{:S(2)}) collective-permute-start(bf16[8,1,128,384]{3,2,1,0:T(8,128)(2,1)S(1)} %copy-done.10), channel_id=1, source_target_pairs={{0,1},{1,2},{2,3},{3,4},{4,5},{5,6},{6,7},{7,8},{8,9},{9,10},{10,1... | collective-permute-start | bytes 2359304 | tf_op jit(solution)/shard_map/ppermute | solution.py:30
  126.9 4.0 %collective-permute-start.4 = (bf16[8,1,128,384]{3,2,1,0:T(8,128)(2,1)}, bf16[8,1,128,384]{3,2,1,0:T(8,128)(2,1)}, u32[]{:S(2)}, u32[]{:S(2)}) collective-permute-start(bf16[8,1,128,384]{3,2,1,0:T(8,128)(2,1)} %get-tuple-element.22), channel_id=1, source_target_pairs={{1,0},{2,1},{3,2},{4,3},{5,4},{6,5},{7,6},{8,7},{9,8},{10,9},{11,1... | collective-permute-start | bytes 2359304 | tf_op jit(solution)/shard_map/ppermute | solution.py:30
  132.9 10.7 %collective-permute-done.2 = bf16[8,1,128,384]{3,2,1,0:T(8,128)(2,1)S(1)} collective-permute-done((bf16[8,1,128,384]{3,2,1,0:T(8,128)(2,1)}, bf16[8,1,128,384]{3,2,1,0:T(8,128)(2,1)S(1)}, u32[]{:S(2)}, u32[]{:S(2)}) %collective-permute-start.2) | collective-permute-done | bytes 786464 | tf_op jit(solution)/shard_map/ppermute | solution.py:30
  143.6 3.8 %collective-permute-done.3 = bf16[8,1,128,384]{3,2,1,0:T(8,128)(2,1)S(1)} collective-permute-done((bf16[8,1,128,384]{3,2,1,0:T(8,128)(2,1)S(1)}, bf16[8,1,128,384]{3,2,1,0:T(8,128)(2,1)S(1)}, u32[]{:S(2)}, u32[]{:S(2)}) %collective-permute-start.3) | collective-permute-done | bytes 786464 | tf_op jit(solution)/shard_map/ppermute | solution.py:30
  148.6 4.9 %all-to-all-start.3 = ((bf16[8,1,128,384]{3,2,1,0:T(8,128)(2,1)}), bf16[8,1,128,384]{3,2,1,0:T(8,128)(2,1)S(1)}, u32[]{:S(2)}, u32[]{:S(2)}) async-start(bf16[8,1,128,384]{3,2,1,0:T(8,128)(2,1)} %add_convert_fusion.1), calls=%async_computation.3 | async-start | bytes 1572864 | tf_op jit(solution)/shard_map/all_to_all | solution.py:185
  153.6 6.5 %collective-permute-done.4 = bf16[8,1,128,384]{3,2,1,0:T(8,128)(2,1)} collective-permute-done((bf16[8,1,128,384]{3,2,1,0:T(8,128)(2,1)}, bf16[8,1,128,384]{3,2,1,0:T(8,128)(2,1)}, u32[]{:S(2)}, u32[]{:S(2)}) %collective-permute-start.4) | collective-permute-done | bytes 786464 | tf_op jit(solution)/shard_map/ppermute | solution.py:30
  160.1 3.8 %collective-permute-done.5 = bf16[8,1,128,384]{3,2,1,0:T(8,128)(2,1)} collective-permute-done((bf16[8,1,128,384]{3,2,1,0:T(8,128)(2,1)}, bf16[8,1,128,384]{3,2,1,0:T(8,128)(2,1)}, u32[]{:S(2)}, u32[]{:S(2)}) %collective-permute-start.5) | collective-permute-done | bytes 786464 | tf_op jit(solution)/shard_map/ppermute | solution.py:30
  163.9 2.6 %add_convert_fusion = bf16[8,1,128,384]{3,2,1,0:T(8,128)(2,1)} fusion(bf16[8,1,128,384]{3,2,1,0:T(8,128)(2,1)} %collective-permute-done.5, bf16[8,1,128,384]{3,2,1,0:T(8,128)(2,1)} %collective-permute-done.4, bf16[8,1,128,384]{3,2,1,0:T(8,128)(2,1)S(1)} %copy-done.7), kind=kLoop, calls=%fused_computation.3 | loop fusion | flops 2359296 | bytes 3145728 | tf_op jit(solution)/shard_map/convert_element_type | solution.py:207
  166.7 4.2 %all-to-all-start.4 = ((bf16[8,1,128,384]{3,2,1,0:T(8,128)(2,1)}), bf16[8,1,128,384]{3,2,1,0:T(8,128)(2,1)S(1)}, u32[]{:S(2)}, u32[]{:S(2)}) async-start(bf16[8,1,128,384]{3,2,1,0:T(8,128)(2,1)} %add_convert_fusion), calls=%async_computation.4 | async-start | bytes 1572864 | tf_op jit(solution)/shard_map/all_to_all | solution.py:185
  170.9 2.7 %shard_map.96 = (bf16[128,3072]{1,0:T(8,128)(2,1)}, bf16[128,3072]{1,0:T(8,128)(2,1)}) custom-call(bf16[8,2,128,384]{3,2,1,0:T(8,128)(2,1)} %copy-done.2), custom_call_target="tpu_custom_call" | custom-call | tf_op jit(solution)/shard_map/pallas_call | solution.py:171
  173.6 2.1 %shard_map.97 = bf16[128,3072]{1,0:T(8,128)(2,1)} custom-call(bf16[8,1,128,384]{3,2,1,0:T(8,128)(2,1)} %copy-done.3), custom_call_target="tpu_custom_call" | custom-call | tf_op jit(solution)/shard_map/pallas_call | solution.py:171
  175.7 8.4 %all-to-all-done.4.refs_0_ = bf16[8,1,128,384]{3,2,1,0:T(8,128)(2,1)S(1)} async-done(((bf16[8,1,128,384]{3,2,1,0:T(8,128)(2,1)}), bf16[8,1,128,384]{3,2,1,0:T(8,128)(2,1)S(1)}, u32[]{:S(2)}, u32[]{:S(2)}) %all-to-all-start.4) | async-done | bytes 786464 | tf_op jit(solution)/shard_map/all_to_all | solution.py:185
  184.9 2.1 %shard_map.98 = bf16[128,3072]{1,0:T(8,128)(2,1)} custom-call(bf16[8,1,128,384]{3,2,1,0:T(8,128)(2,1)} %copy-done.4), custom_call_target="tpu_custom_call" | custom-call | tf_op jit(solution)/shard_map/pallas_call | solution.py:171
  (52 shorter events, 14.9 us)
Async XLA Ops:
  0.6 42.7 %copy-start = (s32[256,256]{1,0:T(8,128)S(1)}, s32[256,256]{1,0:T(8,128)}, u32[]{:S(2)}) copy-start(s32[256,256]{1,0:T(8,128)} %param.10) | copy-start | bytes 786436
  3.3 4.6 %copy-start.1 = (s32[256]{0:T(256)S(1)}, s32[256]{0:T(256)}, u32[]{:S(2)}) copy-start(s32[256]{0:T(256)} %param.11) | copy-start | bytes 3076
  3.3 26.2 %all-to-all-start.1 = ((bf16[8,2,128,384]{3,2,1,0:T(8,128)(2,1)}), bf16[8,2,128,384]{3,2,1,0:T(8,128)(2,1)S(1)}, u32[]{:S(2)}, u32[]{:S(2)}) async-start(bf16[8,2,128,384]{3,2,1,0:T(8,128)(2,1)} %shard_map.94), calls=%async_computation.1 | async-start | bytes 3145728 | tf_op jit(solution)/shard_map/all_to_all | solution.py:181
  29.5 11.6 %copy-start.5 = (bf16[8,2,128,384]{3,2,1,0:T(8,128)(2,1)}, bf16[8,2,128,384]{3,2,1,0:T(8,128)(2,1)S(1)}, u32[]{:S(2)}) copy-start(bf16[8,2,128,384]{3,2,1,0:T(8,128)(2,1)S(1)} %all-to-all-done.1.ko_ref.vo_ref) | copy-start | bytes 4718596
  29.5 25.1 %all-to-all-start = ((bf16[8,2,128,384]{3,2,1,0:T(8,128)(2,1)}), bf16[8,2,128,384]{3,2,1,0:T(8,128)(2,1)S(1)}, u32[]{:S(2)}, u32[]{:S(2)}) async-start(bf16[8,2,128,384]{3,2,1,0:T(8,128)(2,1)} %shard_map.93), calls=%async_computation | async-start | bytes 3145728 | tf_op jit(solution)/shard_map/all_to_all | solution.py:181
  33.1 42.2 %collective-permute-start.1 = (bf16[8,2,128,384]{3,2,1,0:T(8,128)(2,1)S(1)}, bf16[8,2,128,384]{3,2,1,0:T(8,128)(2,1)}, u32[]{:S(2)}, u32[]{:S(2)}) collective-permute-start(bf16[8,2,128,384]{3,2,1,0:T(8,128)(2,1)S(1)} %all-to-all-done.1.ko_ref.vo_ref), channel_id=1, source_target_pairs={{1,0},{2,1},{3,2},{4,3},{5,4},{6,5},{7,6},{8,7},{9,8},{10,9},{11,1... | collective-permute-start | bytes 4718600 | tf_op jit(solution)/shard_map/ppermute | solution.py:30
  41.1 40.5 %collective-permute-start = (bf16[8,2,128,384]{3,2,1,0:T(8,128)(2,1)S(1)}, bf16[8,2,128,384]{3,2,1,0:T(8,128)(2,1)}, u32[]{:S(2)}, u32[]{:S(2)}) collective-permute-start(bf16[8,2,128,384]{3,2,1,0:T(8,128)(2,1)S(1)} %all-to-all-done.1.ko_ref.vo_ref), channel_id=1, source_target_pairs={{0,1},{1,2},{2,3},{3,4},{4,5},{5,6},{6,7},{7,8},{8,9},{9,10},{10,1... | collective-permute-start | bytes 4718600 | tf_op jit(solution)/shard_map/ppermute | solution.py:30
  46.3 1.5 copy-start.9
  54.6 27.1 %copy-start.6 = (bf16[8,2,128,384]{3,2,1,0:T(8,128)(2,1)}, bf16[8,2,128,384]{3,2,1,0:T(8,128)(2,1)S(1)}, u32[]{:S(2)}) copy-start(bf16[8,2,128,384]{3,2,1,0:T(8,128)(2,1)S(1)} %all-to-all-done.qg_ref) | copy-start | bytes 4718596
  116.5 6.5 %copy-start.10 = (bf16[8,1,128,384]{3,2,1,0:T(8,128)(2,1)S(1)}, bf16[8,1,128,384]{3,2,1,0:T(8,128)(2,1)}, u32[]{:S(2)}) copy-start(bf16[8,1,128,384]{3,2,1,0:T(8,128)(2,1)} %get-tuple-element.20) | copy-start | bytes 2359300
  116.5 30.9 %copy-start.8 = (bf16[8,1,128,384]{3,2,1,0:T(8,128)(2,1)S(1)}, bf16[8,1,128,384]{3,2,1,0:T(8,128)(2,1)}, u32[]{:S(2)}) copy-start(bf16[8,1,128,384]{3,2,1,0:T(8,128)(2,1)} %get-tuple-element.18) | copy-start | bytes 2359300
  116.5 32.1 %all-to-all-start.2 = ((bf16[8,2,128,384]{3,2,1,0:T(8,128)(2,1)}), bf16[8,2,128,384]{3,2,1,0:T(8,128)(2,1)S(1)}, u32[]{:S(2)}, u32[]{:S(2)}) async-start(bf16[8,2,128,384]{3,2,1,0:T(8,128)(2,1)} %get-tuple-element.15), calls=%async_computation.2 | async-start | bytes 3145728 | tf_op jit(solution)/shard_map/all_to_all | solution.py:185
  121.1 22.5 %collective-permute-start.2 = (bf16[8,1,128,384]{3,2,1,0:T(8,128)(2,1)}, bf16[8,1,128,384]{3,2,1,0:T(8,128)(2,1)S(1)}, u32[]{:S(2)}, u32[]{:S(2)}) collective-permute-start(bf16[8,1,128,384]{3,2,1,0:T(8,128)(2,1)} %get-tuple-element.19), channel_id=1, source_target_pairs={{1,0},{2,1},{3,2},{4,3},{5,4},{6,5},{7,6},{8,7},{9,8},{10,9},{11,1... | collective-permute-start | bytes 2359304 | tf_op jit(solution)/shard_map/ppermute | solution.py:30
  123.0 24.4 %collective-permute-start.3 = (bf16[8,1,128,384]{3,2,1,0:T(8,128)(2,1)S(1)}, bf16[8,1,128,384]{3,2,1,0:T(8,128)(2,1)S(1)}, u32[]{:S(2)}, u32[]{:S(2)}) collective-permute-start(bf16[8,1,128,384]{3,2,1,0:T(8,128)(2,1)S(1)} %copy-done.10), channel_id=1, source_target_pairs={{0,1},{1,2},{2,3},{3,4},{4,5},{5,6},{6,7},{7,8},{8,9},{9,10},{10,1... | collective-permute-start | bytes 2359304 | tf_op jit(solution)/shard_map/ppermute | solution.py:30
  126.9 33.1 %collective-permute-start.4 = (bf16[8,1,128,384]{3,2,1,0:T(8,128)(2,1)}, bf16[8,1,128,384]{3,2,1,0:T(8,128)(2,1)}, u32[]{:S(2)}, u32[]{:S(2)}) collective-permute-start(bf16[8,1,128,384]{3,2,1,0:T(8,128)(2,1)} %get-tuple-element.22), channel_id=1, source_target_pairs={{1,0},{2,1},{3,2},{4,3},{5,4},{6,5},{7,6},{8,7},{9,8},{10,9},{11,1... | collective-permute-start | bytes 2359304 | tf_op jit(solution)/shard_map/ppermute | solution.py:30
  131.0 32.9 %collective-permute-start.5 = (bf16[8,1,128,384]{3,2,1,0:T(8,128)(2,1)}, bf16[8,1,128,384]{3,2,1,0:T(8,128)(2,1)}, u32[]{:S(2)}, u32[]{:S(2)}) collective-permute-start(bf16[8,1,128,384]{3,2,1,0:T(8,128)(2,1)} %get-tuple-element.23), channel_id=1, source_target_pairs={{0,1},{1,2},{2,3},{3,4},{4,5},{5,6},{6,7},{7,8},{8,9},{9,10},{10,1... | collective-permute-start | bytes 2359304 | tf_op jit(solution)/shard_map/ppermute | solution.py:30
  148.6 15.3 %copy-start.7 = (bf16[8,1,128,384]{3,2,1,0:T(8,128)(2,1)S(1)}, bf16[8,1,128,384]{3,2,1,0:T(8,128)(2,1)}, u32[]{:S(2)}) copy-start(bf16[8,1,128,384]{3,2,1,0:T(8,128)(2,1)} %get-tuple-element.21) | copy-start | bytes 2359300
  148.6 17.8 %copy-start.2 = (bf16[8,2,128,384]{3,2,1,0:T(8,128)(2,1)}, bf16[8,2,128,384]{3,2,1,0:T(8,128)(2,1)S(1)}, u32[]{:S(2)}) copy-start(bf16[8,2,128,384]{3,2,1,0:T(8,128)(2,1)S(1)} %all-to-all-done.2.refs_0_) | copy-start | bytes 4718596
  148.6 18.1 %all-to-all-start.3 = ((bf16[8,1,128,384]{3,2,1,0:T(8,128)(2,1)}), bf16[8,1,128,384]{3,2,1,0:T(8,128)(2,1)S(1)}, u32[]{:S(2)}, u32[]{:S(2)}) async-start(bf16[8,1,128,384]{3,2,1,0:T(8,128)(2,1)} %add_convert_fusion.1), calls=%async_computation.3 | async-start | bytes 1572864 | tf_op jit(solution)/shard_map/all_to_all | solution.py:185
  166.7 6.9 %copy-start.3 = (bf16[8,1,128,384]{3,2,1,0:T(8,128)(2,1)}, bf16[8,1,128,384]{3,2,1,0:T(8,128)(2,1)S(1)}, u32[]{:S(2)}) copy-start(bf16[8,1,128,384]{3,2,1,0:T(8,128)(2,1)S(1)} %all-to-all-done.3.refs_0_) | copy-start | bytes 2359300
  166.7 17.3 %all-to-all-start.4 = ((bf16[8,1,128,384]{3,2,1,0:T(8,128)(2,1)}), bf16[8,1,128,384]{3,2,1,0:T(8,128)(2,1)S(1)}, u32[]{:S(2)}, u32[]{:S(2)}) async-start(bf16[8,1,128,384]{3,2,1,0:T(8,128)(2,1)} %add_convert_fusion), calls=%async_computation.4 | async-start | bytes 1572864 | tf_op jit(solution)/shard_map/all_to_all | solution.py:185
  184.0 0.9 copy-start.4
